TPU v7x, 256 devices: a whole 4x4x8 slice. The times are simulated.
256 devices in a mesh: tm: 16 (over z, x_hi), height: 4 (over x_lo, core), mp: 4 (over y).
Axes of the slice: x: 4 (x_hi: 2, x_lo: 2; x = x_hi * 2 + x_lo), y: 4, z: 8, core: 2. Of those that a mesh axis runs over, the one named last changes fastest.
Arguments:
- image_q: bfloat16 [16, 4, 384, 3072], P('tm', 'height', None, 'mp'), may hold values from -8 to 8
- image_kv: bfloat16 [16, 4, 2, 384, 3072], P('tm', 'height', None, None, 'mp'), may hold values from -8 to 8
- text_kv: bfloat16 [2, 256, 3072], P(None, 'tm', 'mp'), may hold values from -8 to 8
- residual: bfloat16 [16, 4, 384, 3072], P('tm', 'height', None, 'mp'), may hold values from -3 to 3
- out_weight: bfloat16 [3072, 3072], P('mp'), may hold values from -0.109375 to 0.109375
- out_gate: float32 [3072], P('mp'), may hold values from 0.5 to 2
- head_reach: int32 [24, 2], P('mp'), may hold values from 0 to 1, as said below
- tile_extent: int32 [2, 16, 4], replicated, may hold values from 1 to 8, as said below
Outputs:
- updated_tokens: bfloat16 [16, 4, 384, 3072], P('tm', 'height', None, 'mp')
Inputs may be any that keep to these rules, and one draw needn't show every extreme that they name: `head_reach`: in each column exactly 16 heads have reach 1, the others 0. `tile_extent`: valid frames are 6 except in the last tile row along time, where they are below 6; valid rows are 8 except in the last tile row along height, where they are below 8.
All inputs are finite; a program needn't handle non-finite values.
Results may differ from a plain program's by a relative error of at most 0.015.
Values may be sent and summed in bfloat16 or wider, within the bound.
No kernel may reach another device: no remote copies, remote signals or barrier semaphores. Data moves between devices by JAX's collectives and lax.ppermute only.
A program may use at most 128 MiB of HBM per device.

v0:
```python
import math

import jax
import jax.numpy as jnp
from jax import lax
from jax.sharding import PartitionSpec as P

HD = 128
TXT = 256
TILE_F = 6
TILE_R = 8
TILE_C = 8


def with_halo(array, sides, width):
    for axis, dim in sides:
        devices, length = (lax.axis_size(axis), array.shape[dim])
        up = [(i, (i + 1) % devices) for i in range(devices - 1)]
        down = [(j, i) for i, j in up]
        last = lax.slice_in_dim(array, length - width, length, axis=dim)
        leading = lax.slice_in_dim(array, 0, width, axis=dim)
        before = lax.ppermute(last, axis, up)
        after = lax.ppermute(leading, axis, down)
        array = jnp.concatenate([before, array, after], axis=dim)
    return array


def token_masks(extent_pair):
    positions = jnp.arange(TILE_F * TILE_R * TILE_C, dtype=jnp.int32)
    frame_of = positions // (TILE_R * TILE_C)
    row_of = positions // TILE_C % TILE_R
    frame_ok = frame_of < extent_pair[0][..., None]
    row_ok = row_of < extent_pair[1][..., None]
    return jnp.logical_and(frame_ok, row_ok)


def extend_tiles(image_kv):
    return with_halo(image_kv, (("tm", 0), ("height", 1)), 1)


def per_device(image_q, image_kv, text_kv, residual, out_weight, out_gate, head_reach, tile_extent):
    tiles_local = image_q.shape[0]
    tile_len = image_q.shape[2]
    col_width = image_q.shape[3]
    heads_here = col_width // HD
    text_both = lax.all_gather(text_kv, "tm", axis=1, tiled=True)
    extended = extend_tiles(image_kv)
    time_start = lax.axis_index("tm") * tiles_local
    height_start = lax.axis_index("height")
    zero_index = jnp.int32(0)
    padded_ext = jnp.pad(tile_extent, ((0, 0), (1, 1), (1, 1)))
    local_ext = lax.dynamic_slice(
        padded_ext, (zero_index, time_start, height_start), (2, tiles_local + 2, 3)
    )
    key_valid = token_masks(local_ext)
    flat_valid = key_valid[1:-1, 1]
    flat_q = image_q.reshape(tiles_local, tile_len, col_width)
    offsets = jnp.abs(jnp.arange(3, dtype=jnp.int32) - 1)
    scale_factor = 1.0 / math.sqrt(HD)

    def one_tile(tile_index):
        key_rows = jnp.concatenate([extended[:, :, 0].reshape(-1, col_width), text_both[0]], axis=0)
        value_rows = jnp.concatenate(
            [extended[:, :, 1].reshape(-1, col_width), text_both[1]], axis=0
        )
        queries = lax.dynamic_index_in_dim(flat_q, tile_index, 0, keepdims=False)

        def one_head(packed):
            head_id, reaches = packed
            column_start = head_id * HD
            q_head = lax.dynamic_slice_in_dim(queries, column_start, HD, 1)
            k_head = lax.dynamic_slice_in_dim(key_rows, column_start, HD, 1)
            v_head = lax.dynamic_slice_in_dim(value_rows, column_start, HD, 1)
            image_ok = jnp.logical_and(key_valid, offsets[:, None, None] <= reaches[0])
            image_ok = jnp.logical_and(image_ok, offsets[None, :, None] <= reaches[1])
            allowed = jnp.concatenate([image_ok.reshape(-1), jnp.ones((TXT,), jnp.bool_)])
            scores = (
                lax.dot_general(
                    q_head, k_head, (((1,), (1,)), ((), ())), preferred_element_type=jnp.float32
                )
                * scale_factor
            )
            masked = jnp.where(allowed[None, :], scores, -1e30)
            top_score = jnp.max(masked, axis=1, keepdims=True)
            weights = jnp.where(allowed[None, :], jnp.exp(masked - top_score), 0.0)
            row_total = jnp.sum(weights, axis=1, keepdims=True)
            return (
                jnp.dot(weights.astype(jnp.bfloat16), v_head, preferred_element_type=jnp.float32)
                / row_total
            )

        per_head = lax.map(one_head, (jnp.arange(heads_here, dtype=jnp.int32), head_reach))
        joined = jnp.transpose(per_head, (1, 0, 2)).reshape(tile_len, col_width)
        valid_rows = lax.dynamic_index_in_dim(flat_valid, tile_index, 0, keepdims=False)
        return jnp.where(valid_rows[:, None], joined, 0.0).astype(jnp.bfloat16)

    attended = lax.map(one_tile, jnp.arange(tiles_local, dtype=jnp.int32))
    projected = jnp.dot(
        attended.reshape(-1, col_width), out_weight, preferred_element_type=jnp.float32
    )
    summed = lax.psum_scatter(
        projected.reshape(tiles_local, 1, tile_len, -1).astype(jnp.bfloat16),
        "mp",
        scatter_dimension=3,
        tiled=True,
    ).astype(jnp.float32)
    return (residual.astype(jnp.float32) + out_gate * summed).astype(jnp.bfloat16)


def solution(mesh):
    return jax.shard_map(
        per_device,
        mesh=mesh,
        in_specs=(
            P("tm", "height", None, "mp"),
            P("tm", "height", None, None, "mp"),
            P(None, "tm", "mp"),
            P("tm", "height", None, "mp"),
            P("mp", None),
            P("mp"),
            P("mp", None),
            P(),
        ),
        out_specs=P("tm", "height", None, "mp"),
        check_vma=False,
    )
```

profile of v0, /device:TPU:97, one launch (start us, length us, event | category | flops | bytes accessed | tf_op | source)
XLA Modules:
  0.0 286.9 jit_solution(14104560325803142447)
XLA Ops:
  6.5 4.8 %collective-permute-start = (bf16[1,1,2,384,768]{4,3,2,1,0:T(8,128)(2,1)}, bf16[1,1,2,384,768]{4,3,2,1,0:T(8,128)(2,1)S(1)}, u32[]{:S(2)}, u32[]{:S(2)}) collective-permute-start(bf16[1,1,2,384,768]{4,3,2,1,0:T(8,128)(2,1)} %param.11), channel_id=1, source_target_pairs={{0,16},{16,32},{32,48},{48,64},{64,80},{80,96},{96,112},{112,128},... | collective-permute-start | bytes 3538952 | tf_op jit(solution)/shard_map/ppermute | solution.py:22
  11.3 3.0 %collective-permute-start.1 = (bf16[1,1,2,384,768]{4,3,2,1,0:T(8,128)(2,1)}, bf16[1,1,2,384,768]{4,3,2,1,0:T(8,128)(2,1)S(1)}, u32[]{:S(2)}, u32[]{:S(2)}) collective-permute-start(bf16[1,1,2,384,768]{4,3,2,1,0:T(8,128)(2,1)} %param.11), channel_id=1, source_target_pairs={{16,0},{32,16},{48,32},{64,48},{80,64},{96,80},{112,96},{128,112},... | collective-permute-start | bytes 3538952 | tf_op jit(solution)/shard_map/ppermute | solution.py:23
  14.4 47.2 %collective-permute-done = bf16[1,1,2,384,768]{4,3,2,1,0:T(8,128)(2,1)S(1)} collective-permute-done((bf16[1,1,2,384,768]{4,3,2,1,0:T(8,128)(2,1)}, bf16[1,1,2,384,768]{4,3,2,1,0:T(8,128)(2,1)S(1)}, u32[]{:S(2)}, u32[]{:S(2)}) %collective-permute-start) | collective-permute-done | bytes 1179680 | tf_op jit(solution)/shard_map/ppermute | solution.py:22
  61.6 1.4 constant_dynamic-update-slice_fusion.2
  63.0 1.4 collective-permute-done.1
  64.4 3.5 %collective-permute-start.2 = (bf16[3,1,2,384,768]{4,3,2,1,0:T(8,128)(2,1)S(1)}, bf16[3,1,2,384,768]{4,3,2,1,0:T(8,128)(2,1)}, u32[]{:S(2)}, u32[]{:S(2)}) collective-permute-start(bf16[3,1,2,384,768]{4,3,2,1,0:T(8,128)(2,1)S(1)} %constant_dynamic-update-slice_fusion.1), channel_id=1, source_target_pairs={{0,4},{4,8},{8,12},{1,5},{5,9},{9,13},{2,6},{6,10},{10,14},{3,7},{... | collective-permute-start | bytes 10616840 | tf_op jit(solution)/shard_map/ppermute | solution.py:22
  67.9 2.6 collective-permute-start.3
  70.6 0.1 copy.11
  70.7 0.1 copy.12
  70.8 0.6 slice.44
  71.4 0.6 slice.45
  72.0 1.7 and_reduce_fusion
  73.7 71.0 %all_gather.3 = bf16[2,256,768]{2,1,0:T(8,128)(2,1)S(1)} all-gather(bf16[2,16,768]{2,1,0:T(8,128)(2,1)} %param.12), channel_id=1, replica_groups=mesh['tm'=16,'height'=4,'mp'=4] {'tm'}, dimensions={1}, use_global_device_ids=true | all-gather | bytes 835584 | tf_op jit(solution)/shard_map/all_gather | solution.py:46
  144.7 1.0 slice_bitcast_fusion
  145.7 8.2 %pad_maximum_fusion = bf16[3,3,2,384,768]{4,3,2,1,0:T(8,128)(2,1)} fusion(bf16[3,1,2,384,768]{4,3,2,1,0:T(8,128)(2,1)} %collective-permute-done.3, bf16[3,1,2,384,768]{4,3,2,1,0:T(8,128)(2,1)S(1)} %constant_dynamic-update-slice_fusion.1, bf16[3,1,2,384,768]{4,3,2,1,0:T(8,128)(2,1)} %collective-permute-done.2), kind=kLoop, calls=%fused_computation.26 | loop fusion | flops 10616832 | bytes 21233664 | tf_op jit(solution)/shard_map/concatenate | solution.py:24
  153.9 9.0 %fusion.37 = (bf16[3,3,1,384,768]{4,3,2,1,0:T(8,128)(2,1)}, bf16[3,3,1,384,768]{4,3,2,1,0:T(8,128)(2,1)}) fusion(bf16[3,3,2,384,768]{4,3,2,1,0:T(8,128)(2,1)} %pad_maximum_fusion), kind=kLoop, calls=%fused_computation.60 | loop fusion | bytes 21233664 | tf_op jit(solution)/shard_map/while/body/eval_jaxpr/slice | solution.py:64
  162.9 9.5 %pad_maximum_fusion.1 = (bf16[3712,768]{1,0:T(8,128)(2,1)}, bf16[3712,768]{1,0:T(8,128)(2,1)}) fusion(bf16[256,768]{1,0:T(8,128)(2,1)S(1)} %copy-done.1, bf16[3456,768]{1,0:T(8,128)(2,1)} %bitcast.33, bf16[256,768]{1,0:T(8,128)(2,1)S(1)} %copy-done, bf16[3456,768]{1,0:T(8,128)(2,1)} %bitcast.32), kind=kLoop, calls=%fused_computation.27 | loop fusion | flops 22806528 | bytes 22806528 | tf_op jit(solution)/shard_map/while/body/eval_jaxpr/concatenate | solution.py:62
  172.4 54.3 %while.19 = (s32[]{:T(128)}, bf16[6,384,128]{1,2,0:T(8,128)(2,1)S(1)}, s32[6,2]{0,1:T(2,128)S(1)}, s32[6]{0:T(128)S(1)}, bf16[384,768]{1,0:T(8,128)(2,1)}, /*ind...) while((s32[]{:T(128)}, ...), condition=%wide.region_3.4_spmd.clone.clone, body=%wide.region_0.3_spmd.clone.clone.sunk | while | flops 742752384 | bytes 19636056 | solution.py:92
  172.5 0.5 fusion.50
  173.0 1.2 fusion.51
  174.3 0.6 dynamic_slice.60
  175.6 2.4 fusion.53
  178.0 1.2 fusion.54
  179.1 2.2 fusion.55
  181.3 0.1 copy.17
  181.5 0.5 fusion.50
  182.1 1.2 fusion.51
  183.4 0.6 dynamic_slice.60
  184.6 2.4 fusion.53
  187.0 1.2 fusion.54
  188.2 2.2 fusion.55
  190.4 0.1 copy.17
  190.6 0.5 fusion.50
  191.1 1.2 fusion.51
  192.4 0.6 dynamic_slice.60
  193.7 2.4 fusion.53
  196.1 1.2 fusion.54
  197.2 2.2 fusion.55
  199.4 0.1 copy.17
  199.7 0.5 fusion.50
  200.2 1.2 fusion.51
  201.5 0.6 dynamic_slice.60
  202.7 2.4 fusion.53
  205.1 1.2 fusion.54
  206.3 2.2 fusion.55
  208.5 0.1 copy.17
  208.7 0.5 fusion.50
  209.2 1.2 fusion.51
  210.6 0.6 dynamic_slice.60
  211.8 2.4 fusion.53
  214.2 1.2 fusion.54
  215.3 2.2 fusion.55
  217.5 0.1 copy.17
  217.8 0.5 fusion.50
  218.3 1.2 fusion.51
  219.6 0.6 dynamic_slice.60
  220.9 2.4 fusion.53
  223.2 1.2 fusion.54
  224.4 2.2 fusion.55
  226.6 0.1 copy.17
  226.7 0.2 fusion.28
  226.9 5.9 %fusion.27 = bf16[1,1,384,3072]{3,2,1,0:T(8,128)(2,1)} fusion(bf16[384,768]{0,1:T(8,128)(2,1)S(1)} %fusion.28, bf16[768,3072]{1,0:T(8,128)(2,1)} %param.14), kind=kOutput, calls=%fused_computation.30 | convolution fusion | flops 1813118976 | bytes 7667712 | tf_op jit(solution)/shard_map/dot_general | solution.py:98
  232.8 45.2 %reduce-scatter.2.cloned.1.call-done = bf16[1,1,384,768]{3,2,1,0:T(8,128)(2,1)} async-done(((bf16[1,1,384,3072]{3,2,1,0:T(8,128)(2,1)}), bf16[1,1,384,768]{3,2,1,0:T(8,128)(2,1)}) %reduce-scatter.2.cloned.1.call-update) | async-done | bytes 589840 | tf_op jit(solution)/shard_map/reduce_scatter | solution.py:101
  278.0 2.1 add_convert_fusion
  (56 shorter events, 1.6 us)
Async XLA Ops:
  6.5 64.0 %copy-start.6 = (s32[2,16,4]{1,2,0:T(4,128)S(1)}, s32[2,16,4]{1,2,0:T(4,128)}, u32[]{:S(2)}) copy-start(s32[2,16,4]{1,2,0:T(4,128)} %param.17) | copy-start | bytes 1540
  6.5 271.5 %reduce-scatter.2.cloned.1.call-start = ((), (), s32[]{:S(2)}) async-start(), calls=%async_computation.1 | async-start | bytes 2949120 | tf_op jit(solution)/shard_map/reduce_scatter | solution.py:101
  6.5 55.0 %collective-permute-start = (bf16[1,1,2,384,768]{4,3,2,1,0:T(8,128)(2,1)}, bf16[1,1,2,384,768]{4,3,2,1,0:T(8,128)(2,1)S(1)}, u32[]{:S(2)}, u32[]{:S(2)}) collective-permute-start(bf16[1,1,2,384,768]{4,3,2,1,0:T(8,128)(2,1)} %param.11), channel_id=1, source_target_pairs={{0,16},{16,32},{32,48},{48,64},{64,80},{80,96},{96,112},{112,128},... | collective-permute-start | bytes 3538952 | tf_op jit(solution)/shard_map/ppermute | solution.py:22
  11.3 53.0 %collective-permute-start.1 = (bf16[1,1,2,384,768]{4,3,2,1,0:T(8,128)(2,1)}, bf16[1,1,2,384,768]{4,3,2,1,0:T(8,128)(2,1)S(1)}, u32[]{:S(2)}, u32[]{:S(2)}) collective-permute-start(bf16[1,1,2,384,768]{4,3,2,1,0:T(8,128)(2,1)} %param.11), channel_id=1, source_target_pairs={{16,0},{32,16},{48,32},{64,48},{80,64},{96,80},{112,96},{128,112},... | collective-permute-start | bytes 3538952 | tf_op jit(solution)/shard_map/ppermute | solution.py:23
  64.4 81.3 %collective-permute-start.2 = (bf16[3,1,2,384,768]{4,3,2,1,0:T(8,128)(2,1)S(1)}, bf16[3,1,2,384,768]{4,3,2,1,0:T(8,128)(2,1)}, u32[]{:S(2)}, u32[]{:S(2)}) collective-permute-start(bf16[3,1,2,384,768]{4,3,2,1,0:T(8,128)(2,1)S(1)} %constant_dynamic-update-slice_fusion.1), channel_id=1, source_target_pairs={{0,4},{4,8},{8,12},{1,5},{5,9},{9,13},{2,6},{6,10},{10,14},{3,7},{... | collective-permute-start | bytes 10616840 | tf_op jit(solution)/shard_map/ppermute | solution.py:22
  67.9 77.8 %collective-permute-start.3 = (bf16[3,1,2,384,768]{4,3,2,1,0:T(8,128)(2,1)S(1)}, bf16[3,1,2,384,768]{4,3,2,1,0:T(8,128)(2,1)}, u32[]{:S(2)}, u32[]{:S(2)}) collective-permute-start(bf16[3,1,2,384,768]{4,3,2,1,0:T(8,128)(2,1)S(1)} %constant_dynamic-update-slice_fusion.1), channel_id=1, source_target_pairs={{4,0},{8,4},{12,8},{5,1},{9,5},{13,9},{6,2},{10,6},{14,10},{7,3},{... | collective-permute-start | bytes 10616840 | tf_op jit(solution)/shard_map/ppermute | solution.py:23
  153.9 9.0 %copy-start = (bf16[256,768]{1,0:T(8,128)(2,1)S(1)}, bf16[256,768]{1,0:T(8,128)(2,1)}, u32[]{:S(2)}) copy-start(bf16[256,768]{1,0:T(8,128)(2,1)} %get-tuple-element.164) | copy-start | bytes 1179652
  153.9 9.0 %copy-start.1 = (bf16[256,768]{1,0:T(8,128)(2,1)S(1)}, bf16[256,768]{1,0:T(8,128)(2,1)}, u32[]{:S(2)}) copy-start(bf16[256,768]{1,0:T(8,128)(2,1)} %get-tuple-element.165) | copy-start | bytes 1179652
  162.9 9.5 %copy-start.3 = (bf16[6,384,128]{1,2,0:T(8,128)(2,1)S(1)}, bf16[6,384,128]{1,2,0:T(8,128)(2,1)}, u32[]{:S(2)}) copy-start(bf16[6,384,128]{1,2,0:T(8,128)(2,1)} %custom-call.1) | copy-start | bytes 1769476
  162.9 9.5 %copy-start.4 = (s32[6,2]{0,1:T(2,128)S(1)}, s32[6,2]{0,1:T(2,128)}, u32[]{:S(2)}) copy-start(s32[6,2]{0,1:T(2,128)} %param.16) | copy-start | bytes 148
  172.4 54.3 %copy-start.7 = (pred[384]{0:T(512)(128)(4,1)S(1)}, pred[384]{0:T(512)(128)(4,1)}, u32[]{:S(2)}) copy-start(pred[384]{0:T(512)(128)(4,1)} %and_reduce_fusion) | copy-start | bytes 1156
  226.9 51.1 %copy-start.2 = (bf16[1,1,384,768]{3,2,1,0:T(8,128)(2,1)S(1)}, bf16[1,1,384,768]{3,2,1,0:T(8,128)(2,1)}, u32[]{:S(2)}) copy-start(bf16[1,1,384,768]{3,2,1,0:T(8,128)(2,1)} %param.13) | copy-start | bytes 1769476
  226.9 51.1 %copy-start.5 = (f32[768]{0:T(1024)S(1)}, f32[768]{0:T(1024)}, u32[]{:S(2)}) copy-start(f32[768]{0:T(1024)} %param.15) | copy-start | bytes 9220
Sparse Core Ops, SparseCore 0:
  233.0 45.0 reduce-scatter.1
where the time goes:
time: 290 us; the launch traced here: 287 us
  waiting for transfers between devices  93.7 us (32%)
  blocking collectives  71 us (24%)
  other arithmetic  36.3 us (13%)
  matrix products  33.1 us (11%)
  local copies, waits for them, and re-layouts  21.1 us (7%)
  starting transfers between devices  13.9 us (5%)
  between operations  13.5 us (5%)
  loops' own time  4.28 us (1%)
    all_gather x1, blocking collectives, per_device(): text_both = lax.all_gather(text_kv, 'tm', axis=1, tiled=True)  71 us
    ppermute x2, waiting for transfers between devices, with_halo(): before = lax.ppermute(last, axis, up)  47.2 us
    reduce_scatter x1, waiting for transfers between devices, per_device(): lax.psum_scatter(projected.reshape(tiles_local, 1, tile_len, -1).astype(j...  45.2 us
    dot_general x6, matrix products, one_head(): lax.dot_general(q_head, k_head, (((1,), (1,)), ((), ())), preferred_eleme...  14.3 us
    dot_general x6, matrix products, one_head(): jnp.dot(weights.astype(jnp.bfloat16), v_head, preferred_element_type=jnp....  12.9 us
    concatenate x1, other arithmetic, one_tile(): jnp.concatenate([extended[:, :, 0].reshape(-1, col_width), text_both[0]],...  9.48 us
    slice x1, local copies, waits for them, and re-layouts, one_tile(): extended[:, :, 1].reshape(-1, col_width)  8.97 us
    ppermute x2, starting transfers between devices, with_halo(): before = lax.ppermute(last, axis, up)  8.27 us
  transfers between devices with their start and end apart: 5, of which 3 were waited for; matrix products, arithmetic and copies ran while one was open for 2% of the time, Pallas kernels for 0%

commit v1 on v0

v1 whole, which is shorter than its diff:
```python
import math

import jax
import jax.numpy as jnp
from jax import lax
from jax.experimental import pallas as pl
from jax.experimental.pallas import tpu as pltpu
from jax.sharding import PartitionSpec as P

HD = 128
TXT = 256
TILE_F = 6
TILE_R = 8
TILE_C = 8
NEG = -1e30


def token_masks(extent_pair):
    positions = jnp.arange(TILE_F * TILE_R * TILE_C, dtype=jnp.int32)
    frame_of = positions // (TILE_R * TILE_C)
    row_of = positions // TILE_C % TILE_R
    frame_ok = frame_of < extent_pair[0][..., None]
    row_ok = row_of < extent_pair[1][..., None]
    return jnp.logical_and(frame_ok, row_ok)


def shift_pairs(devices, step):
    return [(i, i + step) for i in range(devices) if 0 <= i + step < devices]


def attention_kernel(reach_ref, q_ref, text_ref, *rest):
    tile_refs = rest[:9]
    bias_ref, qvalid_ref, o_ref, m_ref, l_ref, acc_ref = rest[9:]
    head = pl.program_id(0)
    scale = 1.0 / math.sqrt(HD)
    q = q_ref[...]
    dims = (((1,), (1,)), ((), ()))
    s = lax.dot_general(q, text_ref[0], dims, preferred_element_type=jnp.float32) * scale
    m = jnp.max(s, axis=1, keepdims=True)
    p = jnp.exp(s - m)
    m_ref[...] = m
    l_ref[...] = jnp.sum(p, axis=1, keepdims=True)
    acc_ref[...] = jnp.dot(p.astype(jnp.bfloat16), text_ref[1], preferred_element_type=jnp.float32)
    reach_t = reach_ref[head, 0]
    reach_h = reach_ref[head, 1]
    for b in range(9):
        off_t, off_h = abs(b // 3 - 1), abs(b % 3 - 1)
        tile_ref = tile_refs[b]

        def block(tile_ref=tile_ref, b=b):
            s = lax.dot_general(q, tile_ref[0], dims, preferred_element_type=jnp.float32)
            s = s * scale + bias_ref[b]
            m_old = m_ref[...]
            m_new = jnp.maximum(m_old, jnp.max(s, axis=1, keepdims=True))
            alpha = jnp.exp(m_old - m_new)
            p = jnp.exp(s - m_new)
            l_ref[...] = alpha * l_ref[...] + jnp.sum(p, axis=1, keepdims=True)
            acc_ref[...] = alpha * acc_ref[...] + jnp.dot(
                p.astype(jnp.bfloat16), tile_ref[1], preferred_element_type=jnp.float32
            )
            m_ref[...] = m_new

        if off_t == 0 and off_h == 0:
            block()
        else:
            pl.when(jnp.logical_and(reach_t >= off_t, reach_h >= off_h))(block)
    out = acc_ref[...] / l_ref[...]
    out = jnp.where(qvalid_ref[...] > 0, out, 0.0)
    o_ref[...] = out.astype(o_ref.dtype)


def attend(reach, queries, text, tiles, bias, qvalid):
    tile_len, col_width = queries.shape
    heads = col_width // HD
    tile_specs = []
    tile_args = []
    for array, index in tiles:
        if index is None:
            tile_specs.append(pl.BlockSpec((2, tile_len, HD), lambda h, r: (0, 0, h)))
        else:
            tile_specs.append(
                pl.BlockSpec((None, 2, tile_len, HD), lambda h, r, i=index: (i, 0, 0, h))
            )
        tile_args.append(array)
    grid_spec = pltpu.PrefetchScalarGridSpec(
        num_scalar_prefetch=1,
        grid=(heads,),
        in_specs=[
            pl.BlockSpec((tile_len, HD), lambda h, r: (0, h)),
            pl.BlockSpec((2, text.shape[1], HD), lambda h, r: (0, 0, h)),
            *tile_specs,
            pl.BlockSpec(bias.shape, lambda h, r: (0, 0, 0)),
            pl.BlockSpec(qvalid.shape, lambda h, r: (0, 0)),
        ],
        out_specs=pl.BlockSpec((tile_len, HD), lambda h, r: (0, h)),
        scratch_shapes=[
            pltpu.VMEM((tile_len, 1), jnp.float32),
            pltpu.VMEM((tile_len, 1), jnp.float32),
            pltpu.VMEM((tile_len, HD), jnp.float32),
        ],
    )
    return pl.pallas_call(
        attention_kernel,
        grid_spec=grid_spec,
        out_shape=jax.ShapeDtypeStruct((tile_len, col_width), jnp.bfloat16),
    )(reach, queries, text, *tile_args, bias, qvalid)


def per_device(image_q, image_kv, text_kv, residual, out_weight, out_gate, head_reach, tile_extent):
    tile_len = image_q.shape[2]
    col_width = image_q.shape[3]
    tm_size = lax.axis_size("tm")
    height_size = lax.axis_size("height")
    mp_size = lax.axis_size("mp")

    gathered = lax.all_gather(text_kv, "tm", axis=0)
    text = jnp.transpose(gathered, (1, 0, 2, 3)).reshape(2, -1, col_width)

    own = image_kv[0, 0]
    t_before = lax.ppermute(own, "tm", shift_pairs(tm_size, 1))
    t_after = lax.ppermute(own, "tm", shift_pairs(tm_size, -1))
    h_before = lax.ppermute(own, "height", shift_pairs(height_size, 1))
    h_after = lax.ppermute(own, "height", shift_pairs(height_size, -1))
    time_pair = jnp.stack([t_before, t_after])
    c_before = lax.ppermute(time_pair, "height", shift_pairs(height_size, 1))
    c_after = lax.ppermute(time_pair, "height", shift_pairs(height_size, -1))
    tiles = [
        (c_before, 0), (t_before, None), (c_after, 0),
        (h_before, None), (own, None), (h_after, None),
        (c_before, 1), (t_after, None), (c_after, 1),
    ]

    time_start = lax.axis_index("tm")
    height_start = lax.axis_index("height")
    zero_index = jnp.int32(0)
    padded_ext = jnp.pad(tile_extent, ((0, 0), (1, 1), (1, 1)))
    local_ext = lax.dynamic_slice(padded_ext, (zero_index, time_start, height_start), (2, 3, 3))
    key_valid = token_masks(local_ext)
    bias = jnp.where(key_valid, 0.0, NEG).astype(jnp.float32).reshape(9, 1, tile_len)
    qvalid = key_valid[1, 1].astype(jnp.float32).reshape(tile_len, 1)

    attended = attend(head_reach, image_q[0, 0], text, tiles, bias, qvalid)

    mp_index = lax.axis_index("mp")
    chunk = out_weight.shape[1] // mp_size
    received = []
    for step in (2, 1, 3):
        target = (mp_index + step) % mp_size
        w_part = lax.dynamic_slice_in_dim(out_weight, target * chunk, chunk, 1)
        part = jnp.dot(attended, w_part, preferred_element_type=jnp.float32).astype(jnp.bfloat16)
        pairs = [(i, (i + step) % mp_size) for i in range(mp_size)]
        received.append(lax.ppermute(part, "mp", pairs))
    w_own = lax.dynamic_slice_in_dim(out_weight, mp_index * chunk, chunk, 1)
    branch = jnp.dot(attended, w_own, preferred_element_type=jnp.float32).astype(jnp.bfloat16)
    branch = branch.astype(jnp.float32)
    for part in received:
        branch = branch + part.astype(jnp.float32)
    updated = residual[0, 0].astype(jnp.float32) + out_gate * branch
    return updated.astype(jnp.bfloat16)[None, None]


def solution(mesh):
    return jax.shard_map(
        per_device,
        mesh=mesh,
        in_specs=(
            P("tm", "height", None, "mp"),
            P("tm", "height", None, None, "mp"),
            P(None, "tm", "mp"),
            P("tm", "height", None, "mp"),
            P("mp", None),
            P("mp"),
            P("mp", None),
            P(),
        ),
        out_specs=P("tm", "height", None, "mp"),
        check_vma=False,
    )
```

time: 290 us -> 231 us (0.80)
  the two profiles are of different devices: /device:TPU:97 before, /device:TPU:2 now
where the time goes in v1:
time: 231 us; the launch traced here: 230 us
  blocking collectives  83.8 us (36%)
  waiting for transfers between devices  61.7 us (27%)
  Pallas kernels  35.2 us (15%)
  starting transfers between devices  27.8 us (12%)
  matrix products  10.5 us (5%)
  local copies, waits for them, and re-layouts  6.49 us (3%)
  other arithmetic  4.36 us (2%)
    all_gather x1, blocking collectives, per_device(): gathered = lax.all_gather(text_kv, 'tm', axis=0)  83.8 us
    pallas_call x1, Pallas kernels, attend(): pl.pallas_call(attention_kernel, grid_spec=grid_spec, out_shape=jax.Shape...  35.2 us
    ppermute x1, waiting for transfers between devices, per_device(): t_before = lax.ppermute(own, 'tm', shift_pairs(tm_size, 1))  24.4 us
    ppermute x1, waiting for transfers between devices, per_device(): t_after = lax.ppermute(own, 'tm', shift_pairs(tm_size, -1))  23.9 us
    ppermute x3, waiting for transfers between devices, per_device(): received.append(lax.ppermute(part, 'mp', pairs))  13.4 us
    ppermute x3, starting transfers between devices, per_device(): received.append(lax.ppermute(part, 'mp', pairs))  9.28 us
    dot_general x3, matrix products, per_device(): jnp.dot(attended, w_part, preferred_element_type=jnp.float32)  7.64 us
    ppermute x1, starting transfers between devices, per_device(): t_before = lax.ppermute(own, 'tm', shift_pairs(tm_size, 1))  6.13 us
  transfers between devices with their start and end apart: 9, of which 4 were waited for; matrix products, arithmetic and copies ran while one was open for 6% of the time, Pallas kernels for 0%

profile of v1, /device:TPU:2, one launch (start us, length us, event | category | flops | bytes accessed | tf_op | source)
XLA Modules:
  0.0 230.1 jit_solution(15769469923383473045)
XLA Ops:
  0.0 1.3 collective-permute-start.1
  1.3 6.1 %collective-permute-start = (bf16[2,384,768]{2,1,0:T(8,128)(2,1)}, bf16[2,384,768]{2,1,0:T(8,128)(2,1)S(1)}, u32[]{:S(2)}, u32[]{:S(2)}) collective-permute-start(bf16[2,384,768]{2,1,0:T(8,128)(2,1)} %bitcast.5.rest_4_), channel_id=1, source_target_pairs={{0,16},{16,32},{32,48},{48,64},{64,80},{80,96},{96,112},{112,128},... | collective-permute-start | bytes 3538952 | tf_op jit(solution)/shard_map/ppermute | solution.py:120
  7.4 23.9 %collective-permute-done.1.rest_7_ = bf16[2,384,768]{2,1,0:T(8,128)(2,1)S(1)} collective-permute-done((bf16[2,384,768]{2,1,0:T(8,128)(2,1)}, bf16[2,384,768]{2,1,0:T(8,128)(2,1)S(1)}, u32[]{:S(2)}, u32[]{:S(2)}) %collective-permute-start.1) | collective-permute-done | bytes 1179680 | tf_op jit(solution)/shard_map/ppermute | solution.py:121
  31.3 0.0 copy-start.1
  31.3 24.4 %collective-permute-done.rest_1_ = bf16[2,384,768]{2,1,0:T(8,128)(2,1)S(1)} collective-permute-done((bf16[2,384,768]{2,1,0:T(8,128)(2,1)}, bf16[2,384,768]{2,1,0:T(8,128)(2,1)S(1)}, u32[]{:S(2)}, u32[]{:S(2)}) %collective-permute-start) | collective-permute-done | bytes 1179680 | tf_op jit(solution)/shard_map/ppermute | solution.py:120
  55.7 0.0 copy-start.2
  55.7 0.0 copy-start.6
  55.7 1.8 pad_maximum_fusion
  57.5 0.0 copy-done.1
  57.5 0.0 copy-done.2
  57.5 1.9 collective-permute-start.2
  59.4 3.6 %collective-permute-start.3 = (bf16[2,2,384,768]{3,2,1,0:T(8,128)(2,1)}, bf16[2,2,384,768]{3,2,1,0:T(8,128)(2,1)}, u32[]{:S(2)}, u32[]{:S(2)}) collective-permute-start(bf16[2,2,384,768]{3,2,1,0:T(8,128)(2,1)} %pad_maximum_fusion), channel_id=1, source_target_pairs={{4,0},{8,4},{12,8},{5,1},{9,5},{13,9},{6,2},{10,6},{14,10},{7,3},{... | collective-permute-start | bytes 7077896 | tf_op jit(solution)/shard_map/ppermute | solution.py:126
  63.1 2.1 collective-permute-start.4
  65.2 3.5 %collective-permute-start.5 = (bf16[2,384,768]{2,1,0:T(8,128)(2,1)}, bf16[2,384,768]{2,1,0:T(8,128)(2,1)}, u32[]{:S(2)}, u32[]{:S(2)}) collective-permute-start(bf16[2,384,768]{2,1,0:T(8,128)(2,1)} %bitcast.5.rest_4_), channel_id=1, source_target_pairs={{4,0},{8,4},{12,8},{5,1},{9,5},{13,9},{6,2},{10,6},{14,10},{7,3},{... | collective-permute-start | bytes 3538952 | tf_op jit(solution)/shard_map/ppermute | solution.py:123
  68.7 0.0 copy-done.6
  68.7 0.7 copy.27.reach_ref
  69.4 0.0 copy-start.5
  69.4 83.8 %all-gather = bf16[32,16,768]{2,1,0:T(8,128)(2,1)S(1)} all-gather(bf16[2,16,768]{2,1,0:T(8,128)(2,1)} %param.10), channel_id=2, replica_groups=mesh['tm'=16,'height'=4,'mp'=4] {'tm'}, dimensions={0}, use_global_device_ids=true | all-gather | bytes 835584 | tf_op jit(solution)/shard_map/all_gather | solution.py:116
  153.2 1.0 copy.22
  154.1 0.0 copy-done.5
  154.1 0.1 pad_dynamic-slice_fusion
  154.2 0.1 copy.24
  154.3 0.1 lt.108
  154.4 0.1 copy.23
  154.5 0.6 lt.103
  155.1 0.7 slice.13
  155.7 0.6 slice.12
  156.3 1.3 fusion.18
  157.6 0.8 copy.28.rest_10_
  158.4 1.3 and_select_fusion.rest_9_
  159.8 0.0 collective-permute-done.4.rest_3_
  159.8 0.0 copy-start.3
  159.8 0.0 collective-permute-done.5.rest_5_
  159.8 0.0 collective-permute-done.2.rest_0_.rest_6_
  159.8 0.0 copy-start
  159.8 0.0 collective-permute-done.3.rest_2_.rest_8_
  159.8 1.0 copy-done.3
  160.8 0.8 copy-done
  161.6 35.2 %shard_map.82 = bf16[384,768]{1,0:T(8,128)(2,1)} custom-call(s32[6,2]{1,0:T(8,128)} %copy.27.reach_ref, bf16[384,768]{1,0:T(8,128)(2,1)} %bitcast.25, bf16[2,256,768]{2,1,0:T(8,128)(2,1)} %bitcast.23, bf16[2,2,384,768]{3,2,1,0:T(8,128)(2,1)} %copy-done, bf16[2,384,768]{2,1,0:T(8,128)(2,1)} %copy-done.2, ...), custom_call_target="tpu_custom_call" | custom-call | tf_op jit(solution)/shard_map/pallas_call | solution.py:102
  196.8 0.0 copy-start.4
  196.8 2.1 convolution_convert_fusion
  199.0 7.9 %collective-permute-start.8 = (bf16[384,768]{1,0:T(8,128)(2,1)S(1)}, bf16[384,768]{1,0:T(8,128)(2,1)S(1)}, u32[]{:S(2)}, u32[]{:S(2)}) collective-permute-start(bf16[384,768]{1,0:T(8,128)(2,1)S(1)} %convolution_convert_fusion), channel_id=1, source_target_pairs={{0,3},{1,0},{2,1},{3,2},{4,7},{5,4},{6,5},{7,6},{8,11},{9,8},{10,9... | collective-permute-start | bytes 1769480 | tf_op jit(solution)/shard_map/ppermute | solution.py:152
  206.8 0.0 copy-done.4
  206.8 2.7 %convolution_convert_fusion.1 = bf16[384,768]{1,0:T(8,128)(2,1)} fusion(bf16[384,768]{1,0:T(8,128)(2,1)S(1)} %copy-done.4, bf16[768,3072]{1,0:T(8,128)(2,1)} %param.12, s32[]{:T(128)S(6)} %select_n.86), kind=kOutput, calls=%fused_computation.2 | convolution fusion | flops 453279744 | bytes 2359300 | tf_op jit(solution)/shard_map/dot_general | solution.py:150
  209.6 0.0 copy-start.7
  209.6 0.0 copy-start.8
  209.6 0.0 collective-permute-start.7
  209.6 2.8 %convolution_convert_fusion.2 = bf16[384,768]{1,0:T(8,128)(2,1)} fusion(bf16[384,768]{1,0:T(8,128)(2,1)S(1)} %copy-done.4, bf16[768,3072]{1,0:T(8,128)(2,1)} %param.12, s32[]{:T(128)S(6)} %select_n.84), kind=kOutput, calls=%fused_computation.3 | convolution fusion | flops 453279744 | bytes 2359300 | tf_op jit(solution)/shard_map/dot_general | solution.py:150
  212.3 1.4 collective-permute-start.6
  213.8 0.5 collective-permute-done.8
  214.2 12.9 %collective-permute-done.7 = bf16[384,768]{1,0:T(8,128)(2,1)S(1)} collective-permute-done((bf16[384,768]{1,0:T(8,128)(2,1)}, bf16[384,768]{1,0:T(8,128)(2,1)S(1)}, u32[]{:S(2)}, u32[]{:S(2)}) %collective-permute-start.7) | collective-permute-done | bytes 589856 | tf_op jit(solution)/shard_map/ppermute | solution.py:152
  227.2 0.0 collective-permute-done.6
  227.2 0.0 copy-done.7
  227.2 0.0 copy-done.8
  227.2 2.9 %fusion.7 = bf16[1,1,384,768]{3,2,1,0:T(8,128)(2,1)} fusion(bf16[384,768]{1,0:T(8,128)(2,1)S(1)} %copy-done.4, bf16[384,768]{1,0:T(8,128)(2,1)S(1)} %collective-permute-done.8, bf16[384,768]{1,0:T(8,128)(2,1)S(1)} %collective-permute-done.7, bf16[384,768]{1,0:T(8,128)(2,1)S(1)} %collective-permute-done.6, bf16[768,3072]{1,0:T(8,128)(2,1)} %param.12, ...), kind=kOutput, calls=%fused_computation.12 | convolution fusion | flops 456523776 | bytes 4721668 | tf_op jit(solution)/shard_map/dot_general | solution.py:154
  (1 shorter events, 0.0 us)
Async XLA Ops:
  0.0 31.3 %collective-permute-start.1 = (bf16[2,384,768]{2,1,0:T(8,128)(2,1)}, bf16[2,384,768]{2,1,0:T(8,128)(2,1)S(1)}, u32[]{:S(2)}, u32[]{:S(2)}) collective-permute-start(bf16[2,384,768]{2,1,0:T(8,128)(2,1)} %bitcast.5.rest_4_), channel_id=1, source_target_pairs={{16,0},{32,16},{48,32},{64,48},{80,64},{96,80},{112,96},{128,112},... | collective-permute-start | bytes 3538952 | tf_op jit(solution)/shard_map/ppermute | solution.py:121
  1.3 54.4 %collective-permute-start = (bf16[2,384,768]{2,1,0:T(8,128)(2,1)}, bf16[2,384,768]{2,1,0:T(8,128)(2,1)S(1)}, u32[]{:S(2)}, u32[]{:S(2)}) collective-permute-start(bf16[2,384,768]{2,1,0:T(8,128)(2,1)} %bitcast.5.rest_4_), channel_id=1, source_target_pairs={{0,16},{16,32},{32,48},{48,64},{64,80},{80,96},{96,112},{112,128},... | collective-permute-start | bytes 3538952 | tf_op jit(solution)/shard_map/ppermute | solution.py:120
  31.3 26.2 %copy-start.1 = (bf16[2,384,768]{2,1,0:T(8,128)(2,1)}, bf16[2,384,768]{2,1,0:T(8,128)(2,1)S(1)}, u32[]{:S(2)}) copy-start(bf16[2,384,768]{2,1,0:T(8,128)(2,1)S(1)} %collective-permute-done.1.rest_7_) | copy-start | bytes 3538948
  55.7 1.8 copy-start.2
  55.7 13.0 %copy-start.6 = (s32[6,2]{0,1:T(2,128)S(1)}, s32[6,2]{0,1:T(2,128)}, u32[]{:S(2)}) copy-start(s32[6,2]{0,1:T(2,128)} %param.14) | copy-start | bytes 148
  57.5 102.3 %collective-permute-start.2 = (bf16[2,2,384,768]{3,2,1,0:T(8,128)(2,1)}, bf16[2,2,384,768]{3,2,1,0:T(8,128)(2,1)S(1)}, u32[]{:S(2)}, u32[]{:S(2)}) collective-permute-start(bf16[2,2,384,768]{3,2,1,0:T(8,128)(2,1)} %pad_maximum_fusion), channel_id=1, source_target_pairs={{0,4},{4,8},{8,12},{1,5},{5,9},{9,13},{2,6},{6,10},{10,14},{3,7},{... | collective-permute-start | bytes 7077896 | tf_op jit(solution)/shard_map/ppermute | solution.py:125
  59.4 100.4 %collective-permute-start.3 = (bf16[2,2,384,768]{3,2,1,0:T(8,128)(2,1)}, bf16[2,2,384,768]{3,2,1,0:T(8,128)(2,1)}, u32[]{:S(2)}, u32[]{:S(2)}) collective-permute-start(bf16[2,2,384,768]{3,2,1,0:T(8,128)(2,1)} %pad_maximum_fusion), channel_id=1, source_target_pairs={{4,0},{8,4},{12,8},{5,1},{9,5},{13,9},{6,2},{10,6},{14,10},{7,3},{... | collective-permute-start | bytes 7077896 | tf_op jit(solution)/shard_map/ppermute | solution.py:126
  63.1 96.7 %collective-permute-start.4 = (bf16[2,384,768]{2,1,0:T(8,128)(2,1)}, bf16[2,384,768]{2,1,0:T(8,128)(2,1)S(1)}, u32[]{:S(2)}, u32[]{:S(2)}) collective-permute-start(bf16[2,384,768]{2,1,0:T(8,128)(2,1)} %bitcast.5.rest_4_), channel_id=1, source_target_pairs={{0,4},{4,8},{8,12},{1,5},{5,9},{9,13},{2,6},{6,10},{10,14},{3,7},{... | collective-permute-start | bytes 3538952 | tf_op jit(solution)/shard_map/ppermute | solution.py:122
  65.2 94.6 %collective-permute-start.5 = (bf16[2,384,768]{2,1,0:T(8,128)(2,1)}, bf16[2,384,768]{2,1,0:T(8,128)(2,1)}, u32[]{:S(2)}, u32[]{:S(2)}) collective-permute-start(bf16[2,384,768]{2,1,0:T(8,128)(2,1)} %bitcast.5.rest_4_), channel_id=1, source_target_pairs={{4,0},{8,4},{12,8},{5,1},{9,5},{13,9},{6,2},{10,6},{14,10},{7,3},{... | collective-permute-start | bytes 3538952 | tf_op jit(solution)/shard_map/ppermute | solution.py:123
  69.4 84.7 %copy-start.5 = (s32[2,16,4]{1,2,0:T(4,128)S(1)}, s32[2,16,4]{1,2,0:T(4,128)}, u32[]{:S(2)}) copy-start(s32[2,16,4]{1,2,0:T(4,128)} %param.15) | copy-start | bytes 1540
  159.8 1.0 copy-start.3
  159.8 1.8 copy-start
  196.8 10.0 %copy-start.4 = (bf16[384,768]{1,0:T(8,128)(2,1)S(1)}, bf16[384,768]{1,0:T(8,128)(2,1)}, u32[]{:S(2)}) copy-start(bf16[384,768]{1,0:T(8,128)(2,1)} %shard_map.82) | copy-start | bytes 1769476
  199.0 15.3 %collective-permute-start.8 = (bf16[384,768]{1,0:T(8,128)(2,1)S(1)}, bf16[384,768]{1,0:T(8,128)(2,1)S(1)}, u32[]{:S(2)}, u32[]{:S(2)}) collective-permute-start(bf16[384,768]{1,0:T(8,128)(2,1)S(1)} %convolution_convert_fusion), channel_id=1, source_target_pairs={{0,3},{1,0},{2,1},{3,2},{4,7},{5,4},{6,5},{7,6},{8,11},{9,8},{10,9... | collective-permute-start | bytes 1769480 | tf_op jit(solution)/shard_map/ppermute | solution.py:152
  209.6 17.6 %copy-start.7 = (bf16[1,1,384,768]{3,2,1,0:T(8,128)(2,1)S(1)}, bf16[1,1,384,768]{3,2,1,0:T(8,128)(2,1)}, u32[]{:S(2)}) copy-start(bf16[1,1,384,768]{3,2,1,0:T(8,128)(2,1)} %param.11) | copy-start | bytes 1769476
  209.6 17.6 %copy-start.8 = (f32[768]{0:T(1024)S(1)}, f32[768]{0:T(1024)}, u32[]{:S(2)}) copy-start(f32[768]{0:T(1024)} %param.13) | copy-start | bytes 9220
  209.6 17.6 %collective-permute-start.7 = (bf16[384,768]{1,0:T(8,128)(2,1)}, bf16[384,768]{1,0:T(8,128)(2,1)S(1)}, u32[]{:S(2)}, u32[]{:S(2)}) collective-permute-start(bf16[384,768]{1,0:T(8,128)(2,1)} %convolution_convert_fusion.1), channel_id=1, source_target_pairs={{0,1},{1,2},{2,3},{3,0},{4,5},{5,6},{6,7},{7,4},{8,9},{9,10},{10,1... | collective-permute-start | bytes 1769480 | tf_op jit(solution)/shard_map/ppermute | solution.py:152
  212.3 14.8 %collective-permute-start.6 = (bf16[384,768]{1,0:T(8,128)(2,1)}, bf16[384,768]{1,0:T(8,128)(2,1)S(1)}, u32[]{:S(2)}, u32[]{:S(2)}) collective-permute-start(bf16[384,768]{1,0:T(8,128)(2,1)} %convolution_convert_fusion.2), channel_id=1, source_target_pairs={{0,2},{1,3},{2,0},{3,1},{4,6},{5,7},{6,4},{7,5},{8,10},{9,11},{10,... | collective-permute-start | bytes 1769480 | tf_op jit(solution)/shard_map/ppermute | solution.py:152

commit v2 on v1

v2 whole, which is shorter than its diff:
```python
import math

import jax
import jax.numpy as jnp
from jax import lax
from jax.experimental import pallas as pl
from jax.experimental.pallas import tpu as pltpu
from jax.sharding import PartitionSpec as P

HD = 128
TXT = 256
TILE_F = 6
TILE_R = 8
TILE_C = 8
NEG = -1e30


def token_masks(extent_pair):
    positions = jnp.arange(TILE_F * TILE_R * TILE_C, dtype=jnp.int32)
    frame_of = positions // (TILE_R * TILE_C)
    row_of = positions // TILE_C % TILE_R
    frame_ok = frame_of < extent_pair[0][..., None]
    row_ok = row_of < extent_pair[1][..., None]
    return jnp.logical_and(frame_ok, row_ok)


def shift_pairs(devices, step):
    return [(i, i + step) for i in range(devices) if 0 <= i + step < devices]


def gather_text(text_kv, devices):
    position = lax.axis_index("tm")
    gathered = text_kv
    step = 1
    while step < devices:
        other = lax.ppermute(gathered, "tm", [(i, i ^ step) for i in range(devices)])
        low_first = jnp.concatenate([gathered, other], axis=1)
        high_first = jnp.concatenate([other, gathered], axis=1)
        gathered = jnp.where((position & step) == 0, low_first, high_first)
        step *= 2
    return gathered


def make_kernel(blocks, has_text, has_state, final):
    count = len(blocks)

    def kernel(reach_ref, q_ref, *rest):
        rest = list(rest)
        text_ref = rest.pop(0) if has_text else None
        tile_refs = rest[:count]
        rest = rest[count:]
        bias_ref = rest.pop(0)
        if has_state:
            m_in, l_in, acc_in = rest[:3]
            rest = rest[3:]
        if final:
            qvalid_ref = rest.pop(0)
            o_ref = rest.pop(0)
        else:
            m_out, l_out, acc_out = rest[:3]
            rest = rest[3:]
        m_ref, l_ref, acc_ref = rest
        head = pl.program_id(0)
        scale = 1.0 / math.sqrt(HD)
        q = q_ref[...]
        dims = (((1,), (1,)), ((), ()))
        if has_state:
            m_ref[...] = m_in[...]
            l_ref[...] = l_in[...]
            acc_ref[...] = acc_in[...]
        else:
            m_ref[...] = jnp.full(m_ref.shape, NEG, jnp.float32)
            l_ref[...] = jnp.zeros(l_ref.shape, jnp.float32)
            acc_ref[...] = jnp.zeros(acc_ref.shape, jnp.float32)
        if has_text:
            s = lax.dot_general(q, text_ref[0], dims, preferred_element_type=jnp.float32) * scale
            m_old = m_ref[...]
            m_new = jnp.maximum(m_old, jnp.max(s, axis=1, keepdims=True))
            alpha = jnp.exp(m_old - m_new)
            p = jnp.exp(s - m_new)
            l_ref[...] = alpha * l_ref[...] + jnp.sum(p, axis=1, keepdims=True)
            acc_ref[...] = alpha * acc_ref[...] + jnp.dot(
                p.astype(jnp.bfloat16), text_ref[1], preferred_element_type=jnp.float32
            )
            m_ref[...] = m_new
        reach_t = reach_ref[head, 0]
        reach_h = reach_ref[head, 1]
        for tile_ref, b in zip(tile_refs, blocks):
            off_t, off_h = abs(b // 3 - 1), abs(b % 3 - 1)

            def block(tile_ref=tile_ref, b=b):
                s = lax.dot_general(q, tile_ref[0], dims, preferred_element_type=jnp.float32)
                s = s * scale + bias_ref[b]
                m_old = m_ref[...]
                m_new = jnp.maximum(m_old, jnp.max(s, axis=1, keepdims=True))
                alpha = jnp.exp(m_old - m_new)
                p = jnp.exp(s - m_new)
                l_ref[...] = alpha * l_ref[...] + jnp.sum(p, axis=1, keepdims=True)
                acc_ref[...] = alpha * acc_ref[...] + jnp.dot(
                    p.astype(jnp.bfloat16), tile_ref[1], preferred_element_type=jnp.float32
                )
                m_ref[...] = m_new

            if off_t == 0 and off_h == 0:
                block()
            else:
                pl.when(jnp.logical_and(reach_t >= off_t, reach_h >= off_h))(block)
        if final:
            out = acc_ref[...] / l_ref[...]
            out = jnp.where(qvalid_ref[...] > 0, out, 0.0)
            o_ref[...] = out.astype(o_ref.dtype)
        else:
            m_out[...] = m_ref[...]
            l_out[...] = l_ref[...]
            acc_out[...] = acc_ref[...]

    return kernel


def attend(reach, queries, text, tiles, bias, state=None, qvalid=None):
    tile_len, col_width = queries.shape
    heads = col_width // HD
    blocks = [b for _, _, b in tiles]
    specs = [pl.BlockSpec((tile_len, HD), lambda h, r: (0, h))]
    args = [queries]
    if text is not None:
        specs.append(pl.BlockSpec((2, text.shape[1], HD), lambda h, r: (0, 0, h)))
        args.append(text)
    for array, index, _ in tiles:
        if index is None:
            specs.append(pl.BlockSpec((2, tile_len, HD), lambda h, r: (0, 0, h)))
        else:
            specs.append(
                pl.BlockSpec((None, 2, tile_len, HD), lambda h, r, i=index: (i, 0, 0, h))
            )
        args.append(array)
    specs.append(pl.BlockSpec(bias.shape, lambda h, r: (0, 0, 0)))
    args.append(bias)
    row_spec = pl.BlockSpec((None, tile_len, 1), lambda h, r: (h, 0, 0))
    acc_spec = pl.BlockSpec((tile_len, HD), lambda h, r: (0, h))
    if state is not None:
        specs += [row_spec, row_spec, acc_spec]
        args += list(state)
    final = qvalid is not None
    if final:
        specs.append(pl.BlockSpec(qvalid.shape, lambda h, r: (0, 0)))
        args.append(qvalid)
        out_specs = pl.BlockSpec((tile_len, HD), lambda h, r: (0, h))
        out_shape = jax.ShapeDtypeStruct((tile_len, col_width), jnp.bfloat16)
    else:
        out_specs = [row_spec, row_spec, acc_spec]
        row_shape = jax.ShapeDtypeStruct((heads, tile_len, 1), jnp.float32)
        out_shape = [row_shape, row_shape, jax.ShapeDtypeStruct((tile_len, col_width), jnp.float32)]
    grid_spec = pltpu.PrefetchScalarGridSpec(
        num_scalar_prefetch=1,
        grid=(heads,),
        in_specs=specs,
        out_specs=out_specs,
        scratch_shapes=[
            pltpu.VMEM((tile_len, 1), jnp.float32),
            pltpu.VMEM((tile_len, 1), jnp.float32),
            pltpu.VMEM((tile_len, HD), jnp.float32),
        ],
    )
    kernel = make_kernel(blocks, text is not None, state is not None, final)
    return pl.pallas_call(kernel, grid_spec=grid_spec, out_shape=out_shape)(reach, *args)


def per_device(image_q, image_kv, text_kv, residual, out_weight, out_gate, head_reach, tile_extent):
    tile_len = image_q.shape[2]
    col_width = image_q.shape[3]
    tm_size = lax.axis_size("tm")
    height_size = lax.axis_size("height")
    mp_size = lax.axis_size("mp")

    own = image_kv[0, 0]
    t_before = lax.ppermute(own, "tm", shift_pairs(tm_size, 1))
    t_after = lax.ppermute(own, "tm", shift_pairs(tm_size, -1))
    h_before = lax.ppermute(own, "height", shift_pairs(height_size, 1))
    h_after = lax.ppermute(own, "height", shift_pairs(height_size, -1))
    text = gather_text(text_kv, tm_size)
    time_start = lax.axis_index("tm")
    height_start = lax.axis_index("height")
    zero_index = jnp.int32(0)
    padded_ext = jnp.pad(tile_extent, ((0, 0), (1, 1), (1, 1)))
    local_ext = lax.dynamic_slice(padded_ext, (zero_index, time_start, height_start), (2, 3, 3))
    key_valid = token_masks(local_ext)
    bias = jnp.where(key_valid, 0.0, NEG).astype(jnp.float32).reshape(9, 1, tile_len)
    qvalid = key_valid[1, 1].astype(jnp.float32).reshape(tile_len, 1)

    queries = image_q[0, 0]
    near = [(own, None, 4), (h_before, None, 3), (h_after, None, 5)]
    state = attend(head_reach, queries, None, near, bias)
    t_before, t_after, state = lax.optimization_barrier((t_before, t_after, state))
    time_pair = jnp.stack([t_before, t_after])
    c_before = lax.ppermute(time_pair, "height", shift_pairs(height_size, 1))
    c_after = lax.ppermute(time_pair, "height", shift_pairs(height_size, -1))
    across = [(t_before, None, 1), (t_after, None, 7)]
    state = attend(head_reach, queries, text, across, bias, state)
    corners = [(c_before, 0, 0), (c_after, 0, 2), (c_before, 1, 6), (c_after, 1, 8)]
    attended = attend(head_reach, queries, None, corners, bias, state, qvalid)

    mp_index = lax.axis_index("mp")
    chunk = out_weight.shape[1] // mp_size
    received = []
    for step in (2, 1, 3):
        target = (mp_index + step) % mp_size
        w_part = lax.dynamic_slice_in_dim(out_weight, target * chunk, chunk, 1)
        part = jnp.dot(attended, w_part, preferred_element_type=jnp.float32).astype(jnp.bfloat16)
        pairs = [(i, (i + step) % mp_size) for i in range(mp_size)]
        received.append(lax.ppermute(part, "mp", pairs))
    w_own = lax.dynamic_slice_in_dim(out_weight, mp_index * chunk, chunk, 1)
    branch = jnp.dot(attended, w_own, preferred_element_type=jnp.float32).astype(jnp.bfloat16)
    branch = branch.astype(jnp.float32)
    for part in received:
        branch = branch + part.astype(jnp.float32)
    updated = residual[0, 0].astype(jnp.float32) + out_gate * branch
    return updated.astype(jnp.bfloat16)[None, None]


def solution(mesh):
    return jax.shard_map(
        per_device,
        mesh=mesh,
        in_specs=(
            P("tm", "height", None, "mp"),
            P("tm", "height", None, None, "mp"),
            P(None, "tm", "mp"),
            P("tm", "height", None, "mp"),
            P("mp", None),
            P("mp"),
            P("mp", None),
            P(),
        ),
        out_specs=P("tm", "height", None, "mp"),
        check_vma=False,
    )
```

time: 231 us -> 202 us (0.87)
  the two profiles are of different devices: /device:TPU:2 before, /device:TPU:18 now
where the time goes in v2:
time: 202 us; the launch traced here: 199 us
  waiting for transfers between devices  90.9 us (45%)
  starting transfers between devices  43.7 us (22%)
  Pallas kernels  39.2 us (19%)
  matrix products  10.5 us (5%)
  local copies, waits for them, and re-layouts  8.02 us (4%)
  other arithmetic  6.48 us (3%)
    ppermute x4, waiting for transfers between devices, gather_text(): lax.ppermute(gathered, 'tm', [(i, i ^ step) for i in range(devices)])  41.6 us
    pallas_call x3, Pallas kernels, attend(): pl.pallas_call(kernel, grid_spec=grid_spec, out_shape=out_shape)  39.2 us
    ppermute x1, waiting for transfers between devices, per_device(): h_before = lax.ppermute(own, 'height', shift_pairs(height_size, 1))  34.5 us
    ppermute x4, starting transfers between devices, gather_text(): lax.ppermute(gathered, 'tm', [(i, i ^ step) for i in range(devices)])  16.5 us
    ppermute x3, starting transfers between devices, per_device(): received.append(lax.ppermute(part, 'mp', pairs))  10.7 us
    ppermute x3, waiting for transfers between devices, per_device(): received.append(lax.ppermute(part, 'mp', pairs))  10.1 us
    dot_general x3, matrix products, per_device(): jnp.dot(attended, w_part, preferred_element_type=jnp.float32)  7.59 us
    ppermute x1, waiting for transfers between devices, per_device(): h_after = lax.ppermute(own, 'height', shift_pairs(height_size, -1))  4.23 us
  transfers between devices with their start and end apart: 13, of which 9 were waited for; matrix products, arithmetic and copies ran while one was open for 8% of the time, Pallas kernels for 15%

profile of v2, /device:TPU:18, one launch (start us, length us, event | category | flops | bytes accessed | tf_op | source)
XLA Modules:
  0.0 198.9 jit_solution(5213212368985644113)
XLA Ops:
  0.0 1.9 collective-permute-start.2
  1.9 3.6 %collective-permute-start.3 = (bf16[2,384,768]{2,1,0:T(8,128)(2,1)}, bf16[2,384,768]{2,1,0:T(8,128)(2,1)}, u32[]{:S(2)}, u32[]{:S(2)}) collective-permute-start(bf16[2,384,768]{2,1,0:T(8,128)(2,1)} %bitcast.23), channel_id=1, source_target_pairs={{4,0},{8,4},{12,8},{5,1},{9,5},{13,9},{6,2},{10,6},{14,10},{7,3},{... | collective-permute-start | bytes 3538952 | tf_op jit(solution)/shard_map/ppermute | solution.py:180
  5.6 4.1 %collective-permute-start = (bf16[2,384,768]{2,1,0:T(8,128)(2,1)}, bf16[2,384,768]{2,1,0:T(8,128)(2,1)S(1)}, u32[]{:S(2)}, u32[]{:S(2)}) collective-permute-start(bf16[2,384,768]{2,1,0:T(8,128)(2,1)} %bitcast.24), channel_id=1, source_target_pairs={{0,16},{16,32},{32,48},{48,64},{64,80},{80,96},{96,112},{112,128},... | collective-permute-start | bytes 3538952 | tf_op jit(solution)/shard_map/ppermute | solution.py:177
  9.7 1.3 collective-permute-start.1
  11.0 0.8 pad_dynamic-slice_fusion
  11.8 0.1 copy.16
  11.9 0.6 lt.103
  12.5 0.1 copy.17
  12.6 0.6 lt.108
  13.2 1.3 copy.22.reach_ref
  14.5 1.3 and_select_fusion.rest_3_.rest_4_
  15.9 34.5 %collective-permute-done.2.rest_1_ = bf16[2,384,768]{2,1,0:T(8,128)(2,1)S(1)} collective-permute-done((bf16[2,384,768]{2,1,0:T(8,128)(2,1)}, bf16[2,384,768]{2,1,0:T(8,128)(2,1)S(1)}, u32[]{:S(2)}, u32[]{:S(2)}) %collective-permute-start.2) | collective-permute-done | bytes 1179680 | tf_op jit(solution)/shard_map/ppermute | solution.py:179
  50.3 0.0 copy-start.3
  50.3 4.2 %collective-permute-done.3.rest_2_ = bf16[2,384,768]{2,1,0:T(8,128)(2,1)} collective-permute-done((bf16[2,384,768]{2,1,0:T(8,128)(2,1)}, bf16[2,384,768]{2,1,0:T(8,128)(2,1)}, u32[]{:S(2)}, u32[]{:S(2)}) %collective-permute-start.3) | collective-permute-done | bytes 1179680 | tf_op jit(solution)/shard_map/ppermute | solution.py:180
  54.6 0.0 copy-done.3
  54.6 15.0 %shard_map.82 = (f32[6,384,1]{2,1,0:T(8,128)}, f32[6,384,1]{2,1,0:T(8,128)}, f32[384,768]{1,0:T(8,128)}) custom-call(s32[6,2]{1,0:T(8,128)} %copy.22.reach_ref, bf16[384,768]{1,0:T(8,128)(2,1)} %bitcast.17, bf16[2,384,768]{2,1,0:T(8,128)(2,1)} %bitcast.26, bf16[2,384,768]{2,1,0:T(8,128)(2,1)} %copy-done.3, ...), custom_call_target="tpu_custom_call" | custom-call | tf_op jit(solution)/shard_map/pallas_call | solution.py:166
  69.6 0.6 collective-permute-done.rest_1_
  70.1 0.0 copy-start.1
  70.1 0.0 collective-permute-done.1.rest_2_
  70.2 0.0 copy-start.2
  70.2 1.0 copy-done.2
  71.2 1.6 pad_maximum_fusion
  72.8 0.0 copy-done.1
  72.8 1.9 collective-permute-start.4
  74.8 3.6 %collective-permute-start.5 = (bf16[2,2,384,768]{3,2,1,0:T(8,128)(2,1)}, bf16[2,2,384,768]{3,2,1,0:T(8,128)(2,1)}, u32[]{:S(2)}, u32[]{:S(2)}) collective-permute-start(bf16[2,2,384,768]{3,2,1,0:T(8,128)(2,1)} %pad_maximum_fusion), channel_id=1, source_target_pairs={{4,0},{8,4},{12,8},{5,1},{9,5},{13,9},{6,2},{10,6},{14,10},{7,3},{... | collective-permute-start | bytes 7077896 | tf_op jit(solution)/shard_map/ppermute | solution.py:197
  78.4 4.0 %collective-permute-start.6 = (bf16[2,16,768]{2,1,0:T(8,128)(2,1)}, bf16[2,16,768]{2,1,0:T(8,128)(2,1)S(1)}, u32[]{:S(2)}, u32[]{:S(2)}) collective-permute-start(bf16[2,16,768]{2,1,0:T(8,128)(2,1)} %param.10), channel_id=1, source_target_pairs={{0,16},{16,0},{32,48},{48,32},{64,80},{80,64},{96,112},{112,96},{1... | collective-permute-start | bytes 147464 | tf_op jit(solution)/shard_map/ppermute | solution.py:36
  82.4 27.5 %collective-permute-done.6 = bf16[2,16,768]{2,1,0:T(8,128)(2,1)S(1)} collective-permute-done((bf16[2,16,768]{2,1,0:T(8,128)(2,1)}, bf16[2,16,768]{2,1,0:T(8,128)(2,1)S(1)}, u32[]{:S(2)}, u32[]{:S(2)}) %collective-permute-start.6) | collective-permute-done | bytes 49184 | tf_op jit(solution)/shard_map/ppermute | solution.py:36
  109.9 0.9 maximum_select_fusion.3
  110.8 2.5 %collective-permute-start.7 = (bf16[2,32,768]{2,1,0:T(8,128)(2,1)S(1)}, bf16[2,32,768]{2,1,0:T(8,128)(2,1)S(1)}, u32[]{:S(2)}, u32[]{:S(2)}) collective-permute-start(bf16[2,32,768]{2,1,0:T(8,128)(2,1)S(1)} %maximum_select_fusion.3), channel_id=1, source_target_pairs={{0,32},{16,48},{32,0},{48,16},{64,96},{80,112},{96,64},{112,80},{1... | collective-permute-start | bytes 294920 | tf_op jit(solution)/shard_map/ppermute | solution.py:36
  113.2 2.9 %collective-permute-done.7 = bf16[2,32,768]{2,1,0:T(8,128)(2,1)S(1)} collective-permute-done((bf16[2,32,768]{2,1,0:T(8,128)(2,1)S(1)}, bf16[2,32,768]{2,1,0:T(8,128)(2,1)S(1)}, u32[]{:S(2)}, u32[]{:S(2)}) %collective-permute-start.7) | collective-permute-done | bytes 98336 | tf_op jit(solution)/shard_map/ppermute | solution.py:36
  116.2 3.2 %collective-permute-start.8 = (bf16[2,64,768]{2,1,0:T(8,128)(2,1)S(1)}, bf16[2,64,768]{2,1,0:T(8,128)(2,1)S(1)}, u32[]{:S(2)}, u32[]{:S(2)}) collective-permute-start(bf16[2,64,768]{2,1,0:T(8,128)(2,1)S(1)} %maximum_select_fusion.2), channel_id=1, source_target_pairs={{0,64},{16,80},{32,96},{48,112},{64,0},{80,16},{96,32},{112,48},{1... | collective-permute-start | bytes 589832 | tf_op jit(solution)/shard_map/ppermute | solution.py:36
  119.3 5.8 %collective-permute-done.8 = bf16[2,64,768]{2,1,0:T(8,128)(2,1)S(1)} collective-permute-done((bf16[2,64,768]{2,1,0:T(8,128)(2,1)S(1)}, bf16[2,64,768]{2,1,0:T(8,128)(2,1)S(1)}, u32[]{:S(2)}, u32[]{:S(2)}) %collective-permute-start.8) | collective-permute-done | bytes 196640 | tf_op jit(solution)/shard_map/ppermute | solution.py:36
  125.1 0.1 maximum_select_fusion.1
  125.2 6.9 %collective-permute-start.9 = (bf16[2,128,768]{2,1,0:T(8,128)(2,1)S(1)}, bf16[2,128,768]{2,1,0:T(8,128)(2,1)S(1)}, u32[]{:S(2)}, u32[]{:S(2)}) collective-permute-start(bf16[2,128,768]{2,1,0:T(8,128)(2,1)S(1)} %maximum_select_fusion.1), channel_id=1, source_target_pairs={{0,128},{16,144},{32,160},{48,176},{64,192},{80,208},{96,224},{112... | collective-permute-start | bytes 1179656 | tf_op jit(solution)/shard_map/ppermute | solution.py:36
  132.1 0.6 slice.12
  132.7 0.6 slice.13
  133.3 1.3 fusion.18
  134.6 0.8 copy.23.rest_8_
  135.4 5.4 %collective-permute-done.9 = bf16[2,128,768]{2,1,0:T(8,128)(2,1)S(1)} collective-permute-done((bf16[2,128,768]{2,1,0:T(8,128)(2,1)S(1)}, bf16[2,128,768]{2,1,0:T(8,128)(2,1)S(1)}, u32[]{:S(2)}, u32[]{:S(2)}) %collective-permute-start.9) | collective-permute-done | bytes 393248 | tf_op jit(solution)/shard_map/ppermute | solution.py:36
  140.8 1.2 maximum_select_fusion.rest_0_
  142.0 13.9 %shard_map.83 = (f32[6,384,1]{2,1,0:T(8,128)}, f32[6,384,1]{2,1,0:T(8,128)}, f32[384,768]{1,0:T(8,128)}) custom-call(s32[6,2]{1,0:T(8,128)} %copy.22.reach_ref, bf16[384,768]{1,0:T(8,128)(2,1)} %bitcast.18, bf16[2,256,768]{2,1,0:T(8,128)(2,1)} %maximum_select_fusion.rest_0_, bf16[2,384,768]{2,1,0:T(8,128)(2,1)} %copy-done.1, bf16[2,384,768]{2,1,0:T(8,128)(2,1)} %copy-done.2, ...), custom_call_target="tpu_custom_call" | custom-call | tf_op jit(solution)/shard_map/pallas_call | solution.py:166
  156.0 0.0 collective-permute-done.4.rest_0_.rest_2_
  156.0 0.0 copy-start
  156.0 0.0 collective-permute-done.5.rest_1_.rest_3_
  156.0 1.4 copy-done
  157.4 10.2 %shard_map.84 = bf16[384,768]{1,0:T(8,128)(2,1)} custom-call(s32[6,2]{1,0:T(8,128)} %copy.22.reach_ref, bf16[384,768]{1,0:T(8,128)(2,1)} %bitcast.19, bf16[2,2,384,768]{3,2,1,0:T(8,128)(2,1)} %copy-done, bf16[2,2,384,768]{3,2,1,0:T(8,128)(2,1)} %collective-permute-done.5.rest_1_.rest_3_, bf16[2,2,384,768]{3,2,1,0:T(8,128)(2,1)} %copy-done, ...), custom_call_target="tpu_custom_call" | custom-call | tf_op jit(solution)/shard_map/pallas_call | solution.py:166
  167.6 0.0 copy-start.4
  167.6 2.1 %convolution_convert_fusion.2 = bf16[384,768]{1,0:T(8,128)(2,1)S(1)} fusion(bf16[384,768]{1,0:T(8,128)(2,1)} %shard_map.84, bf16[768,3072]{1,0:T(8,128)(2,1)} %param.12, s32[]{:T(128)S(6)} %select_n.124), kind=kOutput, calls=%fused_computation.3 | convolution fusion | flops 453279744 | bytes 2359300 | tf_op jit(solution)/shard_map/dot_general | solution.py:209
  169.8 4.9 %collective-permute-start.10 = (bf16[384,768]{1,0:T(8,128)(2,1)S(1)}, bf16[384,768]{1,0:T(8,128)(2,1)S(1)}, u32[]{:S(2)}, u32[]{:S(2)}) collective-permute-start(bf16[384,768]{1,0:T(8,128)(2,1)S(1)} %convolution_convert_fusion.2), channel_id=1, source_target_pairs={{0,2},{1,3},{2,0},{3,1},{4,6},{5,7},{6,4},{7,5},{8,10},{9,11},{10,... | collective-permute-start | bytes 1769480 | tf_op jit(solution)/shard_map/ppermute | solution.py:211
  174.7 0.0 copy-done.4
  174.7 2.7 %convolution_convert_fusion.1 = bf16[384,768]{1,0:T(8,128)(2,1)} fusion(bf16[384,768]{1,0:T(8,128)(2,1)S(1)} %copy-done.4, bf16[768,3072]{1,0:T(8,128)(2,1)} %param.12, s32[]{:T(128)S(6)} %select_n.126), kind=kOutput, calls=%fused_computation.2 | convolution fusion | flops 453279744 | bytes 2359300 | tf_op jit(solution)/shard_map/dot_general | solution.py:209
  177.4 0.0 copy-start.5
  177.4 0.0 copy-start.6
  177.4 5.8 %collective-permute-start.11 = (bf16[384,768]{1,0:T(8,128)(2,1)}, bf16[384,768]{1,0:T(8,128)(2,1)S(1)}, u32[]{:S(2)}, u32[]{:S(2)}) collective-permute-start(bf16[384,768]{1,0:T(8,128)(2,1)} %convolution_convert_fusion.1), channel_id=1, source_target_pairs={{0,1},{1,2},{2,3},{3,0},{4,5},{5,6},{6,7},{7,4},{8,9},{9,10},{10,1... | collective-permute-start | bytes 1769480 | tf_op jit(solution)/shard_map/ppermute | solution.py:211
  183.2 2.7 %convolution_convert_fusion = bf16[384,768]{1,0:T(8,128)(2,1)} fusion(bf16[384,768]{1,0:T(8,128)(2,1)S(1)} %copy-done.4, bf16[768,3072]{1,0:T(8,128)(2,1)} %param.12, s32[]{:T(128)S(6)} %select_n.128), kind=kOutput, calls=%fused_computation.1 | convolution fusion | flops 453279744 | bytes 2359300 | tf_op jit(solution)/shard_map/dot_general | solution.py:209
  185.9 0.0 collective-permute-start.12
  185.9 0.0 collective-permute-done.10
  185.9 5.0 %collective-permute-done.11 = bf16[384,768]{1,0:T(8,128)(2,1)S(1)} collective-permute-done((bf16[384,768]{1,0:T(8,128)(2,1)}, bf16[384,768]{1,0:T(8,128)(2,1)S(1)}, u32[]{:S(2)}, u32[]{:S(2)}) %collective-permute-start.11) | collective-permute-done | bytes 589856 | tf_op jit(solution)/shard_map/ppermute | solution.py:211
  190.9 5.1 %collective-permute-done.12 = bf16[384,768]{1,0:T(8,128)(2,1)S(1)} collective-permute-done((bf16[384,768]{1,0:T(8,128)(2,1)}, bf16[384,768]{1,0:T(8,128)(2,1)S(1)}, u32[]{:S(2)}, u32[]{:S(2)}) %collective-permute-start.12) | collective-permute-done | bytes 589856 | tf_op jit(solution)/shard_map/ppermute | solution.py:211
  196.0 0.0 copy-done.5
  196.0 0.0 copy-done.6
  196.0 2.9 %fusion.7 = bf16[1,1,384,768]{3,2,1,0:T(8,128)(2,1)} fusion(bf16[384,768]{1,0:T(8,128)(2,1)S(1)} %copy-done.4, bf16[384,768]{1,0:T(8,128)(2,1)S(1)} %collective-permute-done.12, bf16[384,768]{1,0:T(8,128)(2,1)S(1)} %collective-permute-done.11, bf16[384,768]{1,0:T(8,128)(2,1)S(1)} %collective-permute-done.10, bf16[768,3072]{1,0:T(8,128)(2,1)} %param.12, ...), kind=kOutput, calls=%fused_computation.12 | convolution fusion | flops 456523776 | bytes 4721668 | tf_op jit(solution)/shard_map/dot_general | solution.py:213
  (2 shorter events, 0.0 us)
Async XLA Ops:
  0.0 50.3 %collective-permute-start.2 = (bf16[2,384,768]{2,1,0:T(8,128)(2,1)}, bf16[2,384,768]{2,1,0:T(8,128)(2,1)S(1)}, u32[]{:S(2)}, u32[]{:S(2)}) collective-permute-start(bf16[2,384,768]{2,1,0:T(8,128)(2,1)} %bitcast.22), channel_id=1, source_target_pairs={{0,4},{4,8},{8,12},{1,5},{5,9},{9,13},{2,6},{6,10},{10,14},{3,7},{... | collective-permute-start | bytes 3538952 | tf_op jit(solution)/shard_map/ppermute | solution.py:179
  1.9 52.7 %collective-permute-start.3 = (bf16[2,384,768]{2,1,0:T(8,128)(2,1)}, bf16[2,384,768]{2,1,0:T(8,128)(2,1)}, u32[]{:S(2)}, u32[]{:S(2)}) collective-permute-start(bf16[2,384,768]{2,1,0:T(8,128)(2,1)} %bitcast.23), channel_id=1, source_target_pairs={{4,0},{8,4},{12,8},{5,1},{9,5},{13,9},{6,2},{10,6},{14,10},{7,3},{... | collective-permute-start | bytes 3538952 | tf_op jit(solution)/shard_map/ppermute | solution.py:180
  5.6 64.6 %collective-permute-start = (bf16[2,384,768]{2,1,0:T(8,128)(2,1)}, bf16[2,384,768]{2,1,0:T(8,128)(2,1)S(1)}, u32[]{:S(2)}, u32[]{:S(2)}) collective-permute-start(bf16[2,384,768]{2,1,0:T(8,128)(2,1)} %bitcast.24), channel_id=1, source_target_pairs={{0,16},{16,32},{32,48},{48,64},{64,80},{80,96},{96,112},{112,128},... | collective-permute-start | bytes 3538952 | tf_op jit(solution)/shard_map/ppermute | solution.py:177
  9.7 60.5 %collective-permute-start.1 = (bf16[2,384,768]{2,1,0:T(8,128)(2,1)}, bf16[2,384,768]{2,1,0:T(8,128)(2,1)S(1)}, u32[]{:S(2)}, u32[]{:S(2)}) collective-permute-start(bf16[2,384,768]{2,1,0:T(8,128)(2,1)} %bitcast.25), channel_id=1, source_target_pairs={{16,0},{32,16},{48,32},{64,48},{80,64},{96,80},{112,96},{128,112},... | collective-permute-start | bytes 3538952 | tf_op jit(solution)/shard_map/ppermute | solution.py:178
  50.3 4.2 %copy-start.3 = (bf16[2,384,768]{2,1,0:T(8,128)(2,1)}, bf16[2,384,768]{2,1,0:T(8,128)(2,1)S(1)}, u32[]{:S(2)}) copy-start(bf16[2,384,768]{2,1,0:T(8,128)(2,1)S(1)} %collective-permute-done.2.rest_1_) | copy-start | bytes 3538948
  70.1 2.7 %copy-start.1 = (bf16[2,384,768]{2,1,0:T(8,128)(2,1)}, bf16[2,384,768]{2,1,0:T(8,128)(2,1)S(1)}, u32[]{:S(2)}) copy-start(bf16[2,384,768]{2,1,0:T(8,128)(2,1)S(1)} %collective-permute-done.rest_1_) | copy-start | bytes 3538948
  70.2 1.0 copy-start.2
  72.8 83.1 %collective-permute-start.4 = (bf16[2,2,384,768]{3,2,1,0:T(8,128)(2,1)}, bf16[2,2,384,768]{3,2,1,0:T(8,128)(2,1)S(1)}, u32[]{:S(2)}, u32[]{:S(2)}) collective-permute-start(bf16[2,2,384,768]{3,2,1,0:T(8,128)(2,1)} %pad_maximum_fusion), channel_id=1, source_target_pairs={{0,4},{4,8},{8,12},{1,5},{5,9},{9,13},{2,6},{6,10},{10,14},{3,7},{... | collective-permute-start | bytes 7077896 | tf_op jit(solution)/shard_map/ppermute | solution.py:196
  74.8 81.2 %collective-permute-start.5 = (bf16[2,2,384,768]{3,2,1,0:T(8,128)(2,1)}, bf16[2,2,384,768]{3,2,1,0:T(8,128)(2,1)}, u32[]{:S(2)}, u32[]{:S(2)}) collective-permute-start(bf16[2,2,384,768]{3,2,1,0:T(8,128)(2,1)} %pad_maximum_fusion), channel_id=1, source_target_pairs={{4,0},{8,4},{12,8},{5,1},{9,5},{13,9},{6,2},{10,6},{14,10},{7,3},{... | collective-permute-start | bytes 7077896 | tf_op jit(solution)/shard_map/ppermute | solution.py:197
  78.4 31.5 %collective-permute-start.6 = (bf16[2,16,768]{2,1,0:T(8,128)(2,1)}, bf16[2,16,768]{2,1,0:T(8,128)(2,1)S(1)}, u32[]{:S(2)}, u32[]{:S(2)}) collective-permute-start(bf16[2,16,768]{2,1,0:T(8,128)(2,1)} %param.10), channel_id=1, source_target_pairs={{0,16},{16,0},{32,48},{48,32},{64,80},{80,64},{96,112},{112,96},{1... | collective-permute-start | bytes 147464 | tf_op jit(solution)/shard_map/ppermute | solution.py:36
  110.8 5.4 %collective-permute-start.7 = (bf16[2,32,768]{2,1,0:T(8,128)(2,1)S(1)}, bf16[2,32,768]{2,1,0:T(8,128)(2,1)S(1)}, u32[]{:S(2)}, u32[]{:S(2)}) collective-permute-start(bf16[2,32,768]{2,1,0:T(8,128)(2,1)S(1)} %maximum_select_fusion.3), channel_id=1, source_target_pairs={{0,32},{16,48},{32,0},{48,16},{64,96},{80,112},{96,64},{112,80},{1... | collective-permute-start | bytes 294920 | tf_op jit(solution)/shard_map/ppermute | solution.py:36
  116.2 8.9 %collective-permute-start.8 = (bf16[2,64,768]{2,1,0:T(8,128)(2,1)S(1)}, bf16[2,64,768]{2,1,0:T(8,128)(2,1)S(1)}, u32[]{:S(2)}, u32[]{:S(2)}) collective-permute-start(bf16[2,64,768]{2,1,0:T(8,128)(2,1)S(1)} %maximum_select_fusion.2), channel_id=1, source_target_pairs={{0,64},{16,80},{32,96},{48,112},{64,0},{80,16},{96,32},{112,48},{1... | collective-permute-start | bytes 589832 | tf_op jit(solution)/shard_map/ppermute | solution.py:36
  125.2 15.6 %collective-permute-start.9 = (bf16[2,128,768]{2,1,0:T(8,128)(2,1)S(1)}, bf16[2,128,768]{2,1,0:T(8,128)(2,1)S(1)}, u32[]{:S(2)}, u32[]{:S(2)}) collective-permute-start(bf16[2,128,768]{2,1,0:T(8,128)(2,1)S(1)} %maximum_select_fusion.1), channel_id=1, source_target_pairs={{0,128},{16,144},{32,160},{48,176},{64,192},{80,208},{96,224},{112... | collective-permute-start | bytes 1179656 | tf_op jit(solution)/shard_map/ppermute | solution.py:36
  156.0 1.4 copy-start
  167.6 7.0 %copy-start.4 = (bf16[384,768]{1,0:T(8,128)(2,1)S(1)}, bf16[384,768]{1,0:T(8,128)(2,1)}, u32[]{:S(2)}) copy-start(bf16[384,768]{1,0:T(8,128)(2,1)} %shard_map.84) | copy-start | bytes 1769476
  169.8 16.2 %collective-permute-start.10 = (bf16[384,768]{1,0:T(8,128)(2,1)S(1)}, bf16[384,768]{1,0:T(8,128)(2,1)S(1)}, u32[]{:S(2)}, u32[]{:S(2)}) collective-permute-start(bf16[384,768]{1,0:T(8,128)(2,1)S(1)} %convolution_convert_fusion.2), channel_id=1, source_target_pairs={{0,2},{1,3},{2,0},{3,1},{4,6},{5,7},{6,4},{7,5},{8,10},{9,11},{10,... | collective-permute-start | bytes 1769480 | tf_op jit(solution)/shard_map/ppermute | solution.py:211
  177.4 18.6 %copy-start.5 = (bf16[1,1,384,768]{3,2,1,0:T(8,128)(2,1)S(1)}, bf16[1,1,384,768]{3,2,1,0:T(8,128)(2,1)}, u32[]{:S(2)}) copy-start(bf16[1,1,384,768]{3,2,1,0:T(8,128)(2,1)} %param.11) | copy-start | bytes 1769476
  177.4 18.6 %copy-start.6 = (f32[768]{0:T(1024)S(1)}, f32[768]{0:T(1024)}, u32[]{:S(2)}) copy-start(f32[768]{0:T(1024)} %param.13) | copy-start | bytes 9220
  177.4 13.5 %collective-permute-start.11 = (bf16[384,768]{1,0:T(8,128)(2,1)}, bf16[384,768]{1,0:T(8,128)(2,1)S(1)}, u32[]{:S(2)}, u32[]{:S(2)}) collective-permute-start(bf16[384,768]{1,0:T(8,128)(2,1)} %convolution_convert_fusion.1), channel_id=1, source_target_pairs={{0,1},{1,2},{2,3},{3,0},{4,5},{5,6},{6,7},{7,4},{8,9},{9,10},{10,1... | collective-permute-start | bytes 1769480 | tf_op jit(solution)/shard_map/ppermute | solution.py:211
  185.9 10.1 %collective-permute-start.12 = (bf16[384,768]{1,0:T(8,128)(2,1)}, bf16[384,768]{1,0:T(8,128)(2,1)S(1)}, u32[]{:S(2)}, u32[]{:S(2)}) collective-permute-start(bf16[384,768]{1,0:T(8,128)(2,1)} %convolution_convert_fusion), channel_id=1, source_target_pairs={{0,3},{1,0},{2,1},{3,2},{4,7},{5,4},{6,5},{7,6},{8,11},{9,8},{10,9... | collective-permute-start | bytes 1769480 | tf_op jit(solution)/shard_map/ppermute | solution.py:211

commit v3 on v2

--- a/solution.py
+++ b/solution.py
@@ -190,13 +190,13 @@
 
     queries = image_q[0, 0]
     near = [(own, None, 4), (h_before, None, 3), (h_after, None, 5)]
-    state = attend(head_reach, queries, None, near, bias)
+    state = attend(head_reach, queries, text, near, bias)
     t_before, t_after, state = lax.optimization_barrier((t_before, t_after, state))
     time_pair = jnp.stack([t_before, t_after])
     c_before = lax.ppermute(time_pair, "height", shift_pairs(height_size, 1))
     c_after = lax.ppermute(time_pair, "height", shift_pairs(height_size, -1))
     across = [(t_before, None, 1), (t_after, None, 7)]
-    state = attend(head_reach, queries, text, across, bias, state)
+    state = attend(head_reach, queries, None, across, bias, state)
     corners = [(c_before, 0, 0), (c_after, 0, 2), (c_before, 1, 6), (c_after, 1, 8)]
     attended = attend(head_reach, queries, None, corners, bias, state, qvalid)
 

time: 202 us -> 188 us (0.931)
  the two profiles are of different devices: /device:TPU:18 before, /device:TPU:2 now
where the time goes in v3:
time: 188 us; the launch traced here: 190 us
  waiting for transfers between devices  65.7 us (35%)
  starting transfers between devices  53.1 us (28%)
  Pallas kernels  50.7 us (27%)
  matrix products  10.6 us (6%)
  other arithmetic  5.89 us (3%)
  local copies, waits for them, and re-layouts  4.23 us (2%)
    pallas_call x3, Pallas kernels, attend(): pl.pallas_call(kernel, grid_spec=grid_spec, out_shape=out_shape)  50.7 us
    ppermute x4, waiting for transfers between devices, gather_text(): lax.ppermute(gathered, 'tm', [(i, i ^ step) for i in range(devices)])  43.4 us
    ppermute x4, starting transfers between devices, gather_text(): lax.ppermute(gathered, 'tm', [(i, i ^ step) for i in range(devices)])  34 us
    ppermute x3, waiting for transfers between devices, per_device(): received.append(lax.ppermute(part, 'mp', pairs))  11.7 us
    ppermute x1, waiting for transfers between devices, per_device(): c_before = lax.ppermute(time_pair, 'height', shift_pairs(height_size, 1))  8.69 us
    dot_general x3, matrix products, per_device(): jnp.dot(attended, w_part, preferred_element_type=jnp.float32)  7.65 us
  transfers between devices with their start and end apart: 13, of which 7 were waited for; matrix products, arithmetic and copies ran while one was open for 7% of the time, Pallas kernels for 16%

profile of v3, /device:TPU:2, one launch (start us, length us, event | category | flops | bytes accessed | tf_op | source)
XLA Modules:
  0.0 190.4 jit_solution(3171486858622401048)
XLA Ops:
  0.0 0.0 copy-start.4
  0.0 0.0 copy-start.5
  0.0 2.1 %collective-permute-start.2 = (bf16[2,16,768]{2,1,0:T(8,128)(2,1)}, bf16[2,16,768]{2,1,0:T(8,128)(2,1)S(1)}, u32[]{:S(2)}, u32[]{:S(2)}) collective-permute-start(bf16[2,16,768]{2,1,0:T(8,128)(2,1)} %param.10), channel_id=1, source_target_pairs={{0,16},{16,0},{32,48},{48,32},{64,80},{80,64},{96,112},{112,96},{1... | collective-permute-start | bytes 147464 | tf_op jit(solution)/shard_map/ppermute | solution.py:36
  2.1 1.9 %collective-permute-start.6 = (bf16[2,384,768]{2,1,0:T(8,128)(2,1)}, bf16[2,384,768]{2,1,0:T(8,128)(2,1)}, u32[]{:S(2)}, u32[]{:S(2)}) collective-permute-start(bf16[2,384,768]{2,1,0:T(8,128)(2,1)} %bitcast.22), channel_id=1, source_target_pairs={{0,4},{4,8},{8,12},{1,5},{5,9},{9,13},{2,6},{6,10},{10,14},{3,7},{... | collective-permute-start | bytes 3538952 | tf_op jit(solution)/shard_map/ppermute | solution.py:179
  4.0 3.6 %collective-permute-start.7 = (bf16[2,384,768]{2,1,0:T(8,128)(2,1)}, bf16[2,384,768]{2,1,0:T(8,128)(2,1)}, u32[]{:S(2)}, u32[]{:S(2)}) collective-permute-start(bf16[2,384,768]{2,1,0:T(8,128)(2,1)} %bitcast.23), channel_id=1, source_target_pairs={{4,0},{8,4},{12,8},{5,1},{9,5},{13,9},{6,2},{10,6},{14,10},{7,3},{... | collective-permute-start | bytes 3538952 | tf_op jit(solution)/shard_map/ppermute | solution.py:180
  7.7 3.4 %collective-permute-start = (bf16[2,384,768]{2,1,0:T(8,128)(2,1)}, bf16[2,384,768]{2,1,0:T(8,128)(2,1)S(1)}, u32[]{:S(2)}, u32[]{:S(2)}) collective-permute-start(bf16[2,384,768]{2,1,0:T(8,128)(2,1)} %bitcast.24), channel_id=1, source_target_pairs={{0,16},{16,32},{32,48},{48,64},{64,80},{80,96},{96,112},{112,128},... | collective-permute-start | bytes 3538952 | tf_op jit(solution)/shard_map/ppermute | solution.py:177
  11.1 1.3 collective-permute-start.1
  12.4 0.0 collective-permute-done.2
  12.4 0.9 maximum_select_fusion.3
  13.3 5.6 %collective-permute-start.3 = (bf16[2,32,768]{2,1,0:T(8,128)(2,1)S(1)}, bf16[2,32,768]{2,1,0:T(8,128)(2,1)S(1)}, u32[]{:S(2)}, u32[]{:S(2)}) collective-permute-start(bf16[2,32,768]{2,1,0:T(8,128)(2,1)S(1)} %maximum_select_fusion.3), channel_id=1, source_target_pairs={{0,32},{16,48},{32,0},{48,16},{64,96},{80,112},{96,64},{112,80},{1... | collective-permute-start | bytes 294920 | tf_op jit(solution)/shard_map/ppermute | solution.py:36
  18.9 26.7 %collective-permute-done.3 = bf16[2,32,768]{2,1,0:T(8,128)(2,1)S(1)} collective-permute-done((bf16[2,32,768]{2,1,0:T(8,128)(2,1)S(1)}, bf16[2,32,768]{2,1,0:T(8,128)(2,1)S(1)}, u32[]{:S(2)}, u32[]{:S(2)}) %collective-permute-start.3) | collective-permute-done | bytes 98336 | tf_op jit(solution)/shard_map/ppermute | solution.py:36
  45.6 4.1 %collective-permute-start.4 = (bf16[2,64,768]{2,1,0:T(8,128)(2,1)S(1)}, bf16[2,64,768]{2,1,0:T(8,128)(2,1)S(1)}, u32[]{:S(2)}, u32[]{:S(2)}) collective-permute-start(bf16[2,64,768]{2,1,0:T(8,128)(2,1)S(1)} %maximum_select_fusion.2), channel_id=1, source_target_pairs={{0,64},{16,80},{32,96},{48,112},{64,0},{80,16},{96,32},{112,48},{1... | collective-permute-start | bytes 589832 | tf_op jit(solution)/shard_map/ppermute | solution.py:36
  49.8 6.7 %collective-permute-done.4 = bf16[2,64,768]{2,1,0:T(8,128)(2,1)S(1)} collective-permute-done((bf16[2,64,768]{2,1,0:T(8,128)(2,1)S(1)}, bf16[2,64,768]{2,1,0:T(8,128)(2,1)S(1)}, u32[]{:S(2)}, u32[]{:S(2)}) %collective-permute-start.4) | collective-permute-done | bytes 196640 | tf_op jit(solution)/shard_map/ppermute | solution.py:36
  56.4 0.1 maximum_select_fusion.1
  56.5 22.2 %collective-permute-start.5 = (bf16[2,128,768]{2,1,0:T(8,128)(2,1)S(1)}, bf16[2,128,768]{2,1,0:T(8,128)(2,1)S(1)}, u32[]{:S(2)}, u32[]{:S(2)}) collective-permute-start(bf16[2,128,768]{2,1,0:T(8,128)(2,1)S(1)} %maximum_select_fusion.1), channel_id=1, source_target_pairs={{0,128},{16,144},{32,160},{48,176},{64,192},{80,208},{96,224},{112... | collective-permute-start | bytes 1179656 | tf_op jit(solution)/shard_map/ppermute | solution.py:36
  78.7 0.0 copy-done.4
  78.7 0.1 pad_dynamic-slice_fusion
  78.8 0.1 copy.16
  78.9 0.1 lt.103
  79.0 0.1 copy.17
  79.1 0.1 lt.108
  79.1 0.0 copy-done.5
  79.1 0.7 copy.22.reach_ref
  79.8 0.7 and_select_fusion.rest_4_.rest_2_
  80.5 10.1 %collective-permute-done.5 = bf16[2,128,768]{2,1,0:T(8,128)(2,1)S(1)} collective-permute-done((bf16[2,128,768]{2,1,0:T(8,128)(2,1)S(1)}, bf16[2,128,768]{2,1,0:T(8,128)(2,1)S(1)}, u32[]{:S(2)}, u32[]{:S(2)}) %collective-permute-start.5) | collective-permute-done | bytes 393248 | tf_op jit(solution)/shard_map/ppermute | solution.py:36
  90.6 1.2 maximum_select_fusion.rest_0_
  91.8 0.0 collective-permute-done.6.rest_2_
  91.8 0.0 collective-permute-done.7.rest_3_
  91.8 18.0 %shard_map.82 = (f32[6,384,1]{2,1,0:T(8,128)}, f32[6,384,1]{2,1,0:T(8,128)}, f32[384,768]{1,0:T(8,128)}) custom-call(s32[6,2]{1,0:T(8,128)} %copy.22.reach_ref, bf16[384,768]{1,0:T(8,128)(2,1)} %bitcast.17, bf16[2,256,768]{2,1,0:T(8,128)(2,1)} %maximum_select_fusion.rest_0_, bf16[2,384,768]{2,1,0:T(8,128)(2,1)} %bitcast.26, ...), custom_call_target="tpu_custom_call" | custom-call | tf_op jit(solution)/shard_map/pallas_call | solution.py:166
  109.8 0.0 collective-permute-done.rest_0_
  109.8 0.0 copy-start.1
  109.8 0.0 collective-permute-done.1.rest_1_
  109.8 0.0 copy-start.2
  109.8 1.0 copy-done.2
  110.9 1.6 pad_maximum_fusion
  112.5 0.0 copy-done.1
  112.5 1.9 %collective-permute-start.8 = (bf16[2,2,384,768]{3,2,1,0:T(8,128)(2,1)}, bf16[2,2,384,768]{3,2,1,0:T(8,128)(2,1)S(1)}, u32[]{:S(2)}, u32[]{:S(2)}) collective-permute-start(bf16[2,2,384,768]{3,2,1,0:T(8,128)(2,1)} %pad_maximum_fusion), channel_id=1, source_target_pairs={{0,4},{4,8},{8,12},{1,5},{5,9},{9,13},{2,6},{6,10},{10,14},{3,7},{... | collective-permute-start | bytes 7077896 | tf_op jit(solution)/shard_map/ppermute | solution.py:196
  114.4 3.6 %collective-permute-start.9 = (bf16[2,2,384,768]{3,2,1,0:T(8,128)(2,1)}, bf16[2,2,384,768]{3,2,1,0:T(8,128)(2,1)}, u32[]{:S(2)}, u32[]{:S(2)}) collective-permute-start(bf16[2,2,384,768]{3,2,1,0:T(8,128)(2,1)} %pad_maximum_fusion), channel_id=1, source_target_pairs={{4,0},{8,4},{12,8},{5,1},{9,5},{13,9},{6,2},{10,6},{14,10},{7,3},{... | collective-permute-start | bytes 7077896 | tf_op jit(solution)/shard_map/ppermute | solution.py:197
  118.1 0.7 slice.12
  118.8 0.6 slice.13
  119.4 1.3 fusion.18
  120.7 0.8 copy.23.rest_8_
  121.5 12.7 %shard_map.83 = (f32[6,384,1]{2,1,0:T(8,128)}, f32[6,384,1]{2,1,0:T(8,128)}, f32[384,768]{1,0:T(8,128)}) custom-call(s32[6,2]{1,0:T(8,128)} %copy.22.reach_ref, bf16[384,768]{1,0:T(8,128)(2,1)} %bitcast.18, bf16[2,384,768]{2,1,0:T(8,128)(2,1)} %copy-done.1, bf16[2,384,768]{2,1,0:T(8,128)(2,1)} %copy-done.2, f32[9,1,384]{2,1,0:T(1,128)} %and_select_fusion.rest_4_.rest_2_, ...), custom_call_target="tpu_custom_call" | custom-call | tf_op jit(solution)/shard_map/pallas_call | solution.py:166
  134.2 8.7 %collective-permute-done.8.rest_0_.rest_2_ = bf16[2,2,384,768]{3,2,1,0:T(8,128)(2,1)S(1)} collective-permute-done((bf16[2,2,384,768]{3,2,1,0:T(8,128)(2,1)}, bf16[2,2,384,768]{3,2,1,0:T(8,128)(2,1)S(1)}, u32[]{:S(2)}, u32[]{:S(2)}) %collective-permute-start.8) | collective-permute-done | bytes 2359328 | tf_op jit(solution)/shard_map/ppermute | solution.py:196
  142.9 0.0 copy-start
  142.9 1.9 collective-permute-done.9.rest_1_.rest_3_
  144.7 0.0 copy-done
  144.7 20.1 %shard_map.84 = bf16[384,768]{1,0:T(8,128)(2,1)} custom-call(s32[6,2]{1,0:T(8,128)} %copy.22.reach_ref, bf16[384,768]{1,0:T(8,128)(2,1)} %bitcast.19, bf16[2,2,384,768]{3,2,1,0:T(8,128)(2,1)} %copy-done, bf16[2,2,384,768]{3,2,1,0:T(8,128)(2,1)} %collective-permute-done.9.rest_1_.rest_3_, bf16[2,2,384,768]{3,2,1,0:T(8,128)(2,1)} %copy-done, ...), custom_call_target="tpu_custom_call" | custom-call | tf_op jit(solution)/shard_map/pallas_call | solution.py:166
  164.8 0.0 copy-start.3
  164.8 2.1 %convolution_convert_fusion.2 = bf16[384,768]{1,0:T(8,128)(2,1)S(1)} fusion(bf16[384,768]{1,0:T(8,128)(2,1)} %shard_map.84, bf16[768,3072]{1,0:T(8,128)(2,1)} %param.12, s32[]{:T(128)S(6)} %select_n.124), kind=kOutput, calls=%fused_computation.3 | convolution fusion | flops 453279744 | bytes 2359300 | tf_op jit(solution)/shard_map/dot_general | solution.py:209
  167.0 0.1 collective-permute-start.10
  167.1 0.0 copy-done.3
  167.1 2.7 %convolution_convert_fusion.1 = bf16[384,768]{1,0:T(8,128)(2,1)} fusion(bf16[384,768]{1,0:T(8,128)(2,1)S(1)} %copy-done.3, bf16[768,3072]{1,0:T(8,128)(2,1)} %param.12, s32[]{:T(128)S(6)} %select_n.126), kind=kOutput, calls=%fused_computation.2 | convolution fusion | flops 453279744 | bytes 2359300 | tf_op jit(solution)/shard_map/dot_general | solution.py:209
  169.8 0.0 copy-start.6
  169.8 0.0 copy-start.7
  169.8 0.0 collective-permute-start.11
  169.8 2.8 %convolution_convert_fusion = bf16[384,768]{1,0:T(8,128)(2,1)} fusion(bf16[384,768]{1,0:T(8,128)(2,1)S(1)} %copy-done.3, bf16[768,3072]{1,0:T(8,128)(2,1)} %param.12, s32[]{:T(128)S(6)} %select_n.128), kind=kOutput, calls=%fused_computation.1 | convolution fusion | flops 453279744 | bytes 2359300 | tf_op jit(solution)/shard_map/dot_general | solution.py:209
  172.6 3.2 %collective-permute-start.12 = (bf16[384,768]{1,0:T(8,128)(2,1)}, bf16[384,768]{1,0:T(8,128)(2,1)S(1)}, u32[]{:S(2)}, u32[]{:S(2)}) collective-permute-start(bf16[384,768]{1,0:T(8,128)(2,1)} %convolution_convert_fusion), channel_id=1, source_target_pairs={{0,3},{1,0},{2,1},{3,2},{4,7},{5,4},{6,5},{7,6},{8,11},{9,8},{10,9... | collective-permute-start | bytes 1769480 | tf_op jit(solution)/shard_map/ppermute | solution.py:211
  175.8 5.5 %collective-permute-done.10 = bf16[384,768]{1,0:T(8,128)(2,1)S(1)} collective-permute-done((bf16[384,768]{1,0:T(8,128)(2,1)S(1)}, bf16[384,768]{1,0:T(8,128)(2,1)S(1)}, u32[]{:S(2)}, u32[]{:S(2)}) %collective-permute-start.10) | collective-permute-done | bytes 589856 | tf_op jit(solution)/shard_map/ppermute | solution.py:211
  181.3 6.2 %collective-permute-done.11 = bf16[384,768]{1,0:T(8,128)(2,1)S(1)} collective-permute-done((bf16[384,768]{1,0:T(8,128)(2,1)}, bf16[384,768]{1,0:T(8,128)(2,1)S(1)}, u32[]{:S(2)}, u32[]{:S(2)}) %collective-permute-start.11) | collective-permute-done | bytes 589856 | tf_op jit(solution)/shard_map/ppermute | solution.py:211
  187.5 0.0 collective-permute-done.12
  187.5 0.0 copy-done.6
  187.5 0.0 copy-done.7
  187.5 2.9 %fusion.7 = bf16[1,1,384,768]{3,2,1,0:T(8,128)(2,1)} fusion(bf16[384,768]{1,0:T(8,128)(2,1)S(1)} %copy-done.3, bf16[384,768]{1,0:T(8,128)(2,1)S(1)} %collective-permute-done.12, bf16[384,768]{1,0:T(8,128)(2,1)S(1)} %collective-permute-done.11, bf16[384,768]{1,0:T(8,128)(2,1)S(1)} %collective-permute-done.10, bf16[768,3072]{1,0:T(8,128)(2,1)} %param.12, ...), kind=kOutput, calls=%fused_computation.12 | convolution fusion | flops 456523776 | bytes 4721668 | tf_op jit(solution)/shard_map/dot_general | solution.py:213
  (2 shorter events, 0.0 us)
Async XLA Ops:
  0.0 78.7 %copy-start.4 = (s32[2,16,4]{1,2,0:T(4,128)S(1)}, s32[2,16,4]{1,2,0:T(4,128)}, u32[]{:S(2)}) copy-start(s32[2,16,4]{1,2,0:T(4,128)} %param.15) | copy-start | bytes 1540
  0.0 79.1 %copy-start.5 = (s32[6,2]{0,1:T(2,128)S(1)}, s32[6,2]{0,1:T(2,128)}, u32[]{:S(2)}) copy-start(s32[6,2]{0,1:T(2,128)} %param.14) | copy-start | bytes 148
  0.0 12.4 %collective-permute-start.2 = (bf16[2,16,768]{2,1,0:T(8,128)(2,1)}, bf16[2,16,768]{2,1,0:T(8,128)(2,1)S(1)}, u32[]{:S(2)}, u32[]{:S(2)}) collective-permute-start(bf16[2,16,768]{2,1,0:T(8,128)(2,1)} %param.10), channel_id=1, source_target_pairs={{0,16},{16,0},{32,48},{48,32},{64,80},{80,64},{96,112},{112,96},{1... | collective-permute-start | bytes 147464 | tf_op jit(solution)/shard_map/ppermute | solution.py:36
  2.1 89.7 %collective-permute-start.6 = (bf16[2,384,768]{2,1,0:T(8,128)(2,1)}, bf16[2,384,768]{2,1,0:T(8,128)(2,1)}, u32[]{:S(2)}, u32[]{:S(2)}) collective-permute-start(bf16[2,384,768]{2,1,0:T(8,128)(2,1)} %bitcast.22), channel_id=1, source_target_pairs={{0,4},{4,8},{8,12},{1,5},{5,9},{9,13},{2,6},{6,10},{10,14},{3,7},{... | collective-permute-start | bytes 3538952 | tf_op jit(solution)/shard_map/ppermute | solution.py:179
  4.0 87.8 %collective-permute-start.7 = (bf16[2,384,768]{2,1,0:T(8,128)(2,1)}, bf16[2,384,768]{2,1,0:T(8,128)(2,1)}, u32[]{:S(2)}, u32[]{:S(2)}) collective-permute-start(bf16[2,384,768]{2,1,0:T(8,128)(2,1)} %bitcast.23), channel_id=1, source_target_pairs={{4,0},{8,4},{12,8},{5,1},{9,5},{13,9},{6,2},{10,6},{14,10},{7,3},{... | collective-permute-start | bytes 3538952 | tf_op jit(solution)/shard_map/ppermute | solution.py:180
  7.7 102.1 %collective-permute-start = (bf16[2,384,768]{2,1,0:T(8,128)(2,1)}, bf16[2,384,768]{2,1,0:T(8,128)(2,1)S(1)}, u32[]{:S(2)}, u32[]{:S(2)}) collective-permute-start(bf16[2,384,768]{2,1,0:T(8,128)(2,1)} %bitcast.24), channel_id=1, source_target_pairs={{0,16},{16,32},{32,48},{48,64},{64,80},{80,96},{96,112},{112,128},... | collective-permute-start | bytes 3538952 | tf_op jit(solution)/shard_map/ppermute | solution.py:177
  11.1 98.7 %collective-permute-start.1 = (bf16[2,384,768]{2,1,0:T(8,128)(2,1)}, bf16[2,384,768]{2,1,0:T(8,128)(2,1)S(1)}, u32[]{:S(2)}, u32[]{:S(2)}) collective-permute-start(bf16[2,384,768]{2,1,0:T(8,128)(2,1)} %bitcast.25), channel_id=1, source_target_pairs={{16,0},{32,16},{48,32},{64,48},{80,64},{96,80},{112,96},{128,112},... | collective-permute-start | bytes 3538952 | tf_op jit(solution)/shard_map/ppermute | solution.py:178
  13.3 32.2 %collective-permute-start.3 = (bf16[2,32,768]{2,1,0:T(8,128)(2,1)S(1)}, bf16[2,32,768]{2,1,0:T(8,128)(2,1)S(1)}, u32[]{:S(2)}, u32[]{:S(2)}) collective-permute-start(bf16[2,32,768]{2,1,0:T(8,128)(2,1)S(1)} %maximum_select_fusion.3), channel_id=1, source_target_pairs={{0,32},{16,48},{32,0},{48,16},{64,96},{80,112},{96,64},{112,80},{1... | collective-permute-start | bytes 294920 | tf_op jit(solution)/shard_map/ppermute | solution.py:36
  45.6 10.8 %collective-permute-start.4 = (bf16[2,64,768]{2,1,0:T(8,128)(2,1)S(1)}, bf16[2,64,768]{2,1,0:T(8,128)(2,1)S(1)}, u32[]{:S(2)}, u32[]{:S(2)}) collective-permute-start(bf16[2,64,768]{2,1,0:T(8,128)(2,1)S(1)} %maximum_select_fusion.2), channel_id=1, source_target_pairs={{0,64},{16,80},{32,96},{48,112},{64,0},{80,16},{96,32},{112,48},{1... | collective-permute-start | bytes 589832 | tf_op jit(solution)/shard_map/ppermute | solution.py:36
  56.5 34.1 %collective-permute-start.5 = (bf16[2,128,768]{2,1,0:T(8,128)(2,1)S(1)}, bf16[2,128,768]{2,1,0:T(8,128)(2,1)S(1)}, u32[]{:S(2)}, u32[]{:S(2)}) collective-permute-start(bf16[2,128,768]{2,1,0:T(8,128)(2,1)S(1)} %maximum_select_fusion.1), channel_id=1, source_target_pairs={{0,128},{16,144},{32,160},{48,176},{64,192},{80,208},{96,224},{112... | collective-permute-start | bytes 1179656 | tf_op jit(solution)/shard_map/ppermute | solution.py:36
  109.8 2.7 %copy-start.1 = (bf16[2,384,768]{2,1,0:T(8,128)(2,1)}, bf16[2,384,768]{2,1,0:T(8,128)(2,1)S(1)}, u32[]{:S(2)}) copy-start(bf16[2,384,768]{2,1,0:T(8,128)(2,1)S(1)} %collective-permute-done.rest_0_) | copy-start | bytes 3538948
  109.8 1.1 copy-start.2
  112.5 30.4 %collective-permute-start.8 = (bf16[2,2,384,768]{3,2,1,0:T(8,128)(2,1)}, bf16[2,2,384,768]{3,2,1,0:T(8,128)(2,1)S(1)}, u32[]{:S(2)}, u32[]{:S(2)}) collective-permute-start(bf16[2,2,384,768]{3,2,1,0:T(8,128)(2,1)} %pad_maximum_fusion), channel_id=1, source_target_pairs={{0,4},{4,8},{8,12},{1,5},{5,9},{9,13},{2,6},{6,10},{10,14},{3,7},{... | collective-permute-start | bytes 7077896 | tf_op jit(solution)/shard_map/ppermute | solution.py:196
  114.4 30.3 %collective-permute-start.9 = (bf16[2,2,384,768]{3,2,1,0:T(8,128)(2,1)}, bf16[2,2,384,768]{3,2,1,0:T(8,128)(2,1)}, u32[]{:S(2)}, u32[]{:S(2)}) collective-permute-start(bf16[2,2,384,768]{3,2,1,0:T(8,128)(2,1)} %pad_maximum_fusion), channel_id=1, source_target_pairs={{4,0},{8,4},{12,8},{5,1},{9,5},{13,9},{6,2},{10,6},{14,10},{7,3},{... | collective-permute-start | bytes 7077896 | tf_op jit(solution)/shard_map/ppermute | solution.py:197
  142.9 1.9 copy-start
  164.8 2.3 %copy-start.3 = (bf16[384,768]{1,0:T(8,128)(2,1)S(1)}, bf16[384,768]{1,0:T(8,128)(2,1)}, u32[]{:S(2)}) copy-start(bf16[384,768]{1,0:T(8,128)(2,1)} %shard_map.84) | copy-start | bytes 1769476
  167.0 14.3 %collective-permute-start.10 = (bf16[384,768]{1,0:T(8,128)(2,1)S(1)}, bf16[384,768]{1,0:T(8,128)(2,1)S(1)}, u32[]{:S(2)}, u32[]{:S(2)}) collective-permute-start(bf16[384,768]{1,0:T(8,128)(2,1)S(1)} %convolution_convert_fusion.2), channel_id=1, source_target_pairs={{0,2},{1,3},{2,0},{3,1},{4,6},{5,7},{6,4},{7,5},{8,10},{9,11},{10,... | collective-permute-start | bytes 1769480 | tf_op jit(solution)/shard_map/ppermute | solution.py:211
  169.8 17.7 %copy-start.6 = (bf16[1,1,384,768]{3,2,1,0:T(8,128)(2,1)S(1)}, bf16[1,1,384,768]{3,2,1,0:T(8,128)(2,1)}, u32[]{:S(2)}) copy-start(bf16[1,1,384,768]{3,2,1,0:T(8,128)(2,1)} %param.11) | copy-start | bytes 1769476
  169.8 17.7 %copy-start.7 = (f32[768]{0:T(1024)S(1)}, f32[768]{0:T(1024)}, u32[]{:S(2)}) copy-start(f32[768]{0:T(1024)} %param.13) | copy-start | bytes 9220
  169.8 17.7 %collective-permute-start.11 = (bf16[384,768]{1,0:T(8,128)(2,1)}, bf16[384,768]{1,0:T(8,128)(2,1)S(1)}, u32[]{:S(2)}, u32[]{:S(2)}) collective-permute-start(bf16[384,768]{1,0:T(8,128)(2,1)} %convolution_convert_fusion.1), channel_id=1, source_target_pairs={{0,1},{1,2},{2,3},{3,0},{4,5},{5,6},{6,7},{7,4},{8,9},{9,10},{10,1... | collective-permute-start | bytes 1769480 | tf_op jit(solution)/shard_map/ppermute | solution.py:211
  172.6 14.9 %collective-permute-start.12 = (bf16[384,768]{1,0:T(8,128)(2,1)}, bf16[384,768]{1,0:T(8,128)(2,1)S(1)}, u32[]{:S(2)}, u32[]{:S(2)}) collective-permute-start(bf16[384,768]{1,0:T(8,128)(2,1)} %convolution_convert_fusion), channel_id=1, source_target_pairs={{0,3},{1,0},{2,1},{3,2},{4,7},{5,4},{6,5},{7,6},{8,11},{9,8},{10,9... | collective-permute-start | bytes 1769480 | tf_op jit(solution)/shard_map/ppermute | solution.py:211

commit v4 on v3

--- a/solution.py
+++ b/solution.py
@@ -13,6 +13,7 @@
 TILE_R = 8
 TILE_C = 8
 NEG = -1e30
+OFFLOAD_BYTES = 1 << 20
 
 
 def token_masks(extent_pair):
@@ -29,16 +30,13 @@
 
 
 def gather_text(text_kv, devices):
-    position = lax.axis_index("tm")
-    gathered = text_kv
-    step = 1
-    while step < devices:
-        other = lax.ppermute(gathered, "tm", [(i, i ^ step) for i in range(devices)])
-        low_first = jnp.concatenate([gathered, other], axis=1)
-        high_first = jnp.concatenate([other, gathered], axis=1)
-        gathered = jnp.where((position & step) == 0, low_first, high_first)
-        step *= 2
-    return gathered
+    tokens = text_kv.shape[1]
+    shard_bytes = 2 * text_kv.shape[2] * text_kv.dtype.itemsize
+    padded = max(tokens, -(-OFFLOAD_BYTES // (devices * shard_bytes)))
+    padded = -(-padded // 2) * 2
+    grown = jnp.pad(text_kv, ((0, 0), (0, padded - tokens), (0, 0)))
+    gathered = lax.all_gather(grown, "tm", axis=0)[:, :, :tokens]
+    return jnp.transpose(gathered, (1, 0, 2, 3)).reshape(2, -1, text_kv.shape[2])
 
 
 def make_kernel(blocks, has_text, has_state, final):

time: 188 us -> 222 us (1.18)
  the two profiles are of different devices: /device:TPU:2 before, /device:TPU:1 now
where the time goes in v4:
time: 222 us; the launch traced here: 219 us
  waiting for transfers between devices  111 us (50%)
  Pallas kernels  47.8 us (22%)
  starting transfers between devices  23.4 us (11%)
  between operations  13.6 us (6%)
  matrix products  10.5 us (5%)
  local copies, waits for them, and re-layouts  9.16 us (4%)
  other arithmetic  3.61 us (2%)
    all_gather x1, waiting for transfers between devices, gather_text(): gathered = lax.all_gather(grown, 'tm', axis=0)[:, :, :tokens]  89.3 us
    pallas_call x3, Pallas kernels, attend(): pl.pallas_call(kernel, grid_spec=grid_spec, out_shape=out_shape)  47.8 us
    ppermute x3, waiting for transfers between devices, per_device(): received.append(lax.ppermute(part, 'mp', pairs))  9.25 us
    ppermute x1, waiting for transfers between devices, per_device(): c_before = lax.ppermute(time_pair, 'height', shift_pairs(height_size, 1))  8.08 us
    dot_general x3, matrix products, per_device(): jnp.dot(attended, w_part, preferred_element_type=jnp.float32)  7.58 us
    ppermute x1, starting transfers between devices, per_device(): c_before = lax.ppermute(time_pair, 'height', shift_pairs(height_size, 1))  6.48 us
    ppermute x1, starting transfers between devices, per_device(): h_before = lax.ppermute(own, 'height', shift_pairs(height_size, 1))  4.51 us
  transfers between devices with their start and end apart: 10, of which 5 were waited for; matrix products, arithmetic and copies ran while one was open for 6% of the time, Pallas kernels for 13%

profile of v4, /device:TPU:1, one launch (start us, length us, event | category | flops | bytes accessed | tf_op | source)
XLA Modules:
  0.0 219.1 jit_solution(927035559848649143)
XLA Ops:
  6.5 0.0 all-gather.3.cloned.1.call-start
  6.5 1.4 pad.8
  8.0 0.0 all-gather.3.cloned.1.call-update
  8.0 4.5 %collective-permute-start.2 = (bf16[2,384,768]{2,1,0:T(8,128)(2,1)}, bf16[2,384,768]{2,1,0:T(8,128)(2,1)}, u32[]{:S(2)}, u32[]{:S(2)}) collective-permute-start(bf16[2,384,768]{2,1,0:T(8,128)(2,1)} %bitcast.27), channel_id=1, source_target_pairs={{0,4},{4,8},{8,12},{1,5},{5,9},{9,13},{2,6},{6,10},{10,14},{3,7},{... | collective-permute-start | bytes 3538952 | tf_op jit(solution)/shard_map/ppermute | solution.py:177
  12.5 3.0 %collective-permute-start.3 = (bf16[2,384,768]{2,1,0:T(8,128)(2,1)}, bf16[2,384,768]{2,1,0:T(8,128)(2,1)}, u32[]{:S(2)}, u32[]{:S(2)}) collective-permute-start(bf16[2,384,768]{2,1,0:T(8,128)(2,1)} %bitcast.28), channel_id=1, source_target_pairs={{4,0},{8,4},{12,8},{5,1},{9,5},{13,9},{6,2},{10,6},{14,10},{7,3},{... | collective-permute-start | bytes 3538952 | tf_op jit(solution)/shard_map/ppermute | solution.py:178
  15.5 3.4 %collective-permute-start = (bf16[2,384,768]{2,1,0:T(8,128)(2,1)}, bf16[2,384,768]{2,1,0:T(8,128)(2,1)S(1)}, u32[]{:S(2)}, u32[]{:S(2)}) collective-permute-start(bf16[2,384,768]{2,1,0:T(8,128)(2,1)} %bitcast.29), channel_id=1, source_target_pairs={{0,16},{16,32},{32,48},{48,64},{64,80},{80,96},{96,112},{112,128},... | collective-permute-start | bytes 3538952 | tf_op jit(solution)/shard_map/ppermute | solution.py:175
  18.9 1.3 collective-permute-start.1
  20.2 0.8 pad_dynamic-slice_fusion
  21.0 0.1 copy.27
  21.1 0.1 lt.103
  21.2 0.1 copy.28
  21.3 0.1 lt.108
  21.4 1.4 copy.33.reach_ref
  22.7 0.7 and_select_fusion.rest_4_.rest_2_
  23.4 89.3 %all-gather.3.cloned.1.call-done = bf16[32,22,768]{2,1,0:T(8,128)(2,1)} async-done(((bf16[2,22,768]{2,1,0:T(8,128)(2,1)}), bf16[32,22,768]{2,1,0:T(8,128)(2,1)}) %all-gather.3.cloned.1.call-update) | async-done | bytes 1081360 | tf_op jit(solution)/shard_map/all_gather | solution.py:38
  112.8 1.2 slice.16
  114.0 0.9 copy.35
  114.9 0.0 collective-permute-done.2.rest_2_
  114.9 0.0 collective-permute-done.3.rest_3_
  114.9 16.7 %shard_map.82 = (f32[6,384,1]{2,1,0:T(8,128)}, f32[6,384,1]{2,1,0:T(8,128)}, f32[384,768]{1,0:T(8,128)}) custom-call(s32[6,2]{1,0:T(8,128)} %copy.33.reach_ref, bf16[384,768]{1,0:T(8,128)(2,1)} %bitcast.21, bf16[2,256,768]{2,1,0:T(8,128)(2,1)} %bitcast.26, bf16[2,384,768]{2,1,0:T(8,128)(2,1)} %bitcast.31, ...), custom_call_target="tpu_custom_call" | custom-call | tf_op jit(solution)/shard_map/pallas_call | solution.py:164
  131.6 0.0 collective-permute-done.rest_0_
  131.6 0.0 copy-start.1
  131.6 0.0 collective-permute-done.1.rest_1_
  131.6 0.0 copy-start.2
  131.6 1.0 copy-done.2
  132.6 1.6 pad_maximum_fusion
  134.3 0.0 copy-done.1
  134.3 6.5 %collective-permute-start.4 = (bf16[2,2,384,768]{3,2,1,0:T(8,128)(2,1)}, bf16[2,2,384,768]{3,2,1,0:T(8,128)(2,1)S(1)}, u32[]{:S(2)}, u32[]{:S(2)}) collective-permute-start(bf16[2,2,384,768]{3,2,1,0:T(8,128)(2,1)} %pad_maximum_fusion), channel_id=1, source_target_pairs={{0,4},{4,8},{8,12},{1,5},{5,9},{9,13},{2,6},{6,10},{10,14},{3,7},{... | collective-permute-start | bytes 7077896 | tf_op jit(solution)/shard_map/ppermute | solution.py:194
  140.8 1.9 collective-permute-start.5
  142.7 0.6 slice.17
  143.4 0.6 slice.18
  144.0 1.3 fusion.18
  145.2 0.8 copy.34.rest_8_
  146.1 12.7 %shard_map.83 = (f32[6,384,1]{2,1,0:T(8,128)}, f32[6,384,1]{2,1,0:T(8,128)}, f32[384,768]{1,0:T(8,128)}) custom-call(s32[6,2]{1,0:T(8,128)} %copy.33.reach_ref, bf16[384,768]{1,0:T(8,128)(2,1)} %bitcast.22, bf16[2,384,768]{2,1,0:T(8,128)(2,1)} %copy-done.1, bf16[2,384,768]{2,1,0:T(8,128)(2,1)} %copy-done.2, f32[9,1,384]{2,1,0:T(1,128)} %and_select_fusion.rest_4_.rest_2_, ...), custom_call_target="tpu_custom_call" | custom-call | tf_op jit(solution)/shard_map/pallas_call | solution.py:164
  158.8 8.1 %collective-permute-done.4.rest_0_.rest_2_ = bf16[2,2,384,768]{3,2,1,0:T(8,128)(2,1)S(1)} collective-permute-done((bf16[2,2,384,768]{3,2,1,0:T(8,128)(2,1)}, bf16[2,2,384,768]{3,2,1,0:T(8,128)(2,1)S(1)}, u32[]{:S(2)}, u32[]{:S(2)}) %collective-permute-start.4) | collective-permute-done | bytes 2359328 | tf_op jit(solution)/shard_map/ppermute | solution.py:194
  166.8 0.0 copy-start
  166.8 4.4 %collective-permute-done.5.rest_1_.rest_3_ = bf16[2,2,384,768]{3,2,1,0:T(8,128)(2,1)} collective-permute-done((bf16[2,2,384,768]{3,2,1,0:T(8,128)(2,1)}, bf16[2,2,384,768]{3,2,1,0:T(8,128)(2,1)}, u32[]{:S(2)}, u32[]{:S(2)}) %collective-permute-start.5) | collective-permute-done | bytes 2359328 | tf_op jit(solution)/shard_map/ppermute | solution.py:195
  171.2 0.0 copy-done
  171.2 18.4 %shard_map.84 = bf16[384,768]{1,0:T(8,128)(2,1)} custom-call(s32[6,2]{1,0:T(8,128)} %copy.33.reach_ref, bf16[384,768]{1,0:T(8,128)(2,1)} %bitcast.23, bf16[2,2,384,768]{3,2,1,0:T(8,128)(2,1)} %copy-done, bf16[2,2,384,768]{3,2,1,0:T(8,128)(2,1)} %collective-permute-done.5.rest_1_.rest_3_, bf16[2,2,384,768]{3,2,1,0:T(8,128)(2,1)} %copy-done, ...), custom_call_target="tpu_custom_call" | custom-call | tf_op jit(solution)/shard_map/pallas_call | solution.py:164
  189.7 0.0 copy-start.3
  189.7 2.1 convolution_convert_fusion.2
  191.8 0.1 collective-permute-start.6
  191.9 0.0 copy-done.3
  191.9 2.7 %convolution_convert_fusion.1 = bf16[384,768]{1,0:T(8,128)(2,1)} fusion(bf16[384,768]{1,0:T(8,128)(2,1)S(1)} %copy-done.3, bf16[768,3072]{1,0:T(8,128)(2,1)} %param.12, s32[]{:T(128)S(6)} %select_n.86), kind=kOutput, calls=%fused_computation.2 | convolution fusion | flops 453279744 | bytes 2359300 | tf_op jit(solution)/shard_map/dot_general | solution.py:207
  194.7 0.0 copy-start.4
  194.7 0.0 copy-start.5
  194.7 0.3 collective-permute-start.7
  195.0 2.7 %convolution_convert_fusion = bf16[384,768]{1,0:T(8,128)(2,1)} fusion(bf16[384,768]{1,0:T(8,128)(2,1)S(1)} %copy-done.3, bf16[768,3072]{1,0:T(8,128)(2,1)} %param.12, s32[]{:T(128)S(6)} %select_n.88), kind=kOutput, calls=%fused_computation.1 | convolution fusion | flops 453279744 | bytes 2359300 | tf_op jit(solution)/shard_map/dot_general | solution.py:207
  197.7 2.4 %collective-permute-start.8 = (bf16[384,768]{1,0:T(8,128)(2,1)}, bf16[384,768]{1,0:T(8,128)(2,1)S(1)}, u32[]{:S(2)}, u32[]{:S(2)}) collective-permute-start(bf16[384,768]{1,0:T(8,128)(2,1)} %convolution_convert_fusion), channel_id=1, source_target_pairs={{0,3},{1,0},{2,1},{3,2},{4,7},{5,4},{6,5},{7,6},{8,11},{9,8},{10,9... | collective-permute-start | bytes 1769480 | tf_op jit(solution)/shard_map/ppermute | solution.py:209
  200.1 3.0 %collective-permute-done.6 = bf16[384,768]{1,0:T(8,128)(2,1)S(1)} collective-permute-done((bf16[384,768]{1,0:T(8,128)(2,1)S(1)}, bf16[384,768]{1,0:T(8,128)(2,1)S(1)}, u32[]{:S(2)}, u32[]{:S(2)}) %collective-permute-start.6) | collective-permute-done | bytes 589856 | tf_op jit(solution)/shard_map/ppermute | solution.py:209
  203.1 6.2 %collective-permute-done.7 = bf16[384,768]{1,0:T(8,128)(2,1)S(1)} collective-permute-done((bf16[384,768]{1,0:T(8,128)(2,1)}, bf16[384,768]{1,0:T(8,128)(2,1)S(1)}, u32[]{:S(2)}, u32[]{:S(2)}) %collective-permute-start.7) | collective-permute-done | bytes 589856 | tf_op jit(solution)/shard_map/ppermute | solution.py:209
  209.3 0.0 collective-permute-done.8
  209.3 0.0 copy-done.4
  209.3 0.0 copy-done.5
  209.3 2.9 %fusion.7 = bf16[1,1,384,768]{3,2,1,0:T(8,128)(2,1)} fusion(bf16[384,768]{1,0:T(8,128)(2,1)S(1)} %copy-done.3, bf16[384,768]{1,0:T(8,128)(2,1)S(1)} %collective-permute-done.8, bf16[384,768]{1,0:T(8,128)(2,1)S(1)} %collective-permute-done.7, bf16[384,768]{1,0:T(8,128)(2,1)S(1)} %collective-permute-done.6, bf16[768,3072]{1,0:T(8,128)(2,1)} %param.12, ...), kind=kOutput, calls=%fused_computation.12 | convolution fusion | flops 456523776 | bytes 4721668 | tf_op jit(solution)/shard_map/dot_general | solution.py:211
  (1 shorter events, 0.0 us)
Async XLA Ops:
  6.5 106.2 %all-gather.3.cloned.1.call-start = ((), (), s32[]{:S(2)}) async-start(), calls=%async_computation | async-start | bytes 1253376 | tf_op jit(solution)/shard_map/all_gather | solution.py:38
  8.0 106.9 %collective-permute-start.2 = (bf16[2,384,768]{2,1,0:T(8,128)(2,1)}, bf16[2,384,768]{2,1,0:T(8,128)(2,1)}, u32[]{:S(2)}, u32[]{:S(2)}) collective-permute-start(bf16[2,384,768]{2,1,0:T(8,128)(2,1)} %bitcast.27), channel_id=1, source_target_pairs={{0,4},{4,8},{8,12},{1,5},{5,9},{9,13},{2,6},{6,10},{10,14},{3,7},{... | collective-permute-start | bytes 3538952 | tf_op jit(solution)/shard_map/ppermute | solution.py:177
  12.5 102.4 %collective-permute-start.3 = (bf16[2,384,768]{2,1,0:T(8,128)(2,1)}, bf16[2,384,768]{2,1,0:T(8,128)(2,1)}, u32[]{:S(2)}, u32[]{:S(2)}) collective-permute-start(bf16[2,384,768]{2,1,0:T(8,128)(2,1)} %bitcast.28), channel_id=1, source_target_pairs={{4,0},{8,4},{12,8},{5,1},{9,5},{13,9},{6,2},{10,6},{14,10},{7,3},{... | collective-permute-start | bytes 3538952 | tf_op jit(solution)/shard_map/ppermute | solution.py:178
  15.5 116.1 %collective-permute-start = (bf16[2,384,768]{2,1,0:T(8,128)(2,1)}, bf16[2,384,768]{2,1,0:T(8,128)(2,1)S(1)}, u32[]{:S(2)}, u32[]{:S(2)}) collective-permute-start(bf16[2,384,768]{2,1,0:T(8,128)(2,1)} %bitcast.29), channel_id=1, source_target_pairs={{0,16},{16,32},{32,48},{48,64},{64,80},{80,96},{96,112},{112,128},... | collective-permute-start | bytes 3538952 | tf_op jit(solution)/shard_map/ppermute | solution.py:175
  18.9 112.7 %collective-permute-start.1 = (bf16[2,384,768]{2,1,0:T(8,128)(2,1)}, bf16[2,384,768]{2,1,0:T(8,128)(2,1)S(1)}, u32[]{:S(2)}, u32[]{:S(2)}) collective-permute-start(bf16[2,384,768]{2,1,0:T(8,128)(2,1)} %bitcast.30), channel_id=1, source_target_pairs={{16,0},{32,16},{48,32},{64,48},{80,64},{96,80},{112,96},{128,112},... | collective-permute-start | bytes 3538952 | tf_op jit(solution)/shard_map/ppermute | solution.py:176
  131.6 2.7 %copy-start.1 = (bf16[2,384,768]{2,1,0:T(8,128)(2,1)}, bf16[2,384,768]{2,1,0:T(8,128)(2,1)S(1)}, u32[]{:S(2)}) copy-start(bf16[2,384,768]{2,1,0:T(8,128)(2,1)S(1)} %collective-permute-done.rest_0_) | copy-start | bytes 3538948
  131.6 1.0 copy-start.2
  134.3 32.6 %collective-permute-start.4 = (bf16[2,2,384,768]{3,2,1,0:T(8,128)(2,1)}, bf16[2,2,384,768]{3,2,1,0:T(8,128)(2,1)S(1)}, u32[]{:S(2)}, u32[]{:S(2)}) collective-permute-start(bf16[2,2,384,768]{3,2,1,0:T(8,128)(2,1)} %pad_maximum_fusion), channel_id=1, source_target_pairs={{0,4},{4,8},{8,12},{1,5},{5,9},{9,13},{2,6},{6,10},{10,14},{3,7},{... | collective-permute-start | bytes 7077896 | tf_op jit(solution)/shard_map/ppermute | solution.py:194
  140.8 30.5 %collective-permute-start.5 = (bf16[2,2,384,768]{3,2,1,0:T(8,128)(2,1)}, bf16[2,2,384,768]{3,2,1,0:T(8,128)(2,1)}, u32[]{:S(2)}, u32[]{:S(2)}) collective-permute-start(bf16[2,2,384,768]{3,2,1,0:T(8,128)(2,1)} %pad_maximum_fusion), channel_id=1, source_target_pairs={{4,0},{8,4},{12,8},{5,1},{9,5},{13,9},{6,2},{10,6},{14,10},{7,3},{... | collective-permute-start | bytes 7077896 | tf_op jit(solution)/shard_map/ppermute | solution.py:195
  166.8 4.4 %copy-start = (bf16[2,2,384,768]{3,2,1,0:T(8,128)(2,1)}, bf16[2,2,384,768]{3,2,1,0:T(8,128)(2,1)S(1)}, u32[]{:S(2)}) copy-start(bf16[2,2,384,768]{3,2,1,0:T(8,128)(2,1)S(1)} %collective-permute-done.4.rest_0_.rest_2_) | copy-start | bytes 7077892
  189.7 2.3 %copy-start.3 = (bf16[384,768]{1,0:T(8,128)(2,1)S(1)}, bf16[384,768]{1,0:T(8,128)(2,1)}, u32[]{:S(2)}) copy-start(bf16[384,768]{1,0:T(8,128)(2,1)} %shard_map.84) | copy-start | bytes 1769476
  191.8 11.3 %collective-permute-start.6 = (bf16[384,768]{1,0:T(8,128)(2,1)S(1)}, bf16[384,768]{1,0:T(8,128)(2,1)S(1)}, u32[]{:S(2)}, u32[]{:S(2)}) collective-permute-start(bf16[384,768]{1,0:T(8,128)(2,1)S(1)} %convolution_convert_fusion.2), channel_id=1, source_target_pairs={{0,2},{1,3},{2,0},{3,1},{4,6},{5,7},{6,4},{7,5},{8,10},{9,11},{10,... | collective-permute-start | bytes 1769480 | tf_op jit(solution)/shard_map/ppermute | solution.py:209
  194.7 14.7 %copy-start.4 = (bf16[1,1,384,768]{3,2,1,0:T(8,128)(2,1)S(1)}, bf16[1,1,384,768]{3,2,1,0:T(8,128)(2,1)}, u32[]{:S(2)}) copy-start(bf16[1,1,384,768]{3,2,1,0:T(8,128)(2,1)} %param.11) | copy-start | bytes 1769476
  194.7 14.7 %copy-start.5 = (f32[768]{0:T(1024)S(1)}, f32[768]{0:T(1024)}, u32[]{:S(2)}) copy-start(f32[768]{0:T(1024)} %param.13) | copy-start | bytes 9220
  194.7 14.6 %collective-permute-start.7 = (bf16[384,768]{1,0:T(8,128)(2,1)}, bf16[384,768]{1,0:T(8,128)(2,1)S(1)}, u32[]{:S(2)}, u32[]{:S(2)}) collective-permute-start(bf16[384,768]{1,0:T(8,128)(2,1)} %convolution_convert_fusion.1), channel_id=1, source_target_pairs={{0,1},{1,2},{2,3},{3,0},{4,5},{5,6},{6,7},{7,4},{8,9},{9,10},{10,1... | collective-permute-start | bytes 1769480 | tf_op jit(solution)/shard_map/ppermute | solution.py:209
  197.7 11.6 %collective-permute-start.8 = (bf16[384,768]{1,0:T(8,128)(2,1)}, bf16[384,768]{1,0:T(8,128)(2,1)S(1)}, u32[]{:S(2)}, u32[]{:S(2)}) collective-permute-start(bf16[384,768]{1,0:T(8,128)(2,1)} %convolution_convert_fusion), channel_id=1, source_target_pairs={{0,3},{1,0},{2,1},{3,2},{4,7},{5,4},{6,5},{7,6},{8,11},{9,8},{10,9... | collective-permute-start | bytes 1769480 | tf_op jit(solution)/shard_map/ppermute | solution.py:209
Sparse Core Ops, SparseCore 0:
  9.9 102.7 all-gather.2

commit v5 on v2

--- a/solution.py
+++ b/solution.py
@@ -28,17 +28,26 @@
     return [(i, i + step) for i in range(devices) if 0 <= i + step < devices]
 
 
-def gather_text(text_kv, devices):
-    position = lax.axis_index("tm")
-    gathered = text_kv
-    step = 1
-    while step < devices:
-        other = lax.ppermute(gathered, "tm", [(i, i ^ step) for i in range(devices)])
-        low_first = jnp.concatenate([gathered, other], axis=1)
-        high_first = jnp.concatenate([other, gathered], axis=1)
-        gathered = jnp.where((position & step) == 0, low_first, high_first)
-        step *= 2
-    return gathered
+def text_halves(text_kv):
+    half_width = text_kv.shape[2] // 2
+    half = lax.axis_index("height") % 2
+    return lax.dynamic_slice_in_dim(text_kv, half * half_width, half_width, 2)
+
+
+def exchange(block, devices, steps):
+    parts = [block]
+    for step in steps:
+        parts.append(lax.ppermute(block, "tm", [(i, i ^ step) for i in range(devices)]))
+    return jnp.concatenate(parts, axis=1)
+
+
+def join_halves(mine):
+    half = lax.axis_index("height") % 2
+    pairs = [(i, i ^ 1) for i in range(lax.axis_size("height"))]
+    other = lax.ppermute(mine, "height", pairs)
+    low_first = jnp.concatenate([mine, other], axis=2)
+    high_first = jnp.concatenate([other, mine], axis=2)
+    return jnp.where(half == 0, low_first, high_first)
 
 
 def make_kernel(blocks, has_text, has_state, final):
@@ -178,7 +187,7 @@
     t_after = lax.ppermute(own, "tm", shift_pairs(tm_size, -1))
     h_before = lax.ppermute(own, "height", shift_pairs(height_size, 1))
     h_after = lax.ppermute(own, "height", shift_pairs(height_size, -1))
-    text = gather_text(text_kv, tm_size)
+    text_group = exchange(text_halves(text_kv), tm_size, (1, 2, 3))
     time_start = lax.axis_index("tm")
     height_start = lax.axis_index("height")
     zero_index = jnp.int32(0)
@@ -191,6 +200,8 @@
     queries = image_q[0, 0]
     near = [(own, None, 4), (h_before, None, 3), (h_after, None, 5)]
     state = attend(head_reach, queries, None, near, bias)
+    text_group, state = lax.optimization_barrier((text_group, state))
+    text = join_halves(exchange(text_group, tm_size, (4, 8, 12)))
     t_before, t_after, state = lax.optimization_barrier((t_before, t_after, state))
     time_pair = jnp.stack([t_before, t_after])
     c_before = lax.ppermute(time_pair, "height", shift_pairs(height_size, 1))

time: 202 us -> 199 us (0.985)
  the two profiles are of different devices: /device:TPU:18 before, /device:TPU:35 now
where the time goes in v5:
time: 199 us; the launch traced here: 197 us
  waiting for transfers between devices  82.4 us (41%)
  starting transfers between devices  50.4 us (25%)
  Pallas kernels  41 us (21%)
  matrix products  10.8 us (5%)
  local copies, waits for them, and re-layouts  7.41 us (4%)
  other arithmetic  4.69 us (2%)
    ppermute x6, waiting for transfers between devices, exchange(): lax.ppermute(block, 'tm', [(i, i ^ step) for i in range(devices)])  64 us
    pallas_call x3, Pallas kernels, attend(): pl.pallas_call(kernel, grid_spec=grid_spec, out_shape=out_shape)  41 us
    ppermute x3, waiting for transfers between devices, per_device(): received.append(lax.ppermute(part, 'mp', pairs))  18.3 us
    ppermute x1, starting transfers between devices, per_device(): c_after = lax.ppermute(time_pair, 'height', shift_pairs(height_size, -1))  16 us
    ppermute x3, starting transfers between devices, per_device(): received.append(lax.ppermute(part, 'mp', pairs))  10.1 us
    ppermute x6, starting transfers between devices, exchange(): lax.ppermute(block, 'tm', [(i, i ^ step) for i in range(devices)])  8.81 us
    dot_general x3, matrix products, per_device(): jnp.dot(attended, w_part, preferred_element_type=jnp.float32)  7.66 us
    unnamed x18, local copies, waits for them, and re-layouts  4.24 us
  transfers between devices with their start and end apart: 16, of which 7 were waited for; matrix products, arithmetic and copies ran while one was open for 7% of the time, Pallas kernels for 14%

profile of v5, /device:TPU:35, one launch (start us, length us, event | category | flops | bytes accessed | tf_op | source)
XLA Modules:
  0.0 196.9 jit_solution(13237809321464412963)
XLA Ops:
  0.0 0.0 copy-start
  0.0 1.4 collective-permute-start.5
  1.4 4.2 %collective-permute-start.6 = (bf16[2,384,768]{2,1,0:T(8,128)(2,1)}, bf16[2,384,768]{2,1,0:T(8,128)(2,1)}, u32[]{:S(2)}, u32[]{:S(2)}) collective-permute-start(bf16[2,384,768]{2,1,0:T(8,128)(2,1)} %bitcast.23), channel_id=1, source_target_pairs={{4,0},{8,4},{12,8},{5,1},{9,5},{13,9},{6,2},{10,6},{14,10},{7,3},{... | collective-permute-start | bytes 3538952 | tf_op jit(solution)/shard_map/ppermute | solution.py:189
  5.7 3.7 %collective-permute-start = (bf16[2,384,768]{2,1,0:T(8,128)(2,1)}, bf16[2,384,768]{2,1,0:T(8,128)(2,1)S(1)}, u32[]{:S(2)}, u32[]{:S(2)}) collective-permute-start(bf16[2,384,768]{2,1,0:T(8,128)(2,1)} %bitcast.24), channel_id=1, source_target_pairs={{0,16},{16,32},{32,48},{48,64},{64,80},{80,96},{96,112},{112,128},... | collective-permute-start | bytes 3538952 | tf_op jit(solution)/shard_map/ppermute | solution.py:186
  9.4 3.9 %collective-permute-start.1 = (bf16[2,384,768]{2,1,0:T(8,128)(2,1)}, bf16[2,384,768]{2,1,0:T(8,128)(2,1)S(1)}, u32[]{:S(2)}, u32[]{:S(2)}) collective-permute-start(bf16[2,384,768]{2,1,0:T(8,128)(2,1)} %bitcast.25), channel_id=1, source_target_pairs={{16,0},{32,16},{48,32},{64,48},{80,64},{96,80},{112,96},{128,112},... | collective-permute-start | bytes 3538952 | tf_op jit(solution)/shard_map/ppermute | solution.py:187
  13.4 0.0 copy-done
  13.4 1.0 collective-permute-start.2
  14.4 49.7 %collective-permute-done.2 = bf16[2,16,384]{2,1,0:T(8,128)(2,1)S(1)} collective-permute-done((bf16[2,16,384]{2,1,0:T(8,128)(2,1)S(1)}, bf16[2,16,384]{2,1,0:T(8,128)(2,1)S(1)}, u32[]{:S(2)}, u32[]{:S(2)}) %collective-permute-start.2) | collective-permute-done | bytes 24608 | tf_op jit(solution)/shard_map/ppermute | solution.py:40
  64.1 0.0 collective-permute-start.3
  64.1 0.8 pad_dynamic-slice_fusion
  64.9 0.1 copy.16
  65.0 0.1 lt.111
  65.1 0.1 copy.17
  65.2 0.1 lt.116
  65.3 1.8 collective-permute-done.3
  67.1 0.6 collective-permute-start.4
  67.7 0.7 and_select_fusion.rest_3_.rest_4_
  68.3 1.4 copy.22.reach_ref
  69.7 2.6 %collective-permute-done.4 = bf16[2,16,384]{2,1,0:T(8,128)(2,1)S(1)} collective-permute-done((bf16[2,16,384]{2,1,0:T(8,128)(2,1)S(1)}, bf16[2,16,384]{2,1,0:T(8,128)(2,1)S(1)}, u32[]{:S(2)}, u32[]{:S(2)}) %collective-permute-start.4) | collective-permute-done | bytes 24608 | tf_op jit(solution)/shard_map/ppermute | solution.py:40
  72.3 0.0 collective-permute-done.5.rest_1_
  72.3 0.0 collective-permute-done.6.rest_2_
  72.3 15.0 %shard_map.82 = (f32[6,384,1]{2,1,0:T(8,128)}, f32[6,384,1]{2,1,0:T(8,128)}, f32[384,768]{1,0:T(8,128)}) custom-call(s32[6,2]{1,0:T(8,128)} %copy.22.reach_ref, bf16[384,768]{1,0:T(8,128)(2,1)} %bitcast.17, bf16[2,384,768]{2,1,0:T(8,128)(2,1)} %bitcast.26, bf16[2,384,768]{2,1,0:T(8,128)(2,1)} %collective-permute-done.5.rest_1_, ...), custom_call_target="tpu_custom_call" | custom-call | tf_op jit(solution)/shard_map/pallas_call | solution.py:175
  87.3 0.0 collective-permute-done.rest_1_
  87.3 0.0 copy-start.2
  87.3 0.0 collective-permute-done.1.rest_2_
  87.3 0.0 copy-start.3
  87.3 1.1 copy-done.2
  88.4 0.4 copy-done.3
  88.8 1.6 pad_maximum_fusion
  90.4 1.3 collective-permute-start.7
  91.7 16.0 %collective-permute-start.8 = (bf16[2,2,384,768]{3,2,1,0:T(8,128)(2,1)}, bf16[2,2,384,768]{3,2,1,0:T(8,128)(2,1)}, u32[]{:S(2)}, u32[]{:S(2)}) collective-permute-start(bf16[2,2,384,768]{3,2,1,0:T(8,128)(2,1)} %pad_maximum_fusion), channel_id=1, source_target_pairs={{4,0},{8,4},{12,8},{5,1},{9,5},{13,9},{6,2},{10,6},{14,10},{7,3},{... | collective-permute-start | bytes 7077896 | tf_op jit(solution)/shard_map/ppermute | solution.py:208
  107.7 3.0 %collective-permute-start.9 = (bf16[2,64,384]{2,1,0:T(8,128)(2,1)S(1)}, bf16[2,64,384]{2,1,0:T(8,128)(2,1)S(1)}, u32[]{:S(2)}, u32[]{:S(2)}) collective-permute-start(bf16[2,64,384]{2,1,0:T(8,128)(2,1)S(1)} %pad_maximum_fusion.1), channel_id=1, source_target_pairs={{0,64},{16,80},{32,96},{48,112},{64,0},{80,16},{96,32},{112,48},{1... | collective-permute-start | bytes 294920 | tf_op jit(solution)/shard_map/ppermute | solution.py:40
  110.7 4.2 %collective-permute-start.10 = (bf16[2,64,384]{2,1,0:T(8,128)(2,1)S(1)}, bf16[2,64,384]{2,1,0:T(8,128)(2,1)S(1)}, u32[]{:S(2)}, u32[]{:S(2)}) collective-permute-start(bf16[2,64,384]{2,1,0:T(8,128)(2,1)S(1)} %pad_maximum_fusion.1), channel_id=1, source_target_pairs={{0,128},{16,144},{32,160},{48,176},{64,192},{80,208},{96,224},{112... | collective-permute-start | bytes 294920 | tf_op jit(solution)/shard_map/ppermute | solution.py:40
  114.9 0.0 collective-permute-start.11
  114.9 0.0 collective-permute-done.9
  114.9 3.2 %collective-permute-done.10 = bf16[2,64,384]{2,1,0:T(8,128)(2,1)S(1)} collective-permute-done((bf16[2,64,384]{2,1,0:T(8,128)(2,1)S(1)}, bf16[2,64,384]{2,1,0:T(8,128)(2,1)S(1)}, u32[]{:S(2)}, u32[]{:S(2)}) %collective-permute-start.10) | collective-permute-done | bytes 98336 | tf_op jit(solution)/shard_map/ppermute | solution.py:40
  118.2 6.7 %collective-permute-done.11 = bf16[2,64,384]{2,1,0:T(8,128)(2,1)S(1)} collective-permute-done((bf16[2,64,384]{2,1,0:T(8,128)(2,1)S(1)}, bf16[2,64,384]{2,1,0:T(8,128)(2,1)S(1)}, u32[]{:S(2)}, u32[]{:S(2)}) %collective-permute-start.11) | collective-permute-done | bytes 98336 | tf_op jit(solution)/shard_map/ppermute | solution.py:40
  124.9 0.9 collective-permute-start.12
  125.8 0.6 slice.12
  126.4 0.6 slice.13
  126.9 1.3 fusion.18
  128.2 0.8 copy.23.rest_8_
  129.1 0.0 collective-permute-done.12
  129.1 1.1 maximum_select_fusion.rest_0_
  130.1 13.4 %shard_map.83 = (f32[6,384,1]{2,1,0:T(8,128)}, f32[6,384,1]{2,1,0:T(8,128)}, f32[384,768]{1,0:T(8,128)}) custom-call(s32[6,2]{1,0:T(8,128)} %copy.22.reach_ref, bf16[384,768]{1,0:T(8,128)(2,1)} %bitcast.18, bf16[2,256,768]{2,1,0:T(8,128)(2,1)} %maximum_select_fusion.rest_0_, bf16[2,384,768]{2,1,0:T(8,128)(2,1)} %copy-done.2, bf16[2,384,768]{2,1,0:T(8,128)(2,1)} %copy-done.3, ...), custom_call_target="tpu_custom_call" | custom-call | tf_op jit(solution)/shard_map/pallas_call | solution.py:175
  143.5 0.0 collective-permute-done.7.rest_0_.rest_2_
  143.5 0.0 copy-start.1
  143.5 0.0 collective-permute-done.8.rest_1_.rest_3_
  143.5 1.4 copy-done.1
  144.9 12.7 %shard_map.84 = bf16[384,768]{1,0:T(8,128)(2,1)} custom-call(s32[6,2]{1,0:T(8,128)} %copy.22.reach_ref, bf16[384,768]{1,0:T(8,128)(2,1)} %bitcast.19, bf16[2,2,384,768]{3,2,1,0:T(8,128)(2,1)} %copy-done.1, bf16[2,2,384,768]{3,2,1,0:T(8,128)(2,1)} %collective-permute-done.8.rest_1_.rest_3_, bf16[2,2,384,768]{3,2,1,0:T(8,128)(2,1)} %copy-done.1, ...), custom_call_target="tpu_custom_call" | custom-call | tf_op jit(solution)/shard_map/pallas_call | solution.py:175
  157.6 0.0 copy-start.4
  157.6 2.1 %convolution_convert_fusion.2 = bf16[384,768]{1,0:T(8,128)(2,1)S(1)} fusion(bf16[384,768]{1,0:T(8,128)(2,1)} %shard_map.84, bf16[768,3072]{1,0:T(8,128)(2,1)} %param.12, s32[]{:T(128)S(6)} %select_n.105), kind=kOutput, calls=%fused_computation.3 | convolution fusion | flops 453279744 | bytes 2359300 | tf_op jit(solution)/shard_map/dot_general | solution.py:220
  159.8 7.5 %collective-permute-start.13 = (bf16[384,768]{1,0:T(8,128)(2,1)S(1)}, bf16[384,768]{1,0:T(8,128)(2,1)S(1)}, u32[]{:S(2)}, u32[]{:S(2)}) collective-permute-start(bf16[384,768]{1,0:T(8,128)(2,1)S(1)} %convolution_convert_fusion.2), channel_id=1, source_target_pairs={{0,2},{1,3},{2,0},{3,1},{4,6},{5,7},{6,4},{7,5},{8,10},{9,11},{10,... | collective-permute-start | bytes 1769480 | tf_op jit(solution)/shard_map/ppermute | solution.py:222
  167.3 0.0 copy-done.4
  167.3 2.7 %convolution_convert_fusion.1 = bf16[384,768]{1,0:T(8,128)(2,1)} fusion(bf16[384,768]{1,0:T(8,128)(2,1)S(1)} %copy-done.4, bf16[768,3072]{1,0:T(8,128)(2,1)} %param.12, s32[]{:T(128)S(6)} %select_n.107), kind=kOutput, calls=%fused_computation.2 | convolution fusion | flops 453279744 | bytes 2359300 | tf_op jit(solution)/shard_map/dot_general | solution.py:220
  170.0 0.0 collective-permute-start.14
  170.0 2.8 %convolution_convert_fusion = bf16[384,768]{1,0:T(8,128)(2,1)} fusion(bf16[384,768]{1,0:T(8,128)(2,1)S(1)} %copy-done.4, bf16[768,3072]{1,0:T(8,128)(2,1)} %param.12, s32[]{:T(128)S(6)} %select_n.109), kind=kOutput, calls=%fused_computation.1 | convolution fusion | flops 453279744 | bytes 2359300 | tf_op jit(solution)/shard_map/dot_general | solution.py:220
  172.8 2.6 %collective-permute-start.15 = (bf16[384,768]{1,0:T(8,128)(2,1)}, bf16[384,768]{1,0:T(8,128)(2,1)}, u32[]{:S(2)}, u32[]{:S(2)}) collective-permute-start(bf16[384,768]{1,0:T(8,128)(2,1)} %convolution_convert_fusion), channel_id=1, source_target_pairs={{0,3},{1,0},{2,1},{3,2},{4,7},{5,4},{6,5},{7,6},{8,11},{9,8},{10,9... | collective-permute-start | bytes 1769480 | tf_op jit(solution)/shard_map/ppermute | solution.py:222
  175.4 5.6 %collective-permute-done.13 = bf16[384,768]{1,0:T(8,128)(2,1)S(1)} collective-permute-done((bf16[384,768]{1,0:T(8,128)(2,1)S(1)}, bf16[384,768]{1,0:T(8,128)(2,1)S(1)}, u32[]{:S(2)}, u32[]{:S(2)}) %collective-permute-start.13) | collective-permute-done | bytes 589856 | tf_op jit(solution)/shard_map/ppermute | solution.py:222
  181.0 12.8 %collective-permute-done.14 = bf16[384,768]{1,0:T(8,128)(2,1)S(1)} collective-permute-done((bf16[384,768]{1,0:T(8,128)(2,1)}, bf16[384,768]{1,0:T(8,128)(2,1)S(1)}, u32[]{:S(2)}, u32[]{:S(2)}) %collective-permute-start.14) | collective-permute-done | bytes 589856 | tf_op jit(solution)/shard_map/ppermute | solution.py:222
  193.8 0.0 collective-permute-done.15
  193.8 0.0 copy-done.5
  193.8 0.0 copy-done.6
  193.8 3.1 %fusion.7 = bf16[1,1,384,768]{3,2,1,0:T(8,128)(2,1)} fusion(bf16[384,768]{1,0:T(8,128)(2,1)S(1)} %copy-done.4, bf16[384,768]{1,0:T(8,128)(2,1)} %collective-permute-done.15, bf16[384,768]{1,0:T(8,128)(2,1)S(1)} %collective-permute-done.14, bf16[384,768]{1,0:T(8,128)(2,1)S(1)} %collective-permute-done.13, bf16[768,3072]{1,0:T(8,128)(2,1)} %param.12, ...), kind=kOutput, calls=%fused_computation.12 | convolution fusion | flops 456523776 | bytes 4721668 | tf_op jit(solution)/shard_map/dot_general | solution.py:224
  (9 shorter events, 0.1 us)
Async XLA Ops:
  0.0 13.4 %copy-start = (bf16[2,16,768]{2,1,0:T(8,128)(2,1)S(1)}, bf16[2,16,768]{2,1,0:T(8,128)(2,1)}, u32[]{:S(2)}) copy-start(bf16[2,16,768]{2,1,0:T(8,128)(2,1)} %param.10) | copy-start | bytes 147460
  0.0 72.3 %collective-permute-start.5 = (bf16[2,384,768]{2,1,0:T(8,128)(2,1)}, bf16[2,384,768]{2,1,0:T(8,128)(2,1)}, u32[]{:S(2)}, u32[]{:S(2)}) collective-permute-start(bf16[2,384,768]{2,1,0:T(8,128)(2,1)} %bitcast.22), channel_id=1, source_target_pairs={{0,4},{4,8},{8,12},{1,5},{5,9},{9,13},{2,6},{6,10},{10,14},{3,7},{... | collective-permute-start | bytes 3538952 | tf_op jit(solution)/shard_map/ppermute | solution.py:188
  1.4 70.9 %collective-permute-start.6 = (bf16[2,384,768]{2,1,0:T(8,128)(2,1)}, bf16[2,384,768]{2,1,0:T(8,128)(2,1)}, u32[]{:S(2)}, u32[]{:S(2)}) collective-permute-start(bf16[2,384,768]{2,1,0:T(8,128)(2,1)} %bitcast.23), channel_id=1, source_target_pairs={{4,0},{8,4},{12,8},{5,1},{9,5},{13,9},{6,2},{10,6},{14,10},{7,3},{... | collective-permute-start | bytes 3538952 | tf_op jit(solution)/shard_map/ppermute | solution.py:189
  5.7 81.6 %collective-permute-start = (bf16[2,384,768]{2,1,0:T(8,128)(2,1)}, bf16[2,384,768]{2,1,0:T(8,128)(2,1)S(1)}, u32[]{:S(2)}, u32[]{:S(2)}) collective-permute-start(bf16[2,384,768]{2,1,0:T(8,128)(2,1)} %bitcast.24), channel_id=1, source_target_pairs={{0,16},{16,32},{32,48},{48,64},{64,80},{80,96},{96,112},{112,128},... | collective-permute-start | bytes 3538952 | tf_op jit(solution)/shard_map/ppermute | solution.py:186
  9.4 77.9 %collective-permute-start.1 = (bf16[2,384,768]{2,1,0:T(8,128)(2,1)}, bf16[2,384,768]{2,1,0:T(8,128)(2,1)S(1)}, u32[]{:S(2)}, u32[]{:S(2)}) collective-permute-start(bf16[2,384,768]{2,1,0:T(8,128)(2,1)} %bitcast.25), channel_id=1, source_target_pairs={{16,0},{32,16},{48,32},{64,48},{80,64},{96,80},{112,96},{128,112},... | collective-permute-start | bytes 3538952 | tf_op jit(solution)/shard_map/ppermute | solution.py:187
  13.4 50.7 %collective-permute-start.2 = (bf16[2,16,384]{2,1,0:T(8,128)(2,1)S(1)}, bf16[2,16,384]{2,1,0:T(8,128)(2,1)S(1)}, u32[]{:S(2)}, u32[]{:S(2)}) collective-permute-start(bf16[2,16,384]{2,1,0:T(8,128)(2,1)S(1)} %constant_dynamic-slice_fusion), channel_id=1, source_target_pairs={{0,16},{16,0},{32,48},{48,32},{64,80},{80,64},{96,112},{112,96},{1... | collective-permute-start | bytes 73736 | tf_op jit(solution)/shard_map/ppermute | solution.py:40
  64.1 3.0 %collective-permute-start.3 = (bf16[2,16,384]{2,1,0:T(8,128)(2,1)S(1)}, bf16[2,16,384]{2,1,0:T(8,128)(2,1)S(1)}, u32[]{:S(2)}, u32[]{:S(2)}) collective-permute-start(bf16[2,16,384]{2,1,0:T(8,128)(2,1)S(1)} %constant_dynamic-slice_fusion), channel_id=1, source_target_pairs={{0,32},{16,48},{32,0},{48,16},{64,96},{80,112},{96,64},{112,80},{1... | collective-permute-start | bytes 73736 | tf_op jit(solution)/shard_map/ppermute | solution.py:40
  67.1 5.2 %collective-permute-start.4 = (bf16[2,16,384]{2,1,0:T(8,128)(2,1)S(1)}, bf16[2,16,384]{2,1,0:T(8,128)(2,1)S(1)}, u32[]{:S(2)}, u32[]{:S(2)}) collective-permute-start(bf16[2,16,384]{2,1,0:T(8,128)(2,1)S(1)} %constant_dynamic-slice_fusion), channel_id=1, source_target_pairs={{0,48},{16,32},{32,16},{48,0},{64,112},{80,96},{96,80},{112,64},{1... | collective-permute-start | bytes 73736 | tf_op jit(solution)/shard_map/ppermute | solution.py:40
  87.3 1.1 copy-start.2
  87.3 1.4 copy-start.3
  90.4 53.1 %collective-permute-start.7 = (bf16[2,2,384,768]{3,2,1,0:T(8,128)(2,1)}, bf16[2,2,384,768]{3,2,1,0:T(8,128)(2,1)S(1)}, u32[]{:S(2)}, u32[]{:S(2)}) collective-permute-start(bf16[2,2,384,768]{3,2,1,0:T(8,128)(2,1)} %pad_maximum_fusion), channel_id=1, source_target_pairs={{0,4},{4,8},{8,12},{1,5},{5,9},{9,13},{2,6},{6,10},{10,14},{3,7},{... | collective-permute-start | bytes 7077896 | tf_op jit(solution)/shard_map/ppermute | solution.py:207
  91.7 51.8 %collective-permute-start.8 = (bf16[2,2,384,768]{3,2,1,0:T(8,128)(2,1)}, bf16[2,2,384,768]{3,2,1,0:T(8,128)(2,1)}, u32[]{:S(2)}, u32[]{:S(2)}) collective-permute-start(bf16[2,2,384,768]{3,2,1,0:T(8,128)(2,1)} %pad_maximum_fusion), channel_id=1, source_target_pairs={{4,0},{8,4},{12,8},{5,1},{9,5},{13,9},{6,2},{10,6},{14,10},{7,3},{... | collective-permute-start | bytes 7077896 | tf_op jit(solution)/shard_map/ppermute | solution.py:208
  107.7 7.2 %collective-permute-start.9 = (bf16[2,64,384]{2,1,0:T(8,128)(2,1)S(1)}, bf16[2,64,384]{2,1,0:T(8,128)(2,1)S(1)}, u32[]{:S(2)}, u32[]{:S(2)}) collective-permute-start(bf16[2,64,384]{2,1,0:T(8,128)(2,1)S(1)} %pad_maximum_fusion.1), channel_id=1, source_target_pairs={{0,64},{16,80},{32,96},{48,112},{64,0},{80,16},{96,32},{112,48},{1... | collective-permute-start | bytes 294920 | tf_op jit(solution)/shard_map/ppermute | solution.py:40
  110.7 7.5 %collective-permute-start.10 = (bf16[2,64,384]{2,1,0:T(8,128)(2,1)S(1)}, bf16[2,64,384]{2,1,0:T(8,128)(2,1)S(1)}, u32[]{:S(2)}, u32[]{:S(2)}) collective-permute-start(bf16[2,64,384]{2,1,0:T(8,128)(2,1)S(1)} %pad_maximum_fusion.1), channel_id=1, source_target_pairs={{0,128},{16,144},{32,160},{48,176},{64,192},{80,208},{96,224},{112... | collective-permute-start | bytes 294920 | tf_op jit(solution)/shard_map/ppermute | solution.py:40
  114.9 10.0 %collective-permute-start.11 = (bf16[2,64,384]{2,1,0:T(8,128)(2,1)S(1)}, bf16[2,64,384]{2,1,0:T(8,128)(2,1)S(1)}, u32[]{:S(2)}, u32[]{:S(2)}) collective-permute-start(bf16[2,64,384]{2,1,0:T(8,128)(2,1)S(1)} %pad_maximum_fusion.1), channel_id=1, source_target_pairs={{0,192},{16,208},{32,224},{48,240},{64,128},{80,144},{96,160},{112... | collective-permute-start | bytes 294920 | tf_op jit(solution)/shard_map/ppermute | solution.py:40
  124.9 4.2 %collective-permute-start.12 = (bf16[2,256,384]{2,1,0:T(8,128)(2,1)S(1)}, bf16[2,256,384]{2,1,0:T(8,128)(2,1)S(1)}, u32[]{:S(2)}, u32[]{:S(2)}) collective-permute-start(bf16[2,256,384]{2,1,0:T(8,128)(2,1)S(1)} %constant_dynamic-update-slice_fusion), channel_id=1, source_target_pairs={{0,4},{4,0},{8,12},{12,8},{1,5},{5,1},{9,13},{13,9},{2,6},{6,2},{1... | collective-permute-start | bytes 1179656 | tf_op jit(solution)/shard_map/ppermute | solution.py:47
  143.5 1.4 copy-start.1
  157.6 9.7 %copy-start.4 = (bf16[384,768]{1,0:T(8,128)(2,1)S(1)}, bf16[384,768]{1,0:T(8,128)(2,1)}, u32[]{:S(2)}) copy-start(bf16[384,768]{1,0:T(8,128)(2,1)} %shard_map.84) | copy-start | bytes 1769476
  159.8 21.2 %collective-permute-start.13 = (bf16[384,768]{1,0:T(8,128)(2,1)S(1)}, bf16[384,768]{1,0:T(8,128)(2,1)S(1)}, u32[]{:S(2)}, u32[]{:S(2)}) collective-permute-start(bf16[384,768]{1,0:T(8,128)(2,1)S(1)} %convolution_convert_fusion.2), channel_id=1, source_target_pairs={{0,2},{1,3},{2,0},{3,1},{4,6},{5,7},{6,4},{7,5},{8,10},{9,11},{10,... | collective-permute-start | bytes 1769480 | tf_op jit(solution)/shard_map/ppermute | solution.py:222
  170.0 23.7 %copy-start.5 = (bf16[1,1,384,768]{3,2,1,0:T(8,128)(2,1)S(1)}, bf16[1,1,384,768]{3,2,1,0:T(8,128)(2,1)}, u32[]{:S(2)}) copy-start(bf16[1,1,384,768]{3,2,1,0:T(8,128)(2,1)} %param.11) | copy-start | bytes 1769476
  170.0 23.7 %copy-start.6 = (f32[768]{0:T(1024)S(1)}, f32[768]{0:T(1024)}, u32[]{:S(2)}) copy-start(f32[768]{0:T(1024)} %param.13) | copy-start | bytes 9220
  170.0 23.7 %collective-permute-start.14 = (bf16[384,768]{1,0:T(8,128)(2,1)}, bf16[384,768]{1,0:T(8,128)(2,1)S(1)}, u32[]{:S(2)}, u32[]{:S(2)}) collective-permute-start(bf16[384,768]{1,0:T(8,128)(2,1)} %convolution_convert_fusion.1), channel_id=1, source_target_pairs={{0,1},{1,2},{2,3},{3,0},{4,5},{5,6},{6,7},{7,4},{8,9},{9,10},{10,1... | collective-permute-start | bytes 1769480 | tf_op jit(solution)/shard_map/ppermute | solution.py:222
  172.8 20.9 %collective-permute-start.15 = (bf16[384,768]{1,0:T(8,128)(2,1)}, bf16[384,768]{1,0:T(8,128)(2,1)}, u32[]{:S(2)}, u32[]{:S(2)}) collective-permute-start(bf16[384,768]{1,0:T(8,128)(2,1)} %convolution_convert_fusion), channel_id=1, source_target_pairs={{0,3},{1,0},{2,1},{3,2},{4,7},{5,4},{6,5},{7,6},{8,11},{9,8},{10,9... | collective-permute-start | bytes 1769480 | tf_op jit(solution)/shard_map/ppermute | solution.py:222

commit v6 on v5

--- a/solution.py
+++ b/solution.py
@@ -34,11 +34,12 @@
     return lax.dynamic_slice_in_dim(text_kv, half * half_width, half_width, 2)
 
 
-def exchange(block, devices, steps):
-    parts = [block]
-    for step in steps:
-        parts.append(lax.ppermute(block, "tm", [(i, i ^ step) for i in range(devices)]))
-    return jnp.concatenate(parts, axis=1)
+def exchange(block, devices, step):
+    position = lax.axis_index("tm")
+    other = lax.ppermute(block, "tm", [(i, i ^ step) for i in range(devices)])
+    low_first = jnp.concatenate([block, other], axis=1)
+    high_first = jnp.concatenate([other, block], axis=1)
+    return jnp.where((position & step) == 0, low_first, high_first)
 
 
 def join_halves(mine):
@@ -183,11 +184,17 @@
     mp_size = lax.axis_size("mp")
 
     own = image_kv[0, 0]
-    t_before = lax.ppermute(own, "tm", shift_pairs(tm_size, 1))
-    t_after = lax.ppermute(own, "tm", shift_pairs(tm_size, -1))
     h_before = lax.ppermute(own, "height", shift_pairs(height_size, 1))
     h_after = lax.ppermute(own, "height", shift_pairs(height_size, -1))
-    text_group = exchange(text_halves(text_kv), tm_size, (1, 2, 3))
+    text_group = text_halves(text_kv)
+    step = 1
+    while step < tm_size:
+        text_group = exchange(text_group, tm_size, step)
+        step *= 2
+    text = join_halves(text_group)
+    sent, text = lax.optimization_barrier((own, text))
+    t_before = lax.ppermute(sent, "tm", shift_pairs(tm_size, 1))
+    t_after = lax.ppermute(sent, "tm", shift_pairs(tm_size, -1))
     time_start = lax.axis_index("tm")
     height_start = lax.axis_index("height")
     zero_index = jnp.int32(0)
@@ -200,8 +207,6 @@
     queries = image_q[0, 0]
     near = [(own, None, 4), (h_before, None, 3), (h_after, None, 5)]
     state = attend(head_reach, queries, None, near, bias)
-    text_group, state = lax.optimization_barrier((text_group, state))
-    text = join_halves(exchange(text_group, tm_size, (4, 8, 12)))
     t_before, t_after, state = lax.optimization_barrier((t_before, t_after, state))
     time_pair = jnp.stack([t_before, t_after])
     c_before = lax.ppermute(time_pair, "height", shift_pairs(height_size, 1))

time: 199 us -> 182 us (0.915)
  the two profiles are of different devices: /device:TPU:35 before, /device:TPU:97 now
where the time goes in v6:
time: 182 us; the launch traced here: 181 us
  waiting for transfers between devices  75 us (41%)
  Pallas kernels  42.5 us (23%)
  starting transfers between devices  42.4 us (23%)
  matrix products  10.6 us (6%)
  local copies, waits for them, and re-layouts  5.18 us (3%)
  other arithmetic  4.96 us (3%)
    pallas_call x3, Pallas kernels, attend(): pl.pallas_call(kernel, grid_spec=grid_spec, out_shape=out_shape)  42.5 us
    ppermute x1, waiting for transfers between devices, per_device(): h_before = lax.ppermute(own, 'height', shift_pairs(height_size, 1))  30.4 us
    ppermute x3, waiting for transfers between devices, per_device(): received.append(lax.ppermute(part, 'mp', pairs))  14.6 us
    ppermute x4, waiting for transfers between devices, exchange(): other = lax.ppermute(block, 'tm', [(i, i ^ step) for i in range(devices)])  13.4 us
    ppermute x1, waiting for transfers between devices, per_device(): h_after = lax.ppermute(own, 'height', shift_pairs(height_size, -1))  8.11 us
    ppermute x3, starting transfers between devices, per_device(): received.append(lax.ppermute(part, 'mp', pairs))  7.75 us
    dot_general x3, matrix products, per_device(): jnp.dot(attended, w_part, preferred_element_type=jnp.float32)  7.58 us
    ppermute x4, starting transfers between devices, exchange(): other = lax.ppermute(block, 'tm', [(i, i ^ step) for i in range(devices)])  7.5 us
  transfers between devices with their start and end apart: 14, of which 12 were waited for; matrix products, arithmetic and copies ran while one was open for 6% of the time, Pallas kernels for 16%

profile of v6, /device:TPU:97, one launch (start us, length us, event | category | flops | bytes accessed | tf_op | source)
XLA Modules:
  0.0 180.9 jit_solution(16973446041131917537)
XLA Ops:
  0.0 0.0 copy-start
  0.0 0.8 copy-done
  0.8 2.7 %collective-permute-start = (bf16[2,16,384]{2,1,0:T(8,128)(2,1)S(1)}, bf16[2,16,384]{2,1,0:T(8,128)(2,1)S(1)}, u32[]{:S(2)}, u32[]{:S(2)}) collective-permute-start(bf16[2,16,384]{2,1,0:T(8,128)(2,1)S(1)} %constant_dynamic-slice_fusion), channel_id=1, source_target_pairs={{0,16},{16,0},{32,48},{48,32},{64,80},{80,64},{96,112},{112,96},{1... | collective-permute-start | bytes 73736 | tf_op jit(solution)/shard_map/ppermute | solution.py:39
  3.5 1.4 collective-permute-done
  5.0 0.1 collective-permute-start.1
  5.1 2.9 %collective-permute-done.1 = bf16[2,32,384]{2,1,0:T(8,128)(2,1)S(1)} collective-permute-done((bf16[2,32,384]{2,1,0:T(8,128)(2,1)S(1)}, bf16[2,32,384]{2,1,0:T(8,128)(2,1)S(1)}, u32[]{:S(2)}, u32[]{:S(2)}) %collective-permute-start.1) | collective-permute-done | bytes 49184 | tf_op jit(solution)/shard_map/ppermute | solution.py:39
  8.1 0.1 collective-permute-start.2
  8.2 5.1 %collective-permute-done.2 = bf16[2,64,384]{2,1,0:T(8,128)(2,1)S(1)} collective-permute-done((bf16[2,64,384]{2,1,0:T(8,128)(2,1)S(1)}, bf16[2,64,384]{2,1,0:T(8,128)(2,1)S(1)}, u32[]{:S(2)}, u32[]{:S(2)}) %collective-permute-start.2) | collective-permute-done | bytes 98336 | tf_op jit(solution)/shard_map/ppermute | solution.py:39
  13.3 4.6 %collective-permute-start.3 = (bf16[2,128,384]{2,1,0:T(8,128)(2,1)S(1)}, bf16[2,128,384]{2,1,0:T(8,128)(2,1)S(1)}, u32[]{:S(2)}, u32[]{:S(2)}) collective-permute-start(bf16[2,128,384]{2,1,0:T(8,128)(2,1)S(1)} %maximum_select_fusion.2), channel_id=1, source_target_pairs={{0,128},{16,144},{32,160},{48,176},{64,192},{80,208},{96,224},{112... | collective-permute-start | bytes 589832 | tf_op jit(solution)/shard_map/ppermute | solution.py:39
  17.9 0.0 copy-start.5
  17.9 0.0 copy-start.6
  17.9 3.9 %collective-permute-done.3 = bf16[2,128,384]{2,1,0:T(8,128)(2,1)S(1)} collective-permute-done((bf16[2,128,384]{2,1,0:T(8,128)(2,1)S(1)}, bf16[2,128,384]{2,1,0:T(8,128)(2,1)S(1)}, u32[]{:S(2)}, u32[]{:S(2)}) %collective-permute-start.3) | collective-permute-done | bytes 196640 | tf_op jit(solution)/shard_map/ppermute | solution.py:39
  21.8 0.1 maximum_select_fusion.1
  22.0 6.4 %collective-permute-start.4 = (bf16[2,256,384]{2,1,0:T(8,128)(2,1)S(1)}, bf16[2,256,384]{2,1,0:T(8,128)(2,1)S(1)}, u32[]{:S(2)}, u32[]{:S(2)}) collective-permute-start(bf16[2,256,384]{2,1,0:T(8,128)(2,1)S(1)} %maximum_select_fusion.1), channel_id=1, source_target_pairs={{0,4},{4,0},{8,12},{12,8},{1,5},{5,1},{9,13},{13,9},{2,6},{6,2},{1... | collective-permute-start | bytes 1179656 | tf_op jit(solution)/shard_map/ppermute | solution.py:48
  28.4 3.0 %collective-permute-start.7 = (bf16[2,384,768]{2,1,0:T(8,128)(2,1)}, bf16[2,384,768]{2,1,0:T(8,128)(2,1)}, u32[]{:S(2)}, u32[]{:S(2)}) collective-permute-start(bf16[2,384,768]{2,1,0:T(8,128)(2,1)} %bitcast.2.rest_0_), channel_id=1, source_target_pairs={{0,4},{4,8},{8,12},{1,5},{5,9},{9,13},{2,6},{6,10},{10,14},{3,7},{... | collective-permute-start | bytes 3538952 | tf_op jit(solution)/shard_map/ppermute | solution.py:187
  31.4 2.3 %collective-permute-start.8 = (bf16[2,384,768]{2,1,0:T(8,128)(2,1)}, bf16[2,384,768]{2,1,0:T(8,128)(2,1)}, u32[]{:S(2)}, u32[]{:S(2)}) collective-permute-start(bf16[2,384,768]{2,1,0:T(8,128)(2,1)} %bitcast.2.rest_0_), channel_id=1, source_target_pairs={{4,0},{8,4},{12,8},{5,1},{9,5},{13,9},{6,2},{10,6},{14,10},{7,3},{... | collective-permute-start | bytes 3538952 | tf_op jit(solution)/shard_map/ppermute | solution.py:188
  33.8 0.0 collective-permute-done.4
  33.8 1.1 maximum_select_fusion.rest_0_
  34.9 4.6 %collective-permute-start.5 = (bf16[2,384,768]{2,1,0:T(8,128)(2,1)}, bf16[2,384,768]{2,1,0:T(8,128)(2,1)S(1)}, u32[]{:S(2)}, u32[]{:S(2)}) collective-permute-start(bf16[2,384,768]{2,1,0:T(8,128)(2,1)} %bitcast.2.rest_0_), channel_id=1, source_target_pairs={{0,16},{16,32},{32,48},{48,64},{64,80},{80,96},{96,112},{112,128},... | collective-permute-start | bytes 3538952 | tf_op jit(solution)/shard_map/ppermute | solution.py:196
  39.5 3.0 %collective-permute-start.6 = (bf16[2,384,768]{2,1,0:T(8,128)(2,1)}, bf16[2,384,768]{2,1,0:T(8,128)(2,1)S(1)}, u32[]{:S(2)}, u32[]{:S(2)}) collective-permute-start(bf16[2,384,768]{2,1,0:T(8,128)(2,1)} %bitcast.2.rest_0_), channel_id=1, source_target_pairs={{16,0},{32,16},{48,32},{64,48},{80,64},{96,80},{112,96},{128,112},... | collective-permute-start | bytes 3538952 | tf_op jit(solution)/shard_map/ppermute | solution.py:197
  42.6 0.0 copy-done.5
  42.6 0.1 pad_dynamic-slice_fusion
  42.7 0.1 copy.16
  42.8 0.1 lt.111
  42.8 0.1 copy.17
  42.9 0.1 lt.116
  43.0 0.0 copy-done.6
  43.0 0.7 copy.22.reach_ref
  43.7 0.7 and_select_fusion.rest_3_.rest_4_
  44.4 30.4 %collective-permute-done.7.rest_1_ = bf16[2,384,768]{2,1,0:T(8,128)(2,1)} collective-permute-done((bf16[2,384,768]{2,1,0:T(8,128)(2,1)}, bf16[2,384,768]{2,1,0:T(8,128)(2,1)}, u32[]{:S(2)}, u32[]{:S(2)}) %collective-permute-start.7) | collective-permute-done | bytes 1179680 | tf_op jit(solution)/shard_map/ppermute | solution.py:187
  74.8 8.1 %collective-permute-done.8.rest_2_ = bf16[2,384,768]{2,1,0:T(8,128)(2,1)} collective-permute-done((bf16[2,384,768]{2,1,0:T(8,128)(2,1)}, bf16[2,384,768]{2,1,0:T(8,128)(2,1)}, u32[]{:S(2)}, u32[]{:S(2)}) %collective-permute-start.8) | collective-permute-done | bytes 1179680 | tf_op jit(solution)/shard_map/ppermute | solution.py:188
  82.9 14.5 %shard_map.82 = (f32[6,384,1]{2,1,0:T(8,128)}, f32[6,384,1]{2,1,0:T(8,128)}, f32[384,768]{1,0:T(8,128)}) custom-call(s32[6,2]{1,0:T(8,128)} %copy.22.reach_ref, bf16[384,768]{1,0:T(8,128)(2,1)} %bitcast.17, bf16[2,384,768]{2,1,0:T(8,128)(2,1)} %bitcast.2.rest_0_, bf16[2,384,768]{2,1,0:T(8,128)(2,1)} %collective-permute-done.7.rest_1_, ...), custom_call_target="tpu_custom_call" | custom-call | tf_op jit(solution)/shard_map/pallas_call | solution.py:176
  97.4 0.0 collective-permute-done.5.rest_1_
  97.4 0.0 copy-start.2
  97.5 0.8 collective-permute-done.6.rest_2_
  98.2 0.0 copy-start.3
  98.2 0.3 copy-done.2
  98.5 0.7 copy-done.3
  99.2 1.6 pad_maximum_fusion
  100.9 1.9 %collective-permute-start.10 = (bf16[2,2,384,768]{3,2,1,0:T(8,128)(2,1)}, bf16[2,2,384,768]{3,2,1,0:T(8,128)(2,1)S(1)}, u32[]{:S(2)}, u32[]{:S(2)}) collective-permute-start(bf16[2,2,384,768]{3,2,1,0:T(8,128)(2,1)} %pad_maximum_fusion), channel_id=1, source_target_pairs={{4,0},{8,4},{12,8},{5,1},{9,5},{13,9},{6,2},{10,6},{14,10},{7,3},{... | collective-permute-start | bytes 7077896 | tf_op jit(solution)/shard_map/ppermute | solution.py:213
  102.8 5.8 %collective-permute-start.9 = (bf16[2,2,384,768]{3,2,1,0:T(8,128)(2,1)}, bf16[2,2,384,768]{3,2,1,0:T(8,128)(2,1)}, u32[]{:S(2)}, u32[]{:S(2)}) collective-permute-start(bf16[2,2,384,768]{3,2,1,0:T(8,128)(2,1)} %pad_maximum_fusion), channel_id=1, source_target_pairs={{0,4},{4,8},{8,12},{1,5},{5,9},{9,13},{2,6},{6,10},{10,14},{3,7},{... | collective-permute-start | bytes 7077896 | tf_op jit(solution)/shard_map/ppermute | solution.py:212
  108.7 0.7 slice.12
  109.3 0.6 slice.13
  109.9 1.3 fusion.18
  111.3 0.8 copy.23.rest_8_
  112.1 14.9 %shard_map.83 = (f32[6,384,1]{2,1,0:T(8,128)}, f32[6,384,1]{2,1,0:T(8,128)}, f32[384,768]{1,0:T(8,128)}) custom-call(s32[6,2]{1,0:T(8,128)} %copy.22.reach_ref, bf16[384,768]{1,0:T(8,128)(2,1)} %bitcast.18, bf16[2,256,768]{2,1,0:T(8,128)(2,1)} %maximum_select_fusion.rest_0_, bf16[2,384,768]{2,1,0:T(8,128)(2,1)} %copy-done.2, bf16[2,384,768]{2,1,0:T(8,128)(2,1)} %copy-done.3, ...), custom_call_target="tpu_custom_call" | custom-call | tf_op jit(solution)/shard_map/pallas_call | solution.py:176
  127.0 6.5 %collective-permute-done.10.rest_1_.rest_3_ = bf16[2,2,384,768]{3,2,1,0:T(8,128)(2,1)S(1)} collective-permute-done((bf16[2,2,384,768]{3,2,1,0:T(8,128)(2,1)}, bf16[2,2,384,768]{3,2,1,0:T(8,128)(2,1)S(1)}, u32[]{:S(2)}, u32[]{:S(2)}) %collective-permute-start.10) | collective-permute-done | bytes 2359328 | tf_op jit(solution)/shard_map/ppermute | solution.py:213
  133.4 0.0 copy-start.1
  133.4 1.3 collective-permute-done.9.rest_0_.rest_2_
  134.7 0.1 copy-done.1
  134.8 13.1 %shard_map.84 = bf16[384,768]{1,0:T(8,128)(2,1)} custom-call(s32[6,2]{1,0:T(8,128)} %copy.22.reach_ref, bf16[384,768]{1,0:T(8,128)(2,1)} %bitcast.19, bf16[2,2,384,768]{3,2,1,0:T(8,128)(2,1)} %collective-permute-done.9.rest_0_.rest_2_, bf16[2,2,384,768]{3,2,1,0:T(8,128)(2,1)} %copy-done.1, bf16[2,2,384,768]{3,2,1,0:T(8,128)(2,1)} %collective-permute-done.9.rest_0_.rest_2_, ...), custom_call_target="tpu_custom_call" | custom-call | tf_op jit(solution)/shard_map/pallas_call | solution.py:176
  147.9 2.1 %convolution_convert_fusion.2 = bf16[384,768]{1,0:T(8,128)(2,1)S(1)} fusion(bf16[384,768]{1,0:T(8,128)(2,1)} %shard_map.84, bf16[768,3072]{1,0:T(8,128)(2,1)} %param.12, s32[]{:T(128)S(6)} %select_n.145), kind=kOutput, calls=%fused_computation.3 | convolution fusion | flops 453279744 | bytes 2359300 | tf_op jit(solution)/shard_map/dot_general | solution.py:225
  150.1 4.5 %collective-permute-start.11 = (bf16[384,768]{1,0:T(8,128)(2,1)S(1)}, bf16[384,768]{1,0:T(8,128)(2,1)S(1)}, u32[]{:S(2)}, u32[]{:S(2)}) collective-permute-start(bf16[384,768]{1,0:T(8,128)(2,1)S(1)} %convolution_convert_fusion.2), channel_id=1, source_target_pairs={{0,2},{1,3},{2,0},{3,1},{4,6},{5,7},{6,4},{7,5},{8,10},{9,11},{10,... | collective-permute-start | bytes 1769480 | tf_op jit(solution)/shard_map/ppermute | solution.py:227
  154.5 0.0 copy-done.4
  154.6 2.7 %convolution_convert_fusion.1 = bf16[384,768]{1,0:T(8,128)(2,1)} fusion(bf16[384,768]{1,0:T(8,128)(2,1)S(1)} %copy-done.4, bf16[768,3072]{1,0:T(8,128)(2,1)} %param.12, s32[]{:T(128)S(6)} %select_n.147), kind=kOutput, calls=%fused_computation.2 | convolution fusion | flops 453279744 | bytes 2359300 | tf_op jit(solution)/shard_map/dot_general | solution.py:225
  157.3 3.3 %collective-permute-start.12 = (bf16[384,768]{1,0:T(8,128)(2,1)}, bf16[384,768]{1,0:T(8,128)(2,1)S(1)}, u32[]{:S(2)}, u32[]{:S(2)}) collective-permute-start(bf16[384,768]{1,0:T(8,128)(2,1)} %convolution_convert_fusion.1), channel_id=1, source_target_pairs={{0,1},{1,2},{2,3},{3,0},{4,5},{5,6},{6,7},{7,4},{8,9},{9,10},{10,1... | collective-permute-start | bytes 1769480 | tf_op jit(solution)/shard_map/ppermute | solution.py:227
  160.5 2.7 %convolution_convert_fusion = bf16[384,768]{1,0:T(8,128)(2,1)} fusion(bf16[384,768]{1,0:T(8,128)(2,1)S(1)} %copy-done.4, bf16[768,3072]{1,0:T(8,128)(2,1)} %param.12, s32[]{:T(128)S(6)} %select_n.149), kind=kOutput, calls=%fused_computation.1 | convolution fusion | flops 453279744 | bytes 2359300 | tf_op jit(solution)/shard_map/dot_general | solution.py:225
  163.3 0.0 collective-permute-start.13
  163.3 4.7 %collective-permute-done.11 = bf16[384,768]{1,0:T(8,128)(2,1)S(1)} collective-permute-done((bf16[384,768]{1,0:T(8,128)(2,1)S(1)}, bf16[384,768]{1,0:T(8,128)(2,1)S(1)}, u32[]{:S(2)}, u32[]{:S(2)}) %collective-permute-start.11) | collective-permute-done | bytes 589856 | tf_op jit(solution)/shard_map/ppermute | solution.py:227
  167.9 5.5 %collective-permute-done.12 = bf16[384,768]{1,0:T(8,128)(2,1)S(1)} collective-permute-done((bf16[384,768]{1,0:T(8,128)(2,1)}, bf16[384,768]{1,0:T(8,128)(2,1)S(1)}, u32[]{:S(2)}, u32[]{:S(2)}) %collective-permute-start.12) | collective-permute-done | bytes 589856 | tf_op jit(solution)/shard_map/ppermute | solution.py:227
  173.5 4.4 %collective-permute-done.13 = bf16[384,768]{1,0:T(8,128)(2,1)} collective-permute-done((bf16[384,768]{1,0:T(8,128)(2,1)}, bf16[384,768]{1,0:T(8,128)(2,1)}, u32[]{:S(2)}, u32[]{:S(2)}) %collective-permute-start.13) | collective-permute-done | bytes 589856 | tf_op jit(solution)/shard_map/ppermute | solution.py:227
  177.8 0.0 copy-done.7
  177.8 0.0 copy-done.8
  177.8 3.0 %fusion.7 = bf16[1,1,384,768]{3,2,1,0:T(8,128)(2,1)} fusion(bf16[384,768]{1,0:T(8,128)(2,1)S(1)} %copy-done.4, bf16[384,768]{1,0:T(8,128)(2,1)} %collective-permute-done.13, bf16[384,768]{1,0:T(8,128)(2,1)S(1)} %collective-permute-done.12, bf16[384,768]{1,0:T(8,128)(2,1)S(1)} %collective-permute-done.11, bf16[768,3072]{1,0:T(8,128)(2,1)} %param.12, ...), kind=kOutput, calls=%fused_computation.12 | convolution fusion | flops 456523776 | bytes 4721668 | tf_op jit(solution)/shard_map/dot_general | solution.py:229
  (8 shorter events, 0.1 us)
Async XLA Ops:
  0.0 0.8 copy-start
  0.8 4.2 %collective-permute-start = (bf16[2,16,384]{2,1,0:T(8,128)(2,1)S(1)}, bf16[2,16,384]{2,1,0:T(8,128)(2,1)S(1)}, u32[]{:S(2)}, u32[]{:S(2)}) collective-permute-start(bf16[2,16,384]{2,1,0:T(8,128)(2,1)S(1)} %constant_dynamic-slice_fusion), channel_id=1, source_target_pairs={{0,16},{16,0},{32,48},{48,32},{64,80},{80,64},{96,112},{112,96},{1... | collective-permute-start | bytes 73736 | tf_op jit(solution)/shard_map/ppermute | solution.py:39
  5.0 3.0 %collective-permute-start.1 = (bf16[2,32,384]{2,1,0:T(8,128)(2,1)S(1)}, bf16[2,32,384]{2,1,0:T(8,128)(2,1)S(1)}, u32[]{:S(2)}, u32[]{:S(2)}) collective-permute-start(bf16[2,32,384]{2,1,0:T(8,128)(2,1)S(1)} %maximum_select_fusion.4), channel_id=1, source_target_pairs={{0,32},{16,48},{32,0},{48,16},{64,96},{80,112},{96,64},{112,80},{1... | collective-permute-start | bytes 147464 | tf_op jit(solution)/shard_map/ppermute | solution.py:39
  8.1 5.2 %collective-permute-start.2 = (bf16[2,64,384]{2,1,0:T(8,128)(2,1)S(1)}, bf16[2,64,384]{2,1,0:T(8,128)(2,1)S(1)}, u32[]{:S(2)}, u32[]{:S(2)}) collective-permute-start(bf16[2,64,384]{2,1,0:T(8,128)(2,1)S(1)} %maximum_select_fusion.3), channel_id=1, source_target_pairs={{0,64},{16,80},{32,96},{48,112},{64,0},{80,16},{96,32},{112,48},{1... | collective-permute-start | bytes 294920 | tf_op jit(solution)/shard_map/ppermute | solution.py:39
  13.3 8.5 %collective-permute-start.3 = (bf16[2,128,384]{2,1,0:T(8,128)(2,1)S(1)}, bf16[2,128,384]{2,1,0:T(8,128)(2,1)S(1)}, u32[]{:S(2)}, u32[]{:S(2)}) collective-permute-start(bf16[2,128,384]{2,1,0:T(8,128)(2,1)S(1)} %maximum_select_fusion.2), channel_id=1, source_target_pairs={{0,128},{16,144},{32,160},{48,176},{64,192},{80,208},{96,224},{112... | collective-permute-start | bytes 589832 | tf_op jit(solution)/shard_map/ppermute | solution.py:39
  17.9 24.7 %copy-start.5 = (s32[2,16,4]{1,2,0:T(4,128)S(1)}, s32[2,16,4]{1,2,0:T(4,128)}, u32[]{:S(2)}) copy-start(s32[2,16,4]{1,2,0:T(4,128)} %param.15) | copy-start | bytes 1540
  17.9 25.1 %copy-start.6 = (s32[6,2]{0,1:T(2,128)S(1)}, s32[6,2]{0,1:T(2,128)}, u32[]{:S(2)}) copy-start(s32[6,2]{0,1:T(2,128)} %param.14) | copy-start | bytes 148
  22.0 11.8 %collective-permute-start.4 = (bf16[2,256,384]{2,1,0:T(8,128)(2,1)S(1)}, bf16[2,256,384]{2,1,0:T(8,128)(2,1)S(1)}, u32[]{:S(2)}, u32[]{:S(2)}) collective-permute-start(bf16[2,256,384]{2,1,0:T(8,128)(2,1)S(1)} %maximum_select_fusion.1), channel_id=1, source_target_pairs={{0,4},{4,0},{8,12},{12,8},{1,5},{5,1},{9,13},{13,9},{2,6},{6,2},{1... | collective-permute-start | bytes 1179656 | tf_op jit(solution)/shard_map/ppermute | solution.py:48
  28.4 46.4 %collective-permute-start.7 = (bf16[2,384,768]{2,1,0:T(8,128)(2,1)}, bf16[2,384,768]{2,1,0:T(8,128)(2,1)}, u32[]{:S(2)}, u32[]{:S(2)}) collective-permute-start(bf16[2,384,768]{2,1,0:T(8,128)(2,1)} %bitcast.2.rest_0_), channel_id=1, source_target_pairs={{0,4},{4,8},{8,12},{1,5},{5,9},{9,13},{2,6},{6,10},{10,14},{3,7},{... | collective-permute-start | bytes 3538952 | tf_op jit(solution)/shard_map/ppermute | solution.py:187
  31.4 51.5 %collective-permute-start.8 = (bf16[2,384,768]{2,1,0:T(8,128)(2,1)}, bf16[2,384,768]{2,1,0:T(8,128)(2,1)}, u32[]{:S(2)}, u32[]{:S(2)}) collective-permute-start(bf16[2,384,768]{2,1,0:T(8,128)(2,1)} %bitcast.2.rest_0_), channel_id=1, source_target_pairs={{4,0},{8,4},{12,8},{5,1},{9,5},{13,9},{6,2},{10,6},{14,10},{7,3},{... | collective-permute-start | bytes 3538952 | tf_op jit(solution)/shard_map/ppermute | solution.py:188
  34.9 62.6 %collective-permute-start.5 = (bf16[2,384,768]{2,1,0:T(8,128)(2,1)}, bf16[2,384,768]{2,1,0:T(8,128)(2,1)S(1)}, u32[]{:S(2)}, u32[]{:S(2)}) collective-permute-start(bf16[2,384,768]{2,1,0:T(8,128)(2,1)} %bitcast.2.rest_0_), channel_id=1, source_target_pairs={{0,16},{16,32},{32,48},{48,64},{64,80},{80,96},{96,112},{112,128},... | collective-permute-start | bytes 3538952 | tf_op jit(solution)/shard_map/ppermute | solution.py:196
  39.5 58.7 %collective-permute-start.6 = (bf16[2,384,768]{2,1,0:T(8,128)(2,1)}, bf16[2,384,768]{2,1,0:T(8,128)(2,1)S(1)}, u32[]{:S(2)}, u32[]{:S(2)}) collective-permute-start(bf16[2,384,768]{2,1,0:T(8,128)(2,1)} %bitcast.2.rest_0_), channel_id=1, source_target_pairs={{16,0},{32,16},{48,32},{64,48},{80,64},{96,80},{112,96},{128,112},... | collective-permute-start | bytes 3538952 | tf_op jit(solution)/shard_map/ppermute | solution.py:197
  97.4 1.1 copy-start.2
  98.2 1.0 copy-start.3
  100.9 32.6 %collective-permute-start.10 = (bf16[2,2,384,768]{3,2,1,0:T(8,128)(2,1)}, bf16[2,2,384,768]{3,2,1,0:T(8,128)(2,1)S(1)}, u32[]{:S(2)}, u32[]{:S(2)}) collective-permute-start(bf16[2,2,384,768]{3,2,1,0:T(8,128)(2,1)} %pad_maximum_fusion), channel_id=1, source_target_pairs={{4,0},{8,4},{12,8},{5,1},{9,5},{13,9},{6,2},{10,6},{14,10},{7,3},{... | collective-permute-start | bytes 7077896 | tf_op jit(solution)/shard_map/ppermute | solution.py:213
  102.8 31.9 %collective-permute-start.9 = (bf16[2,2,384,768]{3,2,1,0:T(8,128)(2,1)}, bf16[2,2,384,768]{3,2,1,0:T(8,128)(2,1)}, u32[]{:S(2)}, u32[]{:S(2)}) collective-permute-start(bf16[2,2,384,768]{3,2,1,0:T(8,128)(2,1)} %pad_maximum_fusion), channel_id=1, source_target_pairs={{0,4},{4,8},{8,12},{1,5},{5,9},{9,13},{2,6},{6,10},{10,14},{3,7},{... | collective-permute-start | bytes 7077896 | tf_op jit(solution)/shard_map/ppermute | solution.py:212
  133.4 1.4 copy-start.1
  147.9 6.6 %copy-start.4 = (bf16[384,768]{1,0:T(8,128)(2,1)S(1)}, bf16[384,768]{1,0:T(8,128)(2,1)}, u32[]{:S(2)}) copy-start(bf16[384,768]{1,0:T(8,128)(2,1)} %shard_map.84) | copy-start | bytes 1769476
  150.1 17.9 %collective-permute-start.11 = (bf16[384,768]{1,0:T(8,128)(2,1)S(1)}, bf16[384,768]{1,0:T(8,128)(2,1)S(1)}, u32[]{:S(2)}, u32[]{:S(2)}) collective-permute-start(bf16[384,768]{1,0:T(8,128)(2,1)S(1)} %convolution_convert_fusion.2), channel_id=1, source_target_pairs={{0,2},{1,3},{2,0},{3,1},{4,6},{5,7},{6,4},{7,5},{8,10},{9,11},{10,... | collective-permute-start | bytes 1769480 | tf_op jit(solution)/shard_map/ppermute | solution.py:227
  157.3 20.5 %copy-start.7 = (bf16[1,1,384,768]{3,2,1,0:T(8,128)(2,1)S(1)}, bf16[1,1,384,768]{3,2,1,0:T(8,128)(2,1)}, u32[]{:S(2)}) copy-start(bf16[1,1,384,768]{3,2,1,0:T(8,128)(2,1)} %param.11) | copy-start | bytes 1769476
  157.3 20.6 %copy-start.8 = (f32[768]{0:T(1024)S(1)}, f32[768]{0:T(1024)}, u32[]{:S(2)}) copy-start(f32[768]{0:T(1024)} %param.13) | copy-start | bytes 9220
  157.3 16.2 %collective-permute-start.12 = (bf16[384,768]{1,0:T(8,128)(2,1)}, bf16[384,768]{1,0:T(8,128)(2,1)S(1)}, u32[]{:S(2)}, u32[]{:S(2)}) collective-permute-start(bf16[384,768]{1,0:T(8,128)(2,1)} %convolution_convert_fusion.1), channel_id=1, source_target_pairs={{0,1},{1,2},{2,3},{3,0},{4,5},{5,6},{6,7},{7,4},{8,9},{9,10},{10,1... | collective-permute-start | bytes 1769480 | tf_op jit(solution)/shard_map/ppermute | solution.py:227
  163.3 14.6 %collective-permute-start.13 = (bf16[384,768]{1,0:T(8,128)(2,1)}, bf16[384,768]{1,0:T(8,128)(2,1)}, u32[]{:S(2)}, u32[]{:S(2)}) collective-permute-start(bf16[384,768]{1,0:T(8,128)(2,1)} %convolution_convert_fusion), channel_id=1, source_target_pairs={{0,3},{1,0},{2,1},{3,2},{4,7},{5,4},{6,5},{7,6},{8,11},{9,8},{10,9... | collective-permute-start | bytes 1769480 | tf_op jit(solution)/shard_map/ppermute | solution.py:227

commit v7 on v6

--- a/solution.py
+++ b/solution.py
@@ -34,12 +34,13 @@
     return lax.dynamic_slice_in_dim(text_kv, half * half_width, half_width, 2)
 
 
-def exchange(block, devices, step):
+def exchange(block, devices, group):
     position = lax.axis_index("tm")
-    other = lax.ppermute(block, "tm", [(i, i ^ step) for i in range(devices)])
-    low_first = jnp.concatenate([block, other], axis=1)
-    high_first = jnp.concatenate([other, block], axis=1)
-    return jnp.where((position & step) == 0, low_first, high_first)
+    parts = [block]
+    for offset in range(1, 4):
+        step = offset * group
+        parts.append(lax.ppermute(block, "tm", [(i, i ^ step) for i in range(devices)]))
+    return jnp.concatenate(parts, axis=1)
 
 
 def join_halves(mine):
@@ -187,10 +188,10 @@
     h_before = lax.ppermute(own, "height", shift_pairs(height_size, 1))
     h_after = lax.ppermute(own, "height", shift_pairs(height_size, -1))
     text_group = text_halves(text_kv)
-    step = 1
-    while step < tm_size:
-        text_group = exchange(text_group, tm_size, step)
-        step *= 2
+    group = 1
+    while group < tm_size:
+        text_group = exchange(text_group, tm_size, group)
+        group *= 4
     text = join_halves(text_group)
     sent, text = lax.optimization_barrier((own, text))
     t_before = lax.ppermute(sent, "tm", shift_pairs(tm_size, 1))

time: 182 us -> 180 us (0.989)
  the two profiles are of different devices: /device:TPU:97 before, /device:TPU:33 now
where the time goes in v7:
time: 180 us; the launch traced here: 178 us
  waiting for transfers between devices  74 us (41%)
  Pallas kernels  45.5 us (25%)
  starting transfers between devices  36.6 us (20%)
  matrix products  10.5 us (6%)
  local copies, waits for them, and re-layouts  5.99 us (3%)
  other arithmetic  5.27 us (3%)
    pallas_call x3, Pallas kernels, attend(): pl.pallas_call(kernel, grid_spec=grid_spec, out_shape=out_shape)  45.5 us
    ppermute x1, waiting for transfers between devices, per_device(): h_after = lax.ppermute(own, 'height', shift_pairs(height_size, -1))  33.5 us
    ppermute x6, waiting for transfers between devices, exchange(): lax.ppermute(block, 'tm', [(i, i ^ step) for i in range(devices)])  14 us
    ppermute x3, waiting for transfers between devices, per_device(): received.append(lax.ppermute(part, 'mp', pairs))  12.6 us
    ppermute x6, starting transfers between devices, exchange(): lax.ppermute(block, 'tm', [(i, i ^ step) for i in range(devices)])  12.2 us
    dot_general x3, matrix products, per_device(): jnp.dot(attended, w_part, preferred_element_type=jnp.float32)  7.59 us
    ppermute x1, starting transfers between devices, per_device(): t_after = lax.ppermute(sent, 'tm', shift_pairs(tm_size, -1))  5.57 us
    ppermute x3, starting transfers between devices, per_device(): received.append(lax.ppermute(part, 'mp', pairs))  5.5 us
  transfers between devices with their start and end apart: 16, of which 13 were waited for; matrix products, arithmetic and copies ran while one was open for 7% of the time, Pallas kernels for 17%

profile of v7, /device:TPU:33, one launch (start us, length us, event | category | flops | bytes accessed | tf_op | source)
XLA Modules:
  0.0 178.0 jit_solution(9535286298183623733)
XLA Ops:
  0.0 0.7 constant_dynamic-update-slice_fusion.6
  0.7 2.7 %collective-permute-start = (bf16[2,16,384]{2,1,0:T(8,128)(2,1)S(1)}, bf16[2,16,384]{2,1,0:T(8,128)(2,1)S(1)}, u32[]{:S(2)}, u32[]{:S(2)}) collective-permute-start(bf16[2,16,384]{2,1,0:T(8,128)(2,1)S(1)} %get-tuple-element.32), channel_id=1, source_target_pairs={{0,16},{16,0},{32,48},{48,32},{64,80},{80,64},{96,112},{112,96},{1... | collective-permute-start | bytes 73736 | tf_op jit(solution)/shard_map/ppermute | solution.py:42
  3.5 0.0 collective-permute-start.1
  3.5 1.4 collective-permute-start.2
  4.9 0.0 collective-permute-done
  4.9 1.4 collective-permute-done.1
  6.4 2.2 %collective-permute-done.2 = bf16[2,16,384]{2,1,0:T(8,128)(2,1)S(1)} collective-permute-done((bf16[2,16,384]{2,1,0:T(8,128)(2,1)S(1)}, bf16[2,16,384]{2,1,0:T(8,128)(2,1)S(1)}, u32[]{:S(2)}, u32[]{:S(2)}) %collective-permute-start.2) | collective-permute-done | bytes 24608 | tf_op jit(solution)/shard_map/ppermute | solution.py:42
  8.6 0.0 copy-start.3
  8.6 0.0 copy-start.5
  8.6 3.1 %collective-permute-start.3 = (bf16[2,64,384]{2,1,0:T(8,128)(2,1)S(1)}, bf16[2,64,384]{2,1,0:T(8,128)(2,1)S(1)}, u32[]{:S(2)}, u32[]{:S(2)}) collective-permute-start(bf16[2,64,384]{2,1,0:T(8,128)(2,1)S(1)} %pad_maximum_fusion.1), channel_id=1, source_target_pairs={{0,64},{16,80},{32,96},{48,112},{64,0},{80,16},{96,32},{112,48},{1... | collective-permute-start | bytes 294920 | tf_op jit(solution)/shard_map/ppermute | solution.py:42
  11.7 4.9 %collective-permute-start.4 = (bf16[2,64,384]{2,1,0:T(8,128)(2,1)S(1)}, bf16[2,64,384]{2,1,0:T(8,128)(2,1)S(1)}, u32[]{:S(2)}, u32[]{:S(2)}) collective-permute-start(bf16[2,64,384]{2,1,0:T(8,128)(2,1)S(1)} %pad_maximum_fusion.1), channel_id=1, source_target_pairs={{0,128},{16,144},{32,160},{48,176},{64,192},{80,208},{96,224},{112... | collective-permute-start | bytes 294920 | tf_op jit(solution)/shard_map/ppermute | solution.py:42
  16.6 0.0 collective-permute-start.5
  16.7 0.0 collective-permute-done.3
  16.7 3.0 %collective-permute-done.4 = bf16[2,64,384]{2,1,0:T(8,128)(2,1)S(1)} collective-permute-done((bf16[2,64,384]{2,1,0:T(8,128)(2,1)S(1)}, bf16[2,64,384]{2,1,0:T(8,128)(2,1)S(1)}, u32[]{:S(2)}, u32[]{:S(2)}) %collective-permute-start.4) | collective-permute-done | bytes 98336 | tf_op jit(solution)/shard_map/ppermute | solution.py:42
  19.7 7.3 %collective-permute-done.5 = bf16[2,64,384]{2,1,0:T(8,128)(2,1)S(1)} collective-permute-done((bf16[2,64,384]{2,1,0:T(8,128)(2,1)S(1)}, bf16[2,64,384]{2,1,0:T(8,128)(2,1)S(1)}, u32[]{:S(2)}, u32[]{:S(2)}) %collective-permute-start.5) | collective-permute-done | bytes 98336 | tf_op jit(solution)/shard_map/ppermute | solution.py:42
  27.1 1.0 collective-permute-start.6
  28.1 1.9 %collective-permute-start.10 = (bf16[2,384,768]{2,1,0:T(8,128)(2,1)}, bf16[2,384,768]{2,1,0:T(8,128)(2,1)}, u32[]{:S(2)}, u32[]{:S(2)}) collective-permute-start(bf16[2,384,768]{2,1,0:T(8,128)(2,1)} %bitcast.22), channel_id=1, source_target_pairs={{4,0},{8,4},{12,8},{5,1},{9,5},{13,9},{6,2},{10,6},{14,10},{7,3},{... | collective-permute-start | bytes 3538952 | tf_op jit(solution)/shard_map/ppermute | solution.py:189
  30.0 3.6 %collective-permute-start.9 = (bf16[2,384,768]{2,1,0:T(8,128)(2,1)}, bf16[2,384,768]{2,1,0:T(8,128)(2,1)}, u32[]{:S(2)}, u32[]{:S(2)}) collective-permute-start(bf16[2,384,768]{2,1,0:T(8,128)(2,1)} %bitcast.23), channel_id=1, source_target_pairs={{0,4},{4,8},{8,12},{1,5},{5,9},{9,13},{2,6},{6,10},{10,14},{3,7},{... | collective-permute-start | bytes 3538952 | tf_op jit(solution)/shard_map/ppermute | solution.py:188
  33.7 0.0 collective-permute-done.6
  33.7 1.1 maximum_select_fusion.rest_0_
  34.7 0.0 copy-done.3
  34.7 2.1 %collective-permute-start.7 = (bf16[2,384,768]{2,1,0:T(8,128)(2,1)S(1)}, bf16[2,384,768]{2,1,0:T(8,128)(2,1)S(1)}, u32[]{:S(2)}, u32[]{:S(2)}) collective-permute-start(bf16[2,384,768]{2,1,0:T(8,128)(2,1)S(1)} %bitcast.25), channel_id=1, source_target_pairs={{0,16},{16,32},{32,48},{48,64},{64,80},{80,96},{96,112},{112,128},... | collective-permute-start | bytes 3538952 | tf_op jit(solution)/shard_map/ppermute | solution.py:197
  36.9 5.6 %collective-permute-start.8 = (bf16[2,384,768]{2,1,0:T(8,128)(2,1)S(1)}, bf16[2,384,768]{2,1,0:T(8,128)(2,1)S(1)}, u32[]{:S(2)}, u32[]{:S(2)}) collective-permute-start(bf16[2,384,768]{2,1,0:T(8,128)(2,1)S(1)} %bitcast.26), channel_id=1, source_target_pairs={{16,0},{32,16},{48,32},{64,48},{80,64},{96,80},{112,96},{128,112},... | collective-permute-start | bytes 3538952 | tf_op jit(solution)/shard_map/ppermute | solution.py:198
  42.5 0.0 copy-done.5
  42.5 0.1 pad_dynamic-slice_fusion
  42.6 0.1 copy.16
  42.6 0.6 lt.111
  43.2 0.1 copy.17
  43.3 0.6 lt.116
  43.9 0.0 copy-done.6
  43.9 0.7 copy.22.reach_ref
  44.6 1.3 and_select_fusion.rest_3_.rest_4_
  46.0 33.5 %collective-permute-done.10.rest_2_ = bf16[2,384,768]{2,1,0:T(8,128)(2,1)} collective-permute-done((bf16[2,384,768]{2,1,0:T(8,128)(2,1)}, bf16[2,384,768]{2,1,0:T(8,128)(2,1)}, u32[]{:S(2)}, u32[]{:S(2)}) %collective-permute-start.10) | collective-permute-done | bytes 1179680 | tf_op jit(solution)/shard_map/ppermute | solution.py:189
  79.5 2.2 %collective-permute-done.9.rest_1_ = bf16[2,384,768]{2,1,0:T(8,128)(2,1)} collective-permute-done((bf16[2,384,768]{2,1,0:T(8,128)(2,1)}, bf16[2,384,768]{2,1,0:T(8,128)(2,1)}, u32[]{:S(2)}, u32[]{:S(2)}) %collective-permute-start.9) | collective-permute-done | bytes 1179680 | tf_op jit(solution)/shard_map/ppermute | solution.py:188
  81.7 14.5 %shard_map.82 = (f32[6,384,1]{2,1,0:T(8,128)}, f32[6,384,1]{2,1,0:T(8,128)}, f32[384,768]{1,0:T(8,128)}) custom-call(s32[6,2]{1,0:T(8,128)} %copy.22.reach_ref, bf16[384,768]{1,0:T(8,128)(2,1)} %bitcast.17, bf16[2,384,768]{2,1,0:T(8,128)(2,1)} %bitcast.24, bf16[2,384,768]{2,1,0:T(8,128)(2,1)} %collective-permute-done.9.rest_1_, ...), custom_call_target="tpu_custom_call" | custom-call | tf_op jit(solution)/shard_map/pallas_call | solution.py:177
  96.2 1.3 collective-permute-done.7.rest_1_
  97.6 0.7 collective-permute-done.8.rest_2_
  98.2 1.0 copy-done.2
  99.2 1.6 pad_maximum_fusion
  100.9 0.0 copy-done.1
  100.9 2.4 %collective-permute-start.11 = (bf16[2,2,384,768]{3,2,1,0:T(8,128)(2,1)}, bf16[2,2,384,768]{3,2,1,0:T(8,128)(2,1)S(1)}, u32[]{:S(2)}, u32[]{:S(2)}) collective-permute-start(bf16[2,2,384,768]{3,2,1,0:T(8,128)(2,1)} %pad_maximum_fusion), channel_id=1, source_target_pairs={{0,4},{4,8},{8,12},{1,5},{5,9},{9,13},{2,6},{6,10},{10,14},{3,7},{... | collective-permute-start | bytes 7077896 | tf_op jit(solution)/shard_map/ppermute | solution.py:213
  103.3 2.2 %collective-permute-start.12 = (bf16[2,2,384,768]{3,2,1,0:T(8,128)(2,1)}, bf16[2,2,384,768]{3,2,1,0:T(8,128)(2,1)}, u32[]{:S(2)}, u32[]{:S(2)}) collective-permute-start(bf16[2,2,384,768]{3,2,1,0:T(8,128)(2,1)} %pad_maximum_fusion), channel_id=1, source_target_pairs={{4,0},{8,4},{12,8},{5,1},{9,5},{13,9},{6,2},{10,6},{14,10},{7,3},{... | collective-permute-start | bytes 7077896 | tf_op jit(solution)/shard_map/ppermute | solution.py:214
  105.6 0.6 slice.12
  106.2 0.6 slice.13
  106.7 1.2 fusion.18
  108.0 0.8 copy.23.rest_8_
  108.8 15.4 %shard_map.83 = (f32[6,384,1]{2,1,0:T(8,128)}, f32[6,384,1]{2,1,0:T(8,128)}, f32[384,768]{1,0:T(8,128)}) custom-call(s32[6,2]{1,0:T(8,128)} %copy.22.reach_ref, bf16[384,768]{1,0:T(8,128)(2,1)} %bitcast.18, bf16[2,256,768]{2,1,0:T(8,128)(2,1)} %maximum_select_fusion.rest_0_, bf16[2,384,768]{2,1,0:T(8,128)(2,1)} %copy-done.1, bf16[2,384,768]{2,1,0:T(8,128)(2,1)} %copy-done.2, ...), custom_call_target="tpu_custom_call" | custom-call | tf_op jit(solution)/shard_map/pallas_call | solution.py:177
  124.2 5.2 %collective-permute-done.11.rest_0_.rest_2_ = bf16[2,2,384,768]{3,2,1,0:T(8,128)(2,1)S(1)} collective-permute-done((bf16[2,2,384,768]{3,2,1,0:T(8,128)(2,1)}, bf16[2,2,384,768]{3,2,1,0:T(8,128)(2,1)S(1)}, u32[]{:S(2)}, u32[]{:S(2)}) %collective-permute-start.11) | collective-permute-done | bytes 2359328 | tf_op jit(solution)/shard_map/ppermute | solution.py:213
  129.4 4.4 %collective-permute-done.12.rest_1_.rest_3_ = bf16[2,2,384,768]{3,2,1,0:T(8,128)(2,1)} collective-permute-done((bf16[2,2,384,768]{3,2,1,0:T(8,128)(2,1)}, bf16[2,2,384,768]{3,2,1,0:T(8,128)(2,1)}, u32[]{:S(2)}, u32[]{:S(2)}) %collective-permute-start.12) | collective-permute-done | bytes 2359328 | tf_op jit(solution)/shard_map/ppermute | solution.py:214
  133.8 0.0 copy-done
  133.8 15.6 %shard_map.84 = bf16[384,768]{1,0:T(8,128)(2,1)} custom-call(s32[6,2]{1,0:T(8,128)} %copy.22.reach_ref, bf16[384,768]{1,0:T(8,128)(2,1)} %bitcast.19, bf16[2,2,384,768]{3,2,1,0:T(8,128)(2,1)} %copy-done, bf16[2,2,384,768]{3,2,1,0:T(8,128)(2,1)} %collective-permute-done.12.rest_1_.rest_3_, bf16[2,2,384,768]{3,2,1,0:T(8,128)(2,1)} %copy-done, ...), custom_call_target="tpu_custom_call" | custom-call | tf_op jit(solution)/shard_map/pallas_call | solution.py:177
  149.4 2.1 %convolution_convert_fusion.2 = bf16[384,768]{1,0:T(8,128)(2,1)S(1)} fusion(bf16[384,768]{1,0:T(8,128)(2,1)} %shard_map.84, bf16[768,3072]{1,0:T(8,128)(2,1)} %param.12, s32[]{:T(128)S(6)} %select_n.105), kind=kOutput, calls=%fused_computation.3 | convolution fusion | flops 453279744 | bytes 2359300 | tf_op jit(solution)/shard_map/dot_general | solution.py:226
  151.5 0.1 collective-permute-start.13
  151.6 0.0 copy-done.4
  151.6 2.7 %convolution_convert_fusion.1 = bf16[384,768]{1,0:T(8,128)(2,1)} fusion(bf16[384,768]{1,0:T(8,128)(2,1)S(1)} %copy-done.4, bf16[768,3072]{1,0:T(8,128)(2,1)} %param.12, s32[]{:T(128)S(6)} %select_n.107), kind=kOutput, calls=%fused_computation.2 | convolution fusion | flops 453279744 | bytes 2359300 | tf_op jit(solution)/shard_map/dot_general | solution.py:226
  154.4 4.4 %collective-permute-start.14 = (bf16[384,768]{1,0:T(8,128)(2,1)}, bf16[384,768]{1,0:T(8,128)(2,1)S(1)}, u32[]{:S(2)}, u32[]{:S(2)}) collective-permute-start(bf16[384,768]{1,0:T(8,128)(2,1)} %convolution_convert_fusion.1), channel_id=1, source_target_pairs={{0,1},{1,2},{2,3},{3,0},{4,5},{5,6},{6,7},{7,4},{8,9},{9,10},{10,1... | collective-permute-start | bytes 1769480 | tf_op jit(solution)/shard_map/ppermute | solution.py:228
  158.8 2.7 %convolution_convert_fusion = bf16[384,768]{1,0:T(8,128)(2,1)} fusion(bf16[384,768]{1,0:T(8,128)(2,1)S(1)} %copy-done.4, bf16[768,3072]{1,0:T(8,128)(2,1)} %param.12, s32[]{:T(128)S(6)} %select_n.109), kind=kOutput, calls=%fused_computation.1 | convolution fusion | flops 453279744 | bytes 2359300 | tf_op jit(solution)/shard_map/dot_general | solution.py:226
  161.5 1.0 collective-permute-start.15
  162.5 5.1 %collective-permute-done.13 = bf16[384,768]{1,0:T(8,128)(2,1)S(1)} collective-permute-done((bf16[384,768]{1,0:T(8,128)(2,1)S(1)}, bf16[384,768]{1,0:T(8,128)(2,1)S(1)}, u32[]{:S(2)}, u32[]{:S(2)}) %collective-permute-start.13) | collective-permute-done | bytes 589856 | tf_op jit(solution)/shard_map/ppermute | solution.py:228
  167.6 4.9 %collective-permute-done.14 = bf16[384,768]{1,0:T(8,128)(2,1)S(1)} collective-permute-done((bf16[384,768]{1,0:T(8,128)(2,1)}, bf16[384,768]{1,0:T(8,128)(2,1)S(1)}, u32[]{:S(2)}, u32[]{:S(2)}) %collective-permute-start.14) | collective-permute-done | bytes 589856 | tf_op jit(solution)/shard_map/ppermute | solution.py:228
  172.5 2.6 %collective-permute-done.15 = bf16[384,768]{1,0:T(8,128)(2,1)S(1)} collective-permute-done((bf16[384,768]{1,0:T(8,128)(2,1)}, bf16[384,768]{1,0:T(8,128)(2,1)S(1)}, u32[]{:S(2)}, u32[]{:S(2)}) %collective-permute-start.15) | collective-permute-done | bytes 589856 | tf_op jit(solution)/shard_map/ppermute | solution.py:228
  175.1 0.0 copy-done.7
  175.1 0.0 copy-done.8
  175.1 2.9 %fusion.7 = bf16[1,1,384,768]{3,2,1,0:T(8,128)(2,1)} fusion(bf16[384,768]{1,0:T(8,128)(2,1)S(1)} %copy-done.4, bf16[384,768]{1,0:T(8,128)(2,1)S(1)} %collective-permute-done.15, bf16[384,768]{1,0:T(8,128)(2,1)S(1)} %collective-permute-done.14, bf16[384,768]{1,0:T(8,128)(2,1)S(1)} %collective-permute-done.13, bf16[768,3072]{1,0:T(8,128)(2,1)} %param.12, ...), kind=kOutput, calls=%fused_computation.12 | convolution fusion | flops 456523776 | bytes 4721668 | tf_op jit(solution)/shard_map/dot_general | solution.py:230
  (15 shorter events, 0.1 us)
Async XLA Ops:
  0.7 4.2 %collective-permute-start = (bf16[2,16,384]{2,1,0:T(8,128)(2,1)S(1)}, bf16[2,16,384]{2,1,0:T(8,128)(2,1)S(1)}, u32[]{:S(2)}, u32[]{:S(2)}) collective-permute-start(bf16[2,16,384]{2,1,0:T(8,128)(2,1)S(1)} %get-tuple-element.32), channel_id=1, source_target_pairs={{0,16},{16,0},{32,48},{48,32},{64,80},{80,64},{96,112},{112,96},{1... | collective-permute-start | bytes 73736 | tf_op jit(solution)/shard_map/ppermute | solution.py:42
  3.5 2.9 %collective-permute-start.1 = (bf16[2,16,384]{2,1,0:T(8,128)(2,1)S(1)}, bf16[2,16,384]{2,1,0:T(8,128)(2,1)S(1)}, u32[]{:S(2)}, u32[]{:S(2)}) collective-permute-start(bf16[2,16,384]{2,1,0:T(8,128)(2,1)S(1)} %get-tuple-element.32), channel_id=1, source_target_pairs={{0,32},{16,48},{32,0},{48,16},{64,96},{80,112},{96,64},{112,80},{1... | collective-permute-start | bytes 73736 | tf_op jit(solution)/shard_map/ppermute | solution.py:42
  3.5 5.1 %collective-permute-start.2 = (bf16[2,16,384]{2,1,0:T(8,128)(2,1)S(1)}, bf16[2,16,384]{2,1,0:T(8,128)(2,1)S(1)}, u32[]{:S(2)}, u32[]{:S(2)}) collective-permute-start(bf16[2,16,384]{2,1,0:T(8,128)(2,1)S(1)} %get-tuple-element.32), channel_id=1, source_target_pairs={{0,48},{16,32},{32,16},{48,0},{64,112},{80,96},{96,80},{112,64},{1... | collective-permute-start | bytes 73736 | tf_op jit(solution)/shard_map/ppermute | solution.py:42
  8.6 26.2 %copy-start.3 = (bf16[1,1,2,384,768]{4,3,2,1,0:T(8,128)(2,1)S(1)}, bf16[1,1,2,384,768]{4,3,2,1,0:T(8,128)(2,1)}, u32[]{:S(2)}) copy-start(bf16[1,1,2,384,768]{4,3,2,1,0:T(8,128)(2,1)} %param.9) | copy-start | bytes 3538948
  8.6 33.9 %copy-start.5 = (s32[2,16,4]{1,2,0:T(4,128)S(1)}, s32[2,16,4]{1,2,0:T(4,128)}, u32[]{:S(2)}) copy-start(s32[2,16,4]{1,2,0:T(4,128)} %param.15) | copy-start | bytes 1540
  8.6 8.1 %collective-permute-start.3 = (bf16[2,64,384]{2,1,0:T(8,128)(2,1)S(1)}, bf16[2,64,384]{2,1,0:T(8,128)(2,1)S(1)}, u32[]{:S(2)}, u32[]{:S(2)}) collective-permute-start(bf16[2,64,384]{2,1,0:T(8,128)(2,1)S(1)} %pad_maximum_fusion.1), channel_id=1, source_target_pairs={{0,64},{16,80},{32,96},{48,112},{64,0},{80,16},{96,32},{112,48},{1... | collective-permute-start | bytes 294920 | tf_op jit(solution)/shard_map/ppermute | solution.py:42
  11.7 8.0 %collective-permute-start.4 = (bf16[2,64,384]{2,1,0:T(8,128)(2,1)S(1)}, bf16[2,64,384]{2,1,0:T(8,128)(2,1)S(1)}, u32[]{:S(2)}, u32[]{:S(2)}) collective-permute-start(bf16[2,64,384]{2,1,0:T(8,128)(2,1)S(1)} %pad_maximum_fusion.1), channel_id=1, source_target_pairs={{0,128},{16,144},{32,160},{48,176},{64,192},{80,208},{96,224},{112... | collective-permute-start | bytes 294920 | tf_op jit(solution)/shard_map/ppermute | solution.py:42
  16.6 10.4 %collective-permute-start.5 = (bf16[2,64,384]{2,1,0:T(8,128)(2,1)S(1)}, bf16[2,64,384]{2,1,0:T(8,128)(2,1)S(1)}, u32[]{:S(2)}, u32[]{:S(2)}) collective-permute-start(bf16[2,64,384]{2,1,0:T(8,128)(2,1)S(1)} %pad_maximum_fusion.1), channel_id=1, source_target_pairs={{0,192},{16,208},{32,224},{48,240},{64,128},{80,144},{96,160},{112... | collective-permute-start | bytes 294920 | tf_op jit(solution)/shard_map/ppermute | solution.py:42
  16.6 27.3 %copy-start.6 = (s32[6,2]{0,1:T(2,128)S(1)}, s32[6,2]{0,1:T(2,128)}, u32[]{:S(2)}) copy-start(s32[6,2]{0,1:T(2,128)} %param.14) | copy-start | bytes 148
  27.1 6.6 %collective-permute-start.6 = (bf16[2,256,384]{2,1,0:T(8,128)(2,1)S(1)}, bf16[2,256,384]{2,1,0:T(8,128)(2,1)S(1)}, u32[]{:S(2)}, u32[]{:S(2)}) collective-permute-start(bf16[2,256,384]{2,1,0:T(8,128)(2,1)S(1)} %constant_dynamic-update-slice_fusion), channel_id=1, source_target_pairs={{0,4},{4,0},{8,12},{12,8},{1,5},{5,1},{9,13},{13,9},{2,6},{6,2},{1... | collective-permute-start | bytes 1179656 | tf_op jit(solution)/shard_map/ppermute | solution.py:49
  28.1 51.4 %collective-permute-start.10 = (bf16[2,384,768]{2,1,0:T(8,128)(2,1)}, bf16[2,384,768]{2,1,0:T(8,128)(2,1)}, u32[]{:S(2)}, u32[]{:S(2)}) collective-permute-start(bf16[2,384,768]{2,1,0:T(8,128)(2,1)} %bitcast.22), channel_id=1, source_target_pairs={{4,0},{8,4},{12,8},{5,1},{9,5},{13,9},{6,2},{10,6},{14,10},{7,3},{... | collective-permute-start | bytes 3538952 | tf_op jit(solution)/shard_map/ppermute | solution.py:189
  30.0 51.7 %collective-permute-start.9 = (bf16[2,384,768]{2,1,0:T(8,128)(2,1)}, bf16[2,384,768]{2,1,0:T(8,128)(2,1)}, u32[]{:S(2)}, u32[]{:S(2)}) collective-permute-start(bf16[2,384,768]{2,1,0:T(8,128)(2,1)} %bitcast.23), channel_id=1, source_target_pairs={{0,4},{4,8},{8,12},{1,5},{5,9},{9,13},{2,6},{6,10},{10,14},{3,7},{... | collective-permute-start | bytes 3538952 | tf_op jit(solution)/shard_map/ppermute | solution.py:188
  34.7 62.8 %collective-permute-start.7 = (bf16[2,384,768]{2,1,0:T(8,128)(2,1)S(1)}, bf16[2,384,768]{2,1,0:T(8,128)(2,1)S(1)}, u32[]{:S(2)}, u32[]{:S(2)}) collective-permute-start(bf16[2,384,768]{2,1,0:T(8,128)(2,1)S(1)} %bitcast.25), channel_id=1, source_target_pairs={{0,16},{16,32},{32,48},{48,64},{64,80},{80,96},{96,112},{112,128},... | collective-permute-start | bytes 3538952 | tf_op jit(solution)/shard_map/ppermute | solution.py:197
  36.9 61.4 %collective-permute-start.8 = (bf16[2,384,768]{2,1,0:T(8,128)(2,1)S(1)}, bf16[2,384,768]{2,1,0:T(8,128)(2,1)S(1)}, u32[]{:S(2)}, u32[]{:S(2)}) collective-permute-start(bf16[2,384,768]{2,1,0:T(8,128)(2,1)S(1)} %bitcast.26), channel_id=1, source_target_pairs={{16,0},{32,16},{48,32},{64,48},{80,64},{96,80},{112,96},{128,112},... | collective-permute-start | bytes 3538952 | tf_op jit(solution)/shard_map/ppermute | solution.py:198
  97.6 3.3 %copy-start.1 = (bf16[2,384,768]{2,1,0:T(8,128)(2,1)}, bf16[2,384,768]{2,1,0:T(8,128)(2,1)S(1)}, u32[]{:S(2)}) copy-start(bf16[2,384,768]{2,1,0:T(8,128)(2,1)S(1)} %collective-permute-done.7.rest_1_) | copy-start | bytes 3538948
  98.2 1.0 copy-start.2
  100.9 28.5 %collective-permute-start.11 = (bf16[2,2,384,768]{3,2,1,0:T(8,128)(2,1)}, bf16[2,2,384,768]{3,2,1,0:T(8,128)(2,1)S(1)}, u32[]{:S(2)}, u32[]{:S(2)}) collective-permute-start(bf16[2,2,384,768]{3,2,1,0:T(8,128)(2,1)} %pad_maximum_fusion), channel_id=1, source_target_pairs={{0,4},{4,8},{8,12},{1,5},{5,9},{9,13},{2,6},{6,10},{10,14},{3,7},{... | collective-permute-start | bytes 7077896 | tf_op jit(solution)/shard_map/ppermute | solution.py:213
  103.3 30.5 %collective-permute-start.12 = (bf16[2,2,384,768]{3,2,1,0:T(8,128)(2,1)}, bf16[2,2,384,768]{3,2,1,0:T(8,128)(2,1)}, u32[]{:S(2)}, u32[]{:S(2)}) collective-permute-start(bf16[2,2,384,768]{3,2,1,0:T(8,128)(2,1)} %pad_maximum_fusion), channel_id=1, source_target_pairs={{4,0},{8,4},{12,8},{5,1},{9,5},{13,9},{6,2},{10,6},{14,10},{7,3},{... | collective-permute-start | bytes 7077896 | tf_op jit(solution)/shard_map/ppermute | solution.py:214
  129.4 4.4 %copy-start = (bf16[2,2,384,768]{3,2,1,0:T(8,128)(2,1)}, bf16[2,2,384,768]{3,2,1,0:T(8,128)(2,1)S(1)}, u32[]{:S(2)}) copy-start(bf16[2,2,384,768]{3,2,1,0:T(8,128)(2,1)S(1)} %collective-permute-done.11.rest_0_.rest_2_) | copy-start | bytes 7077892
  149.4 2.3 %copy-start.4 = (bf16[384,768]{1,0:T(8,128)(2,1)S(1)}, bf16[384,768]{1,0:T(8,128)(2,1)}, u32[]{:S(2)}) copy-start(bf16[384,768]{1,0:T(8,128)(2,1)} %shard_map.84) | copy-start | bytes 1769476
  151.5 16.1 %collective-permute-start.13 = (bf16[384,768]{1,0:T(8,128)(2,1)S(1)}, bf16[384,768]{1,0:T(8,128)(2,1)S(1)}, u32[]{:S(2)}, u32[]{:S(2)}) collective-permute-start(bf16[384,768]{1,0:T(8,128)(2,1)S(1)} %convolution_convert_fusion.2), channel_id=1, source_target_pairs={{0,2},{1,3},{2,0},{3,1},{4,6},{5,7},{6,4},{7,5},{8,10},{9,11},{10,... | collective-permute-start | bytes 1769480 | tf_op jit(solution)/shard_map/ppermute | solution.py:228
  154.4 20.8 %copy-start.7 = (bf16[1,1,384,768]{3,2,1,0:T(8,128)(2,1)S(1)}, bf16[1,1,384,768]{3,2,1,0:T(8,128)(2,1)}, u32[]{:S(2)}) copy-start(bf16[1,1,384,768]{3,2,1,0:T(8,128)(2,1)} %param.11) | copy-start | bytes 1769476
  154.4 20.8 %copy-start.8 = (f32[768]{0:T(1024)S(1)}, f32[768]{0:T(1024)}, u32[]{:S(2)}) copy-start(f32[768]{0:T(1024)} %param.13) | copy-start | bytes 9220
  154.4 18.1 %collective-permute-start.14 = (bf16[384,768]{1,0:T(8,128)(2,1)}, bf16[384,768]{1,0:T(8,128)(2,1)S(1)}, u32[]{:S(2)}, u32[]{:S(2)}) collective-permute-start(bf16[384,768]{1,0:T(8,128)(2,1)} %convolution_convert_fusion.1), channel_id=1, source_target_pairs={{0,1},{1,2},{2,3},{3,0},{4,5},{5,6},{6,7},{7,4},{8,9},{9,10},{10,1... | collective-permute-start | bytes 1769480 | tf_op jit(solution)/shard_map/ppermute | solution.py:228
  161.5 13.6 %collective-permute-start.15 = (bf16[384,768]{1,0:T(8,128)(2,1)}, bf16[384,768]{1,0:T(8,128)(2,1)S(1)}, u32[]{:S(2)}, u32[]{:S(2)}) collective-permute-start(bf16[384,768]{1,0:T(8,128)(2,1)} %convolution_convert_fusion), channel_id=1, source_target_pairs={{0,3},{1,0},{2,1},{3,2},{4,7},{5,4},{6,5},{7,6},{8,11},{9,8},{10,9... | collective-permute-start | bytes 1769480 | tf_op jit(solution)/shard_map/ppermute | solution.py:228

commit v8 on v6

--- a/solution.py
+++ b/solution.py
@@ -192,7 +192,7 @@
         text_group = exchange(text_group, tm_size, step)
         step *= 2
     text = join_halves(text_group)
-    sent, text = lax.optimization_barrier((own, text))
+    sent, text, h_before, h_after = lax.optimization_barrier((own, text, h_before, h_after))
     t_before = lax.ppermute(sent, "tm", shift_pairs(tm_size, 1))
     t_after = lax.ppermute(sent, "tm", shift_pairs(tm_size, -1))
     time_start = lax.axis_index("tm")

time: 182 us -> 180 us (0.989)
  starting transfers between devices: 42.4 us -> 34 us
  Pallas kernels: 42.5 us -> 44.9 us
  local copies, waits for them, and re-layouts: 5.18 us -> 7.26 us
    ppermute x1, waiting for transfers between devices: 0.01 us -> 32.6 us  [per_device(): t_before = lax.ppermute(sent, 'tm', shift_pairs(tm_size, 1))]
    ppermute x1, waiting for transfers between devices: 30.4 us -> 0.01 us  [per_device(): h_before = lax.ppermute(own, 'height', shift_pairs(height_size, 1))]
    ppermute x1, waiting for transfers between devices: 8.11 us -> 0.01 us  [per_device(): h_after = lax.ppermute(own, 'height', shift_pairs(height_size, -1))]
    ppermute x4, waiting for transfers between devices: 13.4 us -> 18.7 us  [exchange(): other = lax.ppermute(block, 'tm', [(i, i ^ step) for i in range(devices)])]
    ppermute x1, starting transfers between devices: 6.41 us -> 1.36 us  [join_halves(): other = lax.ppermute(mine, 'height', pairs)]
    ppermute x1, starting transfers between devices: 5.84 us -> 3.16 us  [per_device(): c_before = lax.ppermute(time_pair, 'height', shift_pairs(height_size, 1))]
    pallas_call x3, Pallas kernels: 42.5 us -> 44.9 us  [attend(): pl.pallas_call(kernel, grid_spec=grid_spec, out_shape=out_shape)]
    ppermute x1, waiting for transfers between devices: 6.48 us -> 4.21 us  [per_device(): c_after = lax.ppermute(time_pair, 'height', shift_pairs(height_size, -1))]
  transfers between devices with their start and end apart: 14 -> 14, of which waited for: 12 -> 10; matrix products, arithmetic and copies ran while one was open for 6% -> 7% of each run, Pallas kernels for 16% -> 17%
where the time goes in v8:
time: 180 us; the launch traced here: 178 us
  waiting for transfers between devices  76.3 us (42%)
  Pallas kernels  44.9 us (25%)
  starting transfers between devices  34 us (19%)
  matrix products  10.6 us (6%)
  local copies, waits for them, and re-layouts  7.26 us (4%)
  other arithmetic  4.93 us (3%)
    pallas_call x3, Pallas kernels, attend(): pl.pallas_call(kernel, grid_spec=grid_spec, out_shape=out_shape)  44.9 us
    ppermute x1, waiting for transfers between devices, per_device(): t_before = lax.ppermute(sent, 'tm', shift_pairs(tm_size, 1))  32.6 us
    ppermute x4, waiting for transfers between devices, exchange(): other = lax.ppermute(block, 'tm', [(i, i ^ step) for i in range(devices)])  18.7 us
    ppermute x3, waiting for transfers between devices, per_device(): received.append(lax.ppermute(part, 'mp', pairs))  15.6 us
    dot_general x3, matrix products, per_device(): jnp.dot(attended, w_part, preferred_element_type=jnp.float32)  7.59 us
    ppermute x4, starting transfers between devices, exchange(): other = lax.ppermute(block, 'tm', [(i, i ^ step) for i in range(devices)])  7.11 us
    ppermute x3, starting transfers between devices, per_device(): received.append(lax.ppermute(part, 'mp', pairs))  5.5 us
    ppermute x1, starting transfers between devices, per_device(): h_before = lax.ppermute(own, 'height', shift_pairs(height_size, 1))  4.92 us
  transfers between devices with their start and end apart: 14, of which 10 were waited for; matrix products, arithmetic and copies ran while one was open for 7% of the time, Pallas kernels for 17%

profile of v8, /device:TPU:97, one launch (start us, length us, event | category | flops | bytes accessed | tf_op | source)
XLA Modules:
  0.0 178.3 jit_solution(8925340324932875004)
XLA Ops:
  0.0 0.0 copy-start
  0.0 0.8 copy-done
  0.8 2.7 %collective-permute-start = (bf16[2,16,384]{2,1,0:T(8,128)(2,1)S(1)}, bf16[2,16,384]{2,1,0:T(8,128)(2,1)S(1)}, u32[]{:S(2)}, u32[]{:S(2)}) collective-permute-start(bf16[2,16,384]{2,1,0:T(8,128)(2,1)S(1)} %constant_dynamic-slice_fusion), channel_id=1, source_target_pairs={{0,16},{16,0},{32,48},{48,32},{64,80},{80,64},{96,112},{112,96},{1... | collective-permute-start | bytes 73736 | tf_op jit(solution)/shard_map/ppermute | solution.py:39
  3.5 1.4 collective-permute-done
  5.0 0.1 collective-permute-start.1
  5.1 4.9 %collective-permute-start.5 = (bf16[2,384,768]{2,1,0:T(8,128)(2,1)}, bf16[2,384,768]{2,1,0:T(8,128)(2,1)S(1)}, u32[]{:S(2)}, u32[]{:S(2)}) collective-permute-start(bf16[2,384,768]{2,1,0:T(8,128)(2,1)} %bitcast.2.rest_0_), channel_id=1, source_target_pairs={{0,4},{4,8},{8,12},{1,5},{5,9},{9,13},{2,6},{6,10},{10,14},{3,7},{... | collective-permute-start | bytes 3538952 | tf_op jit(solution)/shard_map/ppermute | solution.py:187
  10.0 1.9 %collective-permute-start.6 = (bf16[2,384,768]{2,1,0:T(8,128)(2,1)}, bf16[2,384,768]{2,1,0:T(8,128)(2,1)S(1)}, u32[]{:S(2)}, u32[]{:S(2)}) collective-permute-start(bf16[2,384,768]{2,1,0:T(8,128)(2,1)} %bitcast.2.rest_0_), channel_id=1, source_target_pairs={{4,0},{8,4},{12,8},{5,1},{9,5},{13,9},{6,2},{10,6},{14,10},{7,3},{... | collective-permute-start | bytes 3538952 | tf_op jit(solution)/shard_map/ppermute | solution.py:188
  12.0 0.0 collective-permute-done.1
  12.0 0.1 collective-permute-start.2
  12.1 7.1 %collective-permute-done.2 = bf16[2,64,384]{2,1,0:T(8,128)(2,1)S(1)} collective-permute-done((bf16[2,64,384]{2,1,0:T(8,128)(2,1)S(1)}, bf16[2,64,384]{2,1,0:T(8,128)(2,1)S(1)}, u32[]{:S(2)}, u32[]{:S(2)}) %collective-permute-start.2) | collective-permute-done | bytes 98336 | tf_op jit(solution)/shard_map/ppermute | solution.py:39
  19.3 4.2 %collective-permute-start.3 = (bf16[2,128,384]{2,1,0:T(8,128)(2,1)S(1)}, bf16[2,128,384]{2,1,0:T(8,128)(2,1)S(1)}, u32[]{:S(2)}, u32[]{:S(2)}) collective-permute-start(bf16[2,128,384]{2,1,0:T(8,128)(2,1)S(1)} %maximum_select_fusion.2), channel_id=1, source_target_pairs={{0,128},{16,144},{32,160},{48,176},{64,192},{80,208},{96,224},{112... | collective-permute-start | bytes 589832 | tf_op jit(solution)/shard_map/ppermute | solution.py:39
  23.5 0.0 copy-start.8
  23.5 10.1 %collective-permute-done.3 = bf16[2,128,384]{2,1,0:T(8,128)(2,1)S(1)} collective-permute-done((bf16[2,128,384]{2,1,0:T(8,128)(2,1)S(1)}, bf16[2,128,384]{2,1,0:T(8,128)(2,1)S(1)}, u32[]{:S(2)}, u32[]{:S(2)}) %collective-permute-start.3) | collective-permute-done | bytes 196640 | tf_op jit(solution)/shard_map/ppermute | solution.py:39
  33.6 0.1 maximum_select_fusion.1
  33.7 1.4 collective-permute-start.4
  35.1 1.3 collective-permute-done.4
  36.4 1.1 maximum_select_fusion.rest_0_
  37.5 0.0 collective-permute-done.5.rest_1_
  37.5 0.0 copy-start.4
  37.5 1.0 copy-done.4
  38.5 0.0 collective-permute-done.6.rest_2_
  38.5 0.0 copy-start.5
  38.6 1.0 copy-done.5
  39.6 4.6 %collective-permute-start.7 = (bf16[2,384,768]{2,1,0:T(8,128)(2,1)}, bf16[2,384,768]{2,1,0:T(8,128)(2,1)S(1)}, u32[]{:S(2)}, u32[]{:S(2)}) collective-permute-start(bf16[2,384,768]{2,1,0:T(8,128)(2,1)} %bitcast.2.rest_0_), channel_id=1, source_target_pairs={{0,16},{16,32},{32,48},{48,64},{64,80},{80,96},{96,112},{112,128},... | collective-permute-start | bytes 3538952 | tf_op jit(solution)/shard_map/ppermute | solution.py:196
  44.2 3.0 %collective-permute-start.8 = (bf16[2,384,768]{2,1,0:T(8,128)(2,1)}, bf16[2,384,768]{2,1,0:T(8,128)(2,1)S(1)}, u32[]{:S(2)}, u32[]{:S(2)}) collective-permute-start(bf16[2,384,768]{2,1,0:T(8,128)(2,1)} %bitcast.2.rest_0_), channel_id=1, source_target_pairs={{16,0},{32,16},{48,32},{64,48},{80,64},{96,80},{112,96},{128,112},... | collective-permute-start | bytes 3538952 | tf_op jit(solution)/shard_map/ppermute | solution.py:197
  47.3 0.0 copy-done.7
  47.3 0.1 pad_dynamic-slice_fusion
  47.4 0.1 copy.16
  47.5 0.1 lt.111
  47.6 0.1 copy.17
  47.6 0.1 lt.116
  47.7 0.0 copy-done.8
  47.7 0.7 copy.22.reach_ref
  48.4 0.7 and_select_fusion.rest_3_.rest_4_
  49.1 13.0 %shard_map.82 = (f32[6,384,1]{2,1,0:T(8,128)}, f32[6,384,1]{2,1,0:T(8,128)}, f32[384,768]{1,0:T(8,128)}) custom-call(s32[6,2]{1,0:T(8,128)} %copy.22.reach_ref, bf16[384,768]{1,0:T(8,128)(2,1)} %bitcast.17, bf16[2,384,768]{2,1,0:T(8,128)(2,1)} %bitcast.2.rest_0_, bf16[2,384,768]{2,1,0:T(8,128)(2,1)} %copy-done.4, bf16[2,384,768]{2,1,0:T(8,128)(2,1)} %copy-done.5, ...), custom_call_target="tpu_custom_call" | custom-call | tf_op jit(solution)/shard_map/pallas_call | solution.py:176
  62.1 32.6 %collective-permute-done.7.rest_1_ = bf16[2,384,768]{2,1,0:T(8,128)(2,1)S(1)} collective-permute-done((bf16[2,384,768]{2,1,0:T(8,128)(2,1)}, bf16[2,384,768]{2,1,0:T(8,128)(2,1)S(1)}, u32[]{:S(2)}, u32[]{:S(2)}) %collective-permute-start.7) | collective-permute-done | bytes 1179680 | tf_op jit(solution)/shard_map/ppermute | solution.py:196
  94.8 2.5 %collective-permute-done.8.rest_2_ = bf16[2,384,768]{2,1,0:T(8,128)(2,1)S(1)} collective-permute-done((bf16[2,384,768]{2,1,0:T(8,128)(2,1)}, bf16[2,384,768]{2,1,0:T(8,128)(2,1)S(1)}, u32[]{:S(2)}, u32[]{:S(2)}) %collective-permute-start.8) | collective-permute-done | bytes 1179680 | tf_op jit(solution)/shard_map/ppermute | solution.py:197
  97.2 0.0 copy-done.2
  97.2 1.0 copy-done.3
  98.3 1.7 pad_maximum_fusion
  99.9 2.4 %collective-permute-start.10 = (bf16[2,2,384,768]{3,2,1,0:T(8,128)(2,1)}, bf16[2,2,384,768]{3,2,1,0:T(8,128)(2,1)S(1)}, u32[]{:S(2)}, u32[]{:S(2)}) collective-permute-start(bf16[2,2,384,768]{3,2,1,0:T(8,128)(2,1)} %pad_maximum_fusion), channel_id=1, source_target_pairs={{4,0},{8,4},{12,8},{5,1},{9,5},{13,9},{6,2},{10,6},{14,10},{7,3},{... | collective-permute-start | bytes 7077896 | tf_op jit(solution)/shard_map/ppermute | solution.py:213
  102.3 3.2 %collective-permute-start.9 = (bf16[2,2,384,768]{3,2,1,0:T(8,128)(2,1)}, bf16[2,2,384,768]{3,2,1,0:T(8,128)(2,1)}, u32[]{:S(2)}, u32[]{:S(2)}) collective-permute-start(bf16[2,2,384,768]{3,2,1,0:T(8,128)(2,1)} %pad_maximum_fusion), channel_id=1, source_target_pairs={{0,4},{4,8},{8,12},{1,5},{5,9},{9,13},{2,6},{6,10},{10,14},{3,7},{... | collective-permute-start | bytes 7077896 | tf_op jit(solution)/shard_map/ppermute | solution.py:212
  105.5 0.6 slice.12
  106.2 0.6 slice.13
  106.8 1.3 fusion.18
  108.1 0.8 copy.23.rest_8_
  108.9 17.2 %shard_map.83 = (f32[6,384,1]{2,1,0:T(8,128)}, f32[6,384,1]{2,1,0:T(8,128)}, f32[384,768]{1,0:T(8,128)}) custom-call(s32[6,2]{1,0:T(8,128)} %copy.22.reach_ref, bf16[384,768]{1,0:T(8,128)(2,1)} %bitcast.18, bf16[2,256,768]{2,1,0:T(8,128)(2,1)} %maximum_select_fusion.rest_0_, bf16[2,384,768]{2,1,0:T(8,128)(2,1)} %copy-done.2, bf16[2,384,768]{2,1,0:T(8,128)(2,1)} %copy-done.3, ...), custom_call_target="tpu_custom_call" | custom-call | tf_op jit(solution)/shard_map/pallas_call | solution.py:176
  126.1 4.2 %collective-permute-done.10.rest_1_.rest_3_ = bf16[2,2,384,768]{3,2,1,0:T(8,128)(2,1)S(1)} collective-permute-done((bf16[2,2,384,768]{3,2,1,0:T(8,128)(2,1)}, bf16[2,2,384,768]{3,2,1,0:T(8,128)(2,1)S(1)}, u32[]{:S(2)}, u32[]{:S(2)}) %collective-permute-start.10) | collective-permute-done | bytes 2359328 | tf_op jit(solution)/shard_map/ppermute | solution.py:213
  130.3 1.3 collective-permute-done.9.rest_0_.rest_2_
  131.6 0.2 copy-done.1
  131.7 14.7 %shard_map.84 = bf16[384,768]{1,0:T(8,128)(2,1)} custom-call(s32[6,2]{1,0:T(8,128)} %copy.22.reach_ref, bf16[384,768]{1,0:T(8,128)(2,1)} %bitcast.19, bf16[2,2,384,768]{3,2,1,0:T(8,128)(2,1)} %collective-permute-done.9.rest_0_.rest_2_, bf16[2,2,384,768]{3,2,1,0:T(8,128)(2,1)} %copy-done.1, bf16[2,2,384,768]{3,2,1,0:T(8,128)(2,1)} %collective-permute-done.9.rest_0_.rest_2_, ...), custom_call_target="tpu_custom_call" | custom-call | tf_op jit(solution)/shard_map/pallas_call | solution.py:176
  146.5 2.1 %convolution_convert_fusion.2 = bf16[384,768]{1,0:T(8,128)(2,1)S(1)} fusion(bf16[384,768]{1,0:T(8,128)(2,1)} %shard_map.84, bf16[768,3072]{1,0:T(8,128)(2,1)} %param.12, s32[]{:T(128)S(6)} %select_n.145), kind=kOutput, calls=%fused_computation.3 | convolution fusion | flops 453279744 | bytes 2359300 | tf_op jit(solution)/shard_map/dot_general | solution.py:225
  148.6 2.8 %collective-permute-start.11 = (bf16[384,768]{1,0:T(8,128)(2,1)S(1)}, bf16[384,768]{1,0:T(8,128)(2,1)S(1)}, u32[]{:S(2)}, u32[]{:S(2)}) collective-permute-start(bf16[384,768]{1,0:T(8,128)(2,1)S(1)} %convolution_convert_fusion.2), channel_id=1, source_target_pairs={{0,2},{1,3},{2,0},{3,1},{4,6},{5,7},{6,4},{7,5},{8,10},{9,11},{10,... | collective-permute-start | bytes 1769480 | tf_op jit(solution)/shard_map/ppermute | solution.py:227
  151.4 0.0 copy-done.6
  151.4 2.7 %convolution_convert_fusion.1 = bf16[384,768]{1,0:T(8,128)(2,1)} fusion(bf16[384,768]{1,0:T(8,128)(2,1)S(1)} %copy-done.6, bf16[768,3072]{1,0:T(8,128)(2,1)} %param.12, s32[]{:T(128)S(6)} %select_n.147), kind=kOutput, calls=%fused_computation.2 | convolution fusion | flops 453279744 | bytes 2359300 | tf_op jit(solution)/shard_map/dot_general | solution.py:225
  154.2 1.6 collective-permute-start.12
  155.7 2.7 %convolution_convert_fusion = bf16[384,768]{1,0:T(8,128)(2,1)} fusion(bf16[384,768]{1,0:T(8,128)(2,1)S(1)} %copy-done.6, bf16[768,3072]{1,0:T(8,128)(2,1)} %param.12, s32[]{:T(128)S(6)} %select_n.149), kind=kOutput, calls=%fused_computation.1 | convolution fusion | flops 453279744 | bytes 2359300 | tf_op jit(solution)/shard_map/dot_general | solution.py:225
  158.5 1.1 collective-permute-start.13
  159.6 6.0 %collective-permute-done.11 = bf16[384,768]{1,0:T(8,128)(2,1)S(1)} collective-permute-done((bf16[384,768]{1,0:T(8,128)(2,1)S(1)}, bf16[384,768]{1,0:T(8,128)(2,1)S(1)}, u32[]{:S(2)}, u32[]{:S(2)}) %collective-permute-start.11) | collective-permute-done | bytes 589856 | tf_op jit(solution)/shard_map/ppermute | solution.py:227
  165.5 9.7 %collective-permute-done.12 = bf16[384,768]{1,0:T(8,128)(2,1)S(1)} collective-permute-done((bf16[384,768]{1,0:T(8,128)(2,1)}, bf16[384,768]{1,0:T(8,128)(2,1)S(1)}, u32[]{:S(2)}, u32[]{:S(2)}) %collective-permute-start.12) | collective-permute-done | bytes 589856 | tf_op jit(solution)/shard_map/ppermute | solution.py:227
  175.2 0.0 collective-permute-done.13
  175.2 0.0 copy-done.9
  175.2 0.0 copy-done.10
  175.2 3.1 %fusion.7 = bf16[1,1,384,768]{3,2,1,0:T(8,128)(2,1)} fusion(bf16[384,768]{1,0:T(8,128)(2,1)S(1)} %copy-done.6, bf16[384,768]{1,0:T(8,128)(2,1)} %collective-permute-done.13, bf16[384,768]{1,0:T(8,128)(2,1)S(1)} %collective-permute-done.12, bf16[384,768]{1,0:T(8,128)(2,1)S(1)} %collective-permute-done.11, bf16[768,3072]{1,0:T(8,128)(2,1)} %param.12, ...), kind=kOutput, calls=%fused_computation.12 | convolution fusion | flops 456523776 | bytes 4721668 | tf_op jit(solution)/shard_map/dot_general | solution.py:229
  (12 shorter events, 0.1 us)
Async XLA Ops:
  0.0 0.8 copy-start
  0.8 4.2 %collective-permute-start = (bf16[2,16,384]{2,1,0:T(8,128)(2,1)S(1)}, bf16[2,16,384]{2,1,0:T(8,128)(2,1)S(1)}, u32[]{:S(2)}, u32[]{:S(2)}) collective-permute-start(bf16[2,16,384]{2,1,0:T(8,128)(2,1)S(1)} %constant_dynamic-slice_fusion), channel_id=1, source_target_pairs={{0,16},{16,0},{32,48},{48,32},{64,80},{80,64},{96,112},{112,96},{1... | collective-permute-start | bytes 73736 | tf_op jit(solution)/shard_map/ppermute | solution.py:39
  5.0 7.0 %collective-permute-start.1 = (bf16[2,32,384]{2,1,0:T(8,128)(2,1)S(1)}, bf16[2,32,384]{2,1,0:T(8,128)(2,1)S(1)}, u32[]{:S(2)}, u32[]{:S(2)}) collective-permute-start(bf16[2,32,384]{2,1,0:T(8,128)(2,1)S(1)} %maximum_select_fusion.4), channel_id=1, source_target_pairs={{0,32},{16,48},{32,0},{48,16},{64,96},{80,112},{96,64},{112,80},{1... | collective-permute-start | bytes 147464 | tf_op jit(solution)/shard_map/ppermute | solution.py:39
  5.1 32.4 %collective-permute-start.5 = (bf16[2,384,768]{2,1,0:T(8,128)(2,1)}, bf16[2,384,768]{2,1,0:T(8,128)(2,1)S(1)}, u32[]{:S(2)}, u32[]{:S(2)}) collective-permute-start(bf16[2,384,768]{2,1,0:T(8,128)(2,1)} %bitcast.2.rest_0_), channel_id=1, source_target_pairs={{0,4},{4,8},{8,12},{1,5},{5,9},{9,13},{2,6},{6,10},{10,14},{3,7},{... | collective-permute-start | bytes 3538952 | tf_op jit(solution)/shard_map/ppermute | solution.py:187
  10.0 28.5 %collective-permute-start.6 = (bf16[2,384,768]{2,1,0:T(8,128)(2,1)}, bf16[2,384,768]{2,1,0:T(8,128)(2,1)S(1)}, u32[]{:S(2)}, u32[]{:S(2)}) collective-permute-start(bf16[2,384,768]{2,1,0:T(8,128)(2,1)} %bitcast.2.rest_0_), channel_id=1, source_target_pairs={{4,0},{8,4},{12,8},{5,1},{9,5},{13,9},{6,2},{10,6},{14,10},{7,3},{... | collective-permute-start | bytes 3538952 | tf_op jit(solution)/shard_map/ppermute | solution.py:188
  12.0 7.2 %collective-permute-start.2 = (bf16[2,64,384]{2,1,0:T(8,128)(2,1)S(1)}, bf16[2,64,384]{2,1,0:T(8,128)(2,1)S(1)}, u32[]{:S(2)}, u32[]{:S(2)}) collective-permute-start(bf16[2,64,384]{2,1,0:T(8,128)(2,1)S(1)} %maximum_select_fusion.3), channel_id=1, source_target_pairs={{0,64},{16,80},{32,96},{48,112},{64,0},{80,16},{96,32},{112,48},{1... | collective-permute-start | bytes 294920 | tf_op jit(solution)/shard_map/ppermute | solution.py:39
  19.3 14.3 %collective-permute-start.3 = (bf16[2,128,384]{2,1,0:T(8,128)(2,1)S(1)}, bf16[2,128,384]{2,1,0:T(8,128)(2,1)S(1)}, u32[]{:S(2)}, u32[]{:S(2)}) collective-permute-start(bf16[2,128,384]{2,1,0:T(8,128)(2,1)S(1)} %maximum_select_fusion.2), channel_id=1, source_target_pairs={{0,128},{16,144},{32,160},{48,176},{64,192},{80,208},{96,224},{112... | collective-permute-start | bytes 589832 | tf_op jit(solution)/shard_map/ppermute | solution.py:39
  23.5 23.8 %copy-start.7 = (s32[2,16,4]{1,2,0:T(4,128)S(1)}, s32[2,16,4]{1,2,0:T(4,128)}, u32[]{:S(2)}) copy-start(s32[2,16,4]{1,2,0:T(4,128)} %param.15) | copy-start | bytes 1540
  23.5 24.3 %copy-start.8 = (s32[6,2]{0,1:T(2,128)S(1)}, s32[6,2]{0,1:T(2,128)}, u32[]{:S(2)}) copy-start(s32[6,2]{0,1:T(2,128)} %param.14) | copy-start | bytes 148
  33.7 2.7 %collective-permute-start.4 = (bf16[2,256,384]{2,1,0:T(8,128)(2,1)S(1)}, bf16[2,256,384]{2,1,0:T(8,128)(2,1)S(1)}, u32[]{:S(2)}, u32[]{:S(2)}) collective-permute-start(bf16[2,256,384]{2,1,0:T(8,128)(2,1)S(1)} %maximum_select_fusion.1), channel_id=1, source_target_pairs={{0,4},{4,0},{8,12},{12,8},{1,5},{5,1},{9,13},{13,9},{2,6},{6,2},{1... | collective-permute-start | bytes 1179656 | tf_op jit(solution)/shard_map/ppermute | solution.py:48
  37.5 1.0 copy-start.4
  38.5 1.0 copy-start.5
  39.6 55.2 %collective-permute-start.7 = (bf16[2,384,768]{2,1,0:T(8,128)(2,1)}, bf16[2,384,768]{2,1,0:T(8,128)(2,1)S(1)}, u32[]{:S(2)}, u32[]{:S(2)}) collective-permute-start(bf16[2,384,768]{2,1,0:T(8,128)(2,1)} %bitcast.2.rest_0_), channel_id=1, source_target_pairs={{0,16},{16,32},{32,48},{48,64},{64,80},{80,96},{96,112},{112,128},... | collective-permute-start | bytes 3538952 | tf_op jit(solution)/shard_map/ppermute | solution.py:196
  44.2 53.0 %collective-permute-start.8 = (bf16[2,384,768]{2,1,0:T(8,128)(2,1)}, bf16[2,384,768]{2,1,0:T(8,128)(2,1)S(1)}, u32[]{:S(2)}, u32[]{:S(2)}) collective-permute-start(bf16[2,384,768]{2,1,0:T(8,128)(2,1)} %bitcast.2.rest_0_), channel_id=1, source_target_pairs={{16,0},{32,16},{48,32},{64,48},{80,64},{96,80},{112,96},{128,112},... | collective-permute-start | bytes 3538952 | tf_op jit(solution)/shard_map/ppermute | solution.py:197
  94.8 2.5 %copy-start.2 = (bf16[2,384,768]{2,1,0:T(8,128)(2,1)}, bf16[2,384,768]{2,1,0:T(8,128)(2,1)S(1)}, u32[]{:S(2)}) copy-start(bf16[2,384,768]{2,1,0:T(8,128)(2,1)S(1)} %collective-permute-done.7.rest_1_) | copy-start | bytes 3538948
  97.2 1.0 copy-start.3
  99.9 30.4 %collective-permute-start.10 = (bf16[2,2,384,768]{3,2,1,0:T(8,128)(2,1)}, bf16[2,2,384,768]{3,2,1,0:T(8,128)(2,1)S(1)}, u32[]{:S(2)}, u32[]{:S(2)}) collective-permute-start(bf16[2,2,384,768]{3,2,1,0:T(8,128)(2,1)} %pad_maximum_fusion), channel_id=1, source_target_pairs={{4,0},{8,4},{12,8},{5,1},{9,5},{13,9},{6,2},{10,6},{14,10},{7,3},{... | collective-permute-start | bytes 7077896 | tf_op jit(solution)/shard_map/ppermute | solution.py:213
  102.3 29.3 %collective-permute-start.9 = (bf16[2,2,384,768]{3,2,1,0:T(8,128)(2,1)}, bf16[2,2,384,768]{3,2,1,0:T(8,128)(2,1)}, u32[]{:S(2)}, u32[]{:S(2)}) collective-permute-start(bf16[2,2,384,768]{3,2,1,0:T(8,128)(2,1)} %pad_maximum_fusion), channel_id=1, source_target_pairs={{0,4},{4,8},{8,12},{1,5},{5,9},{9,13},{2,6},{6,10},{10,14},{3,7},{... | collective-permute-start | bytes 7077896 | tf_op jit(solution)/shard_map/ppermute | solution.py:212
  130.3 1.4 copy-start.1
  146.4 5.0 %copy-start.6 = (bf16[384,768]{1,0:T(8,128)(2,1)S(1)}, bf16[384,768]{1,0:T(8,128)(2,1)}, u32[]{:S(2)}) copy-start(bf16[384,768]{1,0:T(8,128)(2,1)} %shard_map.84) | copy-start | bytes 1769476
  148.6 16.9 %collective-permute-start.11 = (bf16[384,768]{1,0:T(8,128)(2,1)S(1)}, bf16[384,768]{1,0:T(8,128)(2,1)S(1)}, u32[]{:S(2)}, u32[]{:S(2)}) collective-permute-start(bf16[384,768]{1,0:T(8,128)(2,1)S(1)} %convolution_convert_fusion.2), channel_id=1, source_target_pairs={{0,2},{1,3},{2,0},{3,1},{4,6},{5,7},{6,4},{7,5},{8,10},{9,11},{10,... | collective-permute-start | bytes 1769480 | tf_op jit(solution)/shard_map/ppermute | solution.py:227
  154.2 21.0 %copy-start.9 = (bf16[1,1,384,768]{3,2,1,0:T(8,128)(2,1)S(1)}, bf16[1,1,384,768]{3,2,1,0:T(8,128)(2,1)}, u32[]{:S(2)}) copy-start(bf16[1,1,384,768]{3,2,1,0:T(8,128)(2,1)} %param.11) | copy-start | bytes 1769476
  154.2 21.0 %copy-start.10 = (f32[768]{0:T(1024)S(1)}, f32[768]{0:T(1024)}, u32[]{:S(2)}) copy-start(f32[768]{0:T(1024)} %param.13) | copy-start | bytes 9220
  154.2 21.0 %collective-permute-start.12 = (bf16[384,768]{1,0:T(8,128)(2,1)}, bf16[384,768]{1,0:T(8,128)(2,1)S(1)}, u32[]{:S(2)}, u32[]{:S(2)}) collective-permute-start(bf16[384,768]{1,0:T(8,128)(2,1)} %convolution_convert_fusion.1), channel_id=1, source_target_pairs={{0,1},{1,2},{2,3},{3,0},{4,5},{5,6},{6,7},{7,4},{8,9},{9,10},{10,1... | collective-permute-start | bytes 1769480 | tf_op jit(solution)/shard_map/ppermute | solution.py:227
  158.5 16.7 %collective-permute-start.13 = (bf16[384,768]{1,0:T(8,128)(2,1)}, bf16[384,768]{1,0:T(8,128)(2,1)}, u32[]{:S(2)}, u32[]{:S(2)}) collective-permute-start(bf16[384,768]{1,0:T(8,128)(2,1)} %convolution_convert_fusion), channel_id=1, source_target_pairs={{0,3},{1,0},{2,1},{3,2},{4,7},{5,4},{6,5},{7,6},{8,11},{9,8},{10,9... | collective-permute-start | bytes 1769480 | tf_op jit(solution)/shard_map/ppermute | solution.py:227

commit v9 on v8

--- a/solution.py
+++ b/solution.py
@@ -129,6 +129,7 @@
 
 def attend(reach, queries, text, tiles, bias, state=None, qvalid=None):
     tile_len, col_width = queries.shape
+    key_len = tiles[0][0].shape[-2]
     heads = col_width // HD
     blocks = [b for _, _, b in tiles]
     specs = [pl.BlockSpec((tile_len, HD), lambda h, r: (0, h))]
@@ -138,10 +139,10 @@
         args.append(text)
     for array, index, _ in tiles:
         if index is None:
-            specs.append(pl.BlockSpec((2, tile_len, HD), lambda h, r: (0, 0, h)))
+            specs.append(pl.BlockSpec((2, key_len, HD), lambda h, r: (0, 0, h)))
         else:
             specs.append(
-                pl.BlockSpec((None, 2, tile_len, HD), lambda h, r, i=index: (i, 0, 0, h))
+                pl.BlockSpec((None, 2, key_len, HD), lambda h, r, i=index: (i, 0, 0, h))
             )
         args.append(array)
     specs.append(pl.BlockSpec(bias.shape, lambda h, r: (0, 0, 0)))
@@ -214,10 +215,28 @@
     across = [(t_before, None, 1), (t_after, None, 7)]
     state = attend(head_reach, queries, text, across, bias, state)
     corners = [(c_before, 0, 0), (c_after, 0, 2), (c_before, 1, 6), (c_after, 1, 8)]
-    attended = attend(head_reach, queries, None, corners, bias, state, qvalid)
-
     mp_index = lax.axis_index("mp")
     chunk = out_weight.shape[1] // mp_size
+    rows = tile_len // 2
+    outputs = []
+    for start in (0, rows):
+        part_state = (
+            state[0][:, start:start + rows],
+            state[1][:, start:start + rows],
+            state[2][start:start + rows],
+        )
+        attended = attend(
+            head_reach, queries[start:start + rows], None, corners, bias, part_state,
+            qvalid[start:start + rows],
+        )
+        outputs.append(
+            project(attended, out_weight, out_gate, residual[0, 0, start:start + rows],
+                    mp_index, mp_size, chunk)
+        )
+    return jnp.concatenate(outputs, axis=0)[None, None]
+
+
+def project(attended, out_weight, out_gate, residual, mp_index, mp_size, chunk):
     received = []
     for step in (2, 1, 3):
         target = (mp_index + step) % mp_size
@@ -230,8 +249,8 @@
     branch = branch.astype(jnp.float32)
     for part in received:
         branch = branch + part.astype(jnp.float32)
-    updated = residual[0, 0].astype(jnp.float32) + out_gate * branch
-    return updated.astype(jnp.bfloat16)[None, None]
+    updated = residual.astype(jnp.float32) + out_gate * branch
+    return updated.astype(jnp.bfloat16)
 
 
 def solution(mesh):

time: 180 us -> 194 us (1.078)
  waiting for transfers between devices: 76.3 us -> 62.6 us
  Pallas kernels: 44.9 us -> 56.1 us
  local copies, waits for them, and re-layouts: 7.26 us -> 15.4 us
  matrix products: 10.6 us -> 16.7 us
  starting transfers between devices: 34 us -> 36.9 us
    pallas_call x3 -> x4, Pallas kernels: 44.9 us -> 56.1 us  [attend(): pl.pallas_call(kernel, grid_spec=grid_spec, out_shape=out_shape)]
    slice x0 -> x7, local copies, waits for them, and re-layouts: none -> 7.19 us  [the longest x1 2.47 us: per_device(): state[2][start:start + rows]]
    dot_general x4 -> x8, matrix products: 10.6 us -> 16.7 us  [the longest x6 13.3 us: project(): jnp.dot(attended, w_part, preferred_element_type=jnp.float32)]
    ppermute x3 -> x6, waiting for transfers between devices: 15.6 us -> 10.1 us  [project(): received.append(lax.ppermute(part, 'mp', pairs))]
    ppermute x1, waiting for transfers between devices: 4.21 us -> 0.01 us  [per_device(): c_after = lax.ppermute(time_pair, 'height', shift_pairs(height_size, -1))]
    ppermute x3 -> x6, starting transfers between devices: 5.5 us -> 8.37 us  [project(): received.append(lax.ppermute(part, 'mp', pairs))]
    ppermute x1, waiting for transfers between devices: 32.6 us -> 30.1 us  [per_device(): t_before = lax.ppermute(sent, 'tm', shift_pairs(tm_size, 1))]
    unnamed x23 -> x31, local copies, waits for them, and re-layouts: 4.75 us -> 6.6 us
  transfers between devices with their start and end apart: 14 -> 17, of which waited for: 10 -> 8; matrix products, arithmetic and copies ran while one was open for 7% -> 13% of each run, Pallas kernels for 17% -> 23%
where the time goes in v9:
time: 194 us
  waiting for transfers between devices  62.6 us (32%)
  Pallas kernels  56.1 us (29%)
  starting transfers between devices  36.9 us (19%)
  matrix products  16.7 us (9%)
  local copies, waits for them, and re-layouts  15.4 us (8%)
  other arithmetic  5.66 us (3%)
    pallas_call x4, Pallas kernels, attend(): pl.pallas_call(kernel, grid_spec=grid_spec, out_shape=out_shape)  56.1 us
    ppermute x1, waiting for transfers between devices, per_device(): t_before = lax.ppermute(sent, 'tm', shift_pairs(tm_size, 1))  30.1 us
    ppermute x4, waiting for transfers between devices, exchange(): other = lax.ppermute(block, 'tm', [(i, i ^ step) for i in range(devices)])  18.7 us
    dot_general x6, matrix products, project(): jnp.dot(attended, w_part, preferred_element_type=jnp.float32)  13.3 us
    ppermute x6, waiting for transfers between devices, project(): received.append(lax.ppermute(part, 'mp', pairs))  10.1 us
    ppermute x6, starting transfers between devices, project(): received.append(lax.ppermute(part, 'mp', pairs))  8.37 us
    ppermute x4, starting transfers between devices, exchange(): other = lax.ppermute(block, 'tm', [(i, i ^ step) for i in range(devices)])  7.11 us
    unnamed x31, local copies, waits for them, and re-layouts  6.6 us
  transfers between devices with their start and end apart: 17, of which 8 were waited for; matrix products, arithmetic and copies ran while one was open for 13% of the time, Pallas kernels for 23%

profile of v9, /device:TPU:97, one launch (start us, length us, event | category | flops | bytes accessed | tf_op | source)
XLA Modules:
  0.0 193.7 jit_solution(7587109155011588878)
XLA Ops:
  0.0 0.8 copy-done
  0.8 2.7 %collective-permute-start = (bf16[2,16,384]{2,1,0:T(8,128)(2,1)S(1)}, bf16[2,16,384]{2,1,0:T(8,128)(2,1)S(1)}, u32[]{:S(2)}, u32[]{:S(2)}) collective-permute-start(bf16[2,16,384]{2,1,0:T(8,128)(2,1)S(1)} %constant_dynamic-slice_fusion), channel_id=1, source_target_pairs={{0,16},{16,0},{32,48},{48,32},{64,80},{80,64},{96,112},{112,96},{1... | collective-permute-start | bytes 73736 | tf_op jit(solution)/shard_map/ppermute | solution.py:39
  3.5 1.4 collective-permute-done
  5.0 0.1 collective-permute-start.1
  5.1 4.9 %collective-permute-start.5 = (bf16[2,384,768]{2,1,0:T(8,128)(2,1)}, bf16[2,384,768]{2,1,0:T(8,128)(2,1)S(1)}, u32[]{:S(2)}, u32[]{:S(2)}) collective-permute-start(bf16[2,384,768]{2,1,0:T(8,128)(2,1)} %bitcast.2.rest_0_), channel_id=1, source_target_pairs={{0,4},{4,8},{8,12},{1,5},{5,9},{9,13},{2,6},{6,10},{10,14},{3,7},{... | collective-permute-start | bytes 3538952 | tf_op jit(solution)/shard_map/ppermute | solution.py:188
  10.0 1.9 collective-permute-start.6
  12.0 0.0 collective-permute-done.1
  12.0 0.1 collective-permute-start.2
  12.1 7.1 %collective-permute-done.2 = bf16[2,64,384]{2,1,0:T(8,128)(2,1)S(1)} collective-permute-done((bf16[2,64,384]{2,1,0:T(8,128)(2,1)S(1)}, bf16[2,64,384]{2,1,0:T(8,128)(2,1)S(1)}, u32[]{:S(2)}, u32[]{:S(2)}) %collective-permute-start.2) | collective-permute-done | bytes 98336 | tf_op jit(solution)/shard_map/ppermute | solution.py:39
  19.3 4.2 %collective-permute-start.3 = (bf16[2,128,384]{2,1,0:T(8,128)(2,1)S(1)}, bf16[2,128,384]{2,1,0:T(8,128)(2,1)S(1)}, u32[]{:S(2)}, u32[]{:S(2)}) collective-permute-start(bf16[2,128,384]{2,1,0:T(8,128)(2,1)S(1)} %maximum_select_fusion.2), channel_id=1, source_target_pairs={{0,128},{16,144},{32,160},{48,176},{64,192},{80,208},{96,224},{112... | collective-permute-start | bytes 589832 | tf_op jit(solution)/shard_map/ppermute | solution.py:39
  23.5 10.1 %collective-permute-done.3 = bf16[2,128,384]{2,1,0:T(8,128)(2,1)S(1)} collective-permute-done((bf16[2,128,384]{2,1,0:T(8,128)(2,1)S(1)}, bf16[2,128,384]{2,1,0:T(8,128)(2,1)S(1)}, u32[]{:S(2)}, u32[]{:S(2)}) %collective-permute-start.3) | collective-permute-done | bytes 196640 | tf_op jit(solution)/shard_map/ppermute | solution.py:39
  33.6 0.1 maximum_select_fusion.1
  33.7 1.4 collective-permute-start.4
  35.1 1.3 collective-permute-done.4
  36.4 1.1 maximum_select_fusion.rest_0_
  37.5 1.0 copy-done.7
  38.5 1.0 copy-done.8
  39.6 4.6 %collective-permute-start.7 = (bf16[2,384,768]{2,1,0:T(8,128)(2,1)}, bf16[2,384,768]{2,1,0:T(8,128)(2,1)S(1)}, u32[]{:S(2)}, u32[]{:S(2)}) collective-permute-start(bf16[2,384,768]{2,1,0:T(8,128)(2,1)} %bitcast.2.rest_0_), channel_id=1, source_target_pairs={{0,16},{16,32},{32,48},{48,64},{64,80},{80,96},{96,112},{112,128},... | collective-permute-start | bytes 3538952 | tf_op jit(solution)/shard_map/ppermute | solution.py:197
  44.2 3.0 %collective-permute-start.8 = (bf16[2,384,768]{2,1,0:T(8,128)(2,1)}, bf16[2,384,768]{2,1,0:T(8,128)(2,1)S(1)}, u32[]{:S(2)}, u32[]{:S(2)}) collective-permute-start(bf16[2,384,768]{2,1,0:T(8,128)(2,1)} %bitcast.2.rest_0_), channel_id=1, source_target_pairs={{16,0},{32,16},{48,32},{64,48},{80,64},{96,80},{112,96},{128,112},... | collective-permute-start | bytes 3538952 | tf_op jit(solution)/shard_map/ppermute | solution.py:198
  47.3 0.1 pad_dynamic-slice_fusion
  47.4 0.1 copy.17
  47.5 0.1 lt.121
  47.5 0.1 copy.18
  47.6 0.1 lt.126
  47.7 0.7 copy.23.reach_ref
  48.4 0.7 and_select_fusion.rest_3_.rest_4_
  49.1 15.6 %shard_map.82 = (f32[6,384,1]{2,1,0:T(8,128)}, f32[6,384,1]{2,1,0:T(8,128)}, f32[384,768]{1,0:T(8,128)}) custom-call(s32[6,2]{1,0:T(8,128)} %copy.23.reach_ref, bf16[384,768]{1,0:T(8,128)(2,1)} %bitcast.30, bf16[2,384,768]{2,1,0:T(8,128)(2,1)} %bitcast.2.rest_0_, bf16[2,384,768]{2,1,0:T(8,128)(2,1)} %copy-done.7, bf16[2,384,768]{2,1,0:T(8,128)(2,1)} %copy-done.8, ...), custom_call_target="tpu_custom_call" | custom-call | tf_op jit(solution)/shard_map/pallas_call | solution.py:177
  64.7 30.1 %collective-permute-done.7.rest_1_ = bf16[2,384,768]{2,1,0:T(8,128)(2,1)S(1)} collective-permute-done((bf16[2,384,768]{2,1,0:T(8,128)(2,1)}, bf16[2,384,768]{2,1,0:T(8,128)(2,1)S(1)}, u32[]{:S(2)}, u32[]{:S(2)}) %collective-permute-start.7) | collective-permute-done | bytes 1179680 | tf_op jit(solution)/shard_map/ppermute | solution.py:197
  94.8 2.5 %collective-permute-done.8.rest_2_ = bf16[2,384,768]{2,1,0:T(8,128)(2,1)S(1)} collective-permute-done((bf16[2,384,768]{2,1,0:T(8,128)(2,1)}, bf16[2,384,768]{2,1,0:T(8,128)(2,1)S(1)}, u32[]{:S(2)}, u32[]{:S(2)}) %collective-permute-start.8) | collective-permute-done | bytes 1179680 | tf_op jit(solution)/shard_map/ppermute | solution.py:198
  97.2 1.0 copy-done.6
  98.2 1.6 pad_maximum_fusion
  99.9 2.4 %collective-permute-start.10 = (bf16[2,2,384,768]{3,2,1,0:T(8,128)(2,1)}, bf16[2,2,384,768]{3,2,1,0:T(8,128)(2,1)S(1)}, u32[]{:S(2)}, u32[]{:S(2)}) collective-permute-start(bf16[2,2,384,768]{3,2,1,0:T(8,128)(2,1)} %pad_maximum_fusion), channel_id=1, source_target_pairs={{4,0},{8,4},{12,8},{5,1},{9,5},{13,9},{6,2},{10,6},{14,10},{7,3},{... | collective-permute-start | bytes 7077896 | tf_op jit(solution)/shard_map/ppermute | solution.py:214
  102.3 3.2 %collective-permute-start.9 = (bf16[2,2,384,768]{3,2,1,0:T(8,128)(2,1)}, bf16[2,2,384,768]{3,2,1,0:T(8,128)(2,1)}, u32[]{:S(2)}, u32[]{:S(2)}) collective-permute-start(bf16[2,2,384,768]{3,2,1,0:T(8,128)(2,1)} %pad_maximum_fusion), channel_id=1, source_target_pairs={{0,4},{4,8},{8,12},{1,5},{5,9},{9,13},{2,6},{6,10},{10,14},{3,7},{... | collective-permute-start | bytes 7077896 | tf_op jit(solution)/shard_map/ppermute | solution.py:213
  105.5 0.6 slice.78
  106.1 0.6 slice.79
  106.6 1.2 and_convert_fusion
  107.9 0.1 slice_bitcast_fusion.3
  108.0 0.8 copy.24.rest_8_
  108.7 0.8 copy.26.rest_8_
  109.5 0.9 slice_bitcast_fusion.1
  110.3 16.3 %shard_map.83 = (f32[6,384,1]{2,1,0:T(8,128)}, f32[6,384,1]{2,1,0:T(8,128)}, f32[384,768]{1,0:T(8,128)}) custom-call(s32[6,2]{1,0:T(8,128)} %copy.23.reach_ref, bf16[384,768]{1,0:T(8,128)(2,1)} %bitcast.31, bf16[2,256,768]{2,1,0:T(8,128)(2,1)} %maximum_select_fusion.rest_0_, bf16[2,384,768]{2,1,0:T(8,128)(2,1)} %copy-done.5, bf16[2,384,768]{2,1,0:T(8,128)(2,1)} %copy-done.6, ...), custom_call_target="tpu_custom_call" | custom-call | tf_op jit(solution)/shard_map/pallas_call | solution.py:177
  126.6 2.5 %fusion.36 = (f32[192,768]{1,0:T(8,128)}, f32[192,768]{1,0:T(8,128)}) fusion(f32[384,768]{1,0:T(8,128)} %get-tuple-element.34), kind=kLoop, calls=%fused_computation.70 | loop fusion | bytes 2359296 | tf_op jit(solution)/shard_map/slice | solution.py:226
  129.1 1.1 fusion.37
  130.2 0.6 copy-done.9
  130.8 1.2 fusion.38
  132.0 1.4 copy-done.1
  133.4 12.1 %shard_map.84 = bf16[192,768]{1,0:T(8,128)(2,1)} custom-call(s32[6,2]{1,0:T(8,128)} %copy.23.reach_ref, bf16[192,768]{1,0:T(8,128)(2,1)} %get-tuple-element.41.q_ref, bf16[2,2,384,768]{3,2,1,0:T(8,128)(2,1)} %collective-permute-done.9.rest_0_.rest_2_, bf16[2,2,384,768]{3,2,1,0:T(8,128)(2,1)} %copy-done.1, ...), custom_call_target="tpu_custom_call" | custom-call | tf_op jit(solution)/shard_map/pallas_call | solution.py:177
  145.5 1.8 convolution_convert_fusion.6
  147.3 2.8 %collective-permute-start.11 = (bf16[192,768]{1,0:T(8,128)(2,1)S(1)}, bf16[192,768]{1,0:T(8,128)(2,1)S(1)}, u32[]{:S(2)}, u32[]{:S(2)}) collective-permute-start(bf16[192,768]{1,0:T(8,128)(2,1)S(1)} %convolution_convert_fusion.6), channel_id=1, source_target_pairs={{0,2},{1,3},{2,0},{3,1},{4,6},{5,7},{6,4},{7,5},{8,10},{9,11},{10,... | collective-permute-start | bytes 884744 | tf_op jit(solution)/shard_map/ppermute | solution.py:246
  150.1 1.7 convolution_convert_fusion.5
  151.8 0.3 collective-permute-start.12
  152.1 2.4 %convolution_convert_fusion.4 = bf16[192,768]{1,0:T(8,128)(2,1)} fusion(bf16[192,768]{1,0:T(8,128)(2,1)S(1)} %copy-done.2, bf16[768,3072]{1,0:T(8,128)(2,1)} %param.12, s32[]{:T(128)S(6)} %select_n.159), kind=kOutput, calls=%fused_computation.12 | convolution fusion | flops 226639872 | bytes 1769476 | tf_op jit(solution)/shard_map/dot_general | solution.py:244
  154.5 2.7 %collective-permute-start.13 = (bf16[192,768]{1,0:T(8,128)(2,1)}, bf16[192,768]{1,0:T(8,128)(2,1)S(1)}, u32[]{:S(2)}, u32[]{:S(2)}) collective-permute-start(bf16[192,768]{1,0:T(8,128)(2,1)} %convolution_convert_fusion.4), channel_id=1, source_target_pairs={{0,3},{1,0},{2,1},{3,2},{4,7},{5,4},{6,5},{7,6},{8,11},{9,8},{10,9... | collective-permute-start | bytes 884744 | tf_op jit(solution)/shard_map/ppermute | solution.py:246
  157.1 12.1 %shard_map.85 = bf16[192,768]{1,0:T(8,128)(2,1)} custom-call(s32[6,2]{1,0:T(8,128)} %copy.23.reach_ref, bf16[192,768]{1,0:T(8,128)(2,1)} %get-tuple-element.42.q_ref, bf16[2,2,384,768]{3,2,1,0:T(8,128)(2,1)} %collective-permute-done.9.rest_0_.rest_2_, bf16[2,2,384,768]{3,2,1,0:T(8,128)(2,1)} %copy-done.1, ...), custom_call_target="tpu_custom_call" | custom-call | tf_op jit(solution)/shard_map/pallas_call | solution.py:177
  169.2 2.5 %convolution_convert_fusion.2 = bf16[192,768]{1,0:T(8,128)(2,1)} fusion(bf16[192,768]{1,0:T(8,128)(2,1)} %shard_map.85, bf16[768,3072]{1,0:T(8,128)(2,1)} %param.12, s32[]{:T(128)S(6)} %select_n.155), kind=kOutput, calls=%fused_computation.3 | convolution fusion | flops 226639872 | bytes 1769476 | tf_op jit(solution)/shard_map/dot_general | solution.py:244
  171.8 2.4 %convolution_convert_fusion.1 = bf16[192,768]{1,0:T(8,128)(2,1)} fusion(bf16[192,768]{1,0:T(8,128)(2,1)S(1)} %copy-done.3, bf16[768,3072]{1,0:T(8,128)(2,1)} %param.12, s32[]{:T(128)S(6)} %select_n.157), kind=kOutput, calls=%fused_computation.2 | convolution fusion | flops 226639872 | bytes 1769476 | tf_op jit(solution)/shard_map/dot_general | solution.py:244
  174.2 0.0 collective-permute-start.14
  174.2 2.5 %convolution_convert_fusion = bf16[192,768]{1,0:T(8,128)(2,1)} fusion(bf16[192,768]{1,0:T(8,128)(2,1)S(1)} %copy-done.3, bf16[768,3072]{1,0:T(8,128)(2,1)} %param.12, s32[]{:T(128)S(6)} %select_n.159), kind=kOutput, calls=%fused_computation.1 | convolution fusion | flops 226639872 | bytes 1769476 | tf_op jit(solution)/shard_map/dot_general | solution.py:244
  176.6 2.7 %collective-permute-start.16 = (bf16[192,768]{1,0:T(8,128)(2,1)}, bf16[192,768]{1,0:T(8,128)(2,1)S(1)}, u32[]{:S(2)}, u32[]{:S(2)}) collective-permute-start(bf16[192,768]{1,0:T(8,128)(2,1)} %convolution_convert_fusion), channel_id=1, source_target_pairs={{0,3},{1,0},{2,1},{3,2},{4,7},{5,4},{6,5},{7,6},{8,11},{9,8},{10,9... | collective-permute-start | bytes 884744 | tf_op jit(solution)/shard_map/ppermute | solution.py:246
  179.3 1.7 fusion.13
  181.1 1.9 collective-permute-done.14
  182.9 8.2 %collective-permute-done.15 = bf16[192,768]{1,0:T(8,128)(2,1)S(1)} collective-permute-done((bf16[192,768]{1,0:T(8,128)(2,1)}, bf16[192,768]{1,0:T(8,128)(2,1)S(1)}, u32[]{:S(2)}, u32[]{:S(2)}) %collective-permute-start.15) | collective-permute-done | bytes 294944 | tf_op jit(solution)/shard_map/ppermute | solution.py:246
  191.1 1.7 fusion.6
  192.9 0.9 maximum_bitcast_fusion
  (38 shorter events, 0.2 us)
Async XLA Ops:
  0.0 0.8 copy-start
  0.8 4.2 %collective-permute-start = (bf16[2,16,384]{2,1,0:T(8,128)(2,1)S(1)}, bf16[2,16,384]{2,1,0:T(8,128)(2,1)S(1)}, u32[]{:S(2)}, u32[]{:S(2)}) collective-permute-start(bf16[2,16,384]{2,1,0:T(8,128)(2,1)S(1)} %constant_dynamic-slice_fusion), channel_id=1, source_target_pairs={{0,16},{16,0},{32,48},{48,32},{64,80},{80,64},{96,112},{112,96},{1... | collective-permute-start | bytes 73736 | tf_op jit(solution)/shard_map/ppermute | solution.py:39
  5.0 7.0 %collective-permute-start.1 = (bf16[2,32,384]{2,1,0:T(8,128)(2,1)S(1)}, bf16[2,32,384]{2,1,0:T(8,128)(2,1)S(1)}, u32[]{:S(2)}, u32[]{:S(2)}) collective-permute-start(bf16[2,32,384]{2,1,0:T(8,128)(2,1)S(1)} %maximum_select_fusion.4), channel_id=1, source_target_pairs={{0,32},{16,48},{32,0},{48,16},{64,96},{80,112},{96,64},{112,80},{1... | collective-permute-start | bytes 147464 | tf_op jit(solution)/shard_map/ppermute | solution.py:39
  5.1 32.4 %collective-permute-start.5 = (bf16[2,384,768]{2,1,0:T(8,128)(2,1)}, bf16[2,384,768]{2,1,0:T(8,128)(2,1)S(1)}, u32[]{:S(2)}, u32[]{:S(2)}) collective-permute-start(bf16[2,384,768]{2,1,0:T(8,128)(2,1)} %bitcast.2.rest_0_), channel_id=1, source_target_pairs={{0,4},{4,8},{8,12},{1,5},{5,9},{9,13},{2,6},{6,10},{10,14},{3,7},{... | collective-permute-start | bytes 3538952 | tf_op jit(solution)/shard_map/ppermute | solution.py:188
  10.0 28.5 %collective-permute-start.6 = (bf16[2,384,768]{2,1,0:T(8,128)(2,1)}, bf16[2,384,768]{2,1,0:T(8,128)(2,1)S(1)}, u32[]{:S(2)}, u32[]{:S(2)}) collective-permute-start(bf16[2,384,768]{2,1,0:T(8,128)(2,1)} %bitcast.2.rest_0_), channel_id=1, source_target_pairs={{4,0},{8,4},{12,8},{5,1},{9,5},{13,9},{6,2},{10,6},{14,10},{7,3},{... | collective-permute-start | bytes 3538952 | tf_op jit(solution)/shard_map/ppermute | solution.py:189
  12.0 7.2 %collective-permute-start.2 = (bf16[2,64,384]{2,1,0:T(8,128)(2,1)S(1)}, bf16[2,64,384]{2,1,0:T(8,128)(2,1)S(1)}, u32[]{:S(2)}, u32[]{:S(2)}) collective-permute-start(bf16[2,64,384]{2,1,0:T(8,128)(2,1)S(1)} %maximum_select_fusion.3), channel_id=1, source_target_pairs={{0,64},{16,80},{32,96},{48,112},{64,0},{80,16},{96,32},{112,48},{1... | collective-permute-start | bytes 294920 | tf_op jit(solution)/shard_map/ppermute | solution.py:39
  19.3 14.3 %collective-permute-start.3 = (bf16[2,128,384]{2,1,0:T(8,128)(2,1)S(1)}, bf16[2,128,384]{2,1,0:T(8,128)(2,1)S(1)}, u32[]{:S(2)}, u32[]{:S(2)}) collective-permute-start(bf16[2,128,384]{2,1,0:T(8,128)(2,1)S(1)} %maximum_select_fusion.2), channel_id=1, source_target_pairs={{0,128},{16,144},{32,160},{48,176},{64,192},{80,208},{96,224},{112... | collective-permute-start | bytes 589832 | tf_op jit(solution)/shard_map/ppermute | solution.py:39
  23.5 23.8 %copy-start.13 = (s32[2,16,4]{1,2,0:T(4,128)S(1)}, s32[2,16,4]{1,2,0:T(4,128)}, u32[]{:S(2)}) copy-start(s32[2,16,4]{1,2,0:T(4,128)} %param.15) | copy-start | bytes 1540
  23.5 24.3 %copy-start.14 = (s32[6,2]{0,1:T(2,128)S(1)}, s32[6,2]{0,1:T(2,128)}, u32[]{:S(2)}) copy-start(s32[6,2]{0,1:T(2,128)} %param.14) | copy-start | bytes 148
  33.7 2.7 %collective-permute-start.4 = (bf16[2,256,384]{2,1,0:T(8,128)(2,1)S(1)}, bf16[2,256,384]{2,1,0:T(8,128)(2,1)S(1)}, u32[]{:S(2)}, u32[]{:S(2)}) collective-permute-start(bf16[2,256,384]{2,1,0:T(8,128)(2,1)S(1)} %maximum_select_fusion.1), channel_id=1, source_target_pairs={{0,4},{4,0},{8,12},{12,8},{1,5},{5,1},{9,13},{13,9},{2,6},{6,2},{1... | collective-permute-start | bytes 1179656 | tf_op jit(solution)/shard_map/ppermute | solution.py:48
  37.5 1.0 copy-start.7
  38.5 1.0 copy-start.8
  39.6 55.2 %collective-permute-start.7 = (bf16[2,384,768]{2,1,0:T(8,128)(2,1)}, bf16[2,384,768]{2,1,0:T(8,128)(2,1)S(1)}, u32[]{:S(2)}, u32[]{:S(2)}) collective-permute-start(bf16[2,384,768]{2,1,0:T(8,128)(2,1)} %bitcast.2.rest_0_), channel_id=1, source_target_pairs={{0,16},{16,32},{32,48},{48,64},{64,80},{80,96},{96,112},{112,128},... | collective-permute-start | bytes 3538952 | tf_op jit(solution)/shard_map/ppermute | solution.py:197
  44.2 53.0 %collective-permute-start.8 = (bf16[2,384,768]{2,1,0:T(8,128)(2,1)}, bf16[2,384,768]{2,1,0:T(8,128)(2,1)S(1)}, u32[]{:S(2)}, u32[]{:S(2)}) collective-permute-start(bf16[2,384,768]{2,1,0:T(8,128)(2,1)} %bitcast.2.rest_0_), channel_id=1, source_target_pairs={{16,0},{32,16},{48,32},{64,48},{80,64},{96,80},{112,96},{128,112},... | collective-permute-start | bytes 3538952 | tf_op jit(solution)/shard_map/ppermute | solution.py:198
  94.8 2.5 %copy-start.5 = (bf16[2,384,768]{2,1,0:T(8,128)(2,1)}, bf16[2,384,768]{2,1,0:T(8,128)(2,1)S(1)}, u32[]{:S(2)}) copy-start(bf16[2,384,768]{2,1,0:T(8,128)(2,1)S(1)} %collective-permute-done.7.rest_1_) | copy-start | bytes 3538948
  97.2 1.0 copy-start.6
  98.2 11.2 %copy-start.4 = (bf16[1,1,384,768]{3,2,1,0:T(8,128)(2,1)S(1)}, bf16[1,1,384,768]{3,2,1,0:T(8,128)(2,1)}, u32[]{:S(2)}) copy-start(bf16[1,1,384,768]{3,2,1,0:T(8,128)(2,1)} %param.8) | copy-start | bytes 1769476
  99.9 32.1 %collective-permute-start.10 = (bf16[2,2,384,768]{3,2,1,0:T(8,128)(2,1)}, bf16[2,2,384,768]{3,2,1,0:T(8,128)(2,1)S(1)}, u32[]{:S(2)}, u32[]{:S(2)}) collective-permute-start(bf16[2,2,384,768]{3,2,1,0:T(8,128)(2,1)} %pad_maximum_fusion), channel_id=1, source_target_pairs={{4,0},{8,4},{12,8},{5,1},{9,5},{13,9},{6,2},{10,6},{14,10},{7,3},{... | collective-permute-start | bytes 7077896 | tf_op jit(solution)/shard_map/ppermute | solution.py:214
  102.3 29.7 %collective-permute-start.9 = (bf16[2,2,384,768]{3,2,1,0:T(8,128)(2,1)}, bf16[2,2,384,768]{3,2,1,0:T(8,128)(2,1)}, u32[]{:S(2)}, u32[]{:S(2)}) collective-permute-start(bf16[2,2,384,768]{3,2,1,0:T(8,128)(2,1)} %pad_maximum_fusion), channel_id=1, source_target_pairs={{0,4},{4,8},{8,12},{1,5},{5,9},{9,13},{2,6},{6,10},{10,14},{3,7},{... | collective-permute-start | bytes 7077896 | tf_op jit(solution)/shard_map/ppermute | solution.py:213
  126.6 2.5 %copy-start.10 = (f32[6,384,1]{2,1,0:T(8,128)S(1)}, f32[6,384,1]{2,1,0:T(8,128)}, u32[]{:S(2)}) copy-start(f32[6,384,1]{2,1,0:T(8,128)} %get-tuple-element.33) | copy-start | bytes 27652
  129.1 1.7 copy-start.9
  131.9 1.4 copy-start.1
  145.5 4.6 %copy-start.2 = (bf16[192,768]{1,0:T(8,128)(2,1)S(1)}, bf16[192,768]{1,0:T(8,128)(2,1)}, u32[]{:S(2)}) copy-start(bf16[192,768]{1,0:T(8,128)(2,1)} %shard_map.84) | copy-start | bytes 884740
  147.3 29.3 %collective-permute-start.11 = (bf16[192,768]{1,0:T(8,128)(2,1)S(1)}, bf16[192,768]{1,0:T(8,128)(2,1)S(1)}, u32[]{:S(2)}, u32[]{:S(2)}) collective-permute-start(bf16[192,768]{1,0:T(8,128)(2,1)S(1)} %convolution_convert_fusion.6), channel_id=1, source_target_pairs={{0,2},{1,3},{2,0},{3,1},{4,6},{5,7},{6,4},{7,5},{8,10},{9,11},{10,... | collective-permute-start | bytes 884744 | tf_op jit(solution)/shard_map/ppermute | solution.py:246
  151.8 27.5 %collective-permute-start.12 = (bf16[192,768]{1,0:T(8,128)(2,1)S(1)}, bf16[192,768]{1,0:T(8,128)(2,1)S(1)}, u32[]{:S(2)}, u32[]{:S(2)}) collective-permute-start(bf16[192,768]{1,0:T(8,128)(2,1)S(1)} %convolution_convert_fusion.5), channel_id=1, source_target_pairs={{0,1},{1,2},{2,3},{3,0},{4,5},{5,6},{6,7},{7,4},{8,9},{9,10},{10,1... | collective-permute-start | bytes 884744 | tf_op jit(solution)/shard_map/ppermute | solution.py:246
  154.5 24.8 %collective-permute-start.13 = (bf16[192,768]{1,0:T(8,128)(2,1)}, bf16[192,768]{1,0:T(8,128)(2,1)S(1)}, u32[]{:S(2)}, u32[]{:S(2)}) collective-permute-start(bf16[192,768]{1,0:T(8,128)(2,1)} %convolution_convert_fusion.4), channel_id=1, source_target_pairs={{0,3},{1,0},{2,1},{3,2},{4,7},{5,4},{6,5},{7,6},{8,11},{9,8},{10,9... | collective-permute-start | bytes 884744 | tf_op jit(solution)/shard_map/ppermute | solution.py:246
  169.2 2.5 %copy-start.3 = (bf16[192,768]{1,0:T(8,128)(2,1)S(1)}, bf16[192,768]{1,0:T(8,128)(2,1)}, u32[]{:S(2)}) copy-start(bf16[192,768]{1,0:T(8,128)(2,1)} %shard_map.85) | copy-start | bytes 884740
  174.2 5.1 %copy-start.11 = (bf16[1,1,384,768]{3,2,1,0:T(8,128)(2,1)S(1)}, bf16[1,1,384,768]{3,2,1,0:T(8,128)(2,1)}, u32[]{:S(2)}) copy-start(bf16[1,1,384,768]{3,2,1,0:T(8,128)(2,1)} %param.11) | copy-start | bytes 1769476
  174.2 5.2 %copy-start.12 = (f32[768]{0:T(1024)S(1)}, f32[768]{0:T(1024)}, u32[]{:S(2)}) copy-start(f32[768]{0:T(1024)} %param.13) | copy-start | bytes 9220
  174.2 8.8 %collective-permute-start.14 = (bf16[192,768]{1,0:T(8,128)(2,1)}, bf16[192,768]{1,0:T(8,128)(2,1)S(1)}, u32[]{:S(2)}, u32[]{:S(2)}) collective-permute-start(bf16[192,768]{1,0:T(8,128)(2,1)} %convolution_convert_fusion.2), channel_id=1, source_target_pairs={{0,2},{1,3},{2,0},{3,1},{4,6},{5,7},{6,4},{7,5},{8,10},{9,11},{10,... | collective-permute-start | bytes 884744 | tf_op jit(solution)/shard_map/ppermute | solution.py:246
  176.6 14.5 %collective-permute-start.15 = (bf16[192,768]{1,0:T(8,128)(2,1)}, bf16[192,768]{1,0:T(8,128)(2,1)S(1)}, u32[]{:S(2)}, u32[]{:S(2)}) collective-permute-start(bf16[192,768]{1,0:T(8,128)(2,1)} %convolution_convert_fusion.1), channel_id=1, source_target_pairs={{0,1},{1,2},{2,3},{3,0},{4,5},{5,6},{6,7},{7,4},{8,9},{9,10},{10,1... | collective-permute-start | bytes 884744 | tf_op jit(solution)/shard_map/ppermute | solution.py:246
  176.6 14.5 %collective-permute-start.16 = (bf16[192,768]{1,0:T(8,128)(2,1)}, bf16[192,768]{1,0:T(8,128)(2,1)S(1)}, u32[]{:S(2)}, u32[]{:S(2)}) collective-permute-start(bf16[192,768]{1,0:T(8,128)(2,1)} %convolution_convert_fusion), channel_id=1, source_target_pairs={{0,3},{1,0},{2,1},{3,2},{4,7},{5,4},{6,5},{7,6},{8,11},{9,8},{10,9... | collective-permute-start | bytes 884744 | tf_op jit(solution)/shard_map/ppermute | solution.py:246

commit v10 on v8

--- a/solution.py
+++ b/solution.py
@@ -186,15 +186,17 @@
     own = image_kv[0, 0]
     h_before = lax.ppermute(own, "height", shift_pairs(height_size, 1))
     h_after = lax.ppermute(own, "height", shift_pairs(height_size, -1))
-    text_group = text_halves(text_kv)
-    step = 1
+    text_group = exchange(text_halves(text_kv), tm_size, 1)
+    sent, text_group, h_before, h_after = lax.optimization_barrier(
+        (own, text_group, h_before, h_after)
+    )
+    t_before = lax.ppermute(sent, "tm", shift_pairs(tm_size, 1))
+    t_after = lax.ppermute(sent, "tm", shift_pairs(tm_size, -1))
+    step = 2
     while step < tm_size:
         text_group = exchange(text_group, tm_size, step)
         step *= 2
     text = join_halves(text_group)
-    sent, text, h_before, h_after = lax.optimization_barrier((own, text, h_before, h_after))
-    t_before = lax.ppermute(sent, "tm", shift_pairs(tm_size, 1))
-    t_after = lax.ppermute(sent, "tm", shift_pairs(tm_size, -1))
     time_start = lax.axis_index("tm")
     height_start = lax.axis_index("height")
     zero_index = jnp.int32(0)

time: 180 us -> 184 us (1.022)
  the two profiles are of different devices: /device:TPU:97 before, /device:TPU:3 now
where the time goes in v10:
time: 184 us; the launch traced here: 182 us
  starting transfers between devices  69.6 us (38%)
  waiting for transfers between devices  46.6 us (25%)
  Pallas kernels  41 us (22%)
  matrix products  10.6 us (6%)
  local copies, waits for them, and re-layouts  9.45 us (5%)
  other arithmetic  4.89 us (3%)
    pallas_call x3, Pallas kernels, attend(): pl.pallas_call(kernel, grid_spec=grid_spec, out_shape=out_shape)  41 us
    ppermute x1, starting transfers between devices, per_device(): c_after = lax.ppermute(time_pair, 'height', shift_pairs(height_size, -1))  30.8 us
    ppermute x3, waiting for transfers between devices, per_device(): received.append(lax.ppermute(part, 'mp', pairs))  20.8 us
    ppermute x4, starting transfers between devices, exchange(): other = lax.ppermute(block, 'tm', [(i, i ^ step) for i in range(devices)])  18 us
    ppermute x4, waiting for transfers between devices, exchange(): other = lax.ppermute(block, 'tm', [(i, i ^ step) for i in range(devices)])  13.2 us
    ppermute x1, waiting for transfers between devices, per_device(): t_before = lax.ppermute(sent, 'tm', shift_pairs(tm_size, 1))  12.6 us
    dot_general x3, matrix products, per_device(): jnp.dot(attended, w_part, preferred_element_type=jnp.float32)  7.58 us
    ppermute x3, starting transfers between devices, per_device(): received.append(lax.ppermute(part, 'mp', pairs))  6.34 us
  transfers between devices with their start and end apart: 14, of which 8 were waited for; matrix products, arithmetic and copies ran while one was open for 7% of the time, Pallas kernels for 16%

profile of v10, /device:TPU:3, one launch (start us, length us, event | category | flops | bytes accessed | tf_op | source)
XLA Modules:
  0.0 182.3 jit_solution(14230677072578855414)
XLA Ops:
  0.0 0.0 copy-start
  0.0 1.4 collective-permute-start.1
  1.4 3.3 %collective-permute-start.2 = (bf16[2,384,768]{2,1,0:T(8,128)(2,1)}, bf16[2,384,768]{2,1,0:T(8,128)(2,1)S(1)}, u32[]{:S(2)}, u32[]{:S(2)}) collective-permute-start(bf16[2,384,768]{2,1,0:T(8,128)(2,1)} %bitcast.23), channel_id=1, source_target_pairs={{4,0},{8,4},{12,8},{5,1},{9,5},{13,9},{6,2},{10,6},{14,10},{7,3},{... | collective-permute-start | bytes 3538952 | tf_op jit(solution)/shard_map/ppermute | solution.py:188
  4.7 0.0 copy-done
  4.8 1.9 %collective-permute-start = (bf16[2,16,384]{2,1,0:T(8,128)(2,1)S(1)}, bf16[2,16,384]{2,1,0:T(8,128)(2,1)S(1)}, u32[]{:S(2)}, u32[]{:S(2)}) collective-permute-start(bf16[2,16,384]{2,1,0:T(8,128)(2,1)S(1)} %constant_dynamic-slice_fusion), channel_id=1, source_target_pairs={{0,16},{16,0},{32,48},{48,32},{64,80},{80,64},{96,112},{112,96},{1... | collective-permute-start | bytes 73736 | tf_op jit(solution)/shard_map/ppermute | solution.py:39
  6.7 2.3 %collective-permute-done = bf16[2,16,384]{2,1,0:T(8,128)(2,1)S(1)} collective-permute-done((bf16[2,16,384]{2,1,0:T(8,128)(2,1)S(1)}, bf16[2,16,384]{2,1,0:T(8,128)(2,1)S(1)}, u32[]{:S(2)}, u32[]{:S(2)}) %collective-permute-start) | collective-permute-done | bytes 24608 | tf_op jit(solution)/shard_map/ppermute | solution.py:39
  9.0 0.0 collective-permute-done.1.rest_1_
  9.1 0.0 copy-start.4
  9.1 1.0 copy-done.4
  10.1 0.0 collective-permute-done.2.rest_2_
  10.1 0.0 copy-start.5
  10.1 1.0 copy-done.5
  11.1 4.0 %collective-permute-start.3 = (bf16[2,384,768]{2,1,0:T(8,128)(2,1)}, bf16[2,384,768]{2,1,0:T(8,128)(2,1)S(1)}, u32[]{:S(2)}, u32[]{:S(2)}) collective-permute-start(bf16[2,384,768]{2,1,0:T(8,128)(2,1)} %bitcast.24), channel_id=1, source_target_pairs={{0,16},{16,32},{32,48},{48,64},{64,80},{80,96},{96,112},{112,128},... | collective-permute-start | bytes 3538952 | tf_op jit(solution)/shard_map/ppermute | solution.py:193
  15.2 1.3 collective-permute-start.4
  16.5 0.8 pad_dynamic-slice_fusion
  17.3 0.1 copy.16
  17.4 0.1 lt.111
  17.4 0.1 copy.17
  17.5 0.1 lt.116
  17.6 1.4 copy.22.reach_ref
  19.0 0.7 and_select_fusion.rest_3_.rest_4_
  19.7 13.5 %shard_map.82 = (f32[6,384,1]{2,1,0:T(8,128)}, f32[6,384,1]{2,1,0:T(8,128)}, f32[384,768]{1,0:T(8,128)}) custom-call(s32[6,2]{1,0:T(8,128)} %copy.22.reach_ref, bf16[384,768]{1,0:T(8,128)(2,1)} %bitcast.17, bf16[2,384,768]{2,1,0:T(8,128)(2,1)} %bitcast.26, bf16[2,384,768]{2,1,0:T(8,128)(2,1)} %copy-done.4, bf16[2,384,768]{2,1,0:T(8,128)(2,1)} %copy-done.5, ...), custom_call_target="tpu_custom_call" | custom-call | tf_op jit(solution)/shard_map/pallas_call | solution.py:176
  33.1 12.6 %collective-permute-done.3.rest_1_ = bf16[2,384,768]{2,1,0:T(8,128)(2,1)S(1)} collective-permute-done((bf16[2,384,768]{2,1,0:T(8,128)(2,1)}, bf16[2,384,768]{2,1,0:T(8,128)(2,1)S(1)}, u32[]{:S(2)}, u32[]{:S(2)}) %collective-permute-start.3) | collective-permute-done | bytes 1179680 | tf_op jit(solution)/shard_map/ppermute | solution.py:193
  45.8 0.0 copy-start.2
  45.8 0.0 collective-permute-done.4.rest_2_
  45.8 0.0 copy-start.3
  45.8 1.1 copy-done.2
  46.8 0.4 copy-done.3
  47.2 1.6 pad_maximum_fusion
  48.9 1.3 collective-permute-start.5
  50.1 30.8 %collective-permute-start.6 = (bf16[2,2,384,768]{3,2,1,0:T(8,128)(2,1)}, bf16[2,2,384,768]{3,2,1,0:T(8,128)(2,1)}, u32[]{:S(2)}, u32[]{:S(2)}) collective-permute-start(bf16[2,2,384,768]{3,2,1,0:T(8,128)(2,1)} %pad_maximum_fusion), channel_id=1, source_target_pairs={{4,0},{8,4},{12,8},{5,1},{9,5},{13,9},{6,2},{10,6},{14,10},{7,3},{... | collective-permute-start | bytes 7077896 | tf_op jit(solution)/shard_map/ppermute | solution.py:215
  80.9 4.1 %collective-permute-start.7 = (bf16[2,32,384]{2,1,0:T(8,128)(2,1)S(1)}, bf16[2,32,384]{2,1,0:T(8,128)(2,1)S(1)}, u32[]{:S(2)}, u32[]{:S(2)}) collective-permute-start(bf16[2,32,384]{2,1,0:T(8,128)(2,1)S(1)} %maximum_select_fusion.4), channel_id=1, source_target_pairs={{0,32},{16,48},{32,0},{48,16},{64,96},{80,112},{96,64},{112,80},{1... | collective-permute-start | bytes 147464 | tf_op jit(solution)/shard_map/ppermute | solution.py:39
  85.0 1.8 collective-permute-done.7
  86.8 3.1 %collective-permute-start.8 = (bf16[2,64,384]{2,1,0:T(8,128)(2,1)S(1)}, bf16[2,64,384]{2,1,0:T(8,128)(2,1)S(1)}, u32[]{:S(2)}, u32[]{:S(2)}) collective-permute-start(bf16[2,64,384]{2,1,0:T(8,128)(2,1)S(1)} %maximum_select_fusion.3), channel_id=1, source_target_pairs={{0,64},{16,80},{32,96},{48,112},{64,0},{80,16},{96,32},{112,48},{1... | collective-permute-start | bytes 294920 | tf_op jit(solution)/shard_map/ppermute | solution.py:39
  89.9 2.0 %collective-permute-done.8 = bf16[2,64,384]{2,1,0:T(8,128)(2,1)S(1)} collective-permute-done((bf16[2,64,384]{2,1,0:T(8,128)(2,1)S(1)}, bf16[2,64,384]{2,1,0:T(8,128)(2,1)S(1)}, u32[]{:S(2)}, u32[]{:S(2)}) %collective-permute-start.8) | collective-permute-done | bytes 98336 | tf_op jit(solution)/shard_map/ppermute | solution.py:39
  91.9 8.9 %collective-permute-start.9 = (bf16[2,128,384]{2,1,0:T(8,128)(2,1)S(1)}, bf16[2,128,384]{2,1,0:T(8,128)(2,1)S(1)}, u32[]{:S(2)}, u32[]{:S(2)}) collective-permute-start(bf16[2,128,384]{2,1,0:T(8,128)(2,1)S(1)} %maximum_select_fusion.2), channel_id=1, source_target_pairs={{0,128},{16,144},{32,160},{48,176},{64,192},{80,208},{96,224},{112... | collective-permute-start | bytes 589832 | tf_op jit(solution)/shard_map/ppermute | solution.py:39
  100.9 7.0 %collective-permute-done.9 = bf16[2,128,384]{2,1,0:T(8,128)(2,1)S(1)} collective-permute-done((bf16[2,128,384]{2,1,0:T(8,128)(2,1)S(1)}, bf16[2,128,384]{2,1,0:T(8,128)(2,1)S(1)}, u32[]{:S(2)}, u32[]{:S(2)}) %collective-permute-start.9) | collective-permute-done | bytes 196640 | tf_op jit(solution)/shard_map/ppermute | solution.py:39
  107.9 0.1 maximum_select_fusion.1
  108.1 3.2 %collective-permute-start.10 = (bf16[2,256,384]{2,1,0:T(8,128)(2,1)S(1)}, bf16[2,256,384]{2,1,0:T(8,128)(2,1)S(1)}, u32[]{:S(2)}, u32[]{:S(2)}) collective-permute-start(bf16[2,256,384]{2,1,0:T(8,128)(2,1)S(1)} %maximum_select_fusion.1), channel_id=1, source_target_pairs={{0,4},{4,0},{8,12},{12,8},{1,5},{5,1},{9,13},{13,9},{2,6},{6,2},{1... | collective-permute-start | bytes 1179656 | tf_op jit(solution)/shard_map/ppermute | solution.py:48
  111.2 0.6 slice.12
  111.8 0.6 slice.13
  112.4 1.3 fusion.18
  113.7 0.8 copy.23.rest_8_
  114.5 0.0 collective-permute-done.10
  114.5 1.1 maximum_select_fusion.rest_0_
  115.6 14.8 %shard_map.83 = (f32[6,384,1]{2,1,0:T(8,128)}, f32[6,384,1]{2,1,0:T(8,128)}, f32[384,768]{1,0:T(8,128)}) custom-call(s32[6,2]{1,0:T(8,128)} %copy.22.reach_ref, bf16[384,768]{1,0:T(8,128)(2,1)} %bitcast.18, bf16[2,256,768]{2,1,0:T(8,128)(2,1)} %maximum_select_fusion.rest_0_, bf16[2,384,768]{2,1,0:T(8,128)(2,1)} %copy-done.2, bf16[2,384,768]{2,1,0:T(8,128)(2,1)} %copy-done.3, ...), custom_call_target="tpu_custom_call" | custom-call | tf_op jit(solution)/shard_map/pallas_call | solution.py:176
  130.4 0.0 collective-permute-done.5.rest_0_.rest_2_
  130.4 0.0 copy-start.1
  130.4 0.0 collective-permute-done.6.rest_1_.rest_3_
  130.4 1.4 copy-done.1
  131.8 12.7 %shard_map.84 = bf16[384,768]{1,0:T(8,128)(2,1)} custom-call(s32[6,2]{1,0:T(8,128)} %copy.22.reach_ref, bf16[384,768]{1,0:T(8,128)(2,1)} %bitcast.19, bf16[2,2,384,768]{3,2,1,0:T(8,128)(2,1)} %copy-done.1, bf16[2,2,384,768]{3,2,1,0:T(8,128)(2,1)} %collective-permute-done.6.rest_1_.rest_3_, bf16[2,2,384,768]{3,2,1,0:T(8,128)(2,1)} %copy-done.1, ...), custom_call_target="tpu_custom_call" | custom-call | tf_op jit(solution)/shard_map/pallas_call | solution.py:176
  144.5 2.1 %convolution_convert_fusion.2 = bf16[384,768]{1,0:T(8,128)(2,1)S(1)} fusion(bf16[384,768]{1,0:T(8,128)(2,1)} %shard_map.84, bf16[768,3072]{1,0:T(8,128)(2,1)} %param.12, s32[]{:T(128)S(6)} %select_n.145), kind=kOutput, calls=%fused_computation.3 | convolution fusion | flops 453279744 | bytes 2359300 | tf_op jit(solution)/shard_map/dot_general | solution.py:227
  146.7 2.4 %collective-permute-start.11 = (bf16[384,768]{1,0:T(8,128)(2,1)S(1)}, bf16[384,768]{1,0:T(8,128)(2,1)S(1)}, u32[]{:S(2)}, u32[]{:S(2)}) collective-permute-start(bf16[384,768]{1,0:T(8,128)(2,1)S(1)} %convolution_convert_fusion.2), channel_id=1, source_target_pairs={{0,2},{1,3},{2,0},{3,1},{4,6},{5,7},{6,4},{7,5},{8,10},{9,11},{10,... | collective-permute-start | bytes 1769480 | tf_op jit(solution)/shard_map/ppermute | solution.py:229
  149.1 0.0 copy-done.6
  149.1 2.7 %convolution_convert_fusion.1 = bf16[384,768]{1,0:T(8,128)(2,1)} fusion(bf16[384,768]{1,0:T(8,128)(2,1)S(1)} %copy-done.6, bf16[768,3072]{1,0:T(8,128)(2,1)} %param.12, s32[]{:T(128)S(6)} %select_n.147), kind=kOutput, calls=%fused_computation.2 | convolution fusion | flops 453279744 | bytes 2359300 | tf_op jit(solution)/shard_map/dot_general | solution.py:227
  151.8 3.9 %collective-permute-start.12 = (bf16[384,768]{1,0:T(8,128)(2,1)}, bf16[384,768]{1,0:T(8,128)(2,1)S(1)}, u32[]{:S(2)}, u32[]{:S(2)}) collective-permute-start(bf16[384,768]{1,0:T(8,128)(2,1)} %convolution_convert_fusion.1), channel_id=1, source_target_pairs={{0,1},{1,2},{2,3},{3,0},{4,5},{5,6},{6,7},{7,4},{8,9},{9,10},{10,1... | collective-permute-start | bytes 1769480 | tf_op jit(solution)/shard_map/ppermute | solution.py:229
  155.7 2.7 %convolution_convert_fusion = bf16[384,768]{1,0:T(8,128)(2,1)} fusion(bf16[384,768]{1,0:T(8,128)(2,1)S(1)} %copy-done.6, bf16[768,3072]{1,0:T(8,128)(2,1)} %param.12, s32[]{:T(128)S(6)} %select_n.149), kind=kOutput, calls=%fused_computation.1 | convolution fusion | flops 453279744 | bytes 2359300 | tf_op jit(solution)/shard_map/dot_general | solution.py:227
  158.5 0.0 collective-permute-start.13
  158.5 4.9 %collective-permute-done.11 = bf16[384,768]{1,0:T(8,128)(2,1)S(1)} collective-permute-done((bf16[384,768]{1,0:T(8,128)(2,1)S(1)}, bf16[384,768]{1,0:T(8,128)(2,1)S(1)}, u32[]{:S(2)}, u32[]{:S(2)}) %collective-permute-start.11) | collective-permute-done | bytes 589856 | tf_op jit(solution)/shard_map/ppermute | solution.py:229
  163.4 13.0 %collective-permute-done.12 = bf16[384,768]{1,0:T(8,128)(2,1)S(1)} collective-permute-done((bf16[384,768]{1,0:T(8,128)(2,1)}, bf16[384,768]{1,0:T(8,128)(2,1)S(1)}, u32[]{:S(2)}, u32[]{:S(2)}) %collective-permute-start.12) | collective-permute-done | bytes 589856 | tf_op jit(solution)/shard_map/ppermute | solution.py:229
  176.4 2.8 %collective-permute-done.13 = bf16[384,768]{1,0:T(8,128)(2,1)} collective-permute-done((bf16[384,768]{1,0:T(8,128)(2,1)}, bf16[384,768]{1,0:T(8,128)(2,1)}, u32[]{:S(2)}, u32[]{:S(2)}) %collective-permute-start.13) | collective-permute-done | bytes 589856 | tf_op jit(solution)/shard_map/ppermute | solution.py:229
  179.2 0.0 copy-done.7
  179.2 0.0 copy-done.8
  179.2 3.0 %fusion.7 = bf16[1,1,384,768]{3,2,1,0:T(8,128)(2,1)} fusion(bf16[384,768]{1,0:T(8,128)(2,1)S(1)} %copy-done.6, bf16[384,768]{1,0:T(8,128)(2,1)} %collective-permute-done.13, bf16[384,768]{1,0:T(8,128)(2,1)S(1)} %collective-permute-done.12, bf16[384,768]{1,0:T(8,128)(2,1)S(1)} %collective-permute-done.11, bf16[768,3072]{1,0:T(8,128)(2,1)} %param.12, ...), kind=kOutput, calls=%fused_computation.12 | convolution fusion | flops 456523776 | bytes 4721668 | tf_op jit(solution)/shard_map/dot_general | solution.py:231
  (8 shorter events, 0.1 us)
Async XLA Ops:
  0.0 4.7 %copy-start = (bf16[2,16,768]{2,1,0:T(8,128)(2,1)S(1)}, bf16[2,16,768]{2,1,0:T(8,128)(2,1)}, u32[]{:S(2)}) copy-start(bf16[2,16,768]{2,1,0:T(8,128)(2,1)} %param.10) | copy-start | bytes 147460
  0.0 9.0 %collective-permute-start.1 = (bf16[2,384,768]{2,1,0:T(8,128)(2,1)}, bf16[2,384,768]{2,1,0:T(8,128)(2,1)S(1)}, u32[]{:S(2)}, u32[]{:S(2)}) collective-permute-start(bf16[2,384,768]{2,1,0:T(8,128)(2,1)} %bitcast.22), channel_id=1, source_target_pairs={{0,4},{4,8},{8,12},{1,5},{5,9},{9,13},{2,6},{6,10},{10,14},{3,7},{... | collective-permute-start | bytes 3538952 | tf_op jit(solution)/shard_map/ppermute | solution.py:187
  1.4 8.7 %collective-permute-start.2 = (bf16[2,384,768]{2,1,0:T(8,128)(2,1)}, bf16[2,384,768]{2,1,0:T(8,128)(2,1)S(1)}, u32[]{:S(2)}, u32[]{:S(2)}) collective-permute-start(bf16[2,384,768]{2,1,0:T(8,128)(2,1)} %bitcast.23), channel_id=1, source_target_pairs={{4,0},{8,4},{12,8},{5,1},{9,5},{13,9},{6,2},{10,6},{14,10},{7,3},{... | collective-permute-start | bytes 3538952 | tf_op jit(solution)/shard_map/ppermute | solution.py:188
  4.8 4.3 %collective-permute-start = (bf16[2,16,384]{2,1,0:T(8,128)(2,1)S(1)}, bf16[2,16,384]{2,1,0:T(8,128)(2,1)S(1)}, u32[]{:S(2)}, u32[]{:S(2)}) collective-permute-start(bf16[2,16,384]{2,1,0:T(8,128)(2,1)S(1)} %constant_dynamic-slice_fusion), channel_id=1, source_target_pairs={{0,16},{16,0},{32,48},{48,32},{64,80},{80,64},{96,112},{112,96},{1... | collective-permute-start | bytes 73736 | tf_op jit(solution)/shard_map/ppermute | solution.py:39
  9.1 1.1 copy-start.4
  10.1 1.0 copy-start.5
  11.1 34.6 %collective-permute-start.3 = (bf16[2,384,768]{2,1,0:T(8,128)(2,1)}, bf16[2,384,768]{2,1,0:T(8,128)(2,1)S(1)}, u32[]{:S(2)}, u32[]{:S(2)}) collective-permute-start(bf16[2,384,768]{2,1,0:T(8,128)(2,1)} %bitcast.24), channel_id=1, source_target_pairs={{0,16},{16,32},{32,48},{48,64},{64,80},{80,96},{96,112},{112,128},... | collective-permute-start | bytes 3538952 | tf_op jit(solution)/shard_map/ppermute | solution.py:193
  15.2 30.6 %collective-permute-start.4 = (bf16[2,384,768]{2,1,0:T(8,128)(2,1)}, bf16[2,384,768]{2,1,0:T(8,128)(2,1)S(1)}, u32[]{:S(2)}, u32[]{:S(2)}) collective-permute-start(bf16[2,384,768]{2,1,0:T(8,128)(2,1)} %bitcast.25), channel_id=1, source_target_pairs={{16,0},{32,16},{48,32},{64,48},{80,64},{96,80},{112,96},{128,112},... | collective-permute-start | bytes 3538952 | tf_op jit(solution)/shard_map/ppermute | solution.py:194
  45.8 1.1 copy-start.2
  45.8 1.4 copy-start.3
  48.9 81.6 %collective-permute-start.5 = (bf16[2,2,384,768]{3,2,1,0:T(8,128)(2,1)}, bf16[2,2,384,768]{3,2,1,0:T(8,128)(2,1)S(1)}, u32[]{:S(2)}, u32[]{:S(2)}) collective-permute-start(bf16[2,2,384,768]{3,2,1,0:T(8,128)(2,1)} %pad_maximum_fusion), channel_id=1, source_target_pairs={{0,4},{4,8},{8,12},{1,5},{5,9},{9,13},{2,6},{6,10},{10,14},{3,7},{... | collective-permute-start | bytes 7077896 | tf_op jit(solution)/shard_map/ppermute | solution.py:214
  50.1 80.3 %collective-permute-start.6 = (bf16[2,2,384,768]{3,2,1,0:T(8,128)(2,1)}, bf16[2,2,384,768]{3,2,1,0:T(8,128)(2,1)}, u32[]{:S(2)}, u32[]{:S(2)}) collective-permute-start(bf16[2,2,384,768]{3,2,1,0:T(8,128)(2,1)} %pad_maximum_fusion), channel_id=1, source_target_pairs={{4,0},{8,4},{12,8},{5,1},{9,5},{13,9},{6,2},{10,6},{14,10},{7,3},{... | collective-permute-start | bytes 7077896 | tf_op jit(solution)/shard_map/ppermute | solution.py:215
  80.9 5.8 %collective-permute-start.7 = (bf16[2,32,384]{2,1,0:T(8,128)(2,1)S(1)}, bf16[2,32,384]{2,1,0:T(8,128)(2,1)S(1)}, u32[]{:S(2)}, u32[]{:S(2)}) collective-permute-start(bf16[2,32,384]{2,1,0:T(8,128)(2,1)S(1)} %maximum_select_fusion.4), channel_id=1, source_target_pairs={{0,32},{16,48},{32,0},{48,16},{64,96},{80,112},{96,64},{112,80},{1... | collective-permute-start | bytes 147464 | tf_op jit(solution)/shard_map/ppermute | solution.py:39
  86.8 5.1 %collective-permute-start.8 = (bf16[2,64,384]{2,1,0:T(8,128)(2,1)S(1)}, bf16[2,64,384]{2,1,0:T(8,128)(2,1)S(1)}, u32[]{:S(2)}, u32[]{:S(2)}) collective-permute-start(bf16[2,64,384]{2,1,0:T(8,128)(2,1)S(1)} %maximum_select_fusion.3), channel_id=1, source_target_pairs={{0,64},{16,80},{32,96},{48,112},{64,0},{80,16},{96,32},{112,48},{1... | collective-permute-start | bytes 294920 | tf_op jit(solution)/shard_map/ppermute | solution.py:39
  91.9 16.0 %collective-permute-start.9 = (bf16[2,128,384]{2,1,0:T(8,128)(2,1)S(1)}, bf16[2,128,384]{2,1,0:T(8,128)(2,1)S(1)}, u32[]{:S(2)}, u32[]{:S(2)}) collective-permute-start(bf16[2,128,384]{2,1,0:T(8,128)(2,1)S(1)} %maximum_select_fusion.2), channel_id=1, source_target_pairs={{0,128},{16,144},{32,160},{48,176},{64,192},{80,208},{96,224},{112... | collective-permute-start | bytes 589832 | tf_op jit(solution)/shard_map/ppermute | solution.py:39
  108.1 6.4 %collective-permute-start.10 = (bf16[2,256,384]{2,1,0:T(8,128)(2,1)S(1)}, bf16[2,256,384]{2,1,0:T(8,128)(2,1)S(1)}, u32[]{:S(2)}, u32[]{:S(2)}) collective-permute-start(bf16[2,256,384]{2,1,0:T(8,128)(2,1)S(1)} %maximum_select_fusion.1), channel_id=1, source_target_pairs={{0,4},{4,0},{8,12},{12,8},{1,5},{5,1},{9,13},{13,9},{2,6},{6,2},{1... | collective-permute-start | bytes 1179656 | tf_op jit(solution)/shard_map/ppermute | solution.py:48
  130.4 1.4 copy-start.1
  144.5 4.6 %copy-start.6 = (bf16[384,768]{1,0:T(8,128)(2,1)S(1)}, bf16[384,768]{1,0:T(8,128)(2,1)}, u32[]{:S(2)}) copy-start(bf16[384,768]{1,0:T(8,128)(2,1)} %shard_map.84) | copy-start | bytes 1769476
  146.7 16.7 %collective-permute-start.11 = (bf16[384,768]{1,0:T(8,128)(2,1)S(1)}, bf16[384,768]{1,0:T(8,128)(2,1)S(1)}, u32[]{:S(2)}, u32[]{:S(2)}) collective-permute-start(bf16[384,768]{1,0:T(8,128)(2,1)S(1)} %convolution_convert_fusion.2), channel_id=1, source_target_pairs={{0,2},{1,3},{2,0},{3,1},{4,6},{5,7},{6,4},{7,5},{8,10},{9,11},{10,... | collective-permute-start | bytes 1769480 | tf_op jit(solution)/shard_map/ppermute | solution.py:229
  151.8 27.4 %copy-start.7 = (bf16[1,1,384,768]{3,2,1,0:T(8,128)(2,1)S(1)}, bf16[1,1,384,768]{3,2,1,0:T(8,128)(2,1)}, u32[]{:S(2)}) copy-start(bf16[1,1,384,768]{3,2,1,0:T(8,128)(2,1)} %param.11) | copy-start | bytes 1769476
  151.8 27.4 %copy-start.8 = (f32[768]{0:T(1024)S(1)}, f32[768]{0:T(1024)}, u32[]{:S(2)}) copy-start(f32[768]{0:T(1024)} %param.13) | copy-start | bytes 9220
  151.8 24.6 %collective-permute-start.12 = (bf16[384,768]{1,0:T(8,128)(2,1)}, bf16[384,768]{1,0:T(8,128)(2,1)S(1)}, u32[]{:S(2)}, u32[]{:S(2)}) collective-permute-start(bf16[384,768]{1,0:T(8,128)(2,1)} %convolution_convert_fusion.1), channel_id=1, source_target_pairs={{0,1},{1,2},{2,3},{3,0},{4,5},{5,6},{6,7},{7,4},{8,9},{9,10},{10,1... | collective-permute-start | bytes 1769480 | tf_op jit(solution)/shard_map/ppermute | solution.py:229
  158.5 20.8 %collective-permute-start.13 = (bf16[384,768]{1,0:T(8,128)(2,1)}, bf16[384,768]{1,0:T(8,128)(2,1)}, u32[]{:S(2)}, u32[]{:S(2)}) collective-permute-start(bf16[384,768]{1,0:T(8,128)(2,1)} %convolution_convert_fusion), channel_id=1, source_target_pairs={{0,3},{1,0},{2,1},{3,2},{4,7},{5,4},{6,5},{7,6},{8,11},{9,8},{10,9... | collective-permute-start | bytes 1769480 | tf_op jit(solution)/shard_map/ppermute | solution.py:229

commit v11 on v8

--- a/solution.py
+++ b/solution.py
@@ -95,20 +95,31 @@
             m_ref[...] = m_new
         reach_t = reach_ref[head, 0]
         reach_h = reach_ref[head, 1]
+        groups = {}
         for tile_ref, b in zip(tile_refs, blocks):
-            off_t, off_h = abs(b // 3 - 1), abs(b % 3 - 1)
-
-            def block(tile_ref=tile_ref, b=b):
-                s = lax.dot_general(q, tile_ref[0], dims, preferred_element_type=jnp.float32)
-                s = s * scale + bias_ref[b]
+            groups.setdefault((abs(b // 3 - 1), abs(b % 3 - 1)), []).append((tile_ref, b))
+        for (off_t, off_h), members in groups.items():
+
+            def block(members=members):
+                scores = []
+                for tile_ref, b in members:
+                    s = lax.dot_general(q, tile_ref[0], dims, preferred_element_type=jnp.float32)
+                    scores.append(s * scale + bias_ref[b])
                 m_old = m_ref[...]
-                m_new = jnp.maximum(m_old, jnp.max(s, axis=1, keepdims=True))
+                m_new = m_old
+                for s in scores:
+                    m_new = jnp.maximum(m_new, jnp.max(s, axis=1, keepdims=True))
                 alpha = jnp.exp(m_old - m_new)
-                p = jnp.exp(s - m_new)
-                l_ref[...] = alpha * l_ref[...] + jnp.sum(p, axis=1, keepdims=True)
-                acc_ref[...] = alpha * acc_ref[...] + jnp.dot(
-                    p.astype(jnp.bfloat16), tile_ref[1], preferred_element_type=jnp.float32
-                )
+                total = alpha * l_ref[...]
+                acc = alpha * acc_ref[...]
+                for s, (tile_ref, _) in zip(scores, members):
+                    p = jnp.exp(s - m_new)
+                    total = total + jnp.sum(p, axis=1, keepdims=True)
+                    acc = acc + jnp.dot(
+                        p.astype(jnp.bfloat16), tile_ref[1], preferred_element_type=jnp.float32
+                    )
+                l_ref[...] = total
+                acc_ref[...] = acc
                 m_ref[...] = m_new
 
             if off_t == 0 and off_h == 0:
@@ -218,16 +229,15 @@
 
     mp_index = lax.axis_index("mp")
     chunk = out_weight.shape[1] // mp_size
+    projected = jnp.dot(attended, out_weight, preferred_element_type=jnp.float32)
+    projected = projected.astype(jnp.bfloat16)
     received = []
     for step in (2, 1, 3):
         target = (mp_index + step) % mp_size
-        w_part = lax.dynamic_slice_in_dim(out_weight, target * chunk, chunk, 1)
-        part = jnp.dot(attended, w_part, preferred_element_type=jnp.float32).astype(jnp.bfloat16)
+        part = lax.dynamic_slice_in_dim(projected, target * chunk, chunk, 1)
         pairs = [(i, (i + step) % mp_size) for i in range(mp_size)]
         received.append(lax.ppermute(part, "mp", pairs))
-    w_own = lax.dynamic_slice_in_dim(out_weight, mp_index * chunk, chunk, 1)
-    branch = jnp.dot(attended, w_own, preferred_element_type=jnp.float32).astype(jnp.bfloat16)
-    branch = branch.astype(jnp.float32)
+    branch = lax.dynamic_slice_in_dim(projected, mp_index * chunk, chunk, 1).astype(jnp.float32)
     for part in received:
         branch = branch + part.astype(jnp.float32)
     updated = residual[0, 0].astype(jnp.float32) + out_gate * branch

time: 180 us -> 174 us (0.967)
  Pallas kernels: 44.9 us -> 32.2 us
  waiting for transfers between devices: 76.3 us -> 85.4 us
  matrix products: 10.6 us -> 4.52 us
  other arithmetic: 4.93 us -> 7.57 us
    pallas_call x3, Pallas kernels: 44.9 us -> 32.2 us  [attend(): pl.pallas_call(kernel, grid_spec=grid_spec, out_shape=out_shape)]
    dot_general x4 -> x1, matrix products: 10.6 us -> 4.52 us  [per_device(): jnp.dot(attended, out_weight, preferred_element_type=jnp.float32)]
    ppermute x1, waiting for transfers between devices: 4.21 us -> 9.47 us  [per_device(): c_after = lax.ppermute(time_pair, 'height', shift_pairs(height_size, -1))]
    broadcast_in_dim x0 -> x1, other arithmetic: none -> 2.64 us  [per_device(): return updated.astype(jnp.bfloat16)[None, None]]
    ppermute x1, waiting for transfers between devices: 32.6 us -> 35 us  [per_device(): t_before = lax.ppermute(sent, 'tm', shift_pairs(tm_size, 1))]
    unnamed x23 -> x21, local copies, waits for them, and re-layouts: 4.75 us -> 4.76 us
  transfers between devices with their start and end apart: 14 -> 14, of which waited for: 10 -> 11; matrix products, arithmetic and copies ran while one was open for 7% -> 4% of each run, Pallas kernels for 17% -> 13%
where the time goes in v11:
time: 174 us
  waiting for transfers between devices  85.4 us (49%)
  starting transfers between devices  35.3 us (20%)
  Pallas kernels  32.2 us (19%)
  local copies, waits for them, and re-layouts  8.56 us (5%)
  other arithmetic  7.57 us (4%)
  matrix products  4.52 us (3%)
    ppermute x1, waiting for transfers between devices, per_device(): t_before = lax.ppermute(sent, 'tm', shift_pairs(tm_size, 1))  35 us
    pallas_call x3, Pallas kernels, attend(): pl.pallas_call(kernel, grid_spec=grid_spec, out_shape=out_shape)  32.2 us
    ppermute x4, waiting for transfers between devices, exchange(): other = lax.ppermute(block, 'tm', [(i, i ^ step) for i in range(devices)])  18.7 us
    ppermute x3, waiting for transfers between devices, per_device(): received.append(lax.ppermute(part, 'mp', pairs))  17.2 us
    ppermute x1, waiting for transfers between devices, per_device(): c_after = lax.ppermute(time_pair, 'height', shift_pairs(height_size, -1))  9.47 us
    ppermute x4, starting transfers between devices, exchange(): other = lax.ppermute(block, 'tm', [(i, i ^ step) for i in range(devices)])  7.11 us
    ppermute x3, starting transfers between devices, per_device(): received.append(lax.ppermute(part, 'mp', pairs))  6.76 us
    ppermute x1, starting transfers between devices, per_device(): h_before = lax.ppermute(own, 'height', shift_pairs(height_size, 1))  4.92 us
  transfers between devices with their start and end apart: 14, of which 11 were waited for; matrix products, arithmetic and copies ran while one was open for 4% of the time, Pallas kernels for 13%

profile of v11, /device:TPU:97, one launch (start us, length us, event | category | flops | bytes accessed | tf_op | source)
XLA Modules:
  0.0 173.8 jit_solution(18270936775009592215)
XLA Ops:
  0.0 0.0 copy-start
  0.0 0.8 copy-done
  0.8 2.7 %collective-permute-start = (bf16[2,16,384]{2,1,0:T(8,128)(2,1)S(1)}, bf16[2,16,384]{2,1,0:T(8,128)(2,1)S(1)}, u32[]{:S(2)}, u32[]{:S(2)}) collective-permute-start(bf16[2,16,384]{2,1,0:T(8,128)(2,1)S(1)} %constant_dynamic-slice_fusion.3), channel_id=1, source_target_pairs={{0,16},{16,0},{32,48},{48,32},{64,80},{80,64},{96,112},{112,96},{1... | collective-permute-start | bytes 73736 | tf_op jit(solution)/shard_map/ppermute | solution.py:39
  3.5 1.4 collective-permute-done
  5.0 0.1 collective-permute-start.1
  5.1 4.9 %collective-permute-start.5 = (bf16[2,384,768]{2,1,0:T(8,128)(2,1)}, bf16[2,384,768]{2,1,0:T(8,128)(2,1)S(1)}, u32[]{:S(2)}, u32[]{:S(2)}) collective-permute-start(bf16[2,384,768]{2,1,0:T(8,128)(2,1)} %bitcast.2.rest_0_), channel_id=1, source_target_pairs={{0,4},{4,8},{8,12},{1,5},{5,9},{9,13},{2,6},{6,10},{10,14},{3,7},{... | collective-permute-start | bytes 3538952 | tf_op jit(solution)/shard_map/ppermute | solution.py:198
  10.0 1.9 %collective-permute-start.6 = (bf16[2,384,768]{2,1,0:T(8,128)(2,1)}, bf16[2,384,768]{2,1,0:T(8,128)(2,1)S(1)}, u32[]{:S(2)}, u32[]{:S(2)}) collective-permute-start(bf16[2,384,768]{2,1,0:T(8,128)(2,1)} %bitcast.2.rest_0_), channel_id=1, source_target_pairs={{4,0},{8,4},{12,8},{5,1},{9,5},{13,9},{6,2},{10,6},{14,10},{7,3},{... | collective-permute-start | bytes 3538952 | tf_op jit(solution)/shard_map/ppermute | solution.py:199
  12.0 0.0 collective-permute-done.1
  12.0 0.1 collective-permute-start.2
  12.1 7.1 %collective-permute-done.2 = bf16[2,64,384]{2,1,0:T(8,128)(2,1)S(1)} collective-permute-done((bf16[2,64,384]{2,1,0:T(8,128)(2,1)S(1)}, bf16[2,64,384]{2,1,0:T(8,128)(2,1)S(1)}, u32[]{:S(2)}, u32[]{:S(2)}) %collective-permute-start.2) | collective-permute-done | bytes 98336 | tf_op jit(solution)/shard_map/ppermute | solution.py:39
  19.3 4.2 %collective-permute-start.3 = (bf16[2,128,384]{2,1,0:T(8,128)(2,1)S(1)}, bf16[2,128,384]{2,1,0:T(8,128)(2,1)S(1)}, u32[]{:S(2)}, u32[]{:S(2)}) collective-permute-start(bf16[2,128,384]{2,1,0:T(8,128)(2,1)S(1)} %maximum_select_fusion.2), channel_id=1, source_target_pairs={{0,128},{16,144},{32,160},{48,176},{64,192},{80,208},{96,224},{112... | collective-permute-start | bytes 589832 | tf_op jit(solution)/shard_map/ppermute | solution.py:39
  23.5 0.0 copy-start.8
  23.5 0.0 copy-start.9
  23.5 10.1 %collective-permute-done.3 = bf16[2,128,384]{2,1,0:T(8,128)(2,1)S(1)} collective-permute-done((bf16[2,128,384]{2,1,0:T(8,128)(2,1)S(1)}, bf16[2,128,384]{2,1,0:T(8,128)(2,1)S(1)}, u32[]{:S(2)}, u32[]{:S(2)}) %collective-permute-start.3) | collective-permute-done | bytes 196640 | tf_op jit(solution)/shard_map/ppermute | solution.py:39
  33.6 0.1 maximum_select_fusion.1
  33.7 1.4 collective-permute-start.4
  35.1 1.3 collective-permute-done.4
  36.4 1.1 maximum_select_fusion.rest_0_
  37.5 0.0 collective-permute-done.5.rest_1_
  37.5 0.0 copy-start.4
  37.5 1.0 copy-done.4
  38.5 0.0 collective-permute-done.6.rest_2_
  38.6 1.0 copy-done.5
  39.6 4.6 %collective-permute-start.7 = (bf16[2,384,768]{2,1,0:T(8,128)(2,1)}, bf16[2,384,768]{2,1,0:T(8,128)(2,1)S(1)}, u32[]{:S(2)}, u32[]{:S(2)}) collective-permute-start(bf16[2,384,768]{2,1,0:T(8,128)(2,1)} %bitcast.2.rest_0_), channel_id=1, source_target_pairs={{0,16},{16,32},{32,48},{48,64},{64,80},{80,96},{96,112},{112,128},... | collective-permute-start | bytes 3538952 | tf_op jit(solution)/shard_map/ppermute | solution.py:207
  44.2 3.0 %collective-permute-start.8 = (bf16[2,384,768]{2,1,0:T(8,128)(2,1)}, bf16[2,384,768]{2,1,0:T(8,128)(2,1)S(1)}, u32[]{:S(2)}, u32[]{:S(2)}) collective-permute-start(bf16[2,384,768]{2,1,0:T(8,128)(2,1)} %bitcast.2.rest_0_), channel_id=1, source_target_pairs={{16,0},{32,16},{48,32},{64,48},{80,64},{96,80},{112,96},{128,112},... | collective-permute-start | bytes 3538952 | tf_op jit(solution)/shard_map/ppermute | solution.py:208
  47.3 0.0 copy-done.8
  47.3 0.1 pad_dynamic-slice_fusion
  47.4 0.1 copy.16
  47.5 0.1 lt.111
  47.6 0.1 copy.17
  47.6 0.1 lt.116
  47.7 0.0 copy-done.9
  47.7 0.7 copy.22.reach_ref
  48.4 0.7 and_select_fusion.rest_3_.rest_4_
  49.1 10.7 %shard_map.82 = (f32[6,384,1]{2,1,0:T(8,128)}, f32[6,384,1]{2,1,0:T(8,128)}, f32[384,768]{1,0:T(8,128)}) custom-call(s32[6,2]{1,0:T(8,128)} %copy.22.reach_ref, bf16[384,768]{1,0:T(8,128)(2,1)} %bitcast.15, bf16[2,384,768]{2,1,0:T(8,128)(2,1)} %bitcast.2.rest_0_, bf16[2,384,768]{2,1,0:T(8,128)(2,1)} %copy-done.4, bf16[2,384,768]{2,1,0:T(8,128)(2,1)} %copy-done.5, ...), custom_call_target="tpu_custom_call" | custom-call | tf_op jit(solution)/shard_map/pallas_call | solution.py:187
  59.8 35.0 %collective-permute-done.7.rest_1_ = bf16[2,384,768]{2,1,0:T(8,128)(2,1)S(1)} collective-permute-done((bf16[2,384,768]{2,1,0:T(8,128)(2,1)}, bf16[2,384,768]{2,1,0:T(8,128)(2,1)S(1)}, u32[]{:S(2)}, u32[]{:S(2)}) %collective-permute-start.7) | collective-permute-done | bytes 1179680 | tf_op jit(solution)/shard_map/ppermute | solution.py:207
  94.8 2.5 %collective-permute-done.8.rest_2_ = bf16[2,384,768]{2,1,0:T(8,128)(2,1)S(1)} collective-permute-done((bf16[2,384,768]{2,1,0:T(8,128)(2,1)}, bf16[2,384,768]{2,1,0:T(8,128)(2,1)S(1)}, u32[]{:S(2)}, u32[]{:S(2)}) %collective-permute-start.8) | collective-permute-done | bytes 1179680 | tf_op jit(solution)/shard_map/ppermute | solution.py:208
  97.2 0.0 copy-done.2
  97.2 1.0 copy-done.3
  98.3 1.7 pad_maximum_fusion
  99.9 2.4 %collective-permute-start.10 = (bf16[2,2,384,768]{3,2,1,0:T(8,128)(2,1)}, bf16[2,2,384,768]{3,2,1,0:T(8,128)(2,1)S(1)}, u32[]{:S(2)}, u32[]{:S(2)}) collective-permute-start(bf16[2,2,384,768]{3,2,1,0:T(8,128)(2,1)} %pad_maximum_fusion), channel_id=1, source_target_pairs={{4,0},{8,4},{12,8},{5,1},{9,5},{13,9},{6,2},{10,6},{14,10},{7,3},{... | collective-permute-start | bytes 7077896 | tf_op jit(solution)/shard_map/ppermute | solution.py:224
  102.3 3.2 %collective-permute-start.9 = (bf16[2,2,384,768]{3,2,1,0:T(8,128)(2,1)}, bf16[2,2,384,768]{3,2,1,0:T(8,128)(2,1)}, u32[]{:S(2)}, u32[]{:S(2)}) collective-permute-start(bf16[2,2,384,768]{3,2,1,0:T(8,128)(2,1)} %pad_maximum_fusion), channel_id=1, source_target_pairs={{0,4},{4,8},{8,12},{1,5},{5,9},{9,13},{2,6},{6,10},{10,14},{3,7},{... | collective-permute-start | bytes 7077896 | tf_op jit(solution)/shard_map/ppermute | solution.py:223
  105.5 0.6 slice.12
  106.2 0.6 slice.13
  106.8 1.3 fusion.8
  108.1 0.8 copy.23.rest_8_
  108.9 11.9 %shard_map.83 = (f32[6,384,1]{2,1,0:T(8,128)}, f32[6,384,1]{2,1,0:T(8,128)}, f32[384,768]{1,0:T(8,128)}) custom-call(s32[6,2]{1,0:T(8,128)} %copy.22.reach_ref, bf16[384,768]{1,0:T(8,128)(2,1)} %bitcast.16, bf16[2,256,768]{2,1,0:T(8,128)(2,1)} %maximum_select_fusion.rest_0_, bf16[2,384,768]{2,1,0:T(8,128)(2,1)} %copy-done.2, bf16[2,384,768]{2,1,0:T(8,128)(2,1)} %copy-done.3, ...), custom_call_target="tpu_custom_call" | custom-call | tf_op jit(solution)/shard_map/pallas_call | solution.py:187
  120.8 9.5 %collective-permute-done.10.rest_1_.rest_3_ = bf16[2,2,384,768]{3,2,1,0:T(8,128)(2,1)S(1)} collective-permute-done((bf16[2,2,384,768]{3,2,1,0:T(8,128)(2,1)}, bf16[2,2,384,768]{3,2,1,0:T(8,128)(2,1)S(1)}, u32[]{:S(2)}, u32[]{:S(2)}) %collective-permute-start.10) | collective-permute-done | bytes 2359328 | tf_op jit(solution)/shard_map/ppermute | solution.py:224
  130.3 1.3 collective-permute-done.9.rest_0_.rest_2_
  131.6 0.2 copy-done.1
  131.7 9.6 %shard_map.84 = bf16[384,768]{1,0:T(8,128)(2,1)} custom-call(s32[6,2]{1,0:T(8,128)} %copy.22.reach_ref, bf16[384,768]{1,0:T(8,128)(2,1)} %bitcast.17, bf16[2,2,384,768]{3,2,1,0:T(8,128)(2,1)} %collective-permute-done.9.rest_0_.rest_2_, bf16[2,2,384,768]{3,2,1,0:T(8,128)(2,1)} %copy-done.1, bf16[2,2,384,768]{3,2,1,0:T(8,128)(2,1)} %collective-permute-done.9.rest_0_.rest_2_, ...), custom_call_target="tpu_custom_call" | custom-call | tf_op jit(solution)/shard_map/pallas_call | solution.py:187
  141.3 4.5 %convolution_convert_fusion = bf16[384,3072]{1,0:T(8,128)(2,1)S(1)} fusion(bf16[384,768]{1,0:T(8,128)(2,1)} %shard_map.84, bf16[768,3072]{1,0:T(8,128)(2,1)} %param.12), kind=kOutput, calls=%fused_computation | convolution fusion | flops 1813118976 | bytes 7667712 | tf_op jit(solution)/shard_map/dot_general | solution.py:232
  145.9 0.0 copy-start.6
  145.9 0.0 copy-start.7
  145.9 1.3 constant_dynamic-slice_fusion.2
  147.2 4.1 %collective-permute-start.11 = (bf16[384,768]{1,0:T(8,128)(2,1)}, bf16[384,768]{1,0:T(8,128)(2,1)}, u32[]{:S(2)}, u32[]{:S(2)}) collective-permute-start(bf16[384,768]{1,0:T(8,128)(2,1)} %get-tuple-element.35), channel_id=1, source_target_pairs={{0,2},{1,3},{2,0},{3,1},{4,6},{5,7},{6,4},{7,5},{8,10},{9,11},{10,... | collective-permute-start | bytes 1769480 | tf_op jit(solution)/shard_map/ppermute | solution.py:239
  151.3 0.8 collective-permute-start.12
  152.1 1.9 %collective-permute-start.13 = (bf16[384,768]{1,0:T(8,128)(2,1)}, bf16[384,768]{1,0:T(8,128)(2,1)}, u32[]{:S(2)}, u32[]{:S(2)}) collective-permute-start(bf16[384,768]{1,0:T(8,128)(2,1)} %get-tuple-element.36), channel_id=1, source_target_pairs={{0,3},{1,0},{2,1},{3,2},{4,7},{5,4},{6,5},{7,6},{8,11},{9,8},{10,9... | collective-permute-start | bytes 1769480 | tf_op jit(solution)/shard_map/ppermute | solution.py:239
  154.0 9.2 %collective-permute-done.11 = bf16[384,768]{1,0:T(8,128)(2,1)} collective-permute-done((bf16[384,768]{1,0:T(8,128)(2,1)}, bf16[384,768]{1,0:T(8,128)(2,1)}, u32[]{:S(2)}, u32[]{:S(2)}) %collective-permute-start.11) | collective-permute-done | bytes 589856 | tf_op jit(solution)/shard_map/ppermute | solution.py:239
  163.2 6.2 %collective-permute-done.12 = bf16[384,768]{1,0:T(8,128)(2,1)} collective-permute-done((bf16[384,768]{1,0:T(8,128)(2,1)}, bf16[384,768]{1,0:T(8,128)(2,1)}, u32[]{:S(2)}, u32[]{:S(2)}) %collective-permute-start.12) | collective-permute-done | bytes 589856 | tf_op jit(solution)/shard_map/ppermute | solution.py:239
  169.4 1.7 %collective-permute-done.13 = bf16[384,768]{1,0:T(8,128)(2,1)} collective-permute-done((bf16[384,768]{1,0:T(8,128)(2,1)}, bf16[384,768]{1,0:T(8,128)(2,1)}, u32[]{:S(2)}, u32[]{:S(2)}) %collective-permute-start.13) | collective-permute-done | bytes 589856 | tf_op jit(solution)/shard_map/ppermute | solution.py:239
  171.1 0.0 copy-done.6
  171.1 0.0 copy-done.7
  171.1 2.6 %fusion.1 = bf16[1,1,384,768]{3,2,1,0:T(8,128)(2,1)} fusion(bf16[384,768]{1,0:T(8,128)(2,1)} %collective-permute-done.13, bf16[384,768]{1,0:T(8,128)(2,1)} %collective-permute-done.12, bf16[384,768]{1,0:T(8,128)(2,1)} %collective-permute-done.11, bf16[1,1,384,768]{3,2,1,0:T(8,128)(2,1)S(1)} %copy-done.6, bf16[384,3072]{1,0:T(8,128)(2,1)S(1)} %convolution_convert_fusion, ...), kind=kLoop, calls=%fused_computation.5 | loop fusion | flops 3244032 | bytes 3542020 | tf_op jit(solution)/shard_map/broadcast_in_dim | solution.py:244
  (9 shorter events, 0.1 us)
Async XLA Ops:
  0.0 0.8 copy-start
  0.8 4.2 %collective-permute-start = (bf16[2,16,384]{2,1,0:T(8,128)(2,1)S(1)}, bf16[2,16,384]{2,1,0:T(8,128)(2,1)S(1)}, u32[]{:S(2)}, u32[]{:S(2)}) collective-permute-start(bf16[2,16,384]{2,1,0:T(8,128)(2,1)S(1)} %constant_dynamic-slice_fusion.3), channel_id=1, source_target_pairs={{0,16},{16,0},{32,48},{48,32},{64,80},{80,64},{96,112},{112,96},{1... | collective-permute-start | bytes 73736 | tf_op jit(solution)/shard_map/ppermute | solution.py:39
  5.0 7.0 %collective-permute-start.1 = (bf16[2,32,384]{2,1,0:T(8,128)(2,1)S(1)}, bf16[2,32,384]{2,1,0:T(8,128)(2,1)S(1)}, u32[]{:S(2)}, u32[]{:S(2)}) collective-permute-start(bf16[2,32,384]{2,1,0:T(8,128)(2,1)S(1)} %maximum_select_fusion.4), channel_id=1, source_target_pairs={{0,32},{16,48},{32,0},{48,16},{64,96},{80,112},{96,64},{112,80},{1... | collective-permute-start | bytes 147464 | tf_op jit(solution)/shard_map/ppermute | solution.py:39
  5.1 32.4 %collective-permute-start.5 = (bf16[2,384,768]{2,1,0:T(8,128)(2,1)}, bf16[2,384,768]{2,1,0:T(8,128)(2,1)S(1)}, u32[]{:S(2)}, u32[]{:S(2)}) collective-permute-start(bf16[2,384,768]{2,1,0:T(8,128)(2,1)} %bitcast.2.rest_0_), channel_id=1, source_target_pairs={{0,4},{4,8},{8,12},{1,5},{5,9},{9,13},{2,6},{6,10},{10,14},{3,7},{... | collective-permute-start | bytes 3538952 | tf_op jit(solution)/shard_map/ppermute | solution.py:198
  10.0 28.5 %collective-permute-start.6 = (bf16[2,384,768]{2,1,0:T(8,128)(2,1)}, bf16[2,384,768]{2,1,0:T(8,128)(2,1)S(1)}, u32[]{:S(2)}, u32[]{:S(2)}) collective-permute-start(bf16[2,384,768]{2,1,0:T(8,128)(2,1)} %bitcast.2.rest_0_), channel_id=1, source_target_pairs={{4,0},{8,4},{12,8},{5,1},{9,5},{13,9},{6,2},{10,6},{14,10},{7,3},{... | collective-permute-start | bytes 3538952 | tf_op jit(solution)/shard_map/ppermute | solution.py:199
  12.0 7.2 %collective-permute-start.2 = (bf16[2,64,384]{2,1,0:T(8,128)(2,1)S(1)}, bf16[2,64,384]{2,1,0:T(8,128)(2,1)S(1)}, u32[]{:S(2)}, u32[]{:S(2)}) collective-permute-start(bf16[2,64,384]{2,1,0:T(8,128)(2,1)S(1)} %maximum_select_fusion.3), channel_id=1, source_target_pairs={{0,64},{16,80},{32,96},{48,112},{64,0},{80,16},{96,32},{112,48},{1... | collective-permute-start | bytes 294920 | tf_op jit(solution)/shard_map/ppermute | solution.py:39
  19.3 14.3 %collective-permute-start.3 = (bf16[2,128,384]{2,1,0:T(8,128)(2,1)S(1)}, bf16[2,128,384]{2,1,0:T(8,128)(2,1)S(1)}, u32[]{:S(2)}, u32[]{:S(2)}) collective-permute-start(bf16[2,128,384]{2,1,0:T(8,128)(2,1)S(1)} %maximum_select_fusion.2), channel_id=1, source_target_pairs={{0,128},{16,144},{32,160},{48,176},{64,192},{80,208},{96,224},{112... | collective-permute-start | bytes 589832 | tf_op jit(solution)/shard_map/ppermute | solution.py:39
  23.5 23.8 %copy-start.8 = (s32[2,16,4]{1,2,0:T(4,128)S(1)}, s32[2,16,4]{1,2,0:T(4,128)}, u32[]{:S(2)}) copy-start(s32[2,16,4]{1,2,0:T(4,128)} %param.15) | copy-start | bytes 1540
  23.5 24.3 %copy-start.9 = (s32[6,2]{0,1:T(2,128)S(1)}, s32[6,2]{0,1:T(2,128)}, u32[]{:S(2)}) copy-start(s32[6,2]{0,1:T(2,128)} %param.14) | copy-start | bytes 148
  33.7 2.7 %collective-permute-start.4 = (bf16[2,256,384]{2,1,0:T(8,128)(2,1)S(1)}, bf16[2,256,384]{2,1,0:T(8,128)(2,1)S(1)}, u32[]{:S(2)}, u32[]{:S(2)}) collective-permute-start(bf16[2,256,384]{2,1,0:T(8,128)(2,1)S(1)} %maximum_select_fusion.1), channel_id=1, source_target_pairs={{0,4},{4,0},{8,12},{12,8},{1,5},{5,1},{9,13},{13,9},{2,6},{6,2},{1... | collective-permute-start | bytes 1179656 | tf_op jit(solution)/shard_map/ppermute | solution.py:48
  37.5 1.0 copy-start.4
  38.5 1.0 copy-start.5
  39.6 55.2 %collective-permute-start.7 = (bf16[2,384,768]{2,1,0:T(8,128)(2,1)}, bf16[2,384,768]{2,1,0:T(8,128)(2,1)S(1)}, u32[]{:S(2)}, u32[]{:S(2)}) collective-permute-start(bf16[2,384,768]{2,1,0:T(8,128)(2,1)} %bitcast.2.rest_0_), channel_id=1, source_target_pairs={{0,16},{16,32},{32,48},{48,64},{64,80},{80,96},{96,112},{112,128},... | collective-permute-start | bytes 3538952 | tf_op jit(solution)/shard_map/ppermute | solution.py:207
  44.2 53.0 %collective-permute-start.8 = (bf16[2,384,768]{2,1,0:T(8,128)(2,1)}, bf16[2,384,768]{2,1,0:T(8,128)(2,1)S(1)}, u32[]{:S(2)}, u32[]{:S(2)}) collective-permute-start(bf16[2,384,768]{2,1,0:T(8,128)(2,1)} %bitcast.2.rest_0_), channel_id=1, source_target_pairs={{16,0},{32,16},{48,32},{64,48},{80,64},{96,80},{112,96},{128,112},... | collective-permute-start | bytes 3538952 | tf_op jit(solution)/shard_map/ppermute | solution.py:208
  94.8 2.5 %copy-start.2 = (bf16[2,384,768]{2,1,0:T(8,128)(2,1)}, bf16[2,384,768]{2,1,0:T(8,128)(2,1)S(1)}, u32[]{:S(2)}) copy-start(bf16[2,384,768]{2,1,0:T(8,128)(2,1)S(1)} %collective-permute-done.7.rest_1_) | copy-start | bytes 3538948
  97.2 1.0 copy-start.3
  99.9 30.4 %collective-permute-start.10 = (bf16[2,2,384,768]{3,2,1,0:T(8,128)(2,1)}, bf16[2,2,384,768]{3,2,1,0:T(8,128)(2,1)S(1)}, u32[]{:S(2)}, u32[]{:S(2)}) collective-permute-start(bf16[2,2,384,768]{3,2,1,0:T(8,128)(2,1)} %pad_maximum_fusion), channel_id=1, source_target_pairs={{4,0},{8,4},{12,8},{5,1},{9,5},{13,9},{6,2},{10,6},{14,10},{7,3},{... | collective-permute-start | bytes 7077896 | tf_op jit(solution)/shard_map/ppermute | solution.py:224
  102.3 29.3 %collective-permute-start.9 = (bf16[2,2,384,768]{3,2,1,0:T(8,128)(2,1)}, bf16[2,2,384,768]{3,2,1,0:T(8,128)(2,1)}, u32[]{:S(2)}, u32[]{:S(2)}) collective-permute-start(bf16[2,2,384,768]{3,2,1,0:T(8,128)(2,1)} %pad_maximum_fusion), channel_id=1, source_target_pairs={{0,4},{4,8},{8,12},{1,5},{5,9},{9,13},{2,6},{6,10},{10,14},{3,7},{... | collective-permute-start | bytes 7077896 | tf_op jit(solution)/shard_map/ppermute | solution.py:223
  130.3 1.4 copy-start.1
  145.9 25.2 %copy-start.6 = (bf16[1,1,384,768]{3,2,1,0:T(8,128)(2,1)S(1)}, bf16[1,1,384,768]{3,2,1,0:T(8,128)(2,1)}, u32[]{:S(2)}) copy-start(bf16[1,1,384,768]{3,2,1,0:T(8,128)(2,1)} %param.11) | copy-start | bytes 1769476
  145.9 25.2 %copy-start.7 = (f32[768]{0:T(1024)S(1)}, f32[768]{0:T(1024)}, u32[]{:S(2)}) copy-start(f32[768]{0:T(1024)} %param.13) | copy-start | bytes 9220
  147.2 16.0 %collective-permute-start.11 = (bf16[384,768]{1,0:T(8,128)(2,1)}, bf16[384,768]{1,0:T(8,128)(2,1)}, u32[]{:S(2)}, u32[]{:S(2)}) collective-permute-start(bf16[384,768]{1,0:T(8,128)(2,1)} %get-tuple-element.35), channel_id=1, source_target_pairs={{0,2},{1,3},{2,0},{3,1},{4,6},{5,7},{6,4},{7,5},{8,10},{9,11},{10,... | collective-permute-start | bytes 1769480 | tf_op jit(solution)/shard_map/ppermute | solution.py:239
  151.3 18.1 %collective-permute-start.12 = (bf16[384,768]{1,0:T(8,128)(2,1)}, bf16[384,768]{1,0:T(8,128)(2,1)}, u32[]{:S(2)}, u32[]{:S(2)}) collective-permute-start(bf16[384,768]{1,0:T(8,128)(2,1)} %get-tuple-element.37), channel_id=1, source_target_pairs={{0,1},{1,2},{2,3},{3,0},{4,5},{5,6},{6,7},{7,4},{8,9},{9,10},{10,1... | collective-permute-start | bytes 1769480 | tf_op jit(solution)/shard_map/ppermute | solution.py:239
  152.1 19.0 %collective-permute-start.13 = (bf16[384,768]{1,0:T(8,128)(2,1)}, bf16[384,768]{1,0:T(8,128)(2,1)}, u32[]{:S(2)}, u32[]{:S(2)}) collective-permute-start(bf16[384,768]{1,0:T(8,128)(2,1)} %get-tuple-element.36), channel_id=1, source_target_pairs={{0,3},{1,0},{2,1},{3,2},{4,7},{5,4},{6,5},{7,6},{8,11},{9,8},{10,9... | collective-permute-start | bytes 1769480 | tf_op jit(solution)/shard_map/ppermute | solution.py:239

commit v12 on v11

--- a/solution.py
+++ b/solution.py
@@ -26,6 +26,17 @@
 
 def shift_pairs(devices, step):
     return [(i, i + step) for i in range(devices) if 0 <= i + step < devices]
+
+
+def diagonal_pairs(tm_size, height_size, step):
+    pairs = []
+    for t in range(tm_size):
+        if not 0 <= t + step < tm_size:
+            continue
+        for h in range(1, height_size - 1, 2):
+            pairs.append((t * height_size + h, (t + step) * height_size + h + 1))
+            pairs.append((t * height_size + h + 1, (t + step) * height_size + h))
+    return pairs
 
 
 def text_halves(text_kv):
@@ -206,6 +217,8 @@
     sent, text, h_before, h_after = lax.optimization_barrier((own, text, h_before, h_after))
     t_before = lax.ppermute(sent, "tm", shift_pairs(tm_size, 1))
     t_after = lax.ppermute(sent, "tm", shift_pairs(tm_size, -1))
+    diag_prev = lax.ppermute(sent, ("tm", "height"), diagonal_pairs(tm_size, height_size, 1))
+    diag_next = lax.ppermute(sent, ("tm", "height"), diagonal_pairs(tm_size, height_size, -1))
     time_start = lax.axis_index("tm")
     height_start = lax.axis_index("height")
     zero_index = jnp.int32(0)
@@ -218,13 +231,24 @@
     queries = image_q[0, 0]
     near = [(own, None, 4), (h_before, None, 3), (h_after, None, 5)]
     state = attend(head_reach, queries, None, near, bias)
-    t_before, t_after, state = lax.optimization_barrier((t_before, t_after, state))
+    t_before, t_after, diag_prev, diag_next, state = lax.optimization_barrier(
+        (t_before, t_after, diag_prev, diag_next, state)
+    )
     time_pair = jnp.stack([t_before, t_after])
-    c_before = lax.ppermute(time_pair, "height", shift_pairs(height_size, 1))
-    c_after = lax.ppermute(time_pair, "height", shift_pairs(height_size, -1))
+    even = [i for i in range(0, height_size - 1, 2)]
+    near_before = lax.ppermute(time_pair, "height", [(i, i + 1) for i in even])
+    near_after = lax.ppermute(time_pair, "height", [(i + 1, i) for i in even])
     across = [(t_before, None, 1), (t_after, None, 7)]
     state = attend(head_reach, queries, text, across, bias, state)
-    corners = [(c_before, 0, 0), (c_after, 0, 2), (c_before, 1, 6), (c_after, 1, 8)]
+    height_index = lax.axis_index("height")
+    from_before = jnp.logical_and(height_index % 2 == 0, height_index > 0)
+    from_after = jnp.logical_and(height_index % 2 == 1, height_index < height_size - 1)
+    corners = [
+        (jnp.where(from_before, diag_prev, near_before[0]), None, 0),
+        (jnp.where(from_after, diag_prev, near_after[0]), None, 2),
+        (jnp.where(from_before, diag_next, near_before[1]), None, 6),
+        (jnp.where(from_after, diag_next, near_after[1]), None, 8),
+    ]
     attended = attend(head_reach, queries, None, corners, bias, state, qvalid)
 
     mp_index = lax.axis_index("mp")

time: 174 us -> 200 us (1.15); the launches traced: 174 us -> 197 us
  waiting for transfers between devices: 85.4 us -> 98.1 us
  starting transfers between devices: 35.3 us -> 41.7 us
  other arithmetic: 7.57 us -> 12.3 us
    ppermute x2 -> x4, waiting for transfers between devices: 10.8 us -> 54 us  [the longest x2 54 us: per_device(): lax.ppermute(sent, ('tm', 'height'), diagonal_pairs(tm_size, height_size,...]
    ppermute x1, waiting for transfers between devices: 35 us -> 0.01 us  [per_device(): t_before = lax.ppermute(sent, 'tm', shift_pairs(tm_size, 1))]
    ppermute x2 -> x4, starting transfers between devices: 5.55 us -> 13.3 us  [the longest x2 7.44 us: per_device(): lax.ppermute(sent, ('tm', 'height'), diagonal_pairs(tm_size, height_size,...]
    ppermute x3, waiting for transfers between devices: 17.2 us -> 24 us  [per_device(): received.append(lax.ppermute(part, 'mp', pairs))]
    select_n x0 -> x1, other arithmetic: none -> 4.66 us  [per_device(): jnp.where(from_before, diag_next, near_before[1])]
    ppermute x1, waiting for transfers between devices: 2.46 us -> 0.01 us  [per_device(): t_after = lax.ppermute(sent, 'tm', shift_pairs(tm_size, -1))]
    unnamed x21 -> x19, local copies, waits for them, and re-layouts: 4.76 us -> 2.96 us
  transfers between devices with their start and end apart: 14 -> 16, of which waited for: 11 -> 7; matrix products, arithmetic and copies ran while one was open for 4% -> 3% of each run, Pallas kernels for 13% -> 12%
where the time goes in v12:
time: 200 us; the launch traced here: 197 us
  waiting for transfers between devices  98.1 us (49%)
  starting transfers between devices  41.7 us (21%)
  Pallas kernels  32.9 us (16%)
  other arithmetic  12.3 us (6%)
  local copies, waits for them, and re-layouts  6.69 us (3%)
  matrix products  4.52 us (2%)
    ppermute x2, waiting for transfers between devices, per_device(): lax.ppermute(sent, ('tm', 'height'), diagonal_pairs(tm_size, height_size,...  54 us
    pallas_call x3, Pallas kernels, attend(): pl.pallas_call(kernel, grid_spec=grid_spec, out_shape=out_shape)  32.9 us
    ppermute x3, waiting for transfers between devices, per_device(): received.append(lax.ppermute(part, 'mp', pairs))  24 us
    ppermute x4, waiting for transfers between devices, exchange(): other = lax.ppermute(block, 'tm', [(i, i ^ step) for i in range(devices)])  18.7 us
    ppermute x2, starting transfers between devices, per_device(): lax.ppermute(sent, ('tm', 'height'), diagonal_pairs(tm_size, height_size,...  7.44 us
    ppermute x4, starting transfers between devices, exchange(): other = lax.ppermute(block, 'tm', [(i, i ^ step) for i in range(devices)])  7.11 us
    ppermute x3, starting transfers between devices, per_device(): received.append(lax.ppermute(part, 'mp', pairs))  5.43 us
    ppermute x1, starting transfers between devices, per_device(): h_before = lax.ppermute(own, 'height', shift_pairs(height_size, 1))  4.92 us
  transfers between devices with their start and end apart: 16, of which 7 were waited for; matrix products, arithmetic and copies ran while one was open for 3% of the time, Pallas kernels for 12%

profile of v12, /device:TPU:97, one launch (start us, length us, event | category | flops | bytes accessed | tf_op | source)
XLA Modules:
  0.0 196.6 jit_solution(18281124472668843927)
XLA Ops:
  0.0 0.0 copy-start
  0.0 0.8 copy-done
  0.8 2.7 %collective-permute-start = (bf16[2,16,384]{2,1,0:T(8,128)(2,1)S(1)}, bf16[2,16,384]{2,1,0:T(8,128)(2,1)S(1)}, u32[]{:S(2)}, u32[]{:S(2)}) collective-permute-start(bf16[2,16,384]{2,1,0:T(8,128)(2,1)S(1)} %constant_dynamic-slice_fusion.3), channel_id=1, source_target_pairs={{0,16},{16,0},{32,48},{48,32},{64,80},{80,64},{96,112},{112,96},{1... | collective-permute-start | bytes 73736 | tf_op jit(solution)/shard_map/ppermute | solution.py:50
  3.5 1.4 collective-permute-done
  5.0 0.1 collective-permute-start.1
  5.1 4.9 %collective-permute-start.5 = (bf16[2,384,768]{2,1,0:T(8,128)(2,1)}, bf16[2,384,768]{2,1,0:T(8,128)(2,1)S(1)}, u32[]{:S(2)}, u32[]{:S(2)}) collective-permute-start(bf16[2,384,768]{2,1,0:T(8,128)(2,1)} %bitcast.2.rest_0_), channel_id=1, source_target_pairs={{0,4},{4,8},{8,12},{1,5},{5,9},{9,13},{2,6},{6,10},{10,14},{3,7},{... | collective-permute-start | bytes 3538952 | tf_op jit(solution)/shard_map/ppermute | solution.py:209
  10.0 1.9 collective-permute-start.6
  12.0 0.0 collective-permute-done.1
  12.0 0.1 collective-permute-start.2
  12.1 7.1 %collective-permute-done.2 = bf16[2,64,384]{2,1,0:T(8,128)(2,1)S(1)} collective-permute-done((bf16[2,64,384]{2,1,0:T(8,128)(2,1)S(1)}, bf16[2,64,384]{2,1,0:T(8,128)(2,1)S(1)}, u32[]{:S(2)}, u32[]{:S(2)}) %collective-permute-start.2) | collective-permute-done | bytes 98336 | tf_op jit(solution)/shard_map/ppermute | solution.py:50
  19.3 4.2 %collective-permute-start.3 = (bf16[2,128,384]{2,1,0:T(8,128)(2,1)S(1)}, bf16[2,128,384]{2,1,0:T(8,128)(2,1)S(1)}, u32[]{:S(2)}, u32[]{:S(2)}) collective-permute-start(bf16[2,128,384]{2,1,0:T(8,128)(2,1)S(1)} %maximum_select_fusion.2), channel_id=1, source_target_pairs={{0,128},{16,144},{32,160},{48,176},{64,192},{80,208},{96,224},{112... | collective-permute-start | bytes 589832 | tf_op jit(solution)/shard_map/ppermute | solution.py:50
  23.5 10.1 %collective-permute-done.3 = bf16[2,128,384]{2,1,0:T(8,128)(2,1)S(1)} collective-permute-done((bf16[2,128,384]{2,1,0:T(8,128)(2,1)S(1)}, bf16[2,128,384]{2,1,0:T(8,128)(2,1)S(1)}, u32[]{:S(2)}, u32[]{:S(2)}) %collective-permute-start.3) | collective-permute-done | bytes 196640 | tf_op jit(solution)/shard_map/ppermute | solution.py:50
  33.6 0.1 maximum_select_fusion.1
  33.7 1.4 collective-permute-start.4
  35.1 1.3 collective-permute-done.4
  36.4 1.1 maximum_select_fusion.rest_0_
  37.5 0.0 collective-permute-done.5.rest_1_
  37.5 0.0 collective-permute-done.6.rest_2_
  37.5 1.1 copy-done.3
  38.6 2.4 %collective-permute-start.10 = (bf16[2,384,768]{2,1,0:T(8,128)(2,1)}, bf16[2,384,768]{2,1,0:T(8,128)(2,1)}, u32[]{:S(2)}, u32[]{:S(2)}) collective-permute-start(bf16[2,384,768]{2,1,0:T(8,128)(2,1)} %bitcast.2.rest_0_), channel_id=1, source_target_pairs={{20,8},{24,4},{36,24},{40,20},{52,40},{56,36},{68,56},{72,52},{84,... | collective-permute-start | bytes 3538952 | tf_op jit(solution)/shard_map/ppermute | solution.py:221
  41.1 0.0 copy-done.4
  41.1 4.1 %collective-permute-start.7 = (bf16[2,384,768]{2,1,0:T(8,128)(2,1)}, bf16[2,384,768]{2,1,0:T(8,128)(2,1)S(1)}, u32[]{:S(2)}, u32[]{:S(2)}) collective-permute-start(bf16[2,384,768]{2,1,0:T(8,128)(2,1)} %bitcast.2.rest_0_), channel_id=1, source_target_pairs={{0,16},{16,32},{32,48},{48,64},{64,80},{80,96},{96,112},{112,128},... | collective-permute-start | bytes 3538952 | tf_op jit(solution)/shard_map/ppermute | solution.py:218
  45.2 3.6 %collective-permute-start.8 = (bf16[2,384,768]{2,1,0:T(8,128)(2,1)}, bf16[2,384,768]{2,1,0:T(8,128)(2,1)S(1)}, u32[]{:S(2)}, u32[]{:S(2)}) collective-permute-start(bf16[2,384,768]{2,1,0:T(8,128)(2,1)} %bitcast.2.rest_0_), channel_id=1, source_target_pairs={{16,0},{32,16},{48,32},{64,48},{80,64},{96,80},{112,96},{128,112},... | collective-permute-start | bytes 3538952 | tf_op jit(solution)/shard_map/ppermute | solution.py:219
  48.8 5.0 %collective-permute-start.9 = (bf16[2,384,768]{2,1,0:T(8,128)(2,1)}, bf16[2,384,768]{2,1,0:T(8,128)(2,1)}, u32[]{:S(2)}, u32[]{:S(2)}) collective-permute-start(bf16[2,384,768]{2,1,0:T(8,128)(2,1)} %bitcast.2.rest_0_), channel_id=1, source_target_pairs={{4,24},{8,20},{20,40},{24,36},{36,56},{40,52},{52,72},{56,68},{68,... | collective-permute-start | bytes 3538952 | tf_op jit(solution)/shard_map/ppermute | solution.py:220
  53.8 0.0 copy-done.7
  53.8 0.1 pad_dynamic-slice_fusion
  53.9 0.1 copy.16
  54.0 0.1 lt.118
  54.1 0.1 copy.17
  54.2 0.1 lt.123
  54.2 0.0 copy-done.8
  54.2 0.7 copy.22.reach_ref
  54.9 0.7 and_select_fusion.rest_3_.rest_4_
  55.6 11.2 %shard_map.82 = (f32[6,384,1]{2,1,0:T(8,128)}, f32[6,384,1]{2,1,0:T(8,128)}, f32[384,768]{1,0:T(8,128)}) custom-call(s32[6,2]{1,0:T(8,128)} %copy.22.reach_ref, bf16[384,768]{1,0:T(8,128)(2,1)} %bitcast.31, bf16[2,384,768]{2,1,0:T(8,128)(2,1)} %bitcast.2.rest_0_, bf16[2,384,768]{2,1,0:T(8,128)(2,1)} %copy-done.3, bf16[2,384,768]{2,1,0:T(8,128)(2,1)} %copy-done.4, ...), custom_call_target="tpu_custom_call" | custom-call | tf_op jit(solution)/shard_map/pallas_call | solution.py:198
  66.8 54.0 %collective-permute-done.10 = bf16[2,384,768]{2,1,0:T(8,128)(2,1)} collective-permute-done((bf16[2,384,768]{2,1,0:T(8,128)(2,1)}, bf16[2,384,768]{2,1,0:T(8,128)(2,1)}, u32[]{:S(2)}, u32[]{:S(2)}) %collective-permute-start.10) | collective-permute-done | bytes 1179680 | tf_op jit(solution)/shard_map/ppermute | solution.py:221
  120.9 0.0 collective-permute-done.7.rest_1_
  120.9 0.0 collective-permute-done.8.rest_2_
  120.9 0.0 copy-start.2
  120.9 0.0 collective-permute-done.9
  120.9 1.8 pad_maximum_fusion
  122.7 0.0 copy-done.1
  122.7 0.4 copy-done.2
  123.1 1.3 collective-permute-start.11
  124.4 4.6 %collective-permute-start.12 = (bf16[2,2,384,768]{3,2,1,0:T(8,128)(2,1)}, bf16[2,2,384,768]{3,2,1,0:T(8,128)(2,1)S(1)}, u32[]{:S(2)}, u32[]{:S(2)}) collective-permute-start(bf16[2,2,384,768]{3,2,1,0:T(8,128)(2,1)} %pad_maximum_fusion), channel_id=1, source_target_pairs={{4,0},{12,8},{5,1},{13,9},{6,2},{14,10},{7,3},{15,11},{20,16},{28,... | collective-permute-start | bytes 7077896 | tf_op jit(solution)/shard_map/ppermute | solution.py:240
  129.0 0.6 slice.32
  129.6 0.6 slice.33
  130.2 1.2 fusion.12
  131.4 0.8 copy.23.rest_8_
  132.2 12.1 %shard_map.83 = (f32[6,384,1]{2,1,0:T(8,128)}, f32[6,384,1]{2,1,0:T(8,128)}, f32[384,768]{1,0:T(8,128)}) custom-call(s32[6,2]{1,0:T(8,128)} %copy.22.reach_ref, bf16[384,768]{1,0:T(8,128)(2,1)} %bitcast.32, bf16[2,256,768]{2,1,0:T(8,128)(2,1)} %maximum_select_fusion.rest_0_, bf16[2,384,768]{2,1,0:T(8,128)(2,1)} %copy-done.1, bf16[2,384,768]{2,1,0:T(8,128)(2,1)} %copy-done.2, ...), custom_call_target="tpu_custom_call" | custom-call | tf_op jit(solution)/shard_map/pallas_call | solution.py:198
  144.3 0.0 collective-permute-done.11
  144.3 0.0 collective-permute-done.12
  144.3 4.7 %fusion.1 = (bf16[2,384,768]{2,1,0:T(8,128)(2,1)}, bf16[2,384,768]{2,1,0:T(8,128)(2,1)}, bf16[2,384,768]{2,1,0:T(8,128)(2,1)}, bf16[2,384,768]{2,1,0:T(8,128)(2,1)}) fusion(bf16[2,384,768]{2,1,0:T(8,128)(2,1)} %collective-permute-done.10, bf16[2,2,384,768]{3,2,1,0:T(8,128)(2,1)} %collective-permute-done.11, pred[]{:T(512)S(6)} %and.97, ...), kind=kLoop, calls=%fused_computation.5 | loop fusion | flops 2359296 | bytes 11796482 | tf_op jit(solution)/shard_map/jit(_where)/select_n | solution.py:249
  149.0 9.6 %shard_map.84 = bf16[384,768]{1,0:T(8,128)(2,1)} custom-call(s32[6,2]{1,0:T(8,128)} %copy.22.reach_ref, bf16[384,768]{1,0:T(8,128)(2,1)} %bitcast.33, bf16[2,384,768]{2,1,0:T(8,128)(2,1)} %get-tuple-element.45.rest_0_, bf16[2,384,768]{2,1,0:T(8,128)(2,1)} %get-tuple-element.46.rest_1_, bf16[2,384,768]{2,1,0:T(8,128)(2,1)} %get-tuple-element.44.rest_2_, ...), custom_call_target="tpu_custom_call" | custom-call | tf_op jit(solution)/shard_map/pallas_call | solution.py:198
  158.6 4.5 %convolution_convert_fusion = bf16[384,3072]{1,0:T(8,128)(2,1)S(1)} fusion(bf16[384,768]{1,0:T(8,128)(2,1)} %shard_map.84, bf16[768,3072]{1,0:T(8,128)(2,1)} %param.12), kind=kOutput, calls=%fused_computation | convolution fusion | flops 1813118976 | bytes 7667712 | tf_op jit(solution)/shard_map/dot_general | solution.py:256
  163.1 0.0 copy-start.5
  163.2 0.0 copy-start.6
  163.2 1.3 constant_dynamic-slice_fusion.2
  164.4 2.4 %collective-permute-start.13 = (bf16[384,768]{1,0:T(8,128)(2,1)}, bf16[384,768]{1,0:T(8,128)(2,1)}, u32[]{:S(2)}, u32[]{:S(2)}) collective-permute-start(bf16[384,768]{1,0:T(8,128)(2,1)} %get-tuple-element.39), channel_id=1, source_target_pairs={{0,2},{1,3},{2,0},{3,1},{4,6},{5,7},{6,4},{7,5},{8,10},{9,11},{10,... | collective-permute-start | bytes 1769480 | tf_op jit(solution)/shard_map/ppermute | solution.py:263
  166.9 0.6 collective-permute-start.14
  167.5 2.4 %collective-permute-start.15 = (bf16[384,768]{1,0:T(8,128)(2,1)}, bf16[384,768]{1,0:T(8,128)(2,1)}, u32[]{:S(2)}, u32[]{:S(2)}) collective-permute-start(bf16[384,768]{1,0:T(8,128)(2,1)} %get-tuple-element.40), channel_id=1, source_target_pairs={{0,3},{1,0},{2,1},{3,2},{4,7},{5,4},{6,5},{7,6},{8,11},{9,8},{10,9... | collective-permute-start | bytes 1769480 | tf_op jit(solution)/shard_map/ppermute | solution.py:263
  169.9 11.5 %collective-permute-done.13 = bf16[384,768]{1,0:T(8,128)(2,1)} collective-permute-done((bf16[384,768]{1,0:T(8,128)(2,1)}, bf16[384,768]{1,0:T(8,128)(2,1)}, u32[]{:S(2)}, u32[]{:S(2)}) %collective-permute-start.13) | collective-permute-done | bytes 589856 | tf_op jit(solution)/shard_map/ppermute | solution.py:263
  181.4 12.6 %collective-permute-done.14 = bf16[384,768]{1,0:T(8,128)(2,1)} collective-permute-done((bf16[384,768]{1,0:T(8,128)(2,1)}, bf16[384,768]{1,0:T(8,128)(2,1)}, u32[]{:S(2)}, u32[]{:S(2)}) %collective-permute-start.14) | collective-permute-done | bytes 589856 | tf_op jit(solution)/shard_map/ppermute | solution.py:263
  193.9 0.0 collective-permute-done.15
  193.9 2.6 %fusion.5 = bf16[1,1,384,768]{3,2,1,0:T(8,128)(2,1)} fusion(bf16[384,768]{1,0:T(8,128)(2,1)} %collective-permute-done.15, bf16[384,768]{1,0:T(8,128)(2,1)} %collective-permute-done.14, bf16[384,768]{1,0:T(8,128)(2,1)} %collective-permute-done.13, bf16[1,1,384,768]{3,2,1,0:T(8,128)(2,1)S(1)} %copy-done.5, bf16[384,3072]{1,0:T(8,128)(2,1)S(1)} %convolution_convert_fusion, ...), kind=kLoop, calls=%fused_computation.13 | loop fusion | flops 3244032 | bytes 3542020 | tf_op jit(solution)/shard_map/broadcast_in_dim | solution.py:268
  (12 shorter events, 0.1 us)
Async XLA Ops:
  0.0 0.8 copy-start
  0.8 4.2 %collective-permute-start = (bf16[2,16,384]{2,1,0:T(8,128)(2,1)S(1)}, bf16[2,16,384]{2,1,0:T(8,128)(2,1)S(1)}, u32[]{:S(2)}, u32[]{:S(2)}) collective-permute-start(bf16[2,16,384]{2,1,0:T(8,128)(2,1)S(1)} %constant_dynamic-slice_fusion.3), channel_id=1, source_target_pairs={{0,16},{16,0},{32,48},{48,32},{64,80},{80,64},{96,112},{112,96},{1... | collective-permute-start | bytes 73736 | tf_op jit(solution)/shard_map/ppermute | solution.py:50
  5.0 7.0 %collective-permute-start.1 = (bf16[2,32,384]{2,1,0:T(8,128)(2,1)S(1)}, bf16[2,32,384]{2,1,0:T(8,128)(2,1)S(1)}, u32[]{:S(2)}, u32[]{:S(2)}) collective-permute-start(bf16[2,32,384]{2,1,0:T(8,128)(2,1)S(1)} %maximum_select_fusion.4), channel_id=1, source_target_pairs={{0,32},{16,48},{32,0},{48,16},{64,96},{80,112},{96,64},{112,80},{1... | collective-permute-start | bytes 147464 | tf_op jit(solution)/shard_map/ppermute | solution.py:50
  5.1 32.4 %collective-permute-start.5 = (bf16[2,384,768]{2,1,0:T(8,128)(2,1)}, bf16[2,384,768]{2,1,0:T(8,128)(2,1)S(1)}, u32[]{:S(2)}, u32[]{:S(2)}) collective-permute-start(bf16[2,384,768]{2,1,0:T(8,128)(2,1)} %bitcast.2.rest_0_), channel_id=1, source_target_pairs={{0,4},{4,8},{8,12},{1,5},{5,9},{9,13},{2,6},{6,10},{10,14},{3,7},{... | collective-permute-start | bytes 3538952 | tf_op jit(solution)/shard_map/ppermute | solution.py:209
  10.0 27.5 %collective-permute-start.6 = (bf16[2,384,768]{2,1,0:T(8,128)(2,1)}, bf16[2,384,768]{2,1,0:T(8,128)(2,1)S(1)}, u32[]{:S(2)}, u32[]{:S(2)}) collective-permute-start(bf16[2,384,768]{2,1,0:T(8,128)(2,1)} %bitcast.2.rest_0_), channel_id=1, source_target_pairs={{4,0},{8,4},{12,8},{5,1},{9,5},{13,9},{6,2},{10,6},{14,10},{7,3},{... | collective-permute-start | bytes 3538952 | tf_op jit(solution)/shard_map/ppermute | solution.py:210
  12.0 7.2 %collective-permute-start.2 = (bf16[2,64,384]{2,1,0:T(8,128)(2,1)S(1)}, bf16[2,64,384]{2,1,0:T(8,128)(2,1)S(1)}, u32[]{:S(2)}, u32[]{:S(2)}) collective-permute-start(bf16[2,64,384]{2,1,0:T(8,128)(2,1)S(1)} %maximum_select_fusion.3), channel_id=1, source_target_pairs={{0,64},{16,80},{32,96},{48,112},{64,0},{80,16},{96,32},{112,48},{1... | collective-permute-start | bytes 294920 | tf_op jit(solution)/shard_map/ppermute | solution.py:50
  19.3 14.3 %collective-permute-start.3 = (bf16[2,128,384]{2,1,0:T(8,128)(2,1)S(1)}, bf16[2,128,384]{2,1,0:T(8,128)(2,1)S(1)}, u32[]{:S(2)}, u32[]{:S(2)}) collective-permute-start(bf16[2,128,384]{2,1,0:T(8,128)(2,1)S(1)} %maximum_select_fusion.2), channel_id=1, source_target_pairs={{0,128},{16,144},{32,160},{48,176},{64,192},{80,208},{96,224},{112... | collective-permute-start | bytes 589832 | tf_op jit(solution)/shard_map/ppermute | solution.py:50
  23.5 30.3 %copy-start.7 = (s32[2,16,4]{1,2,0:T(4,128)S(1)}, s32[2,16,4]{1,2,0:T(4,128)}, u32[]{:S(2)}) copy-start(s32[2,16,4]{1,2,0:T(4,128)} %param.15) | copy-start | bytes 1540
  23.5 30.8 %copy-start.8 = (s32[6,2]{0,1:T(2,128)S(1)}, s32[6,2]{0,1:T(2,128)}, u32[]{:S(2)}) copy-start(s32[6,2]{0,1:T(2,128)} %param.14) | copy-start | bytes 148
  33.7 2.7 %collective-permute-start.4 = (bf16[2,256,384]{2,1,0:T(8,128)(2,1)S(1)}, bf16[2,256,384]{2,1,0:T(8,128)(2,1)S(1)}, u32[]{:S(2)}, u32[]{:S(2)}) collective-permute-start(bf16[2,256,384]{2,1,0:T(8,128)(2,1)S(1)} %maximum_select_fusion.1), channel_id=1, source_target_pairs={{0,4},{4,0},{8,12},{12,8},{1,5},{5,1},{9,13},{13,9},{2,6},{6,2},{1... | collective-permute-start | bytes 1179656 | tf_op jit(solution)/shard_map/ppermute | solution.py:59
  37.5 1.1 copy-start.3
  38.6 2.4 %copy-start.4 = (bf16[2,384,768]{2,1,0:T(8,128)(2,1)}, bf16[2,384,768]{2,1,0:T(8,128)(2,1)S(1)}, u32[]{:S(2)}) copy-start(bf16[2,384,768]{2,1,0:T(8,128)(2,1)S(1)} %collective-permute-done.6.rest_2_) | copy-start | bytes 3538948
  38.6 82.2 %collective-permute-start.10 = (bf16[2,384,768]{2,1,0:T(8,128)(2,1)}, bf16[2,384,768]{2,1,0:T(8,128)(2,1)}, u32[]{:S(2)}, u32[]{:S(2)}) collective-permute-start(bf16[2,384,768]{2,1,0:T(8,128)(2,1)} %bitcast.2.rest_0_), channel_id=1, source_target_pairs={{20,8},{24,4},{36,24},{40,20},{52,40},{56,36},{68,56},{72,52},{84,... | collective-permute-start | bytes 3538952 | tf_op jit(solution)/shard_map/ppermute | solution.py:221
  41.1 79.8 %collective-permute-start.7 = (bf16[2,384,768]{2,1,0:T(8,128)(2,1)}, bf16[2,384,768]{2,1,0:T(8,128)(2,1)S(1)}, u32[]{:S(2)}, u32[]{:S(2)}) collective-permute-start(bf16[2,384,768]{2,1,0:T(8,128)(2,1)} %bitcast.2.rest_0_), channel_id=1, source_target_pairs={{0,16},{16,32},{32,48},{48,64},{64,80},{80,96},{96,112},{112,128},... | collective-permute-start | bytes 3538952 | tf_op jit(solution)/shard_map/ppermute | solution.py:218
  45.2 75.7 %collective-permute-start.8 = (bf16[2,384,768]{2,1,0:T(8,128)(2,1)}, bf16[2,384,768]{2,1,0:T(8,128)(2,1)S(1)}, u32[]{:S(2)}, u32[]{:S(2)}) collective-permute-start(bf16[2,384,768]{2,1,0:T(8,128)(2,1)} %bitcast.2.rest_0_), channel_id=1, source_target_pairs={{16,0},{32,16},{48,32},{64,48},{80,64},{96,80},{112,96},{128,112},... | collective-permute-start | bytes 3538952 | tf_op jit(solution)/shard_map/ppermute | solution.py:219
  48.8 72.1 %collective-permute-start.9 = (bf16[2,384,768]{2,1,0:T(8,128)(2,1)}, bf16[2,384,768]{2,1,0:T(8,128)(2,1)}, u32[]{:S(2)}, u32[]{:S(2)}) collective-permute-start(bf16[2,384,768]{2,1,0:T(8,128)(2,1)} %bitcast.2.rest_0_), channel_id=1, source_target_pairs={{4,24},{8,20},{20,40},{24,36},{36,56},{40,52},{52,72},{56,68},{68,... | collective-permute-start | bytes 3538952 | tf_op jit(solution)/shard_map/ppermute | solution.py:220
  120.9 1.8 copy-start.1
  120.9 2.2 %copy-start.2 = (bf16[2,384,768]{2,1,0:T(8,128)(2,1)}, bf16[2,384,768]{2,1,0:T(8,128)(2,1)S(1)}, u32[]{:S(2)}) copy-start(bf16[2,384,768]{2,1,0:T(8,128)(2,1)S(1)} %collective-permute-done.8.rest_2_) | copy-start | bytes 3538948
  123.1 21.2 %collective-permute-start.11 = (bf16[2,2,384,768]{3,2,1,0:T(8,128)(2,1)}, bf16[2,2,384,768]{3,2,1,0:T(8,128)(2,1)}, u32[]{:S(2)}, u32[]{:S(2)}) collective-permute-start(bf16[2,2,384,768]{3,2,1,0:T(8,128)(2,1)} %pad_maximum_fusion), channel_id=1, source_target_pairs={{0,4},{8,12},{1,5},{9,13},{2,6},{10,14},{3,7},{11,15},{16,20},{24,... | collective-permute-start | bytes 7077896 | tf_op jit(solution)/shard_map/ppermute | solution.py:239
  124.4 20.0 %collective-permute-start.12 = (bf16[2,2,384,768]{3,2,1,0:T(8,128)(2,1)}, bf16[2,2,384,768]{3,2,1,0:T(8,128)(2,1)S(1)}, u32[]{:S(2)}, u32[]{:S(2)}) collective-permute-start(bf16[2,2,384,768]{3,2,1,0:T(8,128)(2,1)} %pad_maximum_fusion), channel_id=1, source_target_pairs={{4,0},{12,8},{5,1},{13,9},{6,2},{14,10},{7,3},{15,11},{20,16},{28,... | collective-permute-start | bytes 7077896 | tf_op jit(solution)/shard_map/ppermute | solution.py:240
  163.1 30.8 %copy-start.5 = (bf16[1,1,384,768]{3,2,1,0:T(8,128)(2,1)S(1)}, bf16[1,1,384,768]{3,2,1,0:T(8,128)(2,1)}, u32[]{:S(2)}) copy-start(bf16[1,1,384,768]{3,2,1,0:T(8,128)(2,1)} %param.11) | copy-start | bytes 1769476
  163.2 30.8 %copy-start.6 = (f32[768]{0:T(1024)S(1)}, f32[768]{0:T(1024)}, u32[]{:S(2)}) copy-start(f32[768]{0:T(1024)} %param.13) | copy-start | bytes 9220
  164.4 16.9 %collective-permute-start.13 = (bf16[384,768]{1,0:T(8,128)(2,1)}, bf16[384,768]{1,0:T(8,128)(2,1)}, u32[]{:S(2)}, u32[]{:S(2)}) collective-permute-start(bf16[384,768]{1,0:T(8,128)(2,1)} %get-tuple-element.39), channel_id=1, source_target_pairs={{0,2},{1,3},{2,0},{3,1},{4,6},{5,7},{6,4},{7,5},{8,10},{9,11},{10,... | collective-permute-start | bytes 1769480 | tf_op jit(solution)/shard_map/ppermute | solution.py:263
  166.9 27.0 %collective-permute-start.14 = (bf16[384,768]{1,0:T(8,128)(2,1)}, bf16[384,768]{1,0:T(8,128)(2,1)}, u32[]{:S(2)}, u32[]{:S(2)}) collective-permute-start(bf16[384,768]{1,0:T(8,128)(2,1)} %get-tuple-element.41), channel_id=1, source_target_pairs={{0,1},{1,2},{2,3},{3,0},{4,5},{5,6},{6,7},{7,4},{8,9},{9,10},{10,1... | collective-permute-start | bytes 1769480 | tf_op jit(solution)/shard_map/ppermute | solution.py:263
  167.5 26.4 %collective-permute-start.15 = (bf16[384,768]{1,0:T(8,128)(2,1)}, bf16[384,768]{1,0:T(8,128)(2,1)}, u32[]{:S(2)}, u32[]{:S(2)}) collective-permute-start(bf16[384,768]{1,0:T(8,128)(2,1)} %get-tuple-element.40), channel_id=1, source_target_pairs={{0,3},{1,0},{2,1},{3,2},{4,7},{5,4},{6,5},{7,6},{8,11},{9,8},{10,9... | collective-permute-start | bytes 1769480 | tf_op jit(solution)/shard_map/ppermute | solution.py:263

commit v13 on v11

--- a/solution.py
+++ b/solution.py
@@ -28,6 +28,19 @@
     return [(i, i + step) for i in range(devices) if 0 <= i + step < devices]
 
 
+def diagonal_pairs(tm_size, height_size, step, rise):
+    pairs = []
+    for t in range(tm_size):
+        if not 0 <= t + step < tm_size:
+            continue
+        for h in range(1, height_size - 1, 2):
+            if rise:
+                pairs.append((t * height_size + h, (t + step) * height_size + h + 1))
+            else:
+                pairs.append((t * height_size + h + 1, (t + step) * height_size + h))
+    return pairs
+
+
 def text_halves(text_kv):
     half_width = text_kv.shape[2] // 2
     half = lax.axis_index("height") % 2
@@ -51,7 +64,14 @@
     return jnp.where(half == 0, low_first, high_first)
 
 
-def make_kernel(blocks, has_text, has_state, final):
+def load(tile_ref, part):
+    main, extra = tile_ref
+    if extra is None:
+        return main[part]
+    return main[part] + extra[part]
+
+
+def make_kernel(blocks, extras, has_text, has_state, final):
     count = len(blocks)
 
     def kernel(reach_ref, q_ref, *rest):
@@ -59,6 +79,9 @@
         text_ref = rest.pop(0) if has_text else None
         tile_refs = rest[:count]
         rest = rest[count:]
+        extra_refs = rest[:len(extras)]
+        rest = rest[len(extras):]
+        extra_of = dict(zip(extras, extra_refs))
         bias_ref = rest.pop(0)
         if has_state:
             m_in, l_in, acc_in = rest[:3]
@@ -97,13 +120,14 @@
         reach_h = reach_ref[head, 1]
         groups = {}
         for tile_ref, b in zip(tile_refs, blocks):
+            tile_ref = (tile_ref, extra_of.get(b))
             groups.setdefault((abs(b // 3 - 1), abs(b % 3 - 1)), []).append((tile_ref, b))
         for (off_t, off_h), members in groups.items():
 
             def block(members=members):
                 scores = []
                 for tile_ref, b in members:
-                    s = lax.dot_general(q, tile_ref[0], dims, preferred_element_type=jnp.float32)
+                    s = lax.dot_general(q, load(tile_ref, 0), dims, preferred_element_type=jnp.float32)
                     scores.append(s * scale + bias_ref[b])
                 m_old = m_ref[...]
                 m_new = m_old
@@ -116,7 +140,7 @@
                     p = jnp.exp(s - m_new)
                     total = total + jnp.sum(p, axis=1, keepdims=True)
                     acc = acc + jnp.dot(
-                        p.astype(jnp.bfloat16), tile_ref[1], preferred_element_type=jnp.float32
+                        p.astype(jnp.bfloat16), load(tile_ref, 1), preferred_element_type=jnp.float32
                     )
                 l_ref[...] = total
                 acc_ref[...] = acc
@@ -138,7 +162,7 @@
     return kernel
 
 
-def attend(reach, queries, text, tiles, bias, state=None, qvalid=None):
+def attend(reach, queries, text, tiles, bias, state=None, qvalid=None, extra=None):
     tile_len, col_width = queries.shape
     heads = col_width // HD
     blocks = [b for _, _, b in tiles]
@@ -147,7 +171,7 @@
     if text is not None:
         specs.append(pl.BlockSpec((2, text.shape[1], HD), lambda h, r: (0, 0, h)))
         args.append(text)
-    for array, index, _ in tiles:
+    def add_tile(array, index):
         if index is None:
             specs.append(pl.BlockSpec((2, tile_len, HD), lambda h, r: (0, 0, h)))
         else:
@@ -155,6 +179,12 @@
                 pl.BlockSpec((None, 2, tile_len, HD), lambda h, r, i=index: (i, 0, 0, h))
             )
         args.append(array)
+
+    for array, index, _ in tiles:
+        add_tile(array, index)
+    extras = [b for b in blocks if b in (extra or {})]
+    for b in extras:
+        add_tile(*extra[b])
     specs.append(pl.BlockSpec(bias.shape, lambda h, r: (0, 0, 0)))
     args.append(bias)
     row_spec = pl.BlockSpec((None, tile_len, 1), lambda h, r: (h, 0, 0))
@@ -183,7 +213,7 @@
             pltpu.VMEM((tile_len, HD), jnp.float32),
         ],
     )
-    kernel = make_kernel(blocks, text is not None, state is not None, final)
+    kernel = make_kernel(blocks, extras, text is not None, state is not None, final)
     return pl.pallas_call(kernel, grid_spec=grid_spec, out_shape=out_shape)(reach, *args)
 
 
@@ -218,14 +248,21 @@
     queries = image_q[0, 0]
     near = [(own, None, 4), (h_before, None, 3), (h_after, None, 5)]
     state = attend(head_reach, queries, None, near, bias)
-    t_before, t_after, state = lax.optimization_barrier((t_before, t_after, state))
+    t_before, t_after, sent, state = lax.optimization_barrier((t_before, t_after, sent, state))
     time_pair = jnp.stack([t_before, t_after])
-    c_before = lax.ppermute(time_pair, "height", shift_pairs(height_size, 1))
-    c_after = lax.ppermute(time_pair, "height", shift_pairs(height_size, -1))
+    even = list(range(0, height_size - 1, 2))
+    odd = list(range(1, height_size - 1, 2))
+    near_before = lax.ppermute(time_pair, "height", [(i, i + 1) for i in even])
+    near_after = lax.ppermute(time_pair, "height", [(i + 1, i) for i in even])
+    cross_before = lax.ppermute(t_before, "height", [(i, i + 1) for i in odd])
+    cross_after = lax.ppermute(t_before, "height", [(i + 1, i) for i in odd])
+    diag_down = lax.ppermute(sent, ("tm", "height"), diagonal_pairs(tm_size, height_size, -1, True))
+    diag_up = lax.ppermute(sent, ("tm", "height"), diagonal_pairs(tm_size, height_size, -1, False))
     across = [(t_before, None, 1), (t_after, None, 7)]
     state = attend(head_reach, queries, text, across, bias, state)
-    corners = [(c_before, 0, 0), (c_after, 0, 2), (c_before, 1, 6), (c_after, 1, 8)]
-    attended = attend(head_reach, queries, None, corners, bias, state, qvalid)
+    corners = [(near_before, 0, 0), (near_after, 0, 2), (near_before, 1, 6), (near_after, 1, 8)]
+    extra = {0: (cross_before, None), 2: (cross_after, None), 6: (diag_down, None), 8: (diag_up, None)}
+    attended = attend(head_reach, queries, None, corners, bias, state, qvalid, extra)
 
     mp_index = lax.axis_index("mp")
     chunk = out_weight.shape[1] // mp_size

time: 174 us -> 183 us (1.052); the launches traced: 174 us -> 180 us
  starting transfers between devices: 35.3 us -> 41.7 us
  waiting for transfers between devices: 85.4 us -> 82 us
  Pallas kernels: 32.2 us -> 35.5 us
  local copies, waits for them, and re-layouts: 8.56 us -> 6.71 us
    ppermute x2 -> x6, waiting for transfers between devices: 10.8 us -> 1.69 us  [the longest x2 1.68 us: per_device(): lax.ppermute(sent, ('tm', 'height'), diagonal_pairs(tm_size, height_size,...]
    ppermute x2 -> x6, starting transfers between devices: 5.55 us -> 13.7 us  [the longest x2 6.65 us: per_device(): lax.ppermute(sent, ('tm', 'height'), diagonal_pairs(tm_size, height_size,...]
    ppermute x3, waiting for transfers between devices: 17.2 us -> 23.2 us  [per_device(): received.append(lax.ppermute(part, 'mp', pairs))]
    pallas_call x3, Pallas kernels: 32.2 us -> 35.5 us  [attend(): pl.pallas_call(kernel, grid_spec=grid_spec, out_shape=out_shape)]
    unnamed x21 -> x17, local copies, waits for them, and re-layouts: 4.76 us -> 2.96 us
  transfers between devices with their start and end apart: 14 -> 18, of which waited for: 11 -> 9; matrix products, arithmetic and copies ran while one was open for 4% -> 5% of each run, Pallas kernels for 13% -> 13%
where the time goes in v13:
time: 183 us; the launch traced here: 180 us
  waiting for transfers between devices  82 us (45%)
  starting transfers between devices  41.7 us (23%)
  Pallas kernels  35.5 us (19%)
  other arithmetic  8.85 us (5%)
  local copies, waits for them, and re-layouts  6.71 us (4%)
  matrix products  4.52 us (2%)
    pallas_call x3, Pallas kernels, attend(): pl.pallas_call(kernel, grid_spec=grid_spec, out_shape=out_shape)  35.5 us
    ppermute x1, waiting for transfers between devices, per_device(): t_before = lax.ppermute(sent, 'tm', shift_pairs(tm_size, 1))  34.7 us
    ppermute x3, waiting for transfers between devices, per_device(): received.append(lax.ppermute(part, 'mp', pairs))  23.2 us
    ppermute x4, waiting for transfers between devices, exchange(): other = lax.ppermute(block, 'tm', [(i, i ^ step) for i in range(devices)])  18.7 us
    ppermute x4, starting transfers between devices, exchange(): other = lax.ppermute(block, 'tm', [(i, i ^ step) for i in range(devices)])  7.11 us
    ppermute x2, starting transfers between devices, per_device(): lax.ppermute(sent, ('tm', 'height'), diagonal_pairs(tm_size, height_size,...  6.65 us
    ppermute x3, starting transfers between devices, per_device(): received.append(lax.ppermute(part, 'mp', pairs))  5.01 us
    ppermute x1, starting transfers between devices, per_device(): h_before = lax.ppermute(own, 'height', shift_pairs(height_size, 1))  4.92 us
  transfers between devices with their start and end apart: 18, of which 9 were waited for; matrix products, arithmetic and copies ran while one was open for 5% of the time, Pallas kernels for 13%

profile of v13, /device:TPU:97, one launch (start us, length us, event | category | flops | bytes accessed | tf_op | source)
XLA Modules:
  0.0 179.6 jit_solution(16391821953874713891)
XLA Ops:
  0.0 0.0 copy-start
  0.0 0.8 copy-done
  0.8 2.7 %collective-permute-start = (bf16[2,16,384]{2,1,0:T(8,128)(2,1)S(1)}, bf16[2,16,384]{2,1,0:T(8,128)(2,1)S(1)}, u32[]{:S(2)}, u32[]{:S(2)}) collective-permute-start(bf16[2,16,384]{2,1,0:T(8,128)(2,1)S(1)} %constant_dynamic-slice_fusion.3), channel_id=1, source_target_pairs={{0,16},{16,0},{32,48},{48,32},{64,80},{80,64},{96,112},{112,96},{1... | collective-permute-start | bytes 73736 | tf_op jit(solution)/shard_map/ppermute | solution.py:52
  3.5 1.4 collective-permute-done
  5.0 0.1 collective-permute-start.1
  5.1 4.9 %collective-permute-start.5 = (bf16[2,384,768]{2,1,0:T(8,128)(2,1)}, bf16[2,384,768]{2,1,0:T(8,128)(2,1)S(1)}, u32[]{:S(2)}, u32[]{:S(2)}) collective-permute-start(bf16[2,384,768]{2,1,0:T(8,128)(2,1)} %bitcast.2.rest_0_), channel_id=1, source_target_pairs={{0,4},{4,8},{8,12},{1,5},{5,9},{9,13},{2,6},{6,10},{10,14},{3,7},{... | collective-permute-start | bytes 3538952 | tf_op jit(solution)/shard_map/ppermute | solution.py:228
  10.0 1.9 %collective-permute-start.6 = (bf16[2,384,768]{2,1,0:T(8,128)(2,1)}, bf16[2,384,768]{2,1,0:T(8,128)(2,1)}, u32[]{:S(2)}, u32[]{:S(2)}) collective-permute-start(bf16[2,384,768]{2,1,0:T(8,128)(2,1)} %bitcast.2.rest_0_), channel_id=1, source_target_pairs={{4,0},{8,4},{12,8},{5,1},{9,5},{13,9},{6,2},{10,6},{14,10},{7,3},{... | collective-permute-start | bytes 3538952 | tf_op jit(solution)/shard_map/ppermute | solution.py:229
  12.0 0.0 collective-permute-done.1
  12.0 0.1 collective-permute-start.2
  12.1 7.1 %collective-permute-done.2 = bf16[2,64,384]{2,1,0:T(8,128)(2,1)S(1)} collective-permute-done((bf16[2,64,384]{2,1,0:T(8,128)(2,1)S(1)}, bf16[2,64,384]{2,1,0:T(8,128)(2,1)S(1)}, u32[]{:S(2)}, u32[]{:S(2)}) %collective-permute-start.2) | collective-permute-done | bytes 98336 | tf_op jit(solution)/shard_map/ppermute | solution.py:52
  19.3 4.2 %collective-permute-start.3 = (bf16[2,128,384]{2,1,0:T(8,128)(2,1)S(1)}, bf16[2,128,384]{2,1,0:T(8,128)(2,1)S(1)}, u32[]{:S(2)}, u32[]{:S(2)}) collective-permute-start(bf16[2,128,384]{2,1,0:T(8,128)(2,1)S(1)} %maximum_select_fusion.2), channel_id=1, source_target_pairs={{0,128},{16,144},{32,160},{48,176},{64,192},{80,208},{96,224},{112... | collective-permute-start | bytes 589832 | tf_op jit(solution)/shard_map/ppermute | solution.py:52
  23.5 10.1 %collective-permute-done.3 = bf16[2,128,384]{2,1,0:T(8,128)(2,1)S(1)} collective-permute-done((bf16[2,128,384]{2,1,0:T(8,128)(2,1)S(1)}, bf16[2,128,384]{2,1,0:T(8,128)(2,1)S(1)}, u32[]{:S(2)}, u32[]{:S(2)}) %collective-permute-start.3) | collective-permute-done | bytes 196640 | tf_op jit(solution)/shard_map/ppermute | solution.py:52
  33.6 0.1 maximum_select_fusion.1
  33.7 1.4 collective-permute-start.4
  35.1 1.3 collective-permute-done.4
  36.4 1.1 maximum_select_fusion.rest_0_
  37.5 0.0 collective-permute-done.5.rest_1_
  37.5 0.0 collective-permute-done.6.rest_2_
  37.5 4.7 %collective-permute-start.7 = (bf16[2,384,768]{2,1,0:T(8,128)(2,1)}, bf16[2,384,768]{2,1,0:T(8,128)(2,1)}, u32[]{:S(2)}, u32[]{:S(2)}) collective-permute-start(bf16[2,384,768]{2,1,0:T(8,128)(2,1)} %bitcast.2.rest_0_), channel_id=1, source_target_pairs={{0,16},{16,32},{32,48},{48,64},{64,80},{80,96},{96,112},{112,128},... | collective-permute-start | bytes 3538952 | tf_op jit(solution)/shard_map/ppermute | solution.py:237
  42.2 3.0 %collective-permute-start.8 = (bf16[2,384,768]{2,1,0:T(8,128)(2,1)}, bf16[2,384,768]{2,1,0:T(8,128)(2,1)S(1)}, u32[]{:S(2)}, u32[]{:S(2)}) collective-permute-start(bf16[2,384,768]{2,1,0:T(8,128)(2,1)} %bitcast.2.rest_0_), channel_id=1, source_target_pairs={{16,0},{32,16},{48,32},{64,48},{80,64},{96,80},{112,96},{128,112},... | collective-permute-start | bytes 3538952 | tf_op jit(solution)/shard_map/ppermute | solution.py:238
  45.2 0.0 copy-done.6
  45.2 0.1 pad_dynamic-slice_fusion
  45.3 0.1 copy.16
  45.4 0.1 lt.111
  45.5 0.1 copy.17
  45.6 0.1 lt.116
  45.7 0.0 copy-done.7
  45.7 0.7 copy.22.reach_ref
  46.4 0.7 and_select_fusion.rest_3_.rest_8_
  47.1 0.0 copy-done.3
  47.1 11.0 %shard_map.82 = (f32[6,384,1]{2,1,0:T(8,128)}, f32[6,384,1]{2,1,0:T(8,128)}, f32[384,768]{1,0:T(8,128)}) custom-call(s32[6,2]{1,0:T(8,128)} %copy.22.reach_ref, bf16[384,768]{1,0:T(8,128)(2,1)} %bitcast.15, bf16[2,384,768]{2,1,0:T(8,128)(2,1)} %bitcast.2.rest_0_, bf16[2,384,768]{2,1,0:T(8,128)(2,1)} %copy-done.3, ...), custom_call_target="tpu_custom_call" | custom-call | tf_op jit(solution)/shard_map/pallas_call | solution.py:217
  58.1 34.7 %collective-permute-done.7.rest_1_ = bf16[2,384,768]{2,1,0:T(8,128)(2,1)} collective-permute-done((bf16[2,384,768]{2,1,0:T(8,128)(2,1)}, bf16[2,384,768]{2,1,0:T(8,128)(2,1)}, u32[]{:S(2)}, u32[]{:S(2)}) %collective-permute-start.7) | collective-permute-done | bytes 1179680 | tf_op jit(solution)/shard_map/ppermute | solution.py:237
  92.7 2.5 %collective-permute-done.8.rest_2_ = bf16[2,384,768]{2,1,0:T(8,128)(2,1)S(1)} collective-permute-done((bf16[2,384,768]{2,1,0:T(8,128)(2,1)}, bf16[2,384,768]{2,1,0:T(8,128)(2,1)S(1)}, u32[]{:S(2)}, u32[]{:S(2)}) %collective-permute-start.8) | collective-permute-done | bytes 1179680 | tf_op jit(solution)/shard_map/ppermute | solution.py:238
  95.2 3.0 %collective-permute-start.11 = (bf16[2,384,768]{2,1,0:T(8,128)(2,1)}, bf16[2,384,768]{2,1,0:T(8,128)(2,1)}, u32[]{:S(2)}, u32[]{:S(2)}) collective-permute-start(bf16[2,384,768]{2,1,0:T(8,128)(2,1)} %collective-permute-done.7.rest_1_), channel_id=1, source_target_pairs={{4,8},{5,9},{6,10},{7,11},{20,24},{21,25},{22,26},{23,27},{36,40},... | collective-permute-start | bytes 3538952 | tf_op jit(solution)/shard_map/ppermute | solution.py:257
  98.2 2.9 %pad_maximum_fusion = bf16[2,2,384,768]{3,2,1,0:T(8,128)(2,1)} fusion(bf16[1,2,384,768]{3,2,1,0:T(8,128)(2,1)S(1)} %bitcast.18, bf16[1,2,384,768]{3,2,1,0:T(8,128)(2,1)} %bitcast.3), kind=kLoop, calls=%fused_computation.1 | loop fusion | flops 1179648 | bytes 4718592 | tf_op jit(solution)/shard_map/stack | solution.py:252
  101.2 1.4 collective-permute-start.10
  102.6 1.3 collective-permute-start.9
  103.9 1.3 collective-permute-start.12
  105.2 5.4 %collective-permute-start.13 = (bf16[2,384,768]{2,1,0:T(8,128)(2,1)}, bf16[2,384,768]{2,1,0:T(8,128)(2,1)}, u32[]{:S(2)}, u32[]{:S(2)}) collective-permute-start(bf16[2,384,768]{2,1,0:T(8,128)(2,1)} %bitcast.2.rest_0_), channel_id=1, source_target_pairs={{20,8},{36,24},{52,40},{68,56},{84,72},{100,88},{116,104},{132,120... | collective-permute-start | bytes 3538952 | tf_op jit(solution)/shard_map/ppermute | solution.py:259
  110.6 0.0 collective-permute-done.11.rest_4_
  110.6 1.3 collective-permute-start.14
  111.9 0.6 slice.12
  112.5 0.6 slice.13
  113.1 1.3 fusion.8
  114.4 0.8 copy.23.rest_12_
  115.2 12.7 %shard_map.83 = (f32[6,384,1]{2,1,0:T(8,128)}, f32[6,384,1]{2,1,0:T(8,128)}, f32[384,768]{1,0:T(8,128)}) custom-call(s32[6,2]{1,0:T(8,128)} %copy.22.reach_ref, bf16[384,768]{1,0:T(8,128)(2,1)} %bitcast.16, bf16[2,256,768]{2,1,0:T(8,128)(2,1)} %maximum_select_fusion.rest_0_, bf16[2,384,768]{2,1,0:T(8,128)(2,1)} %collective-permute-done.7.rest_1_, ...), custom_call_target="tpu_custom_call" | custom-call | tf_op jit(solution)/shard_map/pallas_call | solution.py:217
  127.9 0.0 collective-permute-done.12.rest_5_
  127.9 0.0 collective-permute-done.13.rest_6_
  128.0 1.7 collective-permute-done.14.rest_7_
  129.6 0.0 collective-permute-done.10.rest_1_.rest_3_
  129.6 0.0 collective-permute-done.9.rest_0_.rest_2_
  129.6 1.4 copy-done.1
  131.1 11.8 %shard_map.84 = bf16[384,768]{1,0:T(8,128)(2,1)} custom-call(s32[6,2]{1,0:T(8,128)} %copy.22.reach_ref, bf16[384,768]{1,0:T(8,128)(2,1)} %bitcast.17, bf16[2,2,384,768]{3,2,1,0:T(8,128)(2,1)} %collective-permute-done.9.rest_0_.rest_2_, bf16[2,2,384,768]{3,2,1,0:T(8,128)(2,1)} %copy-done.1, bf16[2,2,384,768]{3,2,1,0:T(8,128)(2,1)} %collective-permute-done.9.rest_0_.rest_2_, ...), custom_call_target="tpu_custom_call" | custom-call | tf_op jit(solution)/shard_map/pallas_call | solution.py:217
  142.9 4.5 %convolution_convert_fusion = bf16[384,3072]{1,0:T(8,128)(2,1)S(1)} fusion(bf16[384,768]{1,0:T(8,128)(2,1)} %shard_map.84, bf16[768,3072]{1,0:T(8,128)(2,1)} %param.12), kind=kOutput, calls=%fused_computation | convolution fusion | flops 1813118976 | bytes 7667712 | tf_op jit(solution)/shard_map/dot_general | solution.py:269
  147.4 0.0 copy-start.4
  147.4 0.0 copy-start.5
  147.5 1.3 constant_dynamic-slice_fusion.2
  148.7 0.0 collective-permute-start.15
  148.7 2.6 %collective-permute-start.16 = (bf16[384,768]{1,0:T(8,128)(2,1)}, bf16[384,768]{1,0:T(8,128)(2,1)}, u32[]{:S(2)}, u32[]{:S(2)}) collective-permute-start(bf16[384,768]{1,0:T(8,128)(2,1)} %get-tuple-element.39), channel_id=1, source_target_pairs={{0,1},{1,2},{2,3},{3,0},{4,5},{5,6},{6,7},{7,4},{8,9},{9,10},{10,1... | collective-permute-start | bytes 1769480 | tf_op jit(solution)/shard_map/ppermute | solution.py:276
  151.4 2.4 %collective-permute-start.17 = (bf16[384,768]{1,0:T(8,128)(2,1)}, bf16[384,768]{1,0:T(8,128)(2,1)}, u32[]{:S(2)}, u32[]{:S(2)}) collective-permute-start(bf16[384,768]{1,0:T(8,128)(2,1)} %get-tuple-element.38), channel_id=1, source_target_pairs={{0,3},{1,0},{2,1},{3,2},{4,7},{5,4},{6,5},{7,6},{8,11},{9,8},{10,9... | collective-permute-start | bytes 1769480 | tf_op jit(solution)/shard_map/ppermute | solution.py:276
  153.8 12.0 %collective-permute-done.15 = bf16[384,768]{1,0:T(8,128)(2,1)} collective-permute-done((bf16[384,768]{1,0:T(8,128)(2,1)}, bf16[384,768]{1,0:T(8,128)(2,1)}, u32[]{:S(2)}, u32[]{:S(2)}) %collective-permute-start.15) | collective-permute-done | bytes 589856 | tf_op jit(solution)/shard_map/ppermute | solution.py:276
  165.7 11.2 %collective-permute-done.16 = bf16[384,768]{1,0:T(8,128)(2,1)} collective-permute-done((bf16[384,768]{1,0:T(8,128)(2,1)}, bf16[384,768]{1,0:T(8,128)(2,1)}, u32[]{:S(2)}, u32[]{:S(2)}) %collective-permute-start.16) | collective-permute-done | bytes 589856 | tf_op jit(solution)/shard_map/ppermute | solution.py:276
  176.9 0.0 collective-permute-done.17
  176.9 2.6 %fusion.1 = bf16[1,1,384,768]{3,2,1,0:T(8,128)(2,1)} fusion(bf16[384,768]{1,0:T(8,128)(2,1)} %collective-permute-done.17, bf16[384,768]{1,0:T(8,128)(2,1)} %collective-permute-done.16, bf16[384,768]{1,0:T(8,128)(2,1)} %collective-permute-done.15, bf16[1,1,384,768]{3,2,1,0:T(8,128)(2,1)S(1)} %copy-done.4, bf16[384,3072]{1,0:T(8,128)(2,1)S(1)} %convolution_convert_fusion, ...), kind=kLoop, calls=%fused_computation.5 | loop fusion | flops 3244032 | bytes 3542020 | tf_op jit(solution)/shard_map/broadcast_in_dim | solution.py:281
  (13 shorter events, 0.1 us)
Async XLA Ops:
  0.0 0.8 copy-start
  0.8 4.2 %collective-permute-start = (bf16[2,16,384]{2,1,0:T(8,128)(2,1)S(1)}, bf16[2,16,384]{2,1,0:T(8,128)(2,1)S(1)}, u32[]{:S(2)}, u32[]{:S(2)}) collective-permute-start(bf16[2,16,384]{2,1,0:T(8,128)(2,1)S(1)} %constant_dynamic-slice_fusion.3), channel_id=1, source_target_pairs={{0,16},{16,0},{32,48},{48,32},{64,80},{80,64},{96,112},{112,96},{1... | collective-permute-start | bytes 73736 | tf_op jit(solution)/shard_map/ppermute | solution.py:52
  5.0 7.0 %collective-permute-start.1 = (bf16[2,32,384]{2,1,0:T(8,128)(2,1)S(1)}, bf16[2,32,384]{2,1,0:T(8,128)(2,1)S(1)}, u32[]{:S(2)}, u32[]{:S(2)}) collective-permute-start(bf16[2,32,384]{2,1,0:T(8,128)(2,1)S(1)} %maximum_select_fusion.4), channel_id=1, source_target_pairs={{0,32},{16,48},{32,0},{48,16},{64,96},{80,112},{96,64},{112,80},{1... | collective-permute-start | bytes 147464 | tf_op jit(solution)/shard_map/ppermute | solution.py:52
  5.1 32.4 %collective-permute-start.5 = (bf16[2,384,768]{2,1,0:T(8,128)(2,1)}, bf16[2,384,768]{2,1,0:T(8,128)(2,1)S(1)}, u32[]{:S(2)}, u32[]{:S(2)}) collective-permute-start(bf16[2,384,768]{2,1,0:T(8,128)(2,1)} %bitcast.2.rest_0_), channel_id=1, source_target_pairs={{0,4},{4,8},{8,12},{1,5},{5,9},{9,13},{2,6},{6,10},{10,14},{3,7},{... | collective-permute-start | bytes 3538952 | tf_op jit(solution)/shard_map/ppermute | solution.py:228
  10.0 27.5 %collective-permute-start.6 = (bf16[2,384,768]{2,1,0:T(8,128)(2,1)}, bf16[2,384,768]{2,1,0:T(8,128)(2,1)}, u32[]{:S(2)}, u32[]{:S(2)}) collective-permute-start(bf16[2,384,768]{2,1,0:T(8,128)(2,1)} %bitcast.2.rest_0_), channel_id=1, source_target_pairs={{4,0},{8,4},{12,8},{5,1},{9,5},{13,9},{6,2},{10,6},{14,10},{7,3},{... | collective-permute-start | bytes 3538952 | tf_op jit(solution)/shard_map/ppermute | solution.py:229
  12.0 7.2 %collective-permute-start.2 = (bf16[2,64,384]{2,1,0:T(8,128)(2,1)S(1)}, bf16[2,64,384]{2,1,0:T(8,128)(2,1)S(1)}, u32[]{:S(2)}, u32[]{:S(2)}) collective-permute-start(bf16[2,64,384]{2,1,0:T(8,128)(2,1)S(1)} %maximum_select_fusion.3), channel_id=1, source_target_pairs={{0,64},{16,80},{32,96},{48,112},{64,0},{80,16},{96,32},{112,48},{1... | collective-permute-start | bytes 294920 | tf_op jit(solution)/shard_map/ppermute | solution.py:52
  19.3 14.3 %collective-permute-start.3 = (bf16[2,128,384]{2,1,0:T(8,128)(2,1)S(1)}, bf16[2,128,384]{2,1,0:T(8,128)(2,1)S(1)}, u32[]{:S(2)}, u32[]{:S(2)}) collective-permute-start(bf16[2,128,384]{2,1,0:T(8,128)(2,1)S(1)} %maximum_select_fusion.2), channel_id=1, source_target_pairs={{0,128},{16,144},{32,160},{48,176},{64,192},{80,208},{96,224},{112... | collective-permute-start | bytes 589832 | tf_op jit(solution)/shard_map/ppermute | solution.py:52
  23.5 21.8 %copy-start.6 = (s32[2,16,4]{1,2,0:T(4,128)S(1)}, s32[2,16,4]{1,2,0:T(4,128)}, u32[]{:S(2)}) copy-start(s32[2,16,4]{1,2,0:T(4,128)} %param.15) | copy-start | bytes 1540
  23.5 22.2 %copy-start.7 = (s32[6,2]{0,1:T(2,128)S(1)}, s32[6,2]{0,1:T(2,128)}, u32[]{:S(2)}) copy-start(s32[6,2]{0,1:T(2,128)} %param.14) | copy-start | bytes 148
  33.7 2.7 %collective-permute-start.4 = (bf16[2,256,384]{2,1,0:T(8,128)(2,1)S(1)}, bf16[2,256,384]{2,1,0:T(8,128)(2,1)S(1)}, u32[]{:S(2)}, u32[]{:S(2)}) collective-permute-start(bf16[2,256,384]{2,1,0:T(8,128)(2,1)S(1)} %maximum_select_fusion.1), channel_id=1, source_target_pairs={{0,4},{4,0},{8,12},{12,8},{1,5},{5,1},{9,13},{13,9},{2,6},{6,2},{1... | collective-permute-start | bytes 1179656 | tf_op jit(solution)/shard_map/ppermute | solution.py:61
  37.5 9.6 %copy-start.3 = (bf16[2,384,768]{2,1,0:T(8,128)(2,1)}, bf16[2,384,768]{2,1,0:T(8,128)(2,1)S(1)}, u32[]{:S(2)}) copy-start(bf16[2,384,768]{2,1,0:T(8,128)(2,1)S(1)} %collective-permute-done.5.rest_1_) | copy-start | bytes 3538948
  37.5 55.2 %collective-permute-start.7 = (bf16[2,384,768]{2,1,0:T(8,128)(2,1)}, bf16[2,384,768]{2,1,0:T(8,128)(2,1)}, u32[]{:S(2)}, u32[]{:S(2)}) collective-permute-start(bf16[2,384,768]{2,1,0:T(8,128)(2,1)} %bitcast.2.rest_0_), channel_id=1, source_target_pairs={{0,16},{16,32},{32,48},{48,64},{64,80},{80,96},{96,112},{112,128},... | collective-permute-start | bytes 3538952 | tf_op jit(solution)/shard_map/ppermute | solution.py:237
  42.2 53.0 %collective-permute-start.8 = (bf16[2,384,768]{2,1,0:T(8,128)(2,1)}, bf16[2,384,768]{2,1,0:T(8,128)(2,1)S(1)}, u32[]{:S(2)}, u32[]{:S(2)}) collective-permute-start(bf16[2,384,768]{2,1,0:T(8,128)(2,1)} %bitcast.2.rest_0_), channel_id=1, source_target_pairs={{16,0},{32,16},{48,32},{64,48},{80,64},{96,80},{112,96},{128,112},... | collective-permute-start | bytes 3538952 | tf_op jit(solution)/shard_map/ppermute | solution.py:238
  95.2 3.0 %copy-start.2 = (bf16[2,384,768]{2,1,0:T(8,128)(2,1)}, bf16[2,384,768]{2,1,0:T(8,128)(2,1)S(1)}, u32[]{:S(2)}) copy-start(bf16[2,384,768]{2,1,0:T(8,128)(2,1)S(1)} %collective-permute-done.8.rest_2_) | copy-start | bytes 3538948
  95.2 15.4 %collective-permute-start.11 = (bf16[2,384,768]{2,1,0:T(8,128)(2,1)}, bf16[2,384,768]{2,1,0:T(8,128)(2,1)}, u32[]{:S(2)}, u32[]{:S(2)}) collective-permute-start(bf16[2,384,768]{2,1,0:T(8,128)(2,1)} %collective-permute-done.7.rest_1_), channel_id=1, source_target_pairs={{4,8},{5,9},{6,10},{7,11},{20,24},{21,25},{22,26},{23,27},{36,40},... | collective-permute-start | bytes 3538952 | tf_op jit(solution)/shard_map/ppermute | solution.py:257
  101.2 28.5 %collective-permute-start.10 = (bf16[2,2,384,768]{3,2,1,0:T(8,128)(2,1)}, bf16[2,2,384,768]{3,2,1,0:T(8,128)(2,1)S(1)}, u32[]{:S(2)}, u32[]{:S(2)}) collective-permute-start(bf16[2,2,384,768]{3,2,1,0:T(8,128)(2,1)} %pad_maximum_fusion), channel_id=1, source_target_pairs={{4,0},{12,8},{5,1},{13,9},{6,2},{14,10},{7,3},{15,11},{20,16},{28,... | collective-permute-start | bytes 7077896 | tf_op jit(solution)/shard_map/ppermute | solution.py:256
  102.6 27.0 %collective-permute-start.9 = (bf16[2,2,384,768]{3,2,1,0:T(8,128)(2,1)}, bf16[2,2,384,768]{3,2,1,0:T(8,128)(2,1)}, u32[]{:S(2)}, u32[]{:S(2)}) collective-permute-start(bf16[2,2,384,768]{3,2,1,0:T(8,128)(2,1)} %pad_maximum_fusion), channel_id=1, source_target_pairs={{0,4},{8,12},{1,5},{9,13},{2,6},{10,14},{3,7},{11,15},{16,20},{24,... | collective-permute-start | bytes 7077896 | tf_op jit(solution)/shard_map/ppermute | solution.py:255
  103.9 24.0 %collective-permute-start.12 = (bf16[2,384,768]{2,1,0:T(8,128)(2,1)}, bf16[2,384,768]{2,1,0:T(8,128)(2,1)}, u32[]{:S(2)}, u32[]{:S(2)}) collective-permute-start(bf16[2,384,768]{2,1,0:T(8,128)(2,1)} %collective-permute-done.7.rest_1_), channel_id=1, source_target_pairs={{8,4},{9,5},{10,6},{11,7},{24,20},{25,21},{26,22},{27,23},{40,36},... | collective-permute-start | bytes 3538952 | tf_op jit(solution)/shard_map/ppermute | solution.py:258
  105.2 22.7 %collective-permute-start.13 = (bf16[2,384,768]{2,1,0:T(8,128)(2,1)}, bf16[2,384,768]{2,1,0:T(8,128)(2,1)}, u32[]{:S(2)}, u32[]{:S(2)}) collective-permute-start(bf16[2,384,768]{2,1,0:T(8,128)(2,1)} %bitcast.2.rest_0_), channel_id=1, source_target_pairs={{20,8},{36,24},{52,40},{68,56},{84,72},{100,88},{116,104},{132,120... | collective-permute-start | bytes 3538952 | tf_op jit(solution)/shard_map/ppermute | solution.py:259
  110.6 19.0 %collective-permute-start.14 = (bf16[2,384,768]{2,1,0:T(8,128)(2,1)}, bf16[2,384,768]{2,1,0:T(8,128)(2,1)}, u32[]{:S(2)}, u32[]{:S(2)}) collective-permute-start(bf16[2,384,768]{2,1,0:T(8,128)(2,1)} %bitcast.2.rest_0_), channel_id=1, source_target_pairs={{24,4},{40,20},{56,36},{72,52},{88,68},{104,84},{120,100},{136,116... | collective-permute-start | bytes 3538952 | tf_op jit(solution)/shard_map/ppermute | solution.py:260
  129.6 1.5 copy-start.1
  147.4 29.5 %copy-start.4 = (bf16[1,1,384,768]{3,2,1,0:T(8,128)(2,1)S(1)}, bf16[1,1,384,768]{3,2,1,0:T(8,128)(2,1)}, u32[]{:S(2)}) copy-start(bf16[1,1,384,768]{3,2,1,0:T(8,128)(2,1)} %param.11) | copy-start | bytes 1769476
  147.4 29.5 %copy-start.5 = (f32[768]{0:T(1024)S(1)}, f32[768]{0:T(1024)}, u32[]{:S(2)}) copy-start(f32[768]{0:T(1024)} %param.13) | copy-start | bytes 9220
  148.7 17.0 %collective-permute-start.15 = (bf16[384,768]{1,0:T(8,128)(2,1)}, bf16[384,768]{1,0:T(8,128)(2,1)}, u32[]{:S(2)}, u32[]{:S(2)}) collective-permute-start(bf16[384,768]{1,0:T(8,128)(2,1)} %get-tuple-element.37), channel_id=1, source_target_pairs={{0,2},{1,3},{2,0},{3,1},{4,6},{5,7},{6,4},{7,5},{8,10},{9,11},{10,... | collective-permute-start | bytes 1769480 | tf_op jit(solution)/shard_map/ppermute | solution.py:276
  148.7 28.2 %collective-permute-start.16 = (bf16[384,768]{1,0:T(8,128)(2,1)}, bf16[384,768]{1,0:T(8,128)(2,1)}, u32[]{:S(2)}, u32[]{:S(2)}) collective-permute-start(bf16[384,768]{1,0:T(8,128)(2,1)} %get-tuple-element.39), channel_id=1, source_target_pairs={{0,1},{1,2},{2,3},{3,0},{4,5},{5,6},{6,7},{7,4},{8,9},{9,10},{10,1... | collective-permute-start | bytes 1769480 | tf_op jit(solution)/shard_map/ppermute | solution.py:276
  151.4 25.6 %collective-permute-start.17 = (bf16[384,768]{1,0:T(8,128)(2,1)}, bf16[384,768]{1,0:T(8,128)(2,1)}, u32[]{:S(2)}, u32[]{:S(2)}) collective-permute-start(bf16[384,768]{1,0:T(8,128)(2,1)} %get-tuple-element.38), channel_id=1, source_target_pairs={{0,3},{1,0},{2,1},{3,2},{4,7},{5,4},{6,5},{7,6},{8,11},{9,8},{10,9... | collective-permute-start | bytes 1769480 | tf_op jit(solution)/shard_map/ppermute | solution.py:276

commit v14 on v11

--- a/solution.py
+++ b/solution.py
@@ -203,9 +203,6 @@
         text_group = exchange(text_group, tm_size, step)
         step *= 2
     text = join_halves(text_group)
-    sent, text, h_before, h_after = lax.optimization_barrier((own, text, h_before, h_after))
-    t_before = lax.ppermute(sent, "tm", shift_pairs(tm_size, 1))
-    t_after = lax.ppermute(sent, "tm", shift_pairs(tm_size, -1))
     time_start = lax.axis_index("tm")
     height_start = lax.axis_index("height")
     zero_index = jnp.int32(0)
@@ -215,6 +212,11 @@
     bias = jnp.where(key_valid, 0.0, NEG).astype(jnp.float32).reshape(9, 1, tile_len)
     qvalid = key_valid[1, 1].astype(jnp.float32).reshape(tile_len, 1)
 
+    sent, text, h_before, h_after, bias, qvalid = lax.optimization_barrier(
+        (own, text, h_before, h_after, bias, qvalid)
+    )
+    t_before = lax.ppermute(sent, "tm", shift_pairs(tm_size, 1))
+    t_after = lax.ppermute(sent, "tm", shift_pairs(tm_size, -1))
     queries = image_q[0, 0]
     near = [(own, None, 4), (h_before, None, 3), (h_after, None, 5)]
     state = attend(head_reach, queries, None, near, bias)

time: 174 us -> 172 us (0.989)
  waiting for transfers between devices: 85.4 us -> 82.7 us
    ppermute x1, waiting for transfers between devices: 9.47 us -> 13 us  [per_device(): c_after = lax.ppermute(time_pair, 'height', shift_pairs(height_size, -1))]
    ppermute x4, waiting for transfers between devices: 18.7 us -> 16.3 us  [exchange(): other = lax.ppermute(block, 'tm', [(i, i ^ step) for i in range(devices)])]
    ppermute x3, waiting for transfers between devices: 17.2 us -> 14.8 us  [per_device(): received.append(lax.ppermute(part, 'mp', pairs))]
    unnamed x21 -> x19, local copies, waits for them, and re-layouts: 4.76 us -> 4.86 us
  transfers between devices with their start and end apart: 14 -> 14, of which waited for: 11 -> 10; matrix products, arithmetic and copies ran while one was open for 4% -> 4% of each run, Pallas kernels for 13% -> 13%
where the time goes in v14:
time: 172 us
  waiting for transfers between devices  82.7 us (48%)
  starting transfers between devices  34.8 us (20%)
  Pallas kernels  32.4 us (19%)
  local copies, waits for them, and re-layouts  9.34 us (5%)
  other arithmetic  7.58 us (4%)
  matrix products  4.52 us (3%)
    ppermute x1, waiting for transfers between devices, per_device(): t_before = lax.ppermute(sent, 'tm', shift_pairs(tm_size, 1))  35.2 us
    pallas_call x3, Pallas kernels, attend(): pl.pallas_call(kernel, grid_spec=grid_spec, out_shape=out_shape)  32.4 us
    ppermute x4, waiting for transfers between devices, exchange(): other = lax.ppermute(block, 'tm', [(i, i ^ step) for i in range(devices)])  16.3 us
    ppermute x3, waiting for transfers between devices, per_device(): received.append(lax.ppermute(part, 'mp', pairs))  14.8 us
    ppermute x1, waiting for transfers between devices, per_device(): c_after = lax.ppermute(time_pair, 'height', shift_pairs(height_size, -1))  13 us
    ppermute x4, starting transfers between devices, exchange(): other = lax.ppermute(block, 'tm', [(i, i ^ step) for i in range(devices)])  7.11 us
    ppermute x3, starting transfers between devices, per_device(): received.append(lax.ppermute(part, 'mp', pairs))  6.31 us
    ppermute x1, starting transfers between devices, per_device(): h_before = lax.ppermute(own, 'height', shift_pairs(height_size, 1))  4.92 us
  transfers between devices with their start and end apart: 14, of which 10 were waited for; matrix products, arithmetic and copies ran while one was open for 4% of the time, Pallas kernels for 13%

profile of v14, /device:TPU:97, one launch (start us, length us, event | category | flops | bytes accessed | tf_op | source)
XLA Modules:
  0.0 171.6 jit_solution(6362455547242029702)
XLA Ops:
  0.0 0.0 copy-start
  0.0 0.8 copy-done
  0.8 2.7 %collective-permute-start = (bf16[2,16,384]{2,1,0:T(8,128)(2,1)S(1)}, bf16[2,16,384]{2,1,0:T(8,128)(2,1)S(1)}, u32[]{:S(2)}, u32[]{:S(2)}) collective-permute-start(bf16[2,16,384]{2,1,0:T(8,128)(2,1)S(1)} %constant_dynamic-slice_fusion.3), channel_id=1, source_target_pairs={{0,16},{16,0},{32,48},{48,32},{64,80},{80,64},{96,112},{112,96},{1... | collective-permute-start | bytes 73736 | tf_op jit(solution)/shard_map/ppermute | solution.py:39
  3.5 1.4 collective-permute-done
  5.0 0.1 collective-permute-start.1
  5.1 4.9 %collective-permute-start.5 = (bf16[2,384,768]{2,1,0:T(8,128)(2,1)}, bf16[2,384,768]{2,1,0:T(8,128)(2,1)S(1)}, u32[]{:S(2)}, u32[]{:S(2)}) collective-permute-start(bf16[2,384,768]{2,1,0:T(8,128)(2,1)} %bitcast.2.rest_0_), channel_id=1, source_target_pairs={{0,4},{4,8},{8,12},{1,5},{5,9},{9,13},{2,6},{6,10},{10,14},{3,7},{... | collective-permute-start | bytes 3538952 | tf_op jit(solution)/shard_map/ppermute | solution.py:198
  10.0 1.9 %collective-permute-start.6 = (bf16[2,384,768]{2,1,0:T(8,128)(2,1)}, bf16[2,384,768]{2,1,0:T(8,128)(2,1)S(1)}, u32[]{:S(2)}, u32[]{:S(2)}) collective-permute-start(bf16[2,384,768]{2,1,0:T(8,128)(2,1)} %bitcast.2.rest_0_), channel_id=1, source_target_pairs={{4,0},{8,4},{12,8},{5,1},{9,5},{13,9},{6,2},{10,6},{14,10},{7,3},{... | collective-permute-start | bytes 3538952 | tf_op jit(solution)/shard_map/ppermute | solution.py:199
  12.0 0.0 collective-permute-done.1
  12.0 0.1 collective-permute-start.2
  12.1 7.1 %collective-permute-done.2 = bf16[2,64,384]{2,1,0:T(8,128)(2,1)S(1)} collective-permute-done((bf16[2,64,384]{2,1,0:T(8,128)(2,1)S(1)}, bf16[2,64,384]{2,1,0:T(8,128)(2,1)S(1)}, u32[]{:S(2)}, u32[]{:S(2)}) %collective-permute-start.2) | collective-permute-done | bytes 98336 | tf_op jit(solution)/shard_map/ppermute | solution.py:39
  19.3 4.2 %collective-permute-start.3 = (bf16[2,128,384]{2,1,0:T(8,128)(2,1)S(1)}, bf16[2,128,384]{2,1,0:T(8,128)(2,1)S(1)}, u32[]{:S(2)}, u32[]{:S(2)}) collective-permute-start(bf16[2,128,384]{2,1,0:T(8,128)(2,1)S(1)} %maximum_select_fusion.2), channel_id=1, source_target_pairs={{0,128},{16,144},{32,160},{48,176},{64,192},{80,208},{96,224},{112... | collective-permute-start | bytes 589832 | tf_op jit(solution)/shard_map/ppermute | solution.py:39
  23.5 0.8 pad_dynamic-slice_fusion
  24.2 0.1 copy.16
  24.3 0.1 lt.111
  24.4 0.1 copy.17
  24.5 0.1 lt.116
  24.6 0.6 slice.12
  25.2 0.6 slice.13
  25.8 0.0 copy-start.8
  25.8 7.7 %collective-permute-done.3 = bf16[2,128,384]{2,1,0:T(8,128)(2,1)S(1)} collective-permute-done((bf16[2,128,384]{2,1,0:T(8,128)(2,1)S(1)}, bf16[2,128,384]{2,1,0:T(8,128)(2,1)S(1)}, u32[]{:S(2)}, u32[]{:S(2)}) %collective-permute-start.3) | collective-permute-done | bytes 196640 | tf_op jit(solution)/shard_map/ppermute | solution.py:39
  33.6 0.1 maximum_select_fusion.1
  33.7 1.4 collective-permute-start.4
  35.1 1.3 fusion.8
  36.4 0.7 and_select_fusion.rest_3_.rest_4_
  37.1 0.0 collective-permute-done.4
  37.1 1.1 maximum_select_fusion.rest_0_
  38.2 0.0 collective-permute-done.5.rest_1_
  38.2 0.0 copy-start.4
  38.2 1.1 copy-done.4
  39.3 0.0 collective-permute-done.6.rest_2_
  39.3 0.0 copy-start.5
  39.3 1.1 copy-done.5
  40.4 4.6 %collective-permute-start.7 = (bf16[2,384,768]{2,1,0:T(8,128)(2,1)}, bf16[2,384,768]{2,1,0:T(8,128)(2,1)S(1)}, u32[]{:S(2)}, u32[]{:S(2)}) collective-permute-start(bf16[2,384,768]{2,1,0:T(8,128)(2,1)} %bitcast.2.rest_0_), channel_id=1, source_target_pairs={{0,16},{16,32},{32,48},{48,64},{64,80},{80,96},{96,112},{112,128},... | collective-permute-start | bytes 3538952 | tf_op jit(solution)/shard_map/ppermute | solution.py:218
  45.0 3.0 %collective-permute-start.8 = (bf16[2,384,768]{2,1,0:T(8,128)(2,1)}, bf16[2,384,768]{2,1,0:T(8,128)(2,1)S(1)}, u32[]{:S(2)}, u32[]{:S(2)}) collective-permute-start(bf16[2,384,768]{2,1,0:T(8,128)(2,1)} %bitcast.2.rest_0_), channel_id=1, source_target_pairs={{16,0},{32,16},{48,32},{64,48},{80,64},{96,80},{112,96},{128,112},... | collective-permute-start | bytes 3538952 | tf_op jit(solution)/shard_map/ppermute | solution.py:219
  48.1 0.0 copy-done.8
  48.1 0.7 copy.22.reach_ref
  48.8 12.0 %shard_map.82 = (f32[6,384,1]{2,1,0:T(8,128)}, f32[6,384,1]{2,1,0:T(8,128)}, f32[384,768]{1,0:T(8,128)}) custom-call(s32[6,2]{1,0:T(8,128)} %copy.22.reach_ref, bf16[384,768]{1,0:T(8,128)(2,1)} %bitcast.15, bf16[2,384,768]{2,1,0:T(8,128)(2,1)} %bitcast.2.rest_0_, bf16[2,384,768]{2,1,0:T(8,128)(2,1)} %copy-done.4, bf16[2,384,768]{2,1,0:T(8,128)(2,1)} %copy-done.5, ...), custom_call_target="tpu_custom_call" | custom-call | tf_op jit(solution)/shard_map/pallas_call | solution.py:187
  60.8 35.2 %collective-permute-done.7.rest_1_ = bf16[2,384,768]{2,1,0:T(8,128)(2,1)S(1)} collective-permute-done((bf16[2,384,768]{2,1,0:T(8,128)(2,1)}, bf16[2,384,768]{2,1,0:T(8,128)(2,1)S(1)}, u32[]{:S(2)}, u32[]{:S(2)}) %collective-permute-start.7) | collective-permute-done | bytes 1179680 | tf_op jit(solution)/shard_map/ppermute | solution.py:218
  96.0 0.0 copy-start.2
  96.0 2.1 %collective-permute-done.8.rest_2_ = bf16[2,384,768]{2,1,0:T(8,128)(2,1)S(1)} collective-permute-done((bf16[2,384,768]{2,1,0:T(8,128)(2,1)}, bf16[2,384,768]{2,1,0:T(8,128)(2,1)S(1)}, u32[]{:S(2)}, u32[]{:S(2)}) %collective-permute-start.8) | collective-permute-done | bytes 1179680 | tf_op jit(solution)/shard_map/ppermute | solution.py:219
  98.1 0.0 copy-done.2
  98.1 1.0 copy-done.3
  99.1 1.6 pad_maximum_fusion
  100.7 2.4 %collective-permute-start.10 = (bf16[2,2,384,768]{3,2,1,0:T(8,128)(2,1)}, bf16[2,2,384,768]{3,2,1,0:T(8,128)(2,1)S(1)}, u32[]{:S(2)}, u32[]{:S(2)}) collective-permute-start(bf16[2,2,384,768]{3,2,1,0:T(8,128)(2,1)} %pad_maximum_fusion), channel_id=1, source_target_pairs={{4,0},{8,4},{12,8},{5,1},{9,5},{13,9},{6,2},{10,6},{14,10},{7,3},{... | collective-permute-start | bytes 7077896 | tf_op jit(solution)/shard_map/ppermute | solution.py:226
  103.1 3.2 %collective-permute-start.9 = (bf16[2,2,384,768]{3,2,1,0:T(8,128)(2,1)}, bf16[2,2,384,768]{3,2,1,0:T(8,128)(2,1)}, u32[]{:S(2)}, u32[]{:S(2)}) collective-permute-start(bf16[2,2,384,768]{3,2,1,0:T(8,128)(2,1)} %pad_maximum_fusion), channel_id=1, source_target_pairs={{0,4},{4,8},{8,12},{1,5},{5,9},{9,13},{2,6},{6,10},{10,14},{3,7},{... | collective-permute-start | bytes 7077896 | tf_op jit(solution)/shard_map/ppermute | solution.py:225
  106.4 0.8 copy.23.rest_8_
  107.2 10.9 %shard_map.83 = (f32[6,384,1]{2,1,0:T(8,128)}, f32[6,384,1]{2,1,0:T(8,128)}, f32[384,768]{1,0:T(8,128)}) custom-call(s32[6,2]{1,0:T(8,128)} %copy.22.reach_ref, bf16[384,768]{1,0:T(8,128)(2,1)} %bitcast.16, bf16[2,256,768]{2,1,0:T(8,128)(2,1)} %maximum_select_fusion.rest_0_, bf16[2,384,768]{2,1,0:T(8,128)(2,1)} %copy-done.2, bf16[2,384,768]{2,1,0:T(8,128)(2,1)} %copy-done.3, ...), custom_call_target="tpu_custom_call" | custom-call | tf_op jit(solution)/shard_map/pallas_call | solution.py:187
  118.1 13.0 %collective-permute-done.10.rest_1_.rest_3_ = bf16[2,2,384,768]{3,2,1,0:T(8,128)(2,1)S(1)} collective-permute-done((bf16[2,2,384,768]{3,2,1,0:T(8,128)(2,1)}, bf16[2,2,384,768]{3,2,1,0:T(8,128)(2,1)S(1)}, u32[]{:S(2)}, u32[]{:S(2)}) %collective-permute-start.10) | collective-permute-done | bytes 2359328 | tf_op jit(solution)/shard_map/ppermute | solution.py:226
  131.1 1.3 collective-permute-done.9.rest_0_.rest_2_
  132.4 0.1 copy-done.1
  132.5 9.5 %shard_map.84 = bf16[384,768]{1,0:T(8,128)(2,1)} custom-call(s32[6,2]{1,0:T(8,128)} %copy.22.reach_ref, bf16[384,768]{1,0:T(8,128)(2,1)} %bitcast.17, bf16[2,2,384,768]{3,2,1,0:T(8,128)(2,1)} %collective-permute-done.9.rest_0_.rest_2_, bf16[2,2,384,768]{3,2,1,0:T(8,128)(2,1)} %copy-done.1, bf16[2,2,384,768]{3,2,1,0:T(8,128)(2,1)} %collective-permute-done.9.rest_0_.rest_2_, ...), custom_call_target="tpu_custom_call" | custom-call | tf_op jit(solution)/shard_map/pallas_call | solution.py:187
  142.0 4.5 %convolution_convert_fusion = bf16[384,3072]{1,0:T(8,128)(2,1)S(1)} fusion(bf16[384,768]{1,0:T(8,128)(2,1)} %shard_map.84, bf16[768,3072]{1,0:T(8,128)(2,1)} %param.12), kind=kOutput, calls=%fused_computation | convolution fusion | flops 1813118976 | bytes 7667712 | tf_op jit(solution)/shard_map/dot_general | solution.py:234
  146.6 0.0 copy-start.6
  146.6 0.0 copy-start.7
  146.6 1.3 constant_dynamic-slice_fusion.2
  147.9 2.1 %collective-permute-start.11 = (bf16[384,768]{1,0:T(8,128)(2,1)}, bf16[384,768]{1,0:T(8,128)(2,1)}, u32[]{:S(2)}, u32[]{:S(2)}) collective-permute-start(bf16[384,768]{1,0:T(8,128)(2,1)} %get-tuple-element.39), channel_id=1, source_target_pairs={{0,2},{1,3},{2,0},{3,1},{4,6},{5,7},{6,4},{7,5},{8,10},{9,11},{10,... | collective-permute-start | bytes 1769480 | tf_op jit(solution)/shard_map/ppermute | solution.py:241
  149.9 2.5 %collective-permute-start.12 = (bf16[384,768]{1,0:T(8,128)(2,1)}, bf16[384,768]{1,0:T(8,128)(2,1)}, u32[]{:S(2)}, u32[]{:S(2)}) collective-permute-start(bf16[384,768]{1,0:T(8,128)(2,1)} %get-tuple-element.41), channel_id=1, source_target_pairs={{0,1},{1,2},{2,3},{3,0},{4,5},{5,6},{6,7},{7,4},{8,9},{9,10},{10,1... | collective-permute-start | bytes 1769480 | tf_op jit(solution)/shard_map/ppermute | solution.py:241
  152.5 1.7 collective-permute-start.13
  154.2 5.5 %collective-permute-done.11 = bf16[384,768]{1,0:T(8,128)(2,1)} collective-permute-done((bf16[384,768]{1,0:T(8,128)(2,1)}, bf16[384,768]{1,0:T(8,128)(2,1)}, u32[]{:S(2)}, u32[]{:S(2)}) %collective-permute-start.11) | collective-permute-done | bytes 589856 | tf_op jit(solution)/shard_map/ppermute | solution.py:241
  159.7 6.2 %collective-permute-done.12 = bf16[384,768]{1,0:T(8,128)(2,1)} collective-permute-done((bf16[384,768]{1,0:T(8,128)(2,1)}, bf16[384,768]{1,0:T(8,128)(2,1)}, u32[]{:S(2)}, u32[]{:S(2)}) %collective-permute-start.12) | collective-permute-done | bytes 589856 | tf_op jit(solution)/shard_map/ppermute | solution.py:241
  165.9 3.1 %collective-permute-done.13 = bf16[384,768]{1,0:T(8,128)(2,1)} collective-permute-done((bf16[384,768]{1,0:T(8,128)(2,1)}, bf16[384,768]{1,0:T(8,128)(2,1)}, u32[]{:S(2)}, u32[]{:S(2)}) %collective-permute-start.13) | collective-permute-done | bytes 589856 | tf_op jit(solution)/shard_map/ppermute | solution.py:241
  169.0 0.0 copy-done.6
  169.0 0.0 copy-done.7
  169.0 2.6 %fusion.1 = bf16[1,1,384,768]{3,2,1,0:T(8,128)(2,1)} fusion(bf16[384,768]{1,0:T(8,128)(2,1)} %collective-permute-done.13, bf16[384,768]{1,0:T(8,128)(2,1)} %collective-permute-done.12, bf16[384,768]{1,0:T(8,128)(2,1)} %collective-permute-done.11, bf16[1,1,384,768]{3,2,1,0:T(8,128)(2,1)S(1)} %copy-done.6, bf16[384,3072]{1,0:T(8,128)(2,1)S(1)} %convolution_convert_fusion, ...), kind=kLoop, calls=%fused_computation.5 | loop fusion | flops 3244032 | bytes 3542020 | tf_op jit(solution)/shard_map/broadcast_in_dim | solution.py:246
  (7 shorter events, 0.1 us)
Async XLA Ops:
  0.0 0.8 copy-start
  0.8 4.2 %collective-permute-start = (bf16[2,16,384]{2,1,0:T(8,128)(2,1)S(1)}, bf16[2,16,384]{2,1,0:T(8,128)(2,1)S(1)}, u32[]{:S(2)}, u32[]{:S(2)}) collective-permute-start(bf16[2,16,384]{2,1,0:T(8,128)(2,1)S(1)} %constant_dynamic-slice_fusion.3), channel_id=1, source_target_pairs={{0,16},{16,0},{32,48},{48,32},{64,80},{80,64},{96,112},{112,96},{1... | collective-permute-start | bytes 73736 | tf_op jit(solution)/shard_map/ppermute | solution.py:39
  5.0 7.0 %collective-permute-start.1 = (bf16[2,32,384]{2,1,0:T(8,128)(2,1)S(1)}, bf16[2,32,384]{2,1,0:T(8,128)(2,1)S(1)}, u32[]{:S(2)}, u32[]{:S(2)}) collective-permute-start(bf16[2,32,384]{2,1,0:T(8,128)(2,1)S(1)} %maximum_select_fusion.4), channel_id=1, source_target_pairs={{0,32},{16,48},{32,0},{48,16},{64,96},{80,112},{96,64},{112,80},{1... | collective-permute-start | bytes 147464 | tf_op jit(solution)/shard_map/ppermute | solution.py:39
  5.1 33.1 %collective-permute-start.5 = (bf16[2,384,768]{2,1,0:T(8,128)(2,1)}, bf16[2,384,768]{2,1,0:T(8,128)(2,1)S(1)}, u32[]{:S(2)}, u32[]{:S(2)}) collective-permute-start(bf16[2,384,768]{2,1,0:T(8,128)(2,1)} %bitcast.2.rest_0_), channel_id=1, source_target_pairs={{0,4},{4,8},{8,12},{1,5},{5,9},{9,13},{2,6},{6,10},{10,14},{3,7},{... | collective-permute-start | bytes 3538952 | tf_op jit(solution)/shard_map/ppermute | solution.py:198
  10.0 29.3 %collective-permute-start.6 = (bf16[2,384,768]{2,1,0:T(8,128)(2,1)}, bf16[2,384,768]{2,1,0:T(8,128)(2,1)S(1)}, u32[]{:S(2)}, u32[]{:S(2)}) collective-permute-start(bf16[2,384,768]{2,1,0:T(8,128)(2,1)} %bitcast.2.rest_0_), channel_id=1, source_target_pairs={{4,0},{8,4},{12,8},{5,1},{9,5},{13,9},{6,2},{10,6},{14,10},{7,3},{... | collective-permute-start | bytes 3538952 | tf_op jit(solution)/shard_map/ppermute | solution.py:199
  12.0 7.2 %collective-permute-start.2 = (bf16[2,64,384]{2,1,0:T(8,128)(2,1)S(1)}, bf16[2,64,384]{2,1,0:T(8,128)(2,1)S(1)}, u32[]{:S(2)}, u32[]{:S(2)}) collective-permute-start(bf16[2,64,384]{2,1,0:T(8,128)(2,1)S(1)} %maximum_select_fusion.3), channel_id=1, source_target_pairs={{0,64},{16,80},{32,96},{48,112},{64,0},{80,16},{96,32},{112,48},{1... | collective-permute-start | bytes 294920 | tf_op jit(solution)/shard_map/ppermute | solution.py:39
  19.3 14.3 %collective-permute-start.3 = (bf16[2,128,384]{2,1,0:T(8,128)(2,1)S(1)}, bf16[2,128,384]{2,1,0:T(8,128)(2,1)S(1)}, u32[]{:S(2)}, u32[]{:S(2)}) collective-permute-start(bf16[2,128,384]{2,1,0:T(8,128)(2,1)S(1)} %maximum_select_fusion.2), channel_id=1, source_target_pairs={{0,128},{16,144},{32,160},{48,176},{64,192},{80,208},{96,224},{112... | collective-permute-start | bytes 589832 | tf_op jit(solution)/shard_map/ppermute | solution.py:39
  25.8 22.3 %copy-start.8 = (s32[6,2]{0,1:T(2,128)S(1)}, s32[6,2]{0,1:T(2,128)}, u32[]{:S(2)}) copy-start(s32[6,2]{0,1:T(2,128)} %param.14) | copy-start | bytes 148
  33.7 3.4 %collective-permute-start.4 = (bf16[2,256,384]{2,1,0:T(8,128)(2,1)S(1)}, bf16[2,256,384]{2,1,0:T(8,128)(2,1)S(1)}, u32[]{:S(2)}, u32[]{:S(2)}) collective-permute-start(bf16[2,256,384]{2,1,0:T(8,128)(2,1)S(1)} %maximum_select_fusion.1), channel_id=1, source_target_pairs={{0,4},{4,0},{8,12},{12,8},{1,5},{5,1},{9,13},{13,9},{2,6},{6,2},{1... | collective-permute-start | bytes 1179656 | tf_op jit(solution)/shard_map/ppermute | solution.py:48
  38.2 1.1 copy-start.4
  39.3 1.1 copy-start.5
  40.4 55.6 %collective-permute-start.7 = (bf16[2,384,768]{2,1,0:T(8,128)(2,1)}, bf16[2,384,768]{2,1,0:T(8,128)(2,1)S(1)}, u32[]{:S(2)}, u32[]{:S(2)}) collective-permute-start(bf16[2,384,768]{2,1,0:T(8,128)(2,1)} %bitcast.2.rest_0_), channel_id=1, source_target_pairs={{0,16},{16,32},{32,48},{48,64},{64,80},{80,96},{96,112},{112,128},... | collective-permute-start | bytes 3538952 | tf_op jit(solution)/shard_map/ppermute | solution.py:218
  45.0 53.0 %collective-permute-start.8 = (bf16[2,384,768]{2,1,0:T(8,128)(2,1)}, bf16[2,384,768]{2,1,0:T(8,128)(2,1)S(1)}, u32[]{:S(2)}, u32[]{:S(2)}) collective-permute-start(bf16[2,384,768]{2,1,0:T(8,128)(2,1)} %bitcast.2.rest_0_), channel_id=1, source_target_pairs={{16,0},{32,16},{48,32},{64,48},{80,64},{96,80},{112,96},{128,112},... | collective-permute-start | bytes 3538952 | tf_op jit(solution)/shard_map/ppermute | solution.py:219
  96.0 2.1 %copy-start.2 = (bf16[2,384,768]{2,1,0:T(8,128)(2,1)}, bf16[2,384,768]{2,1,0:T(8,128)(2,1)S(1)}, u32[]{:S(2)}) copy-start(bf16[2,384,768]{2,1,0:T(8,128)(2,1)S(1)} %collective-permute-done.7.rest_1_) | copy-start | bytes 3538948
  98.1 1.0 copy-start.3
  100.7 30.4 %collective-permute-start.10 = (bf16[2,2,384,768]{3,2,1,0:T(8,128)(2,1)}, bf16[2,2,384,768]{3,2,1,0:T(8,128)(2,1)S(1)}, u32[]{:S(2)}, u32[]{:S(2)}) collective-permute-start(bf16[2,2,384,768]{3,2,1,0:T(8,128)(2,1)} %pad_maximum_fusion), channel_id=1, source_target_pairs={{4,0},{8,4},{12,8},{5,1},{9,5},{13,9},{6,2},{10,6},{14,10},{7,3},{... | collective-permute-start | bytes 7077896 | tf_op jit(solution)/shard_map/ppermute | solution.py:226
  103.1 29.3 %collective-permute-start.9 = (bf16[2,2,384,768]{3,2,1,0:T(8,128)(2,1)}, bf16[2,2,384,768]{3,2,1,0:T(8,128)(2,1)}, u32[]{:S(2)}, u32[]{:S(2)}) collective-permute-start(bf16[2,2,384,768]{3,2,1,0:T(8,128)(2,1)} %pad_maximum_fusion), channel_id=1, source_target_pairs={{0,4},{4,8},{8,12},{1,5},{5,9},{9,13},{2,6},{6,10},{10,14},{3,7},{... | collective-permute-start | bytes 7077896 | tf_op jit(solution)/shard_map/ppermute | solution.py:225
  131.1 1.4 copy-start.1
  146.6 22.4 %copy-start.6 = (bf16[1,1,384,768]{3,2,1,0:T(8,128)(2,1)S(1)}, bf16[1,1,384,768]{3,2,1,0:T(8,128)(2,1)}, u32[]{:S(2)}) copy-start(bf16[1,1,384,768]{3,2,1,0:T(8,128)(2,1)} %param.11) | copy-start | bytes 1769476
  146.6 22.4 %copy-start.7 = (f32[768]{0:T(1024)S(1)}, f32[768]{0:T(1024)}, u32[]{:S(2)}) copy-start(f32[768]{0:T(1024)} %param.13) | copy-start | bytes 9220
  147.9 11.8 %collective-permute-start.11 = (bf16[384,768]{1,0:T(8,128)(2,1)}, bf16[384,768]{1,0:T(8,128)(2,1)}, u32[]{:S(2)}, u32[]{:S(2)}) collective-permute-start(bf16[384,768]{1,0:T(8,128)(2,1)} %get-tuple-element.39), channel_id=1, source_target_pairs={{0,2},{1,3},{2,0},{3,1},{4,6},{5,7},{6,4},{7,5},{8,10},{9,11},{10,... | collective-permute-start | bytes 1769480 | tf_op jit(solution)/shard_map/ppermute | solution.py:241
  149.9 15.9 %collective-permute-start.12 = (bf16[384,768]{1,0:T(8,128)(2,1)}, bf16[384,768]{1,0:T(8,128)(2,1)}, u32[]{:S(2)}, u32[]{:S(2)}) collective-permute-start(bf16[384,768]{1,0:T(8,128)(2,1)} %get-tuple-element.41), channel_id=1, source_target_pairs={{0,1},{1,2},{2,3},{3,0},{4,5},{5,6},{6,7},{7,4},{8,9},{9,10},{10,1... | collective-permute-start | bytes 1769480 | tf_op jit(solution)/shard_map/ppermute | solution.py:241
  152.5 16.5 %collective-permute-start.13 = (bf16[384,768]{1,0:T(8,128)(2,1)}, bf16[384,768]{1,0:T(8,128)(2,1)}, u32[]{:S(2)}, u32[]{:S(2)}) collective-permute-start(bf16[384,768]{1,0:T(8,128)(2,1)} %get-tuple-element.40), channel_id=1, source_target_pairs={{0,3},{1,0},{2,1},{3,2},{4,7},{5,4},{6,5},{7,6},{8,11},{9,8},{10,9... | collective-permute-start | bytes 1769480 | tf_op jit(solution)/shard_map/ppermute | solution.py:241

commit v15 on v14

--- a/solution.py
+++ b/solution.py
@@ -26,6 +26,17 @@
 
 def shift_pairs(devices, step):
     return [(i, i + step) for i in range(devices) if 0 <= i + step < devices]
+
+
+def diagonal_pairs(tm_size, height_size, step):
+    pairs = []
+    for t in range(tm_size):
+        if not 0 <= t + step < tm_size:
+            continue
+        for h in range(1, height_size - 1, 2):
+            pairs.append((t * height_size + h, (t + step) * height_size + h + 1))
+            pairs.append((t * height_size + h + 1, (t + step) * height_size + h))
+    return pairs
 
 
 def text_halves(text_kv):
@@ -220,13 +231,20 @@
     queries = image_q[0, 0]
     near = [(own, None, 4), (h_before, None, 3), (h_after, None, 5)]
     state = attend(head_reach, queries, None, near, bias)
-    t_before, t_after, state = lax.optimization_barrier((t_before, t_after, state))
-    time_pair = jnp.stack([t_before, t_after])
-    c_before = lax.ppermute(time_pair, "height", shift_pairs(height_size, 1))
-    c_after = lax.ppermute(time_pair, "height", shift_pairs(height_size, -1))
+    t_before, t_after, sent, state = lax.optimization_barrier((t_before, t_after, sent, state))
+    earlier_low = lax.ppermute(t_before, "height", shift_pairs(height_size, 1))
+    earlier_high = lax.ppermute(t_before, "height", shift_pairs(height_size, -1))
+    partner = lax.ppermute(t_after, "height", [(i, i ^ 1) for i in range(height_size)])
+    diagonal = lax.ppermute(sent, ("tm", "height"), diagonal_pairs(tm_size, height_size, -1))
     across = [(t_before, None, 1), (t_after, None, 7)]
     state = attend(head_reach, queries, text, across, bias, state)
-    corners = [(c_before, 0, 0), (c_after, 0, 2), (c_before, 1, 6), (c_after, 1, 8)]
+    odd_height = lax.axis_index("height") % 2 == 1
+    corners = [
+        (earlier_low, None, 0),
+        (earlier_high, None, 2),
+        (jnp.where(odd_height, partner, diagonal), None, 6),
+        (jnp.where(odd_height, diagonal, partner), None, 8),
+    ]
     attended = attend(head_reach, queries, None, corners, bias, state, qvalid)
 
     mp_index = lax.axis_index("mp")

time: 172 us -> 172 us (level); the launches traced: 172 us -> 169 us
  waiting for transfers between devices: 82.7 us -> 78.5 us
  starting transfers between devices: 34.8 us -> 38.9 us
  local copies, waits for them, and re-layouts: 9.34 us -> 7.37 us
    ppermute x2 -> x4, waiting for transfers between devices: 14.3 us -> 0.01 us  [the longest x1 0.01 us: per_device(): lax.ppermute(sent, ('tm', 'height'), diagonal_pairs(tm_size, height_size,...]
    ppermute x3, waiting for transfers between devices: 14.8 us -> 23.2 us  [per_device(): received.append(lax.ppermute(part, 'mp', pairs))]
    select_n x0 -> x1, other arithmetic: none -> 3.27 us  [per_device(): jnp.where(odd_height, diagonal, partner)]
    ppermute x2 -> x4, starting transfers between devices: 5.55 us -> 7.94 us  [the longest x1 3.64 us: per_device(): earlier_low = lax.ppermute(t_before, 'height', shift_pairs(height_size, 1))]
    unnamed x19 -> x17, local copies, waits for them, and re-layouts: 4.86 us -> 2.92 us
  transfers between devices with their start and end apart: 14 -> 16, of which waited for: 10 -> 7; matrix products, arithmetic and copies ran while one was open for 4% -> 6% of each run, Pallas kernels for 13% -> 13%
where the time goes in v15:
time: 172 us; the launch traced here: 169 us
  waiting for transfers between devices  78.5 us (46%)
  starting transfers between devices  38.9 us (23%)
  Pallas kernels  30.7 us (18%)
  other arithmetic  9.21 us (5%)
  local copies, waits for them, and re-layouts  7.37 us (4%)
  matrix products  4.52 us (3%)
    ppermute x1, waiting for transfers between devices, per_device(): t_before = lax.ppermute(sent, 'tm', shift_pairs(tm_size, 1))  36.8 us
    pallas_call x3, Pallas kernels, attend(): pl.pallas_call(kernel, grid_spec=grid_spec, out_shape=out_shape)  30.7 us
    ppermute x3, waiting for transfers between devices, per_device(): received.append(lax.ppermute(part, 'mp', pairs))  23.2 us
    ppermute x4, waiting for transfers between devices, exchange(): other = lax.ppermute(block, 'tm', [(i, i ^ step) for i in range(devices)])  16.3 us
    ppermute x3, starting transfers between devices, per_device(): received.append(lax.ppermute(part, 'mp', pairs))  7.95 us
    ppermute x4, starting transfers between devices, exchange(): other = lax.ppermute(block, 'tm', [(i, i ^ step) for i in range(devices)])  7.11 us
    ppermute x1, starting transfers between devices, per_device(): h_before = lax.ppermute(own, 'height', shift_pairs(height_size, 1))  4.92 us
    ppermute x1, starting transfers between devices, per_device(): t_before = lax.ppermute(sent, 'tm', shift_pairs(tm_size, 1))  4.66 us
  transfers between devices with their start and end apart: 16, of which 7 were waited for; matrix products, arithmetic and copies ran while one was open for 6% of the time, Pallas kernels for 13%

profile of v15, /device:TPU:97, one launch (start us, length us, event | category | flops | bytes accessed | tf_op | source)
XLA Modules:
  0.0 169.4 jit_solution(11066309896103448094)
XLA Ops:
  0.0 0.0 copy-start
  0.0 0.8 copy-done
  0.8 2.7 %collective-permute-start = (bf16[2,16,384]{2,1,0:T(8,128)(2,1)S(1)}, bf16[2,16,384]{2,1,0:T(8,128)(2,1)S(1)}, u32[]{:S(2)}, u32[]{:S(2)}) collective-permute-start(bf16[2,16,384]{2,1,0:T(8,128)(2,1)S(1)} %constant_dynamic-slice_fusion.3), channel_id=1, source_target_pairs={{0,16},{16,0},{32,48},{48,32},{64,80},{80,64},{96,112},{112,96},{1... | collective-permute-start | bytes 73736 | tf_op jit(solution)/shard_map/ppermute | solution.py:50
  3.5 1.4 collective-permute-done
  5.0 0.1 collective-permute-start.1
  5.1 4.9 %collective-permute-start.5 = (bf16[2,384,768]{2,1,0:T(8,128)(2,1)}, bf16[2,384,768]{2,1,0:T(8,128)(2,1)S(1)}, u32[]{:S(2)}, u32[]{:S(2)}) collective-permute-start(bf16[2,384,768]{2,1,0:T(8,128)(2,1)} %bitcast.2.rest_0_), channel_id=1, source_target_pairs={{0,4},{4,8},{8,12},{1,5},{5,9},{9,13},{2,6},{6,10},{10,14},{3,7},{... | collective-permute-start | bytes 3538952 | tf_op jit(solution)/shard_map/ppermute | solution.py:209
  10.0 1.9 %collective-permute-start.6 = (bf16[2,384,768]{2,1,0:T(8,128)(2,1)}, bf16[2,384,768]{2,1,0:T(8,128)(2,1)S(1)}, u32[]{:S(2)}, u32[]{:S(2)}) collective-permute-start(bf16[2,384,768]{2,1,0:T(8,128)(2,1)} %bitcast.2.rest_0_), channel_id=1, source_target_pairs={{4,0},{8,4},{12,8},{5,1},{9,5},{13,9},{6,2},{10,6},{14,10},{7,3},{... | collective-permute-start | bytes 3538952 | tf_op jit(solution)/shard_map/ppermute | solution.py:210
  12.0 0.0 collective-permute-done.1
  12.0 0.1 collective-permute-start.2
  12.1 7.1 %collective-permute-done.2 = bf16[2,64,384]{2,1,0:T(8,128)(2,1)S(1)} collective-permute-done((bf16[2,64,384]{2,1,0:T(8,128)(2,1)S(1)}, bf16[2,64,384]{2,1,0:T(8,128)(2,1)S(1)}, u32[]{:S(2)}, u32[]{:S(2)}) %collective-permute-start.2) | collective-permute-done | bytes 98336 | tf_op jit(solution)/shard_map/ppermute | solution.py:50
  19.3 4.2 %collective-permute-start.3 = (bf16[2,128,384]{2,1,0:T(8,128)(2,1)S(1)}, bf16[2,128,384]{2,1,0:T(8,128)(2,1)S(1)}, u32[]{:S(2)}, u32[]{:S(2)}) collective-permute-start(bf16[2,128,384]{2,1,0:T(8,128)(2,1)S(1)} %maximum_select_fusion.2), channel_id=1, source_target_pairs={{0,128},{16,144},{32,160},{48,176},{64,192},{80,208},{96,224},{112... | collective-permute-start | bytes 589832 | tf_op jit(solution)/shard_map/ppermute | solution.py:50
  23.5 0.8 pad_dynamic-slice_fusion
  24.2 0.1 copy.16
  24.3 0.1 lt.113
  24.4 0.1 copy.17
  24.5 0.1 lt.118
  24.6 0.6 slice.12
  25.2 0.6 slice.13
  25.8 7.8 %collective-permute-done.3 = bf16[2,128,384]{2,1,0:T(8,128)(2,1)S(1)} collective-permute-done((bf16[2,128,384]{2,1,0:T(8,128)(2,1)S(1)}, bf16[2,128,384]{2,1,0:T(8,128)(2,1)S(1)}, u32[]{:S(2)}, u32[]{:S(2)}) %collective-permute-start.3) | collective-permute-done | bytes 196640 | tf_op jit(solution)/shard_map/ppermute | solution.py:50
  33.6 0.1 maximum_select_fusion.1
  33.7 1.4 collective-permute-start.4
  35.1 1.3 fusion.8
  36.4 0.7 and_select_fusion.rest_3_.rest_4_
  37.1 0.0 collective-permute-done.4
  37.1 1.1 maximum_select_fusion.rest_0_
  38.2 0.0 collective-permute-done.5.rest_1_
  38.2 0.0 collective-permute-done.6.rest_2_
  38.2 0.0 copy-start.4
  38.2 4.7 %collective-permute-start.7 = (bf16[2,384,768]{2,1,0:T(8,128)(2,1)}, bf16[2,384,768]{2,1,0:T(8,128)(2,1)}, u32[]{:S(2)}, u32[]{:S(2)}) collective-permute-start(bf16[2,384,768]{2,1,0:T(8,128)(2,1)} %bitcast.2.rest_0_), channel_id=1, source_target_pairs={{0,16},{16,32},{32,48},{48,64},{64,80},{80,96},{96,112},{112,128},... | collective-permute-start | bytes 3538952 | tf_op jit(solution)/shard_map/ppermute | solution.py:229
  42.9 3.0 %collective-permute-start.8 = (bf16[2,384,768]{2,1,0:T(8,128)(2,1)}, bf16[2,384,768]{2,1,0:T(8,128)(2,1)}, u32[]{:S(2)}, u32[]{:S(2)}) collective-permute-start(bf16[2,384,768]{2,1,0:T(8,128)(2,1)} %bitcast.2.rest_0_), channel_id=1, source_target_pairs={{16,0},{32,16},{48,32},{64,48},{80,64},{96,80},{112,96},{128,112},... | collective-permute-start | bytes 3538952 | tf_op jit(solution)/shard_map/ppermute | solution.py:230
  45.9 0.0 copy-done.7
  45.9 0.7 copy.22.reach_ref
  46.6 0.0 copy-done.3
  46.6 0.0 copy-done.4
  46.6 10.5 %shard_map.82 = (f32[6,384,1]{2,1,0:T(8,128)}, f32[6,384,1]{2,1,0:T(8,128)}, f32[384,768]{1,0:T(8,128)}) custom-call(s32[6,2]{1,0:T(8,128)} %copy.22.reach_ref, bf16[384,768]{1,0:T(8,128)(2,1)} %bitcast.13, bf16[2,384,768]{2,1,0:T(8,128)(2,1)} %bitcast.2.rest_0_, bf16[2,384,768]{2,1,0:T(8,128)(2,1)} %copy-done.3, bf16[2,384,768]{2,1,0:T(8,128)(2,1)} %copy-done.4, ...), custom_call_target="tpu_custom_call" | custom-call | tf_op jit(solution)/shard_map/pallas_call | solution.py:198
  57.0 36.8 %collective-permute-done.7.rest_1_ = bf16[2,384,768]{2,1,0:T(8,128)(2,1)} collective-permute-done((bf16[2,384,768]{2,1,0:T(8,128)(2,1)}, bf16[2,384,768]{2,1,0:T(8,128)(2,1)}, u32[]{:S(2)}, u32[]{:S(2)}) %collective-permute-start.7) | collective-permute-done | bytes 1179680 | tf_op jit(solution)/shard_map/ppermute | solution.py:229
  93.8 2.2 %collective-permute-done.8.rest_2_ = bf16[2,384,768]{2,1,0:T(8,128)(2,1)} collective-permute-done((bf16[2,384,768]{2,1,0:T(8,128)(2,1)}, bf16[2,384,768]{2,1,0:T(8,128)(2,1)}, u32[]{:S(2)}, u32[]{:S(2)}) %collective-permute-start.8) | collective-permute-done | bytes 1179680 | tf_op jit(solution)/shard_map/ppermute | solution.py:230
  96.0 0.5 collective-permute-start.11
  96.5 1.9 %collective-permute-start.12 = (bf16[2,384,768]{2,1,0:T(8,128)(2,1)}, bf16[2,384,768]{2,1,0:T(8,128)(2,1)}, u32[]{:S(2)}, u32[]{:S(2)}) collective-permute-start(bf16[2,384,768]{2,1,0:T(8,128)(2,1)} %bitcast.2.rest_0_), channel_id=1, source_target_pairs={{20,8},{24,4},{36,24},{40,20},{52,40},{56,36},{68,56},{72,52},{84,... | collective-permute-start | bytes 3538952 | tf_op jit(solution)/shard_map/ppermute | solution.py:238
  98.4 1.9 %collective-permute-start.10 = (bf16[2,384,768]{2,1,0:T(8,128)(2,1)}, bf16[2,384,768]{2,1,0:T(8,128)(2,1)S(1)}, u32[]{:S(2)}, u32[]{:S(2)}) collective-permute-start(bf16[2,384,768]{2,1,0:T(8,128)(2,1)} %collective-permute-done.7.rest_1_), channel_id=1, source_target_pairs={{4,0},{8,4},{12,8},{5,1},{9,5},{13,9},{6,2},{10,6},{14,10},{7,3},{... | collective-permute-start | bytes 3538952 | tf_op jit(solution)/shard_map/ppermute | solution.py:236
  100.3 3.6 %collective-permute-start.9 = (bf16[2,384,768]{2,1,0:T(8,128)(2,1)}, bf16[2,384,768]{2,1,0:T(8,128)(2,1)S(1)}, u32[]{:S(2)}, u32[]{:S(2)}) collective-permute-start(bf16[2,384,768]{2,1,0:T(8,128)(2,1)} %collective-permute-done.7.rest_1_), channel_id=1, source_target_pairs={{0,4},{4,8},{8,12},{1,5},{5,9},{9,13},{2,6},{6,10},{10,14},{3,7},{... | collective-permute-start | bytes 3538952 | tf_op jit(solution)/shard_map/ppermute | solution.py:235
  104.0 0.8 copy.23.rest_8_
  104.9 12.0 %shard_map.83 = (f32[6,384,1]{2,1,0:T(8,128)}, f32[6,384,1]{2,1,0:T(8,128)}, f32[384,768]{1,0:T(8,128)}) custom-call(s32[6,2]{1,0:T(8,128)} %copy.22.reach_ref, bf16[384,768]{1,0:T(8,128)(2,1)} %bitcast.14, bf16[2,256,768]{2,1,0:T(8,128)(2,1)} %maximum_select_fusion.rest_0_, bf16[2,384,768]{2,1,0:T(8,128)(2,1)} %collective-permute-done.7.rest_1_, ...), custom_call_target="tpu_custom_call" | custom-call | tf_op jit(solution)/shard_map/pallas_call | solution.py:198
  116.8 0.0 collective-permute-done.11
  116.8 0.0 collective-permute-done.12
  116.8 3.3 %broadcast_select_fusion = (bf16[2,384,768]{2,1,0:T(8,128)(2,1)}, bf16[2,384,768]{2,1,0:T(8,128)(2,1)}) fusion(bf16[2,384,768]{2,1,0:T(8,128)(2,1)} %collective-permute-done.12, bf16[2,384,768]{2,1,0:T(8,128)(2,1)} %collective-permute-done.11, pred[]{:T(512)S(6)} %eq.32), kind=kLoop, calls=%fused_computation.3 | loop fusion | flops 1179648 | bytes 4718593 | tf_op jit(solution)/shard_map/jit(_where)/select_n | solution.py:246
  120.1 0.0 collective-permute-done.10.rest_1_
  120.1 0.0 collective-permute-done.9.rest_0_
  120.1 0.0 copy-start.2
  120.1 1.0 copy-done.1
  121.1 0.4 copy-done.2
  121.5 8.3 %shard_map.84 = bf16[384,768]{1,0:T(8,128)(2,1)} custom-call(s32[6,2]{1,0:T(8,128)} %copy.22.reach_ref, bf16[384,768]{1,0:T(8,128)(2,1)} %bitcast.15, bf16[2,384,768]{2,1,0:T(8,128)(2,1)} %copy-done.2, bf16[2,384,768]{2,1,0:T(8,128)(2,1)} %copy-done.1, bf16[2,384,768]{2,1,0:T(8,128)(2,1)} %get-tuple-element.45.rest_2_, ...), custom_call_target="tpu_custom_call" | custom-call | tf_op jit(solution)/shard_map/pallas_call | solution.py:198
  129.8 4.5 %convolution_convert_fusion = bf16[384,3072]{1,0:T(8,128)(2,1)S(1)} fusion(bf16[384,768]{1,0:T(8,128)(2,1)} %shard_map.84, bf16[768,3072]{1,0:T(8,128)(2,1)} %param.12), kind=kOutput, calls=%fused_computation | convolution fusion | flops 1813118976 | bytes 7667712 | tf_op jit(solution)/shard_map/dot_general | solution.py:252
  134.3 0.0 copy-start.5
  134.4 0.0 copy-start.6
  134.4 1.3 constant_dynamic-slice_fusion.2
  135.7 5.3 %collective-permute-start.13 = (bf16[384,768]{1,0:T(8,128)(2,1)}, bf16[384,768]{1,0:T(8,128)(2,1)}, u32[]{:S(2)}, u32[]{:S(2)}) collective-permute-start(bf16[384,768]{1,0:T(8,128)(2,1)} %get-tuple-element.41), channel_id=1, source_target_pairs={{0,2},{1,3},{2,0},{3,1},{4,6},{5,7},{6,4},{7,5},{8,10},{9,11},{10,... | collective-permute-start | bytes 1769480 | tf_op jit(solution)/shard_map/ppermute | solution.py:259
  140.9 0.0 collective-permute-start.14
  140.9 2.7 %collective-permute-start.15 = (bf16[384,768]{1,0:T(8,128)(2,1)}, bf16[384,768]{1,0:T(8,128)(2,1)}, u32[]{:S(2)}, u32[]{:S(2)}) collective-permute-start(bf16[384,768]{1,0:T(8,128)(2,1)} %get-tuple-element.42), channel_id=1, source_target_pairs={{0,3},{1,0},{2,1},{3,2},{4,7},{5,4},{6,5},{7,6},{8,11},{9,8},{10,9... | collective-permute-start | bytes 1769480 | tf_op jit(solution)/shard_map/ppermute | solution.py:259
  143.6 11.3 %collective-permute-done.13 = bf16[384,768]{1,0:T(8,128)(2,1)} collective-permute-done((bf16[384,768]{1,0:T(8,128)(2,1)}, bf16[384,768]{1,0:T(8,128)(2,1)}, u32[]{:S(2)}, u32[]{:S(2)}) %collective-permute-start.13) | collective-permute-done | bytes 589856 | tf_op jit(solution)/shard_map/ppermute | solution.py:259
  154.9 11.9 %collective-permute-done.14 = bf16[384,768]{1,0:T(8,128)(2,1)} collective-permute-done((bf16[384,768]{1,0:T(8,128)(2,1)}, bf16[384,768]{1,0:T(8,128)(2,1)}, u32[]{:S(2)}, u32[]{:S(2)}) %collective-permute-start.14) | collective-permute-done | bytes 589856 | tf_op jit(solution)/shard_map/ppermute | solution.py:259
  166.8 0.0 collective-permute-done.15
  166.8 0.0 copy-done.6
  166.8 2.6 %fusion.1 = bf16[1,1,384,768]{3,2,1,0:T(8,128)(2,1)} fusion(bf16[384,768]{1,0:T(8,128)(2,1)} %collective-permute-done.15, bf16[384,768]{1,0:T(8,128)(2,1)} %collective-permute-done.14, bf16[384,768]{1,0:T(8,128)(2,1)} %collective-permute-done.13, bf16[1,1,384,768]{3,2,1,0:T(8,128)(2,1)S(1)} %copy-done.5, bf16[384,3072]{1,0:T(8,128)(2,1)S(1)} %convolution_convert_fusion, ...), kind=kLoop, calls=%fused_computation.6 | loop fusion | flops 3244032 | bytes 3542020 | tf_op jit(solution)/shard_map/broadcast_in_dim | solution.py:264
  (9 shorter events, 0.1 us)
Async XLA Ops:
  0.0 0.8 copy-start
  0.8 4.2 %collective-permute-start = (bf16[2,16,384]{2,1,0:T(8,128)(2,1)S(1)}, bf16[2,16,384]{2,1,0:T(8,128)(2,1)S(1)}, u32[]{:S(2)}, u32[]{:S(2)}) collective-permute-start(bf16[2,16,384]{2,1,0:T(8,128)(2,1)S(1)} %constant_dynamic-slice_fusion.3), channel_id=1, source_target_pairs={{0,16},{16,0},{32,48},{48,32},{64,80},{80,64},{96,112},{112,96},{1... | collective-permute-start | bytes 73736 | tf_op jit(solution)/shard_map/ppermute | solution.py:50
  5.0 7.0 %collective-permute-start.1 = (bf16[2,32,384]{2,1,0:T(8,128)(2,1)S(1)}, bf16[2,32,384]{2,1,0:T(8,128)(2,1)S(1)}, u32[]{:S(2)}, u32[]{:S(2)}) collective-permute-start(bf16[2,32,384]{2,1,0:T(8,128)(2,1)S(1)} %maximum_select_fusion.4), channel_id=1, source_target_pairs={{0,32},{16,48},{32,0},{48,16},{64,96},{80,112},{96,64},{112,80},{1... | collective-permute-start | bytes 147464 | tf_op jit(solution)/shard_map/ppermute | solution.py:50
  5.1 33.1 %collective-permute-start.5 = (bf16[2,384,768]{2,1,0:T(8,128)(2,1)}, bf16[2,384,768]{2,1,0:T(8,128)(2,1)S(1)}, u32[]{:S(2)}, u32[]{:S(2)}) collective-permute-start(bf16[2,384,768]{2,1,0:T(8,128)(2,1)} %bitcast.2.rest_0_), channel_id=1, source_target_pairs={{0,4},{4,8},{8,12},{1,5},{5,9},{9,13},{2,6},{6,10},{10,14},{3,7},{... | collective-permute-start | bytes 3538952 | tf_op jit(solution)/shard_map/ppermute | solution.py:209
  10.0 28.2 %collective-permute-start.6 = (bf16[2,384,768]{2,1,0:T(8,128)(2,1)}, bf16[2,384,768]{2,1,0:T(8,128)(2,1)S(1)}, u32[]{:S(2)}, u32[]{:S(2)}) collective-permute-start(bf16[2,384,768]{2,1,0:T(8,128)(2,1)} %bitcast.2.rest_0_), channel_id=1, source_target_pairs={{4,0},{8,4},{12,8},{5,1},{9,5},{13,9},{6,2},{10,6},{14,10},{7,3},{... | collective-permute-start | bytes 3538952 | tf_op jit(solution)/shard_map/ppermute | solution.py:210
  12.0 7.2 %collective-permute-start.2 = (bf16[2,64,384]{2,1,0:T(8,128)(2,1)S(1)}, bf16[2,64,384]{2,1,0:T(8,128)(2,1)S(1)}, u32[]{:S(2)}, u32[]{:S(2)}) collective-permute-start(bf16[2,64,384]{2,1,0:T(8,128)(2,1)S(1)} %maximum_select_fusion.3), channel_id=1, source_target_pairs={{0,64},{16,80},{32,96},{48,112},{64,0},{80,16},{96,32},{112,48},{1... | collective-permute-start | bytes 294920 | tf_op jit(solution)/shard_map/ppermute | solution.py:50
  19.3 14.3 %collective-permute-start.3 = (bf16[2,128,384]{2,1,0:T(8,128)(2,1)S(1)}, bf16[2,128,384]{2,1,0:T(8,128)(2,1)S(1)}, u32[]{:S(2)}, u32[]{:S(2)}) collective-permute-start(bf16[2,128,384]{2,1,0:T(8,128)(2,1)S(1)} %maximum_select_fusion.2), channel_id=1, source_target_pairs={{0,128},{16,144},{32,160},{48,176},{64,192},{80,208},{96,224},{112... | collective-permute-start | bytes 589832 | tf_op jit(solution)/shard_map/ppermute | solution.py:50
  25.8 20.1 %copy-start.7 = (s32[6,2]{0,1:T(2,128)S(1)}, s32[6,2]{0,1:T(2,128)}, u32[]{:S(2)}) copy-start(s32[6,2]{0,1:T(2,128)} %param.14) | copy-start | bytes 148
  33.7 3.3 %collective-permute-start.4 = (bf16[2,256,384]{2,1,0:T(8,128)(2,1)S(1)}, bf16[2,256,384]{2,1,0:T(8,128)(2,1)S(1)}, u32[]{:S(2)}, u32[]{:S(2)}) collective-permute-start(bf16[2,256,384]{2,1,0:T(8,128)(2,1)S(1)} %maximum_select_fusion.1), channel_id=1, source_target_pairs={{0,4},{4,0},{8,12},{12,8},{1,5},{5,1},{9,13},{13,9},{2,6},{6,2},{1... | collective-permute-start | bytes 1179656 | tf_op jit(solution)/shard_map/ppermute | solution.py:59
  38.2 8.4 %copy-start.3 = (bf16[2,384,768]{2,1,0:T(8,128)(2,1)}, bf16[2,384,768]{2,1,0:T(8,128)(2,1)S(1)}, u32[]{:S(2)}) copy-start(bf16[2,384,768]{2,1,0:T(8,128)(2,1)S(1)} %collective-permute-done.5.rest_1_) | copy-start | bytes 3538948
  38.2 8.4 %copy-start.4 = (bf16[2,384,768]{2,1,0:T(8,128)(2,1)}, bf16[2,384,768]{2,1,0:T(8,128)(2,1)S(1)}, u32[]{:S(2)}) copy-start(bf16[2,384,768]{2,1,0:T(8,128)(2,1)S(1)} %collective-permute-done.6.rest_2_) | copy-start | bytes 3538948
  38.2 55.6 %collective-permute-start.7 = (bf16[2,384,768]{2,1,0:T(8,128)(2,1)}, bf16[2,384,768]{2,1,0:T(8,128)(2,1)}, u32[]{:S(2)}, u32[]{:S(2)}) collective-permute-start(bf16[2,384,768]{2,1,0:T(8,128)(2,1)} %bitcast.2.rest_0_), channel_id=1, source_target_pairs={{0,16},{16,32},{32,48},{48,64},{64,80},{80,96},{96,112},{112,128},... | collective-permute-start | bytes 3538952 | tf_op jit(solution)/shard_map/ppermute | solution.py:229
  42.9 53.1 %collective-permute-start.8 = (bf16[2,384,768]{2,1,0:T(8,128)(2,1)}, bf16[2,384,768]{2,1,0:T(8,128)(2,1)}, u32[]{:S(2)}, u32[]{:S(2)}) collective-permute-start(bf16[2,384,768]{2,1,0:T(8,128)(2,1)} %bitcast.2.rest_0_), channel_id=1, source_target_pairs={{16,0},{32,16},{48,32},{64,48},{80,64},{96,80},{112,96},{128,112},... | collective-permute-start | bytes 3538952 | tf_op jit(solution)/shard_map/ppermute | solution.py:230
  96.0 20.8 %collective-permute-start.11 = (bf16[2,384,768]{2,1,0:T(8,128)(2,1)}, bf16[2,384,768]{2,1,0:T(8,128)(2,1)}, u32[]{:S(2)}, u32[]{:S(2)}) collective-permute-start(bf16[2,384,768]{2,1,0:T(8,128)(2,1)} %collective-permute-done.8.rest_2_), channel_id=1, source_target_pairs={{0,4},{4,0},{8,12},{12,8},{1,5},{5,1},{9,13},{13,9},{2,6},{6,2},{1... | collective-permute-start | bytes 3538952 | tf_op jit(solution)/shard_map/ppermute | solution.py:237
  96.5 20.3 %collective-permute-start.12 = (bf16[2,384,768]{2,1,0:T(8,128)(2,1)}, bf16[2,384,768]{2,1,0:T(8,128)(2,1)}, u32[]{:S(2)}, u32[]{:S(2)}) collective-permute-start(bf16[2,384,768]{2,1,0:T(8,128)(2,1)} %bitcast.2.rest_0_), channel_id=1, source_target_pairs={{20,8},{24,4},{36,24},{40,20},{52,40},{56,36},{68,56},{72,52},{84,... | collective-permute-start | bytes 3538952 | tf_op jit(solution)/shard_map/ppermute | solution.py:238
  98.4 21.7 %collective-permute-start.10 = (bf16[2,384,768]{2,1,0:T(8,128)(2,1)}, bf16[2,384,768]{2,1,0:T(8,128)(2,1)S(1)}, u32[]{:S(2)}, u32[]{:S(2)}) collective-permute-start(bf16[2,384,768]{2,1,0:T(8,128)(2,1)} %collective-permute-done.7.rest_1_), channel_id=1, source_target_pairs={{4,0},{8,4},{12,8},{5,1},{9,5},{13,9},{6,2},{10,6},{14,10},{7,3},{... | collective-permute-start | bytes 3538952 | tf_op jit(solution)/shard_map/ppermute | solution.py:236
  100.3 19.8 %collective-permute-start.9 = (bf16[2,384,768]{2,1,0:T(8,128)(2,1)}, bf16[2,384,768]{2,1,0:T(8,128)(2,1)S(1)}, u32[]{:S(2)}, u32[]{:S(2)}) collective-permute-start(bf16[2,384,768]{2,1,0:T(8,128)(2,1)} %collective-permute-done.7.rest_1_), channel_id=1, source_target_pairs={{0,4},{4,8},{8,12},{1,5},{5,9},{9,13},{2,6},{6,10},{10,14},{3,7},{... | collective-permute-start | bytes 3538952 | tf_op jit(solution)/shard_map/ppermute | solution.py:235
  120.1 1.0 copy-start.1
  120.1 1.4 copy-start.2
  134.3 32.4 %copy-start.5 = (bf16[1,1,384,768]{3,2,1,0:T(8,128)(2,1)S(1)}, bf16[1,1,384,768]{3,2,1,0:T(8,128)(2,1)}, u32[]{:S(2)}) copy-start(bf16[1,1,384,768]{3,2,1,0:T(8,128)(2,1)} %param.11) | copy-start | bytes 1769476
  134.4 32.4 %copy-start.6 = (f32[768]{0:T(1024)S(1)}, f32[768]{0:T(1024)}, u32[]{:S(2)}) copy-start(f32[768]{0:T(1024)} %param.13) | copy-start | bytes 9220
  135.7 19.2 %collective-permute-start.13 = (bf16[384,768]{1,0:T(8,128)(2,1)}, bf16[384,768]{1,0:T(8,128)(2,1)}, u32[]{:S(2)}, u32[]{:S(2)}) collective-permute-start(bf16[384,768]{1,0:T(8,128)(2,1)} %get-tuple-element.41), channel_id=1, source_target_pairs={{0,2},{1,3},{2,0},{3,1},{4,6},{5,7},{6,4},{7,5},{8,10},{9,11},{10,... | collective-permute-start | bytes 1769480 | tf_op jit(solution)/shard_map/ppermute | solution.py:259
  140.9 25.8 %collective-permute-start.14 = (bf16[384,768]{1,0:T(8,128)(2,1)}, bf16[384,768]{1,0:T(8,128)(2,1)}, u32[]{:S(2)}, u32[]{:S(2)}) collective-permute-start(bf16[384,768]{1,0:T(8,128)(2,1)} %get-tuple-element.43), channel_id=1, source_target_pairs={{0,1},{1,2},{2,3},{3,0},{4,5},{5,6},{6,7},{7,4},{8,9},{9,10},{10,1... | collective-permute-start | bytes 1769480 | tf_op jit(solution)/shard_map/ppermute | solution.py:259
  140.9 25.8 %collective-permute-start.15 = (bf16[384,768]{1,0:T(8,128)(2,1)}, bf16[384,768]{1,0:T(8,128)(2,1)}, u32[]{:S(2)}, u32[]{:S(2)}) collective-permute-start(bf16[384,768]{1,0:T(8,128)(2,1)} %get-tuple-element.42), channel_id=1, source_target_pairs={{0,3},{1,0},{2,1},{3,2},{4,7},{5,4},{6,5},{7,6},{8,11},{9,8},{10,9... | collective-permute-start | bytes 1769480 | tf_op jit(solution)/shard_map/ppermute | solution.py:259

commit v16 on v15

--- a/solution.py
+++ b/solution.py
@@ -230,14 +230,14 @@
     t_after = lax.ppermute(sent, "tm", shift_pairs(tm_size, -1))
     queries = image_q[0, 0]
     near = [(own, None, 4), (h_before, None, 3), (h_after, None, 5)]
-    state = attend(head_reach, queries, None, near, bias)
+    state = attend(head_reach, queries, text, near, bias)
     t_before, t_after, sent, state = lax.optimization_barrier((t_before, t_after, sent, state))
     earlier_low = lax.ppermute(t_before, "height", shift_pairs(height_size, 1))
     earlier_high = lax.ppermute(t_before, "height", shift_pairs(height_size, -1))
     partner = lax.ppermute(t_after, "height", [(i, i ^ 1) for i in range(height_size)])
     diagonal = lax.ppermute(sent, ("tm", "height"), diagonal_pairs(tm_size, height_size, -1))
     across = [(t_before, None, 1), (t_after, None, 7)]
-    state = attend(head_reach, queries, text, across, bias, state)
+    state = attend(head_reach, queries, None, across, bias, state)
     odd_height = lax.axis_index("height") % 2 == 1
     corners = [
         (earlier_low, None, 0),

time: 172 us -> 168 us (0.977)
  waiting for transfers between devices: 78.5 us -> 76.5 us
    ppermute x1, waiting for transfers between devices: 36.8 us -> 34.3 us  [per_device(): t_before = lax.ppermute(sent, 'tm', shift_pairs(tm_size, 1))]
  transfers between devices with their start and end apart: 16 -> 16, of which waited for: 7 -> 8; matrix products, arithmetic and copies ran while one was open for 6% -> 6% of each run, Pallas kernels for 13% -> 13%
where the time goes in v16:
time: 168 us; the launch traced here: 167 us
  waiting for transfers between devices  76.5 us (46%)
  starting transfers between devices  38.7 us (23%)
  Pallas kernels  30.7 us (18%)
  other arithmetic  9.08 us (5%)
  local copies, waits for them, and re-layouts  7.38 us (4%)
  matrix products  4.52 us (3%)
    ppermute x1, waiting for transfers between devices, per_device(): t_before = lax.ppermute(sent, 'tm', shift_pairs(tm_size, 1))  34.3 us
    pallas_call x3, Pallas kernels, attend(): pl.pallas_call(kernel, grid_spec=grid_spec, out_shape=out_shape)  30.7 us
    ppermute x3, waiting for transfers between devices, per_device(): received.append(lax.ppermute(part, 'mp', pairs))  22.1 us
    ppermute x4, waiting for transfers between devices, exchange(): other = lax.ppermute(block, 'tm', [(i, i ^ step) for i in range(devices)])  16.3 us
    ppermute x3, starting transfers between devices, per_device(): received.append(lax.ppermute(part, 'mp', pairs))  7.76 us
    ppermute x4, starting transfers between devices, exchange(): other = lax.ppermute(block, 'tm', [(i, i ^ step) for i in range(devices)])  7.11 us
    ppermute x1, starting transfers between devices, per_device(): h_before = lax.ppermute(own, 'height', shift_pairs(height_size, 1))  4.92 us
    ppermute x1, starting transfers between devices, per_device(): t_before = lax.ppermute(sent, 'tm', shift_pairs(tm_size, 1))  4.66 us
  transfers between devices with their start and end apart: 16, of which 8 were waited for; matrix products, arithmetic and copies ran while one was open for 6% of the time, Pallas kernels for 13%

profile of v16, /device:TPU:97, one launch (start us, length us, event | category | flops | bytes accessed | tf_op | source)
XLA Modules:
  0.0 167.1 jit_solution(18094926491449540106)
XLA Ops:
  0.0 0.0 copy-start
  0.0 0.8 copy-done
  0.8 2.7 %collective-permute-start = (bf16[2,16,384]{2,1,0:T(8,128)(2,1)S(1)}, bf16[2,16,384]{2,1,0:T(8,128)(2,1)S(1)}, u32[]{:S(2)}, u32[]{:S(2)}) collective-permute-start(bf16[2,16,384]{2,1,0:T(8,128)(2,1)S(1)} %constant_dynamic-slice_fusion.3), channel_id=1, source_target_pairs={{0,16},{16,0},{32,48},{48,32},{64,80},{80,64},{96,112},{112,96},{1... | collective-permute-start | bytes 73736 | tf_op jit(solution)/shard_map/ppermute | solution.py:50
  3.5 1.4 collective-permute-done
  5.0 0.1 collective-permute-start.1
  5.1 4.9 %collective-permute-start.5 = (bf16[2,384,768]{2,1,0:T(8,128)(2,1)}, bf16[2,384,768]{2,1,0:T(8,128)(2,1)S(1)}, u32[]{:S(2)}, u32[]{:S(2)}) collective-permute-start(bf16[2,384,768]{2,1,0:T(8,128)(2,1)} %bitcast.2.rest_1_), channel_id=1, source_target_pairs={{0,4},{4,8},{8,12},{1,5},{5,9},{9,13},{2,6},{6,10},{10,14},{3,7},{... | collective-permute-start | bytes 3538952 | tf_op jit(solution)/shard_map/ppermute | solution.py:209
  10.0 1.9 %collective-permute-start.6 = (bf16[2,384,768]{2,1,0:T(8,128)(2,1)}, bf16[2,384,768]{2,1,0:T(8,128)(2,1)S(1)}, u32[]{:S(2)}, u32[]{:S(2)}) collective-permute-start(bf16[2,384,768]{2,1,0:T(8,128)(2,1)} %bitcast.2.rest_1_), channel_id=1, source_target_pairs={{4,0},{8,4},{12,8},{5,1},{9,5},{13,9},{6,2},{10,6},{14,10},{7,3},{... | collective-permute-start | bytes 3538952 | tf_op jit(solution)/shard_map/ppermute | solution.py:210
  12.0 0.0 collective-permute-done.1
  12.0 0.1 collective-permute-start.2
  12.1 7.1 %collective-permute-done.2 = bf16[2,64,384]{2,1,0:T(8,128)(2,1)S(1)} collective-permute-done((bf16[2,64,384]{2,1,0:T(8,128)(2,1)S(1)}, bf16[2,64,384]{2,1,0:T(8,128)(2,1)S(1)}, u32[]{:S(2)}, u32[]{:S(2)}) %collective-permute-start.2) | collective-permute-done | bytes 98336 | tf_op jit(solution)/shard_map/ppermute | solution.py:50
  19.3 4.2 %collective-permute-start.3 = (bf16[2,128,384]{2,1,0:T(8,128)(2,1)S(1)}, bf16[2,128,384]{2,1,0:T(8,128)(2,1)S(1)}, u32[]{:S(2)}, u32[]{:S(2)}) collective-permute-start(bf16[2,128,384]{2,1,0:T(8,128)(2,1)S(1)} %maximum_select_fusion.2), channel_id=1, source_target_pairs={{0,128},{16,144},{32,160},{48,176},{64,192},{80,208},{96,224},{112... | collective-permute-start | bytes 589832 | tf_op jit(solution)/shard_map/ppermute | solution.py:50
  23.5 0.8 pad_dynamic-slice_fusion
  24.2 0.1 copy.16
  24.3 0.1 lt.113
  24.4 0.1 copy.17
  24.5 0.1 lt.118
  24.6 0.6 slice.12
  25.2 0.6 slice.13
  25.8 7.8 %collective-permute-done.3 = bf16[2,128,384]{2,1,0:T(8,128)(2,1)S(1)} collective-permute-done((bf16[2,128,384]{2,1,0:T(8,128)(2,1)S(1)}, bf16[2,128,384]{2,1,0:T(8,128)(2,1)S(1)}, u32[]{:S(2)}, u32[]{:S(2)}) %collective-permute-start.3) | collective-permute-done | bytes 196640 | tf_op jit(solution)/shard_map/ppermute | solution.py:50
  33.6 0.1 maximum_select_fusion.1
  33.7 1.4 collective-permute-start.4
  35.1 1.3 fusion.8
  36.4 0.7 and_select_fusion.rest_4_.rest_2_
  37.1 0.0 collective-permute-done.4
  37.1 1.1 maximum_select_fusion.rest_0_
  38.1 0.0 collective-permute-done.5.rest_2_
  38.1 0.0 collective-permute-done.6.rest_3_
  38.1 0.0 copy-start.4
  38.2 4.7 %collective-permute-start.7 = (bf16[2,384,768]{2,1,0:T(8,128)(2,1)}, bf16[2,384,768]{2,1,0:T(8,128)(2,1)}, u32[]{:S(2)}, u32[]{:S(2)}) collective-permute-start(bf16[2,384,768]{2,1,0:T(8,128)(2,1)} %bitcast.2.rest_1_), channel_id=1, source_target_pairs={{0,16},{16,32},{32,48},{48,64},{64,80},{80,96},{96,112},{112,128},... | collective-permute-start | bytes 3538952 | tf_op jit(solution)/shard_map/ppermute | solution.py:229
  42.8 3.0 %collective-permute-start.8 = (bf16[2,384,768]{2,1,0:T(8,128)(2,1)}, bf16[2,384,768]{2,1,0:T(8,128)(2,1)}, u32[]{:S(2)}, u32[]{:S(2)}) collective-permute-start(bf16[2,384,768]{2,1,0:T(8,128)(2,1)} %bitcast.2.rest_1_), channel_id=1, source_target_pairs={{16,0},{32,16},{48,32},{64,48},{80,64},{96,80},{112,96},{128,112},... | collective-permute-start | bytes 3538952 | tf_op jit(solution)/shard_map/ppermute | solution.py:230
  45.9 0.0 copy-done.7
  45.9 0.7 copy.22.reach_ref
  46.5 0.0 copy-done.3
  46.5 0.0 copy-done.4
  46.5 12.9 %shard_map.82 = (f32[6,384,1]{2,1,0:T(8,128)}, f32[6,384,1]{2,1,0:T(8,128)}, f32[384,768]{1,0:T(8,128)}) custom-call(s32[6,2]{1,0:T(8,128)} %copy.22.reach_ref, bf16[384,768]{1,0:T(8,128)(2,1)} %bitcast.13, bf16[2,256,768]{2,1,0:T(8,128)(2,1)} %maximum_select_fusion.rest_0_, bf16[2,384,768]{2,1,0:T(8,128)(2,1)} %bitcast.2.rest_1_, ...), custom_call_target="tpu_custom_call" | custom-call | tf_op jit(solution)/shard_map/pallas_call | solution.py:198
  59.4 34.3 %collective-permute-done.7.rest_0_ = bf16[2,384,768]{2,1,0:T(8,128)(2,1)} collective-permute-done((bf16[2,384,768]{2,1,0:T(8,128)(2,1)}, bf16[2,384,768]{2,1,0:T(8,128)(2,1)}, u32[]{:S(2)}, u32[]{:S(2)}) %collective-permute-start.7) | collective-permute-done | bytes 1179680 | tf_op jit(solution)/shard_map/ppermute | solution.py:229
  93.8 2.2 %collective-permute-done.8.rest_1_ = bf16[2,384,768]{2,1,0:T(8,128)(2,1)} collective-permute-done((bf16[2,384,768]{2,1,0:T(8,128)(2,1)}, bf16[2,384,768]{2,1,0:T(8,128)(2,1)}, u32[]{:S(2)}, u32[]{:S(2)}) %collective-permute-start.8) | collective-permute-done | bytes 1179680 | tf_op jit(solution)/shard_map/ppermute | solution.py:230
  96.0 0.5 collective-permute-start.11
  96.4 1.9 %collective-permute-start.12 = (bf16[2,384,768]{2,1,0:T(8,128)(2,1)}, bf16[2,384,768]{2,1,0:T(8,128)(2,1)}, u32[]{:S(2)}, u32[]{:S(2)}) collective-permute-start(bf16[2,384,768]{2,1,0:T(8,128)(2,1)} %bitcast.2.rest_1_), channel_id=1, source_target_pairs={{20,8},{24,4},{36,24},{40,20},{52,40},{56,36},{68,56},{72,52},{84,... | collective-permute-start | bytes 3538952 | tf_op jit(solution)/shard_map/ppermute | solution.py:238
  98.4 1.9 %collective-permute-start.10 = (bf16[2,384,768]{2,1,0:T(8,128)(2,1)}, bf16[2,384,768]{2,1,0:T(8,128)(2,1)S(1)}, u32[]{:S(2)}, u32[]{:S(2)}) collective-permute-start(bf16[2,384,768]{2,1,0:T(8,128)(2,1)} %collective-permute-done.7.rest_0_), channel_id=1, source_target_pairs={{4,0},{8,4},{12,8},{5,1},{9,5},{13,9},{6,2},{10,6},{14,10},{7,3},{... | collective-permute-start | bytes 3538952 | tf_op jit(solution)/shard_map/ppermute | solution.py:236
  100.3 3.6 %collective-permute-start.9 = (bf16[2,384,768]{2,1,0:T(8,128)(2,1)}, bf16[2,384,768]{2,1,0:T(8,128)(2,1)S(1)}, u32[]{:S(2)}, u32[]{:S(2)}) collective-permute-start(bf16[2,384,768]{2,1,0:T(8,128)(2,1)} %collective-permute-done.7.rest_0_), channel_id=1, source_target_pairs={{0,4},{4,8},{8,12},{1,5},{5,9},{9,13},{2,6},{6,10},{10,14},{3,7},{... | collective-permute-start | bytes 3538952 | tf_op jit(solution)/shard_map/ppermute | solution.py:235
  104.0 0.8 copy.23.rest_8_
  104.8 9.2 %shard_map.83 = (f32[6,384,1]{2,1,0:T(8,128)}, f32[6,384,1]{2,1,0:T(8,128)}, f32[384,768]{1,0:T(8,128)}) custom-call(s32[6,2]{1,0:T(8,128)} %copy.22.reach_ref, bf16[384,768]{1,0:T(8,128)(2,1)} %bitcast.14, bf16[2,384,768]{2,1,0:T(8,128)(2,1)} %collective-permute-done.7.rest_0_, bf16[2,384,768]{2,1,0:T(8,128)(2,1)} %collective-permute-done.8.rest_1_, ...), custom_call_target="tpu_custom_call" | custom-call | tf_op jit(solution)/shard_map/pallas_call | solution.py:198
  114.0 0.0 collective-permute-done.11
  114.0 1.5 collective-permute-done.12
  115.5 3.2 %broadcast_select_fusion = (bf16[2,384,768]{2,1,0:T(8,128)(2,1)}, bf16[2,384,768]{2,1,0:T(8,128)(2,1)}) fusion(bf16[2,384,768]{2,1,0:T(8,128)(2,1)} %collective-permute-done.12, bf16[2,384,768]{2,1,0:T(8,128)(2,1)} %collective-permute-done.11, pred[]{:T(512)S(6)} %eq.32), kind=kLoop, calls=%fused_computation.3 | loop fusion | flops 1179648 | bytes 4718593 | tf_op jit(solution)/shard_map/jit(_where)/select_n | solution.py:246
  118.6 0.0 collective-permute-done.10.rest_1_
  118.7 0.0 collective-permute-done.9.rest_0_
  118.7 0.0 copy-start.2
  118.7 1.1 copy-done.1
  119.7 0.4 copy-done.2
  120.1 8.6 %shard_map.84 = bf16[384,768]{1,0:T(8,128)(2,1)} custom-call(s32[6,2]{1,0:T(8,128)} %copy.22.reach_ref, bf16[384,768]{1,0:T(8,128)(2,1)} %bitcast.15, bf16[2,384,768]{2,1,0:T(8,128)(2,1)} %copy-done.2, bf16[2,384,768]{2,1,0:T(8,128)(2,1)} %copy-done.1, bf16[2,384,768]{2,1,0:T(8,128)(2,1)} %get-tuple-element.45.rest_2_, ...), custom_call_target="tpu_custom_call" | custom-call | tf_op jit(solution)/shard_map/pallas_call | solution.py:198
  128.8 4.5 %convolution_convert_fusion = bf16[384,3072]{1,0:T(8,128)(2,1)S(1)} fusion(bf16[384,768]{1,0:T(8,128)(2,1)} %shard_map.84, bf16[768,3072]{1,0:T(8,128)(2,1)} %param.12), kind=kOutput, calls=%fused_computation | convolution fusion | flops 1813118976 | bytes 7667712 | tf_op jit(solution)/shard_map/dot_general | solution.py:252
  133.3 0.0 copy-start.5
  133.3 0.0 copy-start.6
  133.3 1.3 constant_dynamic-slice_fusion.2
  134.6 5.1 %collective-permute-start.13 = (bf16[384,768]{1,0:T(8,128)(2,1)}, bf16[384,768]{1,0:T(8,128)(2,1)}, u32[]{:S(2)}, u32[]{:S(2)}) collective-permute-start(bf16[384,768]{1,0:T(8,128)(2,1)} %get-tuple-element.41), channel_id=1, source_target_pairs={{0,2},{1,3},{2,0},{3,1},{4,6},{5,7},{6,4},{7,5},{8,10},{9,11},{10,... | collective-permute-start | bytes 1769480 | tf_op jit(solution)/shard_map/ppermute | solution.py:259
  139.7 0.5 collective-permute-start.14
  140.2 2.2 %collective-permute-start.15 = (bf16[384,768]{1,0:T(8,128)(2,1)}, bf16[384,768]{1,0:T(8,128)(2,1)}, u32[]{:S(2)}, u32[]{:S(2)}) collective-permute-start(bf16[384,768]{1,0:T(8,128)(2,1)} %get-tuple-element.42), channel_id=1, source_target_pairs={{0,3},{1,0},{2,1},{3,2},{4,7},{5,4},{6,5},{7,6},{8,11},{9,8},{10,9... | collective-permute-start | bytes 1769480 | tf_op jit(solution)/shard_map/ppermute | solution.py:259
  142.4 11.3 %collective-permute-done.13 = bf16[384,768]{1,0:T(8,128)(2,1)} collective-permute-done((bf16[384,768]{1,0:T(8,128)(2,1)}, bf16[384,768]{1,0:T(8,128)(2,1)}, u32[]{:S(2)}, u32[]{:S(2)}) %collective-permute-start.13) | collective-permute-done | bytes 589856 | tf_op jit(solution)/shard_map/ppermute | solution.py:259
  153.7 10.8 %collective-permute-done.14 = bf16[384,768]{1,0:T(8,128)(2,1)} collective-permute-done((bf16[384,768]{1,0:T(8,128)(2,1)}, bf16[384,768]{1,0:T(8,128)(2,1)}, u32[]{:S(2)}, u32[]{:S(2)}) %collective-permute-start.14) | collective-permute-done | bytes 589856 | tf_op jit(solution)/shard_map/ppermute | solution.py:259
  164.5 0.0 collective-permute-done.15
  164.5 0.0 copy-done.5
  164.5 2.6 %fusion.1 = bf16[1,1,384,768]{3,2,1,0:T(8,128)(2,1)} fusion(bf16[384,768]{1,0:T(8,128)(2,1)} %collective-permute-done.15, bf16[384,768]{1,0:T(8,128)(2,1)} %collective-permute-done.14, bf16[384,768]{1,0:T(8,128)(2,1)} %collective-permute-done.13, bf16[1,1,384,768]{3,2,1,0:T(8,128)(2,1)S(1)} %copy-done.5, bf16[384,3072]{1,0:T(8,128)(2,1)S(1)} %convolution_convert_fusion, ...), kind=kLoop, calls=%fused_computation.6 | loop fusion | flops 3244032 | bytes 3542020 | tf_op jit(solution)/shard_map/broadcast_in_dim | solution.py:264
  (9 shorter events, 0.1 us)
Async XLA Ops:
  0.0 0.8 copy-start
  0.8 4.2 %collective-permute-start = (bf16[2,16,384]{2,1,0:T(8,128)(2,1)S(1)}, bf16[2,16,384]{2,1,0:T(8,128)(2,1)S(1)}, u32[]{:S(2)}, u32[]{:S(2)}) collective-permute-start(bf16[2,16,384]{2,1,0:T(8,128)(2,1)S(1)} %constant_dynamic-slice_fusion.3), channel_id=1, source_target_pairs={{0,16},{16,0},{32,48},{48,32},{64,80},{80,64},{96,112},{112,96},{1... | collective-permute-start | bytes 73736 | tf_op jit(solution)/shard_map/ppermute | solution.py:50
  5.0 7.0 %collective-permute-start.1 = (bf16[2,32,384]{2,1,0:T(8,128)(2,1)S(1)}, bf16[2,32,384]{2,1,0:T(8,128)(2,1)S(1)}, u32[]{:S(2)}, u32[]{:S(2)}) collective-permute-start(bf16[2,32,384]{2,1,0:T(8,128)(2,1)S(1)} %maximum_select_fusion.4), channel_id=1, source_target_pairs={{0,32},{16,48},{32,0},{48,16},{64,96},{80,112},{96,64},{112,80},{1... | collective-permute-start | bytes 147464 | tf_op jit(solution)/shard_map/ppermute | solution.py:50
  5.1 33.0 %collective-permute-start.5 = (bf16[2,384,768]{2,1,0:T(8,128)(2,1)}, bf16[2,384,768]{2,1,0:T(8,128)(2,1)S(1)}, u32[]{:S(2)}, u32[]{:S(2)}) collective-permute-start(bf16[2,384,768]{2,1,0:T(8,128)(2,1)} %bitcast.2.rest_1_), channel_id=1, source_target_pairs={{0,4},{4,8},{8,12},{1,5},{5,9},{9,13},{2,6},{6,10},{10,14},{3,7},{... | collective-permute-start | bytes 3538952 | tf_op jit(solution)/shard_map/ppermute | solution.py:209
  10.0 28.1 %collective-permute-start.6 = (bf16[2,384,768]{2,1,0:T(8,128)(2,1)}, bf16[2,384,768]{2,1,0:T(8,128)(2,1)S(1)}, u32[]{:S(2)}, u32[]{:S(2)}) collective-permute-start(bf16[2,384,768]{2,1,0:T(8,128)(2,1)} %bitcast.2.rest_1_), channel_id=1, source_target_pairs={{4,0},{8,4},{12,8},{5,1},{9,5},{13,9},{6,2},{10,6},{14,10},{7,3},{... | collective-permute-start | bytes 3538952 | tf_op jit(solution)/shard_map/ppermute | solution.py:210
  12.0 7.2 %collective-permute-start.2 = (bf16[2,64,384]{2,1,0:T(8,128)(2,1)S(1)}, bf16[2,64,384]{2,1,0:T(8,128)(2,1)S(1)}, u32[]{:S(2)}, u32[]{:S(2)}) collective-permute-start(bf16[2,64,384]{2,1,0:T(8,128)(2,1)S(1)} %maximum_select_fusion.3), channel_id=1, source_target_pairs={{0,64},{16,80},{32,96},{48,112},{64,0},{80,16},{96,32},{112,48},{1... | collective-permute-start | bytes 294920 | tf_op jit(solution)/shard_map/ppermute | solution.py:50
  19.3 14.3 %collective-permute-start.3 = (bf16[2,128,384]{2,1,0:T(8,128)(2,1)S(1)}, bf16[2,128,384]{2,1,0:T(8,128)(2,1)S(1)}, u32[]{:S(2)}, u32[]{:S(2)}) collective-permute-start(bf16[2,128,384]{2,1,0:T(8,128)(2,1)S(1)} %maximum_select_fusion.2), channel_id=1, source_target_pairs={{0,128},{16,144},{32,160},{48,176},{64,192},{80,208},{96,224},{112... | collective-permute-start | bytes 589832 | tf_op jit(solution)/shard_map/ppermute | solution.py:50
  25.8 20.1 %copy-start.7 = (s32[6,2]{0,1:T(2,128)S(1)}, s32[6,2]{0,1:T(2,128)}, u32[]{:S(2)}) copy-start(s32[6,2]{0,1:T(2,128)} %param.14) | copy-start | bytes 148
  33.7 3.3 %collective-permute-start.4 = (bf16[2,256,384]{2,1,0:T(8,128)(2,1)S(1)}, bf16[2,256,384]{2,1,0:T(8,128)(2,1)S(1)}, u32[]{:S(2)}, u32[]{:S(2)}) collective-permute-start(bf16[2,256,384]{2,1,0:T(8,128)(2,1)S(1)} %maximum_select_fusion.1), channel_id=1, source_target_pairs={{0,4},{4,0},{8,12},{12,8},{1,5},{5,1},{9,13},{13,9},{2,6},{6,2},{1... | collective-permute-start | bytes 1179656 | tf_op jit(solution)/shard_map/ppermute | solution.py:59
  38.1 8.4 %copy-start.3 = (bf16[2,384,768]{2,1,0:T(8,128)(2,1)}, bf16[2,384,768]{2,1,0:T(8,128)(2,1)S(1)}, u32[]{:S(2)}) copy-start(bf16[2,384,768]{2,1,0:T(8,128)(2,1)S(1)} %collective-permute-done.5.rest_2_) | copy-start | bytes 3538948
  38.1 8.4 %copy-start.4 = (bf16[2,384,768]{2,1,0:T(8,128)(2,1)}, bf16[2,384,768]{2,1,0:T(8,128)(2,1)S(1)}, u32[]{:S(2)}) copy-start(bf16[2,384,768]{2,1,0:T(8,128)(2,1)S(1)} %collective-permute-done.6.rest_3_) | copy-start | bytes 3538948
  38.2 55.6 %collective-permute-start.7 = (bf16[2,384,768]{2,1,0:T(8,128)(2,1)}, bf16[2,384,768]{2,1,0:T(8,128)(2,1)}, u32[]{:S(2)}, u32[]{:S(2)}) collective-permute-start(bf16[2,384,768]{2,1,0:T(8,128)(2,1)} %bitcast.2.rest_1_), channel_id=1, source_target_pairs={{0,16},{16,32},{32,48},{48,64},{64,80},{80,96},{96,112},{112,128},... | collective-permute-start | bytes 3538952 | tf_op jit(solution)/shard_map/ppermute | solution.py:229
  42.8 53.1 %collective-permute-start.8 = (bf16[2,384,768]{2,1,0:T(8,128)(2,1)}, bf16[2,384,768]{2,1,0:T(8,128)(2,1)}, u32[]{:S(2)}, u32[]{:S(2)}) collective-permute-start(bf16[2,384,768]{2,1,0:T(8,128)(2,1)} %bitcast.2.rest_1_), channel_id=1, source_target_pairs={{16,0},{32,16},{48,32},{64,48},{80,64},{96,80},{112,96},{128,112},... | collective-permute-start | bytes 3538952 | tf_op jit(solution)/shard_map/ppermute | solution.py:230
  96.0 18.0 %collective-permute-start.11 = (bf16[2,384,768]{2,1,0:T(8,128)(2,1)}, bf16[2,384,768]{2,1,0:T(8,128)(2,1)}, u32[]{:S(2)}, u32[]{:S(2)}) collective-permute-start(bf16[2,384,768]{2,1,0:T(8,128)(2,1)} %collective-permute-done.8.rest_1_), channel_id=1, source_target_pairs={{0,4},{4,0},{8,12},{12,8},{1,5},{5,1},{9,13},{13,9},{2,6},{6,2},{1... | collective-permute-start | bytes 3538952 | tf_op jit(solution)/shard_map/ppermute | solution.py:237
  96.4 19.0 %collective-permute-start.12 = (bf16[2,384,768]{2,1,0:T(8,128)(2,1)}, bf16[2,384,768]{2,1,0:T(8,128)(2,1)}, u32[]{:S(2)}, u32[]{:S(2)}) collective-permute-start(bf16[2,384,768]{2,1,0:T(8,128)(2,1)} %bitcast.2.rest_1_), channel_id=1, source_target_pairs={{20,8},{24,4},{36,24},{40,20},{52,40},{56,36},{68,56},{72,52},{84,... | collective-permute-start | bytes 3538952 | tf_op jit(solution)/shard_map/ppermute | solution.py:238
  98.4 20.3 %collective-permute-start.10 = (bf16[2,384,768]{2,1,0:T(8,128)(2,1)}, bf16[2,384,768]{2,1,0:T(8,128)(2,1)S(1)}, u32[]{:S(2)}, u32[]{:S(2)}) collective-permute-start(bf16[2,384,768]{2,1,0:T(8,128)(2,1)} %collective-permute-done.7.rest_0_), channel_id=1, source_target_pairs={{4,0},{8,4},{12,8},{5,1},{9,5},{13,9},{6,2},{10,6},{14,10},{7,3},{... | collective-permute-start | bytes 3538952 | tf_op jit(solution)/shard_map/ppermute | solution.py:236
  100.3 18.4 %collective-permute-start.9 = (bf16[2,384,768]{2,1,0:T(8,128)(2,1)}, bf16[2,384,768]{2,1,0:T(8,128)(2,1)S(1)}, u32[]{:S(2)}, u32[]{:S(2)}) collective-permute-start(bf16[2,384,768]{2,1,0:T(8,128)(2,1)} %collective-permute-done.7.rest_0_), channel_id=1, source_target_pairs={{0,4},{4,8},{8,12},{1,5},{5,9},{9,13},{2,6},{6,10},{10,14},{3,7},{... | collective-permute-start | bytes 3538952 | tf_op jit(solution)/shard_map/ppermute | solution.py:235
  118.7 1.1 copy-start.1
  118.7 1.5 copy-start.2
  133.3 31.2 %copy-start.5 = (bf16[1,1,384,768]{3,2,1,0:T(8,128)(2,1)S(1)}, bf16[1,1,384,768]{3,2,1,0:T(8,128)(2,1)}, u32[]{:S(2)}) copy-start(bf16[1,1,384,768]{3,2,1,0:T(8,128)(2,1)} %param.11) | copy-start | bytes 1769476
  133.3 31.2 %copy-start.6 = (f32[768]{0:T(1024)S(1)}, f32[768]{0:T(1024)}, u32[]{:S(2)}) copy-start(f32[768]{0:T(1024)} %param.13) | copy-start | bytes 9220
  134.6 19.1 %collective-permute-start.13 = (bf16[384,768]{1,0:T(8,128)(2,1)}, bf16[384,768]{1,0:T(8,128)(2,1)}, u32[]{:S(2)}, u32[]{:S(2)}) collective-permute-start(bf16[384,768]{1,0:T(8,128)(2,1)} %get-tuple-element.41), channel_id=1, source_target_pairs={{0,2},{1,3},{2,0},{3,1},{4,6},{5,7},{6,4},{7,5},{8,10},{9,11},{10,... | collective-permute-start | bytes 1769480 | tf_op jit(solution)/shard_map/ppermute | solution.py:259
  139.7 24.8 %collective-permute-start.14 = (bf16[384,768]{1,0:T(8,128)(2,1)}, bf16[384,768]{1,0:T(8,128)(2,1)}, u32[]{:S(2)}, u32[]{:S(2)}) collective-permute-start(bf16[384,768]{1,0:T(8,128)(2,1)} %get-tuple-element.43), channel_id=1, source_target_pairs={{0,1},{1,2},{2,3},{3,0},{4,5},{5,6},{6,7},{7,4},{8,9},{9,10},{10,1... | collective-permute-start | bytes 1769480 | tf_op jit(solution)/shard_map/ppermute | solution.py:259
  140.2 24.3 %collective-permute-start.15 = (bf16[384,768]{1,0:T(8,128)(2,1)}, bf16[384,768]{1,0:T(8,128)(2,1)}, u32[]{:S(2)}, u32[]{:S(2)}) collective-permute-start(bf16[384,768]{1,0:T(8,128)(2,1)} %get-tuple-element.42), channel_id=1, source_target_pairs={{0,3},{1,0},{2,1},{3,2},{4,7},{5,4},{6,5},{7,6},{8,11},{9,8},{10,9... | collective-permute-start | bytes 1769480 | tf_op jit(solution)/shard_map/ppermute | solution.py:259

commit v17 on v16

--- a/solution.py
+++ b/solution.py
@@ -62,7 +62,7 @@
     return jnp.where(half == 0, low_first, high_first)
 
 
-def make_kernel(blocks, has_text, has_state, final):
+def make_kernel(blocks, extras, has_text, has_state, final, heads):
     count = len(blocks)
 
     def kernel(reach_ref, q_ref, *rest):
@@ -70,6 +70,8 @@
         text_ref = rest.pop(0) if has_text else None
         tile_refs = rest[:count]
         rest = rest[count:]
+        extra_of = dict(zip(extras, rest[:len(extras)]))
+        rest = rest[len(extras):]
         bias_ref = rest.pop(0)
         if has_state:
             m_in, l_in, acc_in = rest[:3]
@@ -106,6 +108,14 @@
             m_ref[...] = m_new
         reach_t = reach_ref[head, 0]
         reach_h = reach_ref[head, 1]
+        weight = reach_ref[heads, 0].astype(jnp.float32)
+
+        def load(tile_ref, b, part):
+            if b not in extra_of:
+                return tile_ref[part]
+            main = tile_ref[part].astype(jnp.float32)
+            other = extra_of[b][part].astype(jnp.float32)
+            return (main * weight + other * (1.0 - weight)).astype(jnp.bfloat16)
         groups = {}
         for tile_ref, b in zip(tile_refs, blocks):
             groups.setdefault((abs(b // 3 - 1), abs(b % 3 - 1)), []).append((tile_ref, b))
@@ -114,7 +124,7 @@
             def block(members=members):
                 scores = []
                 for tile_ref, b in members:
-                    s = lax.dot_general(q, tile_ref[0], dims, preferred_element_type=jnp.float32)
+                    s = lax.dot_general(q, load(tile_ref, b, 0), dims, preferred_element_type=jnp.float32)
                     scores.append(s * scale + bias_ref[b])
                 m_old = m_ref[...]
                 m_new = m_old
@@ -123,11 +133,11 @@
                 alpha = jnp.exp(m_old - m_new)
                 total = alpha * l_ref[...]
                 acc = alpha * acc_ref[...]
-                for s, (tile_ref, _) in zip(scores, members):
+                for s, (tile_ref, b) in zip(scores, members):
                     p = jnp.exp(s - m_new)
                     total = total + jnp.sum(p, axis=1, keepdims=True)
                     acc = acc + jnp.dot(
-                        p.astype(jnp.bfloat16), tile_ref[1], preferred_element_type=jnp.float32
+                        p.astype(jnp.bfloat16), load(tile_ref, b, 1), preferred_element_type=jnp.float32
                     )
                 l_ref[...] = total
                 acc_ref[...] = acc
@@ -149,7 +159,7 @@
     return kernel
 
 
-def attend(reach, queries, text, tiles, bias, state=None, qvalid=None):
+def attend(reach, queries, text, tiles, bias, state=None, qvalid=None, extra=None):
     tile_len, col_width = queries.shape
     heads = col_width // HD
     blocks = [b for _, _, b in tiles]
@@ -158,7 +168,7 @@
     if text is not None:
         specs.append(pl.BlockSpec((2, text.shape[1], HD), lambda h, r: (0, 0, h)))
         args.append(text)
-    for array, index, _ in tiles:
+    def add_tile(array, index):
         if index is None:
             specs.append(pl.BlockSpec((2, tile_len, HD), lambda h, r: (0, 0, h)))
         else:
@@ -166,6 +176,12 @@
                 pl.BlockSpec((None, 2, tile_len, HD), lambda h, r, i=index: (i, 0, 0, h))
             )
         args.append(array)
+
+    for array, index, _ in tiles:
+        add_tile(array, index)
+    extras = [b for b in blocks if b in (extra or {})]
+    for b in extras:
+        add_tile(*extra[b])
     specs.append(pl.BlockSpec(bias.shape, lambda h, r: (0, 0, 0)))
     args.append(bias)
     row_spec = pl.BlockSpec((None, tile_len, 1), lambda h, r: (h, 0, 0))
@@ -194,7 +210,7 @@
             pltpu.VMEM((tile_len, HD), jnp.float32),
         ],
     )
-    kernel = make_kernel(blocks, text is not None, state is not None, final)
+    kernel = make_kernel(blocks, extras, text is not None, state is not None, final, heads)
     return pl.pallas_call(kernel, grid_spec=grid_spec, out_shape=out_shape)(reach, *args)
 
 
@@ -229,6 +245,8 @@
     t_before = lax.ppermute(sent, "tm", shift_pairs(tm_size, 1))
     t_after = lax.ppermute(sent, "tm", shift_pairs(tm_size, -1))
     queries = image_q[0, 0]
+    odd = (lax.axis_index("height") % 2).astype(head_reach.dtype)
+    reach_odd = jnp.concatenate([head_reach, jnp.stack([odd, odd])[None]], axis=0)
     near = [(own, None, 4), (h_before, None, 3), (h_after, None, 5)]
     state = attend(head_reach, queries, text, near, bias)
     t_before, t_after, sent, state = lax.optimization_barrier((t_before, t_after, sent, state))
@@ -238,14 +256,9 @@
     diagonal = lax.ppermute(sent, ("tm", "height"), diagonal_pairs(tm_size, height_size, -1))
     across = [(t_before, None, 1), (t_after, None, 7)]
     state = attend(head_reach, queries, None, across, bias, state)
-    odd_height = lax.axis_index("height") % 2 == 1
-    corners = [
-        (earlier_low, None, 0),
-        (earlier_high, None, 2),
-        (jnp.where(odd_height, partner, diagonal), None, 6),
-        (jnp.where(odd_height, diagonal, partner), None, 8),
-    ]
-    attended = attend(head_reach, queries, None, corners, bias, state, qvalid)
+    corners = [(earlier_low, None, 0), (earlier_high, None, 2), (partner, None, 6), (diagonal, None, 8)]
+    extra = {6: (diagonal, None), 8: (partner, None)}
+    attended = attend(reach_odd, queries, None, corners, bias, state, qvalid, extra)
 
     mp_index = lax.axis_index("mp")
     chunk = out_weight.shape[1] // mp_size

time: 168 us -> 170 us (1.012)
  the two profiles are of different devices: /device:TPU:97 before, /device:TPU:33 now
where the time goes in v17:
time: 170 us; the launch traced here: 169 us
  waiting for transfers between devices  74.2 us (44%)
  starting transfers between devices  46.5 us (27%)
  Pallas kernels  31.2 us (18%)
  other arithmetic  6.61 us (4%)
  local copies, waits for them, and re-layouts  5.94 us (3%)
  matrix products  4.52 us (3%)
    ppermute x1, waiting for transfers between devices, per_device(): t_before = lax.ppermute(sent, 'tm', shift_pairs(tm_size, 1))  32.1 us
    pallas_call x3, Pallas kernels, attend(): pl.pallas_call(kernel, grid_spec=grid_spec, out_shape=out_shape)  31.2 us
    ppermute x3, waiting for transfers between devices, per_device(): received.append(lax.ppermute(part, 'mp', pairs))  24.1 us
    ppermute x4, waiting for transfers between devices, exchange(): other = lax.ppermute(block, 'tm', [(i, i ^ step) for i in range(devices)])  10.9 us
    ppermute x4, starting transfers between devices, exchange(): other = lax.ppermute(block, 'tm', [(i, i ^ step) for i in range(devices)])  10.1 us
    ppermute x3, starting transfers between devices, per_device(): received.append(lax.ppermute(part, 'mp', pairs))  8.14 us
    ppermute x1, starting transfers between devices, per_device(): lax.ppermute(sent, ('tm', 'height'), diagonal_pairs(tm_size, height_size,...  7.27 us
    ppermute x1, starting transfers between devices, per_device(): h_before = lax.ppermute(own, 'height', shift_pairs(height_size, 1))  4.92 us
  transfers between devices with their start and end apart: 16, of which 9 were waited for; matrix products, arithmetic and copies ran while one was open for 5% of the time, Pallas kernels for 13%

profile of v17, /device:TPU:33, one launch (start us, length us, event | category | flops | bytes accessed | tf_op | source)
XLA Modules:
  0.0 169.2 jit_solution(5626244016236300555)
XLA Ops:
  0.0 0.0 copy-start
  0.0 0.8 copy-done
  0.8 2.7 %collective-permute-start = (bf16[2,16,384]{2,1,0:T(8,128)(2,1)S(1)}, bf16[2,16,384]{2,1,0:T(8,128)(2,1)S(1)}, u32[]{:S(2)}, u32[]{:S(2)}) collective-permute-start(bf16[2,16,384]{2,1,0:T(8,128)(2,1)S(1)} %constant_dynamic-slice_fusion.3), channel_id=1, source_target_pairs={{0,16},{16,0},{32,48},{48,32},{64,80},{80,64},{96,112},{112,96},{1... | collective-permute-start | bytes 73736 | tf_op jit(solution)/shard_map/ppermute | solution.py:50
  3.5 1.4 collective-permute-done
  5.0 0.1 collective-permute-start.1
  5.1 4.9 %collective-permute-start.5 = (bf16[2,384,768]{2,1,0:T(8,128)(2,1)}, bf16[2,384,768]{2,1,0:T(8,128)(2,1)S(1)}, u32[]{:S(2)}, u32[]{:S(2)}) collective-permute-start(bf16[2,384,768]{2,1,0:T(8,128)(2,1)} %bitcast.19), channel_id=1, source_target_pairs={{0,4},{4,8},{8,12},{1,5},{5,9},{9,13},{2,6},{6,10},{10,14},{3,7},{... | collective-permute-start | bytes 3538952 | tf_op jit(solution)/shard_map/ppermute | solution.py:225
  10.0 2.0 %collective-permute-start.6 = (bf16[2,384,768]{2,1,0:T(8,128)(2,1)}, bf16[2,384,768]{2,1,0:T(8,128)(2,1)}, u32[]{:S(2)}, u32[]{:S(2)}) collective-permute-start(bf16[2,384,768]{2,1,0:T(8,128)(2,1)} %bitcast.20), channel_id=1, source_target_pairs={{4,0},{8,4},{12,8},{5,1},{9,5},{13,9},{6,2},{10,6},{14,10},{7,3},{... | collective-permute-start | bytes 3538952 | tf_op jit(solution)/shard_map/ppermute | solution.py:226
  12.0 0.0 collective-permute-done.1
  12.1 3.0 %collective-permute-start.2 = (bf16[2,64,384]{2,1,0:T(8,128)(2,1)S(1)}, bf16[2,64,384]{2,1,0:T(8,128)(2,1)S(1)}, u32[]{:S(2)}, u32[]{:S(2)}) collective-permute-start(bf16[2,64,384]{2,1,0:T(8,128)(2,1)S(1)} %maximum_select_fusion.3), channel_id=1, source_target_pairs={{0,64},{16,80},{32,96},{48,112},{64,0},{80,16},{96,32},{112,48},{1... | collective-permute-start | bytes 294920 | tf_op jit(solution)/shard_map/ppermute | solution.py:50
  15.1 4.3 %collective-permute-done.2 = bf16[2,64,384]{2,1,0:T(8,128)(2,1)S(1)} collective-permute-done((bf16[2,64,384]{2,1,0:T(8,128)(2,1)S(1)}, bf16[2,64,384]{2,1,0:T(8,128)(2,1)S(1)}, u32[]{:S(2)}, u32[]{:S(2)}) %collective-permute-start.2) | collective-permute-done | bytes 98336 | tf_op jit(solution)/shard_map/ppermute | solution.py:50
  19.4 4.2 %collective-permute-start.3 = (bf16[2,128,384]{2,1,0:T(8,128)(2,1)S(1)}, bf16[2,128,384]{2,1,0:T(8,128)(2,1)S(1)}, u32[]{:S(2)}, u32[]{:S(2)}) collective-permute-start(bf16[2,128,384]{2,1,0:T(8,128)(2,1)S(1)} %maximum_select_fusion.2), channel_id=1, source_target_pairs={{0,128},{16,144},{32,160},{48,176},{64,192},{80,208},{96,224},{112... | collective-permute-start | bytes 589832 | tf_op jit(solution)/shard_map/ppermute | solution.py:50
  23.6 0.8 pad_dynamic-slice_fusion
  24.4 0.1 copy.34
  24.5 0.1 lt.113
  24.6 0.1 copy.35
  24.7 0.1 lt.118
  24.8 0.6 slice.12
  25.4 0.6 slice.13
  26.0 5.2 %collective-permute-done.3 = bf16[2,128,384]{2,1,0:T(8,128)(2,1)S(1)} collective-permute-done((bf16[2,128,384]{2,1,0:T(8,128)(2,1)S(1)}, bf16[2,128,384]{2,1,0:T(8,128)(2,1)S(1)}, u32[]{:S(2)}, u32[]{:S(2)}) %collective-permute-start.3) | collective-permute-done | bytes 196640 | tf_op jit(solution)/shard_map/ppermute | solution.py:50
  31.1 0.1 maximum_select_fusion.1
  31.3 1.2 collective-permute-start.4
  32.5 1.3 fusion.8
  33.8 0.7 and_select_fusion.rest_4_.rest_2_.rest_6_
  34.4 0.0 collective-permute-done.4
  34.4 1.1 maximum_select_fusion.rest_0_
  35.6 0.0 collective-permute-done.5.rest_2_
  35.6 0.0 collective-permute-done.6.rest_3_
  35.6 0.0 copy-done.3
  35.6 4.7 %collective-permute-start.7 = (bf16[2,384,768]{2,1,0:T(8,128)(2,1)S(1)}, bf16[2,384,768]{2,1,0:T(8,128)(2,1)}, u32[]{:S(2)}, u32[]{:S(2)}) collective-permute-start(bf16[2,384,768]{2,1,0:T(8,128)(2,1)S(1)} %bitcast.23), channel_id=1, source_target_pairs={{0,16},{16,32},{32,48},{48,64},{64,80},{80,96},{96,112},{112,128},... | collective-permute-start | bytes 3538952 | tf_op jit(solution)/shard_map/ppermute | solution.py:245
  40.2 3.9 %collective-permute-start.8 = (bf16[2,384,768]{2,1,0:T(8,128)(2,1)S(1)}, bf16[2,384,768]{2,1,0:T(8,128)(2,1)}, u32[]{:S(2)}, u32[]{:S(2)}) collective-permute-start(bf16[2,384,768]{2,1,0:T(8,128)(2,1)S(1)} %bitcast.24), channel_id=1, source_target_pairs={{16,0},{32,16},{48,32},{64,48},{80,64},{96,80},{112,96},{128,112},... | collective-permute-start | bytes 3538952 | tf_op jit(solution)/shard_map/ppermute | solution.py:246
  44.1 0.0 copy-done.8
  44.2 0.7 copy.33.reach_ref
  44.8 0.0 copy-done.4
  44.8 13.9 %shard_map.82 = (f32[6,384,1]{2,1,0:T(8,128)}, f32[6,384,1]{2,1,0:T(8,128)}, f32[384,768]{1,0:T(8,128)}) custom-call(s32[6,2]{1,0:T(8,128)} %copy.33.reach_ref, bf16[384,768]{1,0:T(8,128)(2,1)} %bitcast.16, bf16[2,256,768]{2,1,0:T(8,128)(2,1)} %maximum_select_fusion.rest_0_, bf16[2,384,768]{2,1,0:T(8,128)(2,1)} %bitcast.21, bf16[2,384,768]{2,1,0:T(8,128)(2,1)} %copy-done.4, ...), custom_call_target="tpu_custom_call" | custom-call | tf_op jit(solution)/shard_map/pallas_call | solution.py:214
  58.8 32.1 %collective-permute-done.7.rest_0_ = bf16[2,384,768]{2,1,0:T(8,128)(2,1)} collective-permute-done((bf16[2,384,768]{2,1,0:T(8,128)(2,1)S(1)}, bf16[2,384,768]{2,1,0:T(8,128)(2,1)}, u32[]{:S(2)}, u32[]{:S(2)}) %collective-permute-start.7) | collective-permute-done | bytes 1179680 | tf_op jit(solution)/shard_map/ppermute | solution.py:245
  90.9 3.2 %collective-permute-done.8.rest_1_ = bf16[2,384,768]{2,1,0:T(8,128)(2,1)} collective-permute-done((bf16[2,384,768]{2,1,0:T(8,128)(2,1)S(1)}, bf16[2,384,768]{2,1,0:T(8,128)(2,1)}, u32[]{:S(2)}, u32[]{:S(2)}) %collective-permute-start.8) | collective-permute-done | bytes 1179680 | tf_op jit(solution)/shard_map/ppermute | solution.py:246
  94.0 2.4 %collective-permute-start.10 = (bf16[2,384,768]{2,1,0:T(8,128)(2,1)}, bf16[2,384,768]{2,1,0:T(8,128)(2,1)}, u32[]{:S(2)}, u32[]{:S(2)}) collective-permute-start(bf16[2,384,768]{2,1,0:T(8,128)(2,1)} %collective-permute-done.7.rest_0_), channel_id=1, source_target_pairs={{4,0},{8,4},{12,8},{5,1},{9,5},{13,9},{6,2},{10,6},{14,10},{7,3},{... | collective-permute-start | bytes 3538952 | tf_op jit(solution)/shard_map/ppermute | solution.py:254
  96.4 0.1 collective-permute-start.11
  96.5 7.3 %collective-permute-start.12 = (bf16[2,384,768]{2,1,0:T(8,128)(2,1)}, bf16[2,384,768]{2,1,0:T(8,128)(2,1)S(1)}, u32[]{:S(2)}, u32[]{:S(2)}) collective-permute-start(bf16[2,384,768]{2,1,0:T(8,128)(2,1)} %bitcast.22), channel_id=1, source_target_pairs={{20,8},{24,4},{36,24},{40,20},{52,40},{56,36},{68,56},{72,52},{84,... | collective-permute-start | bytes 3538952 | tf_op jit(solution)/shard_map/ppermute | solution.py:256
  103.8 1.9 %collective-permute-start.9 = (bf16[2,384,768]{2,1,0:T(8,128)(2,1)}, bf16[2,384,768]{2,1,0:T(8,128)(2,1)}, u32[]{:S(2)}, u32[]{:S(2)}) collective-permute-start(bf16[2,384,768]{2,1,0:T(8,128)(2,1)} %collective-permute-done.7.rest_0_), channel_id=1, source_target_pairs={{0,4},{4,8},{8,12},{1,5},{5,9},{9,13},{2,6},{6,10},{10,14},{3,7},{... | collective-permute-start | bytes 3538952 | tf_op jit(solution)/shard_map/ppermute | solution.py:253
  105.8 0.1 add_bitcast_fusion
  105.8 0.0 copy-done.6
  105.8 0.6 pad_add_fusion.reach_ref
  106.4 0.8 copy.40.rest_10_
  107.3 7.9 %shard_map.83 = (f32[6,384,1]{2,1,0:T(8,128)}, f32[6,384,1]{2,1,0:T(8,128)}, f32[384,768]{1,0:T(8,128)}) custom-call(s32[6,2]{1,0:T(8,128)} %copy.33.reach_ref, bf16[384,768]{1,0:T(8,128)(2,1)} %bitcast.17, bf16[2,384,768]{2,1,0:T(8,128)(2,1)} %collective-permute-done.7.rest_0_, bf16[2,384,768]{2,1,0:T(8,128)(2,1)} %collective-permute-done.8.rest_1_, ...), custom_call_target="tpu_custom_call" | custom-call | tf_op jit(solution)/shard_map/pallas_call | solution.py:214
  115.2 0.0 collective-permute-done.10.rest_1_
  115.2 0.0 collective-permute-done.11.rest_2_.rest_5_
  115.2 0.0 copy-start.1
  115.2 2.0 %collective-permute-done.12.rest_3_.rest_4_ = bf16[2,384,768]{2,1,0:T(8,128)(2,1)S(1)} collective-permute-done((bf16[2,384,768]{2,1,0:T(8,128)(2,1)}, bf16[2,384,768]{2,1,0:T(8,128)(2,1)S(1)}, u32[]{:S(2)}, u32[]{:S(2)}) %collective-permute-start.12) | collective-permute-done | bytes 1179680 | tf_op jit(solution)/shard_map/ppermute | solution.py:256
  117.2 1.9 %collective-permute-done.9.rest_0_ = bf16[2,384,768]{2,1,0:T(8,128)(2,1)} collective-permute-done((bf16[2,384,768]{2,1,0:T(8,128)(2,1)}, bf16[2,384,768]{2,1,0:T(8,128)(2,1)}, u32[]{:S(2)}, u32[]{:S(2)}) %collective-permute-start.9) | collective-permute-done | bytes 1179680 | tf_op jit(solution)/shard_map/ppermute | solution.py:253
  119.2 0.0 copy-done.1
  119.2 0.0 copy-done.2
  119.2 9.3 %shard_map.84 = bf16[384,768]{1,0:T(8,128)(2,1)} custom-call(s32[7,2]{1,0:T(8,128)} %pad_add_fusion.reach_ref, bf16[384,768]{1,0:T(8,128)(2,1)} %bitcast.18, bf16[2,384,768]{2,1,0:T(8,128)(2,1)} %collective-permute-done.9.rest_0_, bf16[2,384,768]{2,1,0:T(8,128)(2,1)} %collective-permute-done.10.rest_1_, bf16[2,384,768]{2,1,0:T(8,128)(2,1)} %copy-done.1, ...), custom_call_target="tpu_custom_call" | custom-call | tf_op jit(solution)/shard_map/pallas_call | solution.py:214
  128.5 4.5 %convolution_convert_fusion = bf16[384,3072]{1,0:T(8,128)(2,1)S(1)} fusion(bf16[384,768]{1,0:T(8,128)(2,1)} %shard_map.84, bf16[768,3072]{1,0:T(8,128)(2,1)} %param.12), kind=kOutput, calls=%fused_computation | convolution fusion | flops 1813118976 | bytes 7667712 | tf_op jit(solution)/shard_map/dot_general | solution.py:265
  133.0 0.0 copy-start.5
  133.0 0.0 copy-start.7
  133.0 1.3 constant_dynamic-slice_fusion.2
  134.3 5.5 %collective-permute-start.13 = (bf16[384,768]{1,0:T(8,128)(2,1)}, bf16[384,768]{1,0:T(8,128)(2,1)}, u32[]{:S(2)}, u32[]{:S(2)}) collective-permute-start(bf16[384,768]{1,0:T(8,128)(2,1)} %get-tuple-element.41), channel_id=1, source_target_pairs={{0,2},{1,3},{2,0},{3,1},{4,6},{5,7},{6,4},{7,5},{8,10},{9,11},{10,... | collective-permute-start | bytes 1769480 | tf_op jit(solution)/shard_map/ppermute | solution.py:272
  139.8 0.0 collective-permute-start.14
  139.8 2.7 %collective-permute-start.15 = (bf16[384,768]{1,0:T(8,128)(2,1)}, bf16[384,768]{1,0:T(8,128)(2,1)}, u32[]{:S(2)}, u32[]{:S(2)}) collective-permute-start(bf16[384,768]{1,0:T(8,128)(2,1)} %get-tuple-element.42), channel_id=1, source_target_pairs={{0,3},{1,0},{2,1},{3,2},{4,7},{5,4},{6,5},{7,6},{8,11},{9,8},{10,9... | collective-permute-start | bytes 1769480 | tf_op jit(solution)/shard_map/ppermute | solution.py:272
  142.5 10.9 %collective-permute-done.13 = bf16[384,768]{1,0:T(8,128)(2,1)} collective-permute-done((bf16[384,768]{1,0:T(8,128)(2,1)}, bf16[384,768]{1,0:T(8,128)(2,1)}, u32[]{:S(2)}, u32[]{:S(2)}) %collective-permute-start.13) | collective-permute-done | bytes 589856 | tf_op jit(solution)/shard_map/ppermute | solution.py:272
  153.4 13.2 %collective-permute-done.14 = bf16[384,768]{1,0:T(8,128)(2,1)} collective-permute-done((bf16[384,768]{1,0:T(8,128)(2,1)}, bf16[384,768]{1,0:T(8,128)(2,1)}, u32[]{:S(2)}, u32[]{:S(2)}) %collective-permute-start.14) | collective-permute-done | bytes 589856 | tf_op jit(solution)/shard_map/ppermute | solution.py:272
  166.5 0.0 collective-permute-done.15
  166.5 2.6 %fusion.1 = bf16[1,1,384,768]{3,2,1,0:T(8,128)(2,1)} fusion(bf16[384,768]{1,0:T(8,128)(2,1)} %collective-permute-done.15, bf16[384,768]{1,0:T(8,128)(2,1)} %collective-permute-done.14, bf16[384,768]{1,0:T(8,128)(2,1)} %collective-permute-done.13, bf16[1,1,384,768]{3,2,1,0:T(8,128)(2,1)S(1)} %copy-done.5, bf16[384,3072]{1,0:T(8,128)(2,1)S(1)} %convolution_convert_fusion, ...), kind=kLoop, calls=%fused_computation.4 | loop fusion | flops 3244032 | bytes 3542020 | tf_op jit(solution)/shard_map/broadcast_in_dim | solution.py:277
  (12 shorter events, 0.1 us)
Async XLA Ops:
  0.0 0.8 copy-start
  0.8 4.2 %collective-permute-start = (bf16[2,16,384]{2,1,0:T(8,128)(2,1)S(1)}, bf16[2,16,384]{2,1,0:T(8,128)(2,1)S(1)}, u32[]{:S(2)}, u32[]{:S(2)}) collective-permute-start(bf16[2,16,384]{2,1,0:T(8,128)(2,1)S(1)} %constant_dynamic-slice_fusion.3), channel_id=1, source_target_pairs={{0,16},{16,0},{32,48},{48,32},{64,80},{80,64},{96,112},{112,96},{1... | collective-permute-start | bytes 73736 | tf_op jit(solution)/shard_map/ppermute | solution.py:50
  5.0 7.0 %collective-permute-start.1 = (bf16[2,32,384]{2,1,0:T(8,128)(2,1)S(1)}, bf16[2,32,384]{2,1,0:T(8,128)(2,1)S(1)}, u32[]{:S(2)}, u32[]{:S(2)}) collective-permute-start(bf16[2,32,384]{2,1,0:T(8,128)(2,1)S(1)} %maximum_select_fusion.4), channel_id=1, source_target_pairs={{0,32},{16,48},{32,0},{48,16},{64,96},{80,112},{96,64},{112,80},{1... | collective-permute-start | bytes 147464 | tf_op jit(solution)/shard_map/ppermute | solution.py:50
  5.1 30.5 %collective-permute-start.5 = (bf16[2,384,768]{2,1,0:T(8,128)(2,1)}, bf16[2,384,768]{2,1,0:T(8,128)(2,1)S(1)}, u32[]{:S(2)}, u32[]{:S(2)}) collective-permute-start(bf16[2,384,768]{2,1,0:T(8,128)(2,1)} %bitcast.19), channel_id=1, source_target_pairs={{0,4},{4,8},{8,12},{1,5},{5,9},{9,13},{2,6},{6,10},{10,14},{3,7},{... | collective-permute-start | bytes 3538952 | tf_op jit(solution)/shard_map/ppermute | solution.py:225
  10.0 25.5 %collective-permute-start.6 = (bf16[2,384,768]{2,1,0:T(8,128)(2,1)}, bf16[2,384,768]{2,1,0:T(8,128)(2,1)}, u32[]{:S(2)}, u32[]{:S(2)}) collective-permute-start(bf16[2,384,768]{2,1,0:T(8,128)(2,1)} %bitcast.20), channel_id=1, source_target_pairs={{4,0},{8,4},{12,8},{5,1},{9,5},{13,9},{6,2},{10,6},{14,10},{7,3},{... | collective-permute-start | bytes 3538952 | tf_op jit(solution)/shard_map/ppermute | solution.py:226
  12.1 7.3 %collective-permute-start.2 = (bf16[2,64,384]{2,1,0:T(8,128)(2,1)S(1)}, bf16[2,64,384]{2,1,0:T(8,128)(2,1)S(1)}, u32[]{:S(2)}, u32[]{:S(2)}) collective-permute-start(bf16[2,64,384]{2,1,0:T(8,128)(2,1)S(1)} %maximum_select_fusion.3), channel_id=1, source_target_pairs={{0,64},{16,80},{32,96},{48,112},{64,0},{80,16},{96,32},{112,48},{1... | collective-permute-start | bytes 294920 | tf_op jit(solution)/shard_map/ppermute | solution.py:50
  19.4 11.7 %collective-permute-start.3 = (bf16[2,128,384]{2,1,0:T(8,128)(2,1)S(1)}, bf16[2,128,384]{2,1,0:T(8,128)(2,1)S(1)}, u32[]{:S(2)}, u32[]{:S(2)}) collective-permute-start(bf16[2,128,384]{2,1,0:T(8,128)(2,1)S(1)} %maximum_select_fusion.2), channel_id=1, source_target_pairs={{0,128},{16,144},{32,160},{48,176},{64,192},{80,208},{96,224},{112... | collective-permute-start | bytes 589832 | tf_op jit(solution)/shard_map/ppermute | solution.py:50
  26.0 9.6 %copy-start.3 = (bf16[1,1,2,384,768]{4,3,2,1,0:T(8,128)(2,1)S(1)}, bf16[1,1,2,384,768]{4,3,2,1,0:T(8,128)(2,1)}, u32[]{:S(2)}) copy-start(bf16[1,1,2,384,768]{4,3,2,1,0:T(8,128)(2,1)} %param.9) | copy-start | bytes 3538948
  26.0 18.2 %copy-start.8 = (s32[6,2]{0,1:T(2,128)S(1)}, s32[6,2]{0,1:T(2,128)}, u32[]{:S(2)}) copy-start(s32[6,2]{0,1:T(2,128)} %param.14) | copy-start | bytes 148
  31.3 3.2 %collective-permute-start.4 = (bf16[2,256,384]{2,1,0:T(8,128)(2,1)S(1)}, bf16[2,256,384]{2,1,0:T(8,128)(2,1)S(1)}, u32[]{:S(2)}, u32[]{:S(2)}) collective-permute-start(bf16[2,256,384]{2,1,0:T(8,128)(2,1)S(1)} %maximum_select_fusion.1), channel_id=1, source_target_pairs={{0,4},{4,0},{8,12},{12,8},{1,5},{5,1},{9,13},{13,9},{2,6},{6,2},{1... | collective-permute-start | bytes 1179656 | tf_op jit(solution)/shard_map/ppermute | solution.py:59
  35.6 9.3 %copy-start.4 = (bf16[2,384,768]{2,1,0:T(8,128)(2,1)}, bf16[2,384,768]{2,1,0:T(8,128)(2,1)S(1)}, u32[]{:S(2)}) copy-start(bf16[2,384,768]{2,1,0:T(8,128)(2,1)S(1)} %collective-permute-done.5.rest_2_) | copy-start | bytes 3538948
  35.6 55.3 %collective-permute-start.7 = (bf16[2,384,768]{2,1,0:T(8,128)(2,1)S(1)}, bf16[2,384,768]{2,1,0:T(8,128)(2,1)}, u32[]{:S(2)}, u32[]{:S(2)}) collective-permute-start(bf16[2,384,768]{2,1,0:T(8,128)(2,1)S(1)} %bitcast.23), channel_id=1, source_target_pairs={{0,16},{16,32},{32,48},{48,64},{64,80},{80,96},{96,112},{112,128},... | collective-permute-start | bytes 3538952 | tf_op jit(solution)/shard_map/ppermute | solution.py:245
  40.2 53.8 %collective-permute-start.8 = (bf16[2,384,768]{2,1,0:T(8,128)(2,1)S(1)}, bf16[2,384,768]{2,1,0:T(8,128)(2,1)}, u32[]{:S(2)}, u32[]{:S(2)}) collective-permute-start(bf16[2,384,768]{2,1,0:T(8,128)(2,1)S(1)} %bitcast.24), channel_id=1, source_target_pairs={{16,0},{32,16},{48,32},{64,48},{80,64},{96,80},{112,96},{128,112},... | collective-permute-start | bytes 3538952 | tf_op jit(solution)/shard_map/ppermute | solution.py:246
  44.8 61.0 %copy-start.6 = (s32[6,2]{1,0:T(8,128)S(1)}, s32[6,2]{1,0:T(8,128)}, u32[]{:S(2)}) copy-start(s32[6,2]{1,0:T(8,128)} %copy.33.reach_ref) | copy-start | bytes 148
  94.0 21.2 %collective-permute-start.10 = (bf16[2,384,768]{2,1,0:T(8,128)(2,1)}, bf16[2,384,768]{2,1,0:T(8,128)(2,1)}, u32[]{:S(2)}, u32[]{:S(2)}) collective-permute-start(bf16[2,384,768]{2,1,0:T(8,128)(2,1)} %collective-permute-done.7.rest_0_), channel_id=1, source_target_pairs={{4,0},{8,4},{12,8},{5,1},{9,5},{13,9},{6,2},{10,6},{14,10},{7,3},{... | collective-permute-start | bytes 3538952 | tf_op jit(solution)/shard_map/ppermute | solution.py:254
  96.4 18.8 %collective-permute-start.11 = (bf16[2,384,768]{2,1,0:T(8,128)(2,1)}, bf16[2,384,768]{2,1,0:T(8,128)(2,1)S(1)}, u32[]{:S(2)}, u32[]{:S(2)}) collective-permute-start(bf16[2,384,768]{2,1,0:T(8,128)(2,1)} %collective-permute-done.8.rest_1_), channel_id=1, source_target_pairs={{0,4},{4,0},{8,12},{12,8},{1,5},{5,1},{9,13},{13,9},{2,6},{6,2},{1... | collective-permute-start | bytes 3538952 | tf_op jit(solution)/shard_map/ppermute | solution.py:255
  96.5 20.7 %collective-permute-start.12 = (bf16[2,384,768]{2,1,0:T(8,128)(2,1)}, bf16[2,384,768]{2,1,0:T(8,128)(2,1)S(1)}, u32[]{:S(2)}, u32[]{:S(2)}) collective-permute-start(bf16[2,384,768]{2,1,0:T(8,128)(2,1)} %bitcast.22), channel_id=1, source_target_pairs={{20,8},{24,4},{36,24},{40,20},{52,40},{56,36},{68,56},{72,52},{84,... | collective-permute-start | bytes 3538952 | tf_op jit(solution)/shard_map/ppermute | solution.py:256
  103.8 15.4 %collective-permute-start.9 = (bf16[2,384,768]{2,1,0:T(8,128)(2,1)}, bf16[2,384,768]{2,1,0:T(8,128)(2,1)}, u32[]{:S(2)}, u32[]{:S(2)}) collective-permute-start(bf16[2,384,768]{2,1,0:T(8,128)(2,1)} %collective-permute-done.7.rest_0_), channel_id=1, source_target_pairs={{0,4},{4,8},{8,12},{1,5},{5,9},{9,13},{2,6},{6,10},{10,14},{3,7},{... | collective-permute-start | bytes 3538952 | tf_op jit(solution)/shard_map/ppermute | solution.py:253
  115.2 3.9 %copy-start.1 = (bf16[2,384,768]{2,1,0:T(8,128)(2,1)}, bf16[2,384,768]{2,1,0:T(8,128)(2,1)S(1)}, u32[]{:S(2)}) copy-start(bf16[2,384,768]{2,1,0:T(8,128)(2,1)S(1)} %collective-permute-done.11.rest_2_.rest_5_) | copy-start | bytes 3538948
  117.2 1.9 %copy-start.2 = (bf16[2,384,768]{2,1,0:T(8,128)(2,1)}, bf16[2,384,768]{2,1,0:T(8,128)(2,1)S(1)}, u32[]{:S(2)}) copy-start(bf16[2,384,768]{2,1,0:T(8,128)(2,1)S(1)} %collective-permute-done.12.rest_3_.rest_4_) | copy-start | bytes 3538948
  133.0 33.5 %copy-start.5 = (bf16[1,1,384,768]{3,2,1,0:T(8,128)(2,1)S(1)}, bf16[1,1,384,768]{3,2,1,0:T(8,128)(2,1)}, u32[]{:S(2)}) copy-start(bf16[1,1,384,768]{3,2,1,0:T(8,128)(2,1)} %param.11) | copy-start | bytes 1769476
  133.0 33.5 %copy-start.7 = (f32[768]{0:T(1024)S(1)}, f32[768]{0:T(1024)}, u32[]{:S(2)}) copy-start(f32[768]{0:T(1024)} %param.13) | copy-start | bytes 9220
  134.3 19.1 %collective-permute-start.13 = (bf16[384,768]{1,0:T(8,128)(2,1)}, bf16[384,768]{1,0:T(8,128)(2,1)}, u32[]{:S(2)}, u32[]{:S(2)}) collective-permute-start(bf16[384,768]{1,0:T(8,128)(2,1)} %get-tuple-element.41), channel_id=1, source_target_pairs={{0,2},{1,3},{2,0},{3,1},{4,6},{5,7},{6,4},{7,5},{8,10},{9,11},{10,... | collective-permute-start | bytes 1769480 | tf_op jit(solution)/shard_map/ppermute | solution.py:272
  139.8 26.7 %collective-permute-start.14 = (bf16[384,768]{1,0:T(8,128)(2,1)}, bf16[384,768]{1,0:T(8,128)(2,1)}, u32[]{:S(2)}, u32[]{:S(2)}) collective-permute-start(bf16[384,768]{1,0:T(8,128)(2,1)} %get-tuple-element.43), channel_id=1, source_target_pairs={{0,1},{1,2},{2,3},{3,0},{4,5},{5,6},{6,7},{7,4},{8,9},{9,10},{10,1... | collective-permute-start | bytes 1769480 | tf_op jit(solution)/shard_map/ppermute | solution.py:272
  139.8 26.7 %collective-permute-start.15 = (bf16[384,768]{1,0:T(8,128)(2,1)}, bf16[384,768]{1,0:T(8,128)(2,1)}, u32[]{:S(2)}, u32[]{:S(2)}) collective-permute-start(bf16[384,768]{1,0:T(8,128)(2,1)} %get-tuple-element.42), channel_id=1, source_target_pairs={{0,3},{1,0},{2,1},{3,2},{4,7},{5,4},{6,5},{7,6},{8,11},{9,8},{10,9... | collective-permute-start | bytes 1769480 | tf_op jit(solution)/shard_map/ppermute | solution.py:272

commit v18 on v16

--- a/solution.py
+++ b/solution.py
@@ -210,10 +210,9 @@
     h_after = lax.ppermute(own, "height", shift_pairs(height_size, -1))
     text_group = text_halves(text_kv)
     step = 1
-    while step < tm_size:
+    while 2 * step < tm_size:
         text_group = exchange(text_group, tm_size, step)
         step *= 2
-    text = join_halves(text_group)
     time_start = lax.axis_index("tm")
     height_start = lax.axis_index("height")
     zero_index = jnp.int32(0)
@@ -223,11 +222,14 @@
     bias = jnp.where(key_valid, 0.0, NEG).astype(jnp.float32).reshape(9, 1, tile_len)
     qvalid = key_valid[1, 1].astype(jnp.float32).reshape(tile_len, 1)
 
-    sent, text, h_before, h_after, bias, qvalid = lax.optimization_barrier(
-        (own, text, h_before, h_after, bias, qvalid)
+    sent, text_group, h_before, h_after, bias, qvalid = lax.optimization_barrier(
+        (own, text_group, h_before, h_after, bias, qvalid)
     )
     t_before = lax.ppermute(sent, "tm", shift_pairs(tm_size, 1))
     t_after = lax.ppermute(sent, "tm", shift_pairs(tm_size, -1))
+    if step < tm_size:
+        text_group = exchange(text_group, tm_size, step)
+    text = join_halves(text_group)
     queries = image_q[0, 0]
     near = [(own, None, 4), (h_before, None, 3), (h_after, None, 5)]
     state = attend(head_reach, queries, text, near, bias)

time: 168 us -> 157 us (0.935)
  waiting for transfers between devices: 76.5 us -> 68.9 us
  starting transfers between devices: 38.7 us -> 36.9 us
    ppermute x1, waiting for transfers between devices: 34.3 us -> 0.01 us  [per_device(): t_before = lax.ppermute(sent, 'tm', shift_pairs(tm_size, 1))]
    ppermute x4, waiting for transfers between devices: 16.3 us -> 43.2 us  [exchange(): other = lax.ppermute(block, 'tm', [(i, i ^ step) for i in range(devices)])]
    ppermute x1, waiting for transfers between devices: 2.19 us -> 0.01 us  [per_device(): t_after = lax.ppermute(sent, 'tm', shift_pairs(tm_size, -1))]
  transfers between devices with their start and end apart: 16 -> 16, of which waited for: 8 -> 9; matrix products, arithmetic and copies ran while one was open for 6% -> 7% of each run, Pallas kernels for 13% -> 14%
where the time goes in v18:
time: 157 us
  waiting for transfers between devices  68.9 us (44%)
  starting transfers between devices  36.9 us (24%)
  Pallas kernels  30.5 us (19%)
  other arithmetic  9.06 us (6%)
  local copies, waits for them, and re-layouts  6.58 us (4%)
  matrix products  4.52 us (3%)
    ppermute x4, waiting for transfers between devices, exchange(): other = lax.ppermute(block, 'tm', [(i, i ^ step) for i in range(devices)])  43.2 us
    pallas_call x3, Pallas kernels, attend(): pl.pallas_call(kernel, grid_spec=grid_spec, out_shape=out_shape)  30.5 us
    ppermute x3, waiting for transfers between devices, per_device(): received.append(lax.ppermute(part, 'mp', pairs))  22.3 us
    ppermute x3, starting transfers between devices, per_device(): received.append(lax.ppermute(part, 'mp', pairs))  8.72 us
    ppermute x4, starting transfers between devices, exchange(): other = lax.ppermute(block, 'tm', [(i, i ^ step) for i in range(devices)])  7.02 us
    dot_general x1, matrix products, per_device(): jnp.dot(attended, out_weight, preferred_element_type=jnp.float32)  4.52 us
    ppermute x1, starting transfers between devices, per_device(): t_after = lax.ppermute(sent, 'tm', shift_pairs(tm_size, -1))  3.92 us
    ppermute x1, starting transfers between devices, per_device(): h_before = lax.ppermute(own, 'height', shift_pairs(height_size, 1))  3.8 us
  transfers between devices with their start and end apart: 16, of which 9 were waited for; matrix products, arithmetic and copies ran while one was open for 7% of the time, Pallas kernels for 14%

profile of v18, /device:TPU:97, one launch (start us, length us, event | category | flops | bytes accessed | tf_op | source)
XLA Modules:
  0.0 156.8 jit_solution(11680858667768849226)
XLA Ops:
  0.0 0.0 copy-start
  0.0 3.8 %collective-permute-start.3 = (bf16[2,384,768]{2,1,0:T(8,128)(2,1)}, bf16[2,384,768]{2,1,0:T(8,128)(2,1)S(1)}, u32[]{:S(2)}, u32[]{:S(2)}) collective-permute-start(bf16[2,384,768]{2,1,0:T(8,128)(2,1)} %bitcast.2.rest_1_), channel_id=1, source_target_pairs={{0,4},{4,8},{8,12},{1,5},{5,9},{9,13},{2,6},{6,10},{10,14},{3,7},{... | collective-permute-start | bytes 3538952 | tf_op jit(solution)/shard_map/ppermute | solution.py:209
  3.8 1.9 %collective-permute-start.4 = (bf16[2,384,768]{2,1,0:T(8,128)(2,1)}, bf16[2,384,768]{2,1,0:T(8,128)(2,1)S(1)}, u32[]{:S(2)}, u32[]{:S(2)}) collective-permute-start(bf16[2,384,768]{2,1,0:T(8,128)(2,1)} %bitcast.2.rest_1_), channel_id=1, source_target_pairs={{4,0},{8,4},{12,8},{5,1},{9,5},{13,9},{6,2},{10,6},{14,10},{7,3},{... | collective-permute-start | bytes 3538952 | tf_op jit(solution)/shard_map/ppermute | solution.py:210
  5.8 0.0 copy-done
  5.8 2.5 %collective-permute-start = (bf16[2,16,384]{2,1,0:T(8,128)(2,1)S(1)}, bf16[2,16,384]{2,1,0:T(8,128)(2,1)S(1)}, u32[]{:S(2)}, u32[]{:S(2)}) collective-permute-start(bf16[2,16,384]{2,1,0:T(8,128)(2,1)S(1)} %constant_dynamic-slice_fusion.3), channel_id=1, source_target_pairs={{0,16},{16,0},{32,48},{48,32},{64,80},{80,64},{96,112},{112,96},{1... | collective-permute-start | bytes 73736 | tf_op jit(solution)/shard_map/ppermute | solution.py:50
  8.3 0.8 pad_dynamic-slice_fusion
  9.1 0.1 copy.16
  9.2 0.1 lt.113
  9.3 0.1 copy.17
  9.4 0.1 lt.118
  9.5 11.1 %collective-permute-done = bf16[2,16,384]{2,1,0:T(8,128)(2,1)S(1)} collective-permute-done((bf16[2,16,384]{2,1,0:T(8,128)(2,1)S(1)}, bf16[2,16,384]{2,1,0:T(8,128)(2,1)S(1)}, u32[]{:S(2)}, u32[]{:S(2)}) %collective-permute-start) | collective-permute-done | bytes 24608 | tf_op jit(solution)/shard_map/ppermute | solution.py:50
  20.6 0.1 collective-permute-start.1
  20.7 0.7 and_select_fusion.rest_4_.rest_2_
  21.4 0.6 slice.12
  22.0 0.6 slice.13
  22.6 1.1 collective-permute-done.1
  23.6 0.1 collective-permute-start.2
  23.7 1.3 fusion.8
  25.0 4.5 %collective-permute-done.2 = bf16[2,64,384]{2,1,0:T(8,128)(2,1)S(1)} collective-permute-done((bf16[2,64,384]{2,1,0:T(8,128)(2,1)S(1)}, bf16[2,64,384]{2,1,0:T(8,128)(2,1)S(1)}, u32[]{:S(2)}, u32[]{:S(2)}) %collective-permute-start.2) | collective-permute-done | bytes 98336 | tf_op jit(solution)/shard_map/ppermute | solution.py:50
  29.6 0.0 collective-permute-done.3.rest_2_
  29.6 0.0 copy-start.3
  29.6 0.0 collective-permute-done.4.rest_3_
  29.6 0.0 copy-start.4
  29.6 3.8 %collective-permute-start.5 = (bf16[2,384,768]{2,1,0:T(8,128)(2,1)}, bf16[2,384,768]{2,1,0:T(8,128)(2,1)}, u32[]{:S(2)}, u32[]{:S(2)}) collective-permute-start(bf16[2,384,768]{2,1,0:T(8,128)(2,1)} %bitcast.2.rest_1_), channel_id=1, source_target_pairs={{0,16},{16,32},{32,48},{48,64},{64,80},{80,96},{96,112},{112,128},... | collective-permute-start | bytes 3538952 | tf_op jit(solution)/shard_map/ppermute | solution.py:228
  33.4 3.9 %collective-permute-start.6 = (bf16[2,384,768]{2,1,0:T(8,128)(2,1)}, bf16[2,384,768]{2,1,0:T(8,128)(2,1)}, u32[]{:S(2)}, u32[]{:S(2)}) collective-permute-start(bf16[2,384,768]{2,1,0:T(8,128)(2,1)} %bitcast.2.rest_1_), channel_id=1, source_target_pairs={{16,0},{32,16},{48,32},{64,48},{80,64},{96,80},{112,96},{128,112},... | collective-permute-start | bytes 3538952 | tf_op jit(solution)/shard_map/ppermute | solution.py:229
  37.3 4.3 %collective-permute-start.7 = (bf16[2,128,384]{2,1,0:T(8,128)(2,1)S(1)}, bf16[2,128,384]{2,1,0:T(8,128)(2,1)S(1)}, u32[]{:S(2)}, u32[]{:S(2)}) collective-permute-start(bf16[2,128,384]{2,1,0:T(8,128)(2,1)S(1)} %maximum_select_fusion.2), channel_id=1, source_target_pairs={{0,128},{16,144},{32,160},{48,176},{64,192},{80,208},{96,224},{112... | collective-permute-start | bytes 589832 | tf_op jit(solution)/shard_map/ppermute | solution.py:50
  41.6 26.6 %collective-permute-done.7 = bf16[2,128,384]{2,1,0:T(8,128)(2,1)S(1)} collective-permute-done((bf16[2,128,384]{2,1,0:T(8,128)(2,1)S(1)}, bf16[2,128,384]{2,1,0:T(8,128)(2,1)S(1)}, u32[]{:S(2)}, u32[]{:S(2)}) %collective-permute-start.7) | collective-permute-done | bytes 196640 | tf_op jit(solution)/shard_map/ppermute | solution.py:50
  68.2 0.1 maximum_select_fusion.1
  68.3 0.1 collective-permute-start.8
  68.4 0.0 copy-done.7
  68.5 0.7 copy.22.reach_ref
  69.1 1.0 collective-permute-done.8
  70.2 1.1 maximum_select_fusion.rest_0_
  71.2 0.0 copy-done.3
  71.2 0.0 copy-done.4
  71.2 13.5 %shard_map.82 = (f32[6,384,1]{2,1,0:T(8,128)}, f32[6,384,1]{2,1,0:T(8,128)}, f32[384,768]{1,0:T(8,128)}) custom-call(s32[6,2]{1,0:T(8,128)} %copy.22.reach_ref, bf16[384,768]{1,0:T(8,128)(2,1)} %bitcast.13, bf16[2,256,768]{2,1,0:T(8,128)(2,1)} %maximum_select_fusion.rest_0_, bf16[2,384,768]{2,1,0:T(8,128)(2,1)} %bitcast.2.rest_1_, ...), custom_call_target="tpu_custom_call" | custom-call | tf_op jit(solution)/shard_map/pallas_call | solution.py:198
  84.7 0.0 collective-permute-done.5.rest_0_
  84.8 0.0 collective-permute-done.6.rest_1_
  84.8 0.2 collective-permute-start.11
  85.0 1.9 %collective-permute-start.12 = (bf16[2,384,768]{2,1,0:T(8,128)(2,1)}, bf16[2,384,768]{2,1,0:T(8,128)(2,1)}, u32[]{:S(2)}, u32[]{:S(2)}) collective-permute-start(bf16[2,384,768]{2,1,0:T(8,128)(2,1)} %bitcast.2.rest_1_), channel_id=1, source_target_pairs={{20,8},{24,4},{36,24},{40,20},{52,40},{56,36},{68,56},{72,52},{84,... | collective-permute-start | bytes 3538952 | tf_op jit(solution)/shard_map/ppermute | solution.py:240
  86.9 2.1 %collective-permute-start.10 = (bf16[2,384,768]{2,1,0:T(8,128)(2,1)}, bf16[2,384,768]{2,1,0:T(8,128)(2,1)S(1)}, u32[]{:S(2)}, u32[]{:S(2)}) collective-permute-start(bf16[2,384,768]{2,1,0:T(8,128)(2,1)} %collective-permute-done.5.rest_0_), channel_id=1, source_target_pairs={{4,0},{8,4},{12,8},{5,1},{9,5},{13,9},{6,2},{10,6},{14,10},{7,3},{... | collective-permute-start | bytes 3538952 | tf_op jit(solution)/shard_map/ppermute | solution.py:238
  89.0 3.5 %collective-permute-start.9 = (bf16[2,384,768]{2,1,0:T(8,128)(2,1)}, bf16[2,384,768]{2,1,0:T(8,128)(2,1)S(1)}, u32[]{:S(2)}, u32[]{:S(2)}) collective-permute-start(bf16[2,384,768]{2,1,0:T(8,128)(2,1)} %collective-permute-done.5.rest_0_), channel_id=1, source_target_pairs={{0,4},{4,8},{8,12},{1,5},{5,9},{9,13},{2,6},{6,10},{10,14},{3,7},{... | collective-permute-start | bytes 3538952 | tf_op jit(solution)/shard_map/ppermute | solution.py:237
  92.5 0.8 copy.23.rest_8_
  93.4 8.3 %shard_map.83 = (f32[6,384,1]{2,1,0:T(8,128)}, f32[6,384,1]{2,1,0:T(8,128)}, f32[384,768]{1,0:T(8,128)}) custom-call(s32[6,2]{1,0:T(8,128)} %copy.22.reach_ref, bf16[384,768]{1,0:T(8,128)(2,1)} %bitcast.14, bf16[2,384,768]{2,1,0:T(8,128)(2,1)} %collective-permute-done.5.rest_0_, bf16[2,384,768]{2,1,0:T(8,128)(2,1)} %collective-permute-done.6.rest_1_, ...), custom_call_target="tpu_custom_call" | custom-call | tf_op jit(solution)/shard_map/pallas_call | solution.py:198
  101.6 0.0 collective-permute-done.11
  101.6 2.4 %collective-permute-done.12 = bf16[2,384,768]{2,1,0:T(8,128)(2,1)} collective-permute-done((bf16[2,384,768]{2,1,0:T(8,128)(2,1)}, bf16[2,384,768]{2,1,0:T(8,128)(2,1)}, u32[]{:S(2)}, u32[]{:S(2)}) %collective-permute-start.12) | collective-permute-done | bytes 1179680 | tf_op jit(solution)/shard_map/ppermute | solution.py:240
  104.0 3.2 %broadcast_select_fusion = (bf16[2,384,768]{2,1,0:T(8,128)(2,1)}, bf16[2,384,768]{2,1,0:T(8,128)(2,1)}) fusion(bf16[2,384,768]{2,1,0:T(8,128)(2,1)} %collective-permute-done.12, bf16[2,384,768]{2,1,0:T(8,128)(2,1)} %collective-permute-done.11, pred[]{:T(512)S(6)} %eq.32), kind=kLoop, calls=%fused_computation.3 | loop fusion | flops 1179648 | bytes 4718593 | tf_op jit(solution)/shard_map/jit(_where)/select_n | solution.py:248
  107.2 0.0 collective-permute-done.10.rest_1_
  107.2 0.0 collective-permute-done.9.rest_0_
  107.2 1.1 copy-done.1
  108.3 0.4 copy-done.2
  108.7 8.7 %shard_map.84 = bf16[384,768]{1,0:T(8,128)(2,1)} custom-call(s32[6,2]{1,0:T(8,128)} %copy.22.reach_ref, bf16[384,768]{1,0:T(8,128)(2,1)} %bitcast.15, bf16[2,384,768]{2,1,0:T(8,128)(2,1)} %copy-done.2, bf16[2,384,768]{2,1,0:T(8,128)(2,1)} %copy-done.1, bf16[2,384,768]{2,1,0:T(8,128)(2,1)} %get-tuple-element.45.rest_2_, ...), custom_call_target="tpu_custom_call" | custom-call | tf_op jit(solution)/shard_map/pallas_call | solution.py:198
  117.3 4.5 %convolution_convert_fusion = bf16[384,3072]{1,0:T(8,128)(2,1)S(1)} fusion(bf16[384,768]{1,0:T(8,128)(2,1)} %shard_map.84, bf16[768,3072]{1,0:T(8,128)(2,1)} %param.12), kind=kOutput, calls=%fused_computation | convolution fusion | flops 1813118976 | bytes 7667712 | tf_op jit(solution)/shard_map/dot_general | solution.py:254
  121.9 0.0 copy-start.5
  121.9 0.0 copy-start.6
  121.9 1.3 constant_dynamic-slice_fusion.2
  123.2 6.0 %collective-permute-start.13 = (bf16[384,768]{1,0:T(8,128)(2,1)}, bf16[384,768]{1,0:T(8,128)(2,1)}, u32[]{:S(2)}, u32[]{:S(2)}) collective-permute-start(bf16[384,768]{1,0:T(8,128)(2,1)} %get-tuple-element.41), channel_id=1, source_target_pairs={{0,2},{1,3},{2,0},{3,1},{4,6},{5,7},{6,4},{7,5},{8,10},{9,11},{10,... | collective-permute-start | bytes 1769480 | tf_op jit(solution)/shard_map/ppermute | solution.py:261
  129.2 0.3 collective-permute-start.14
  129.6 2.3 %collective-permute-start.15 = (bf16[384,768]{1,0:T(8,128)(2,1)}, bf16[384,768]{1,0:T(8,128)(2,1)}, u32[]{:S(2)}, u32[]{:S(2)}) collective-permute-start(bf16[384,768]{1,0:T(8,128)(2,1)} %get-tuple-element.42), channel_id=1, source_target_pairs={{0,3},{1,0},{2,1},{3,2},{4,7},{5,4},{6,5},{7,6},{8,11},{9,8},{10,9... | collective-permute-start | bytes 1769480 | tf_op jit(solution)/shard_map/ppermute | solution.py:261
  131.9 11.3 %collective-permute-done.13 = bf16[384,768]{1,0:T(8,128)(2,1)} collective-permute-done((bf16[384,768]{1,0:T(8,128)(2,1)}, bf16[384,768]{1,0:T(8,128)(2,1)}, u32[]{:S(2)}, u32[]{:S(2)}) %collective-permute-start.13) | collective-permute-done | bytes 589856 | tf_op jit(solution)/shard_map/ppermute | solution.py:261
  143.2 10.1 %collective-permute-done.14 = bf16[384,768]{1,0:T(8,128)(2,1)} collective-permute-done((bf16[384,768]{1,0:T(8,128)(2,1)}, bf16[384,768]{1,0:T(8,128)(2,1)}, u32[]{:S(2)}, u32[]{:S(2)}) %collective-permute-start.14) | collective-permute-done | bytes 589856 | tf_op jit(solution)/shard_map/ppermute | solution.py:261
  153.3 0.9 collective-permute-done.15
  154.2 0.0 copy-done.5
  154.2 2.6 %fusion.1 = bf16[1,1,384,768]{3,2,1,0:T(8,128)(2,1)} fusion(bf16[384,768]{1,0:T(8,128)(2,1)} %collective-permute-done.15, bf16[384,768]{1,0:T(8,128)(2,1)} %collective-permute-done.14, bf16[384,768]{1,0:T(8,128)(2,1)} %collective-permute-done.13, bf16[1,1,384,768]{3,2,1,0:T(8,128)(2,1)S(1)} %copy-done.5, bf16[384,3072]{1,0:T(8,128)(2,1)S(1)} %convolution_convert_fusion, ...), kind=kLoop, calls=%fused_computation.6 | loop fusion | flops 3244032 | bytes 3542020 | tf_op jit(solution)/shard_map/broadcast_in_dim | solution.py:266
  (9 shorter events, 0.1 us)
Async XLA Ops:
  0.0 5.8 %copy-start = (bf16[2,16,768]{2,1,0:T(8,128)(2,1)S(1)}, bf16[2,16,768]{2,1,0:T(8,128)(2,1)}, u32[]{:S(2)}) copy-start(bf16[2,16,768]{2,1,0:T(8,128)(2,1)} %param.10) | copy-start | bytes 147460
  0.0 68.4 %copy-start.7 = (s32[6,2]{0,1:T(2,128)S(1)}, s32[6,2]{0,1:T(2,128)}, u32[]{:S(2)}) copy-start(s32[6,2]{0,1:T(2,128)} %param.14) | copy-start | bytes 148
  0.0 29.6 %collective-permute-start.3 = (bf16[2,384,768]{2,1,0:T(8,128)(2,1)}, bf16[2,384,768]{2,1,0:T(8,128)(2,1)S(1)}, u32[]{:S(2)}, u32[]{:S(2)}) collective-permute-start(bf16[2,384,768]{2,1,0:T(8,128)(2,1)} %bitcast.2.rest_1_), channel_id=1, source_target_pairs={{0,4},{4,8},{8,12},{1,5},{5,9},{9,13},{2,6},{6,10},{10,14},{3,7},{... | collective-permute-start | bytes 3538952 | tf_op jit(solution)/shard_map/ppermute | solution.py:209
  3.8 25.8 %collective-permute-start.4 = (bf16[2,384,768]{2,1,0:T(8,128)(2,1)}, bf16[2,384,768]{2,1,0:T(8,128)(2,1)S(1)}, u32[]{:S(2)}, u32[]{:S(2)}) collective-permute-start(bf16[2,384,768]{2,1,0:T(8,128)(2,1)} %bitcast.2.rest_1_), channel_id=1, source_target_pairs={{4,0},{8,4},{12,8},{5,1},{9,5},{13,9},{6,2},{10,6},{14,10},{7,3},{... | collective-permute-start | bytes 3538952 | tf_op jit(solution)/shard_map/ppermute | solution.py:210
  5.8 14.8 %collective-permute-start = (bf16[2,16,384]{2,1,0:T(8,128)(2,1)S(1)}, bf16[2,16,384]{2,1,0:T(8,128)(2,1)S(1)}, u32[]{:S(2)}, u32[]{:S(2)}) collective-permute-start(bf16[2,16,384]{2,1,0:T(8,128)(2,1)S(1)} %constant_dynamic-slice_fusion.3), channel_id=1, source_target_pairs={{0,16},{16,0},{32,48},{48,32},{64,80},{80,64},{96,112},{112,96},{1... | collective-permute-start | bytes 73736 | tf_op jit(solution)/shard_map/ppermute | solution.py:50
  20.6 3.0 %collective-permute-start.1 = (bf16[2,32,384]{2,1,0:T(8,128)(2,1)S(1)}, bf16[2,32,384]{2,1,0:T(8,128)(2,1)S(1)}, u32[]{:S(2)}, u32[]{:S(2)}) collective-permute-start(bf16[2,32,384]{2,1,0:T(8,128)(2,1)S(1)} %maximum_select_fusion.4), channel_id=1, source_target_pairs={{0,32},{16,48},{32,0},{48,16},{64,96},{80,112},{96,64},{112,80},{1... | collective-permute-start | bytes 147464 | tf_op jit(solution)/shard_map/ppermute | solution.py:50
  23.6 5.9 %collective-permute-start.2 = (bf16[2,64,384]{2,1,0:T(8,128)(2,1)S(1)}, bf16[2,64,384]{2,1,0:T(8,128)(2,1)S(1)}, u32[]{:S(2)}, u32[]{:S(2)}) collective-permute-start(bf16[2,64,384]{2,1,0:T(8,128)(2,1)S(1)} %maximum_select_fusion.3), channel_id=1, source_target_pairs={{0,64},{16,80},{32,96},{48,112},{64,0},{80,16},{96,32},{112,48},{1... | collective-permute-start | bytes 294920 | tf_op jit(solution)/shard_map/ppermute | solution.py:50
  29.6 41.6 %copy-start.3 = (bf16[2,384,768]{2,1,0:T(8,128)(2,1)}, bf16[2,384,768]{2,1,0:T(8,128)(2,1)S(1)}, u32[]{:S(2)}) copy-start(bf16[2,384,768]{2,1,0:T(8,128)(2,1)S(1)} %collective-permute-done.3.rest_2_) | copy-start | bytes 3538948
  29.6 41.6 %copy-start.4 = (bf16[2,384,768]{2,1,0:T(8,128)(2,1)}, bf16[2,384,768]{2,1,0:T(8,128)(2,1)S(1)}, u32[]{:S(2)}) copy-start(bf16[2,384,768]{2,1,0:T(8,128)(2,1)S(1)} %collective-permute-done.4.rest_3_) | copy-start | bytes 3538948
  29.6 55.1 %collective-permute-start.5 = (bf16[2,384,768]{2,1,0:T(8,128)(2,1)}, bf16[2,384,768]{2,1,0:T(8,128)(2,1)}, u32[]{:S(2)}, u32[]{:S(2)}) collective-permute-start(bf16[2,384,768]{2,1,0:T(8,128)(2,1)} %bitcast.2.rest_1_), channel_id=1, source_target_pairs={{0,16},{16,32},{32,48},{48,64},{64,80},{80,96},{96,112},{112,128},... | collective-permute-start | bytes 3538952 | tf_op jit(solution)/shard_map/ppermute | solution.py:228
  33.4 51.3 %collective-permute-start.6 = (bf16[2,384,768]{2,1,0:T(8,128)(2,1)}, bf16[2,384,768]{2,1,0:T(8,128)(2,1)}, u32[]{:S(2)}, u32[]{:S(2)}) collective-permute-start(bf16[2,384,768]{2,1,0:T(8,128)(2,1)} %bitcast.2.rest_1_), channel_id=1, source_target_pairs={{16,0},{32,16},{48,32},{64,48},{80,64},{96,80},{112,96},{128,112},... | collective-permute-start | bytes 3538952 | tf_op jit(solution)/shard_map/ppermute | solution.py:229
  37.3 30.9 %collective-permute-start.7 = (bf16[2,128,384]{2,1,0:T(8,128)(2,1)S(1)}, bf16[2,128,384]{2,1,0:T(8,128)(2,1)S(1)}, u32[]{:S(2)}, u32[]{:S(2)}) collective-permute-start(bf16[2,128,384]{2,1,0:T(8,128)(2,1)S(1)} %maximum_select_fusion.2), channel_id=1, source_target_pairs={{0,128},{16,144},{32,160},{48,176},{64,192},{80,208},{96,224},{112... | collective-permute-start | bytes 589832 | tf_op jit(solution)/shard_map/ppermute | solution.py:50
  68.3 1.8 %collective-permute-start.8 = (bf16[2,256,384]{2,1,0:T(8,128)(2,1)S(1)}, bf16[2,256,384]{2,1,0:T(8,128)(2,1)S(1)}, u32[]{:S(2)}, u32[]{:S(2)}) collective-permute-start(bf16[2,256,384]{2,1,0:T(8,128)(2,1)S(1)} %maximum_select_fusion.1), channel_id=1, source_target_pairs={{0,4},{4,0},{8,12},{12,8},{1,5},{5,1},{9,13},{13,9},{2,6},{6,2},{1... | collective-permute-start | bytes 1179656 | tf_op jit(solution)/shard_map/ppermute | solution.py:59
  84.8 16.9 %collective-permute-start.11 = (bf16[2,384,768]{2,1,0:T(8,128)(2,1)}, bf16[2,384,768]{2,1,0:T(8,128)(2,1)}, u32[]{:S(2)}, u32[]{:S(2)}) collective-permute-start(bf16[2,384,768]{2,1,0:T(8,128)(2,1)} %collective-permute-done.6.rest_1_), channel_id=1, source_target_pairs={{0,4},{4,0},{8,12},{12,8},{1,5},{5,1},{9,13},{13,9},{2,6},{6,2},{1... | collective-permute-start | bytes 3538952 | tf_op jit(solution)/shard_map/ppermute | solution.py:239
  85.0 19.0 %collective-permute-start.12 = (bf16[2,384,768]{2,1,0:T(8,128)(2,1)}, bf16[2,384,768]{2,1,0:T(8,128)(2,1)}, u32[]{:S(2)}, u32[]{:S(2)}) collective-permute-start(bf16[2,384,768]{2,1,0:T(8,128)(2,1)} %bitcast.2.rest_1_), channel_id=1, source_target_pairs={{20,8},{24,4},{36,24},{40,20},{52,40},{56,36},{68,56},{72,52},{84,... | collective-permute-start | bytes 3538952 | tf_op jit(solution)/shard_map/ppermute | solution.py:240
  86.9 20.3 %collective-permute-start.10 = (bf16[2,384,768]{2,1,0:T(8,128)(2,1)}, bf16[2,384,768]{2,1,0:T(8,128)(2,1)S(1)}, u32[]{:S(2)}, u32[]{:S(2)}) collective-permute-start(bf16[2,384,768]{2,1,0:T(8,128)(2,1)} %collective-permute-done.5.rest_0_), channel_id=1, source_target_pairs={{4,0},{8,4},{12,8},{5,1},{9,5},{13,9},{6,2},{10,6},{14,10},{7,3},{... | collective-permute-start | bytes 3538952 | tf_op jit(solution)/shard_map/ppermute | solution.py:238
  89.0 18.2 %collective-permute-start.9 = (bf16[2,384,768]{2,1,0:T(8,128)(2,1)}, bf16[2,384,768]{2,1,0:T(8,128)(2,1)S(1)}, u32[]{:S(2)}, u32[]{:S(2)}) collective-permute-start(bf16[2,384,768]{2,1,0:T(8,128)(2,1)} %collective-permute-done.5.rest_0_), channel_id=1, source_target_pairs={{0,4},{4,8},{8,12},{1,5},{5,9},{9,13},{2,6},{6,10},{10,14},{3,7},{... | collective-permute-start | bytes 3538952 | tf_op jit(solution)/shard_map/ppermute | solution.py:237
  107.2 1.1 copy-start.1
  107.2 1.5 copy-start.2
  121.9 32.3 %copy-start.5 = (bf16[1,1,384,768]{3,2,1,0:T(8,128)(2,1)S(1)}, bf16[1,1,384,768]{3,2,1,0:T(8,128)(2,1)}, u32[]{:S(2)}) copy-start(bf16[1,1,384,768]{3,2,1,0:T(8,128)(2,1)} %param.11) | copy-start | bytes 1769476
  121.9 32.3 %copy-start.6 = (f32[768]{0:T(1024)S(1)}, f32[768]{0:T(1024)}, u32[]{:S(2)}) copy-start(f32[768]{0:T(1024)} %param.13) | copy-start | bytes 9220
  123.2 20.1 %collective-permute-start.13 = (bf16[384,768]{1,0:T(8,128)(2,1)}, bf16[384,768]{1,0:T(8,128)(2,1)}, u32[]{:S(2)}, u32[]{:S(2)}) collective-permute-start(bf16[384,768]{1,0:T(8,128)(2,1)} %get-tuple-element.41), channel_id=1, source_target_pairs={{0,2},{1,3},{2,0},{3,1},{4,6},{5,7},{6,4},{7,5},{8,10},{9,11},{10,... | collective-permute-start | bytes 1769480 | tf_op jit(solution)/shard_map/ppermute | solution.py:261
  129.2 24.1 %collective-permute-start.14 = (bf16[384,768]{1,0:T(8,128)(2,1)}, bf16[384,768]{1,0:T(8,128)(2,1)}, u32[]{:S(2)}, u32[]{:S(2)}) collective-permute-start(bf16[384,768]{1,0:T(8,128)(2,1)} %get-tuple-element.43), channel_id=1, source_target_pairs={{0,1},{1,2},{2,3},{3,0},{4,5},{5,6},{6,7},{7,4},{8,9},{9,10},{10,1... | collective-permute-start | bytes 1769480 | tf_op jit(solution)/shard_map/ppermute | solution.py:261
  129.6 24.6 %collective-permute-start.15 = (bf16[384,768]{1,0:T(8,128)(2,1)}, bf16[384,768]{1,0:T(8,128)(2,1)}, u32[]{:S(2)}, u32[]{:S(2)}) collective-permute-start(bf16[384,768]{1,0:T(8,128)(2,1)} %get-tuple-element.42), channel_id=1, source_target_pairs={{0,3},{1,0},{2,1},{3,2},{4,7},{5,4},{6,5},{7,6},{8,11},{9,8},{10,9... | collective-permute-start | bytes 1769480 | tf_op jit(solution)/shard_map/ppermute | solution.py:261

commit v19 on v18

--- a/solution.py
+++ b/solution.py
@@ -210,7 +210,7 @@
     h_after = lax.ppermute(own, "height", shift_pairs(height_size, -1))
     text_group = text_halves(text_kv)
     step = 1
-    while 2 * step < tm_size:
+    while 4 * step < tm_size:
         text_group = exchange(text_group, tm_size, step)
         step *= 2
     time_start = lax.axis_index("tm")
@@ -227,8 +227,9 @@
     )
     t_before = lax.ppermute(sent, "tm", shift_pairs(tm_size, 1))
     t_after = lax.ppermute(sent, "tm", shift_pairs(tm_size, -1))
-    if step < tm_size:
+    while step < tm_size:
         text_group = exchange(text_group, tm_size, step)
+        step *= 2
     text = join_halves(text_group)
     queries = image_q[0, 0]
     near = [(own, None, 4), (h_before, None, 3), (h_after, None, 5)]

time: 157 us -> 170 us (1.083)
  the two profiles are of different devices: /device:TPU:97 before, /device:TPU:37 now
where the time goes in v19:
time: 170 us; the launch traced here: 169 us
  waiting for transfers between devices  66.5 us (39%)
  starting transfers between devices  51.6 us (30%)
  Pallas kernels  30.6 us (18%)
  other arithmetic  9.07 us (5%)
  local copies, waits for them, and re-layouts  6.16 us (4%)
  matrix products  4.52 us (3%)
    pallas_call x3, Pallas kernels, attend(): pl.pallas_call(kernel, grid_spec=grid_spec, out_shape=out_shape)  30.6 us
    ppermute x4, waiting for transfers between devices, exchange(): other = lax.ppermute(block, 'tm', [(i, i ^ step) for i in range(devices)])  25.4 us
    ppermute x3, waiting for transfers between devices, per_device(): received.append(lax.ppermute(part, 'mp', pairs))  25.2 us
    ppermute x1, starting transfers between devices, per_device(): lax.ppermute(sent, ('tm', 'height'), diagonal_pairs(tm_size, height_size,...  15.2 us
    ppermute x1, waiting for transfers between devices, per_device(): h_after = lax.ppermute(own, 'height', shift_pairs(height_size, -1))  13.8 us
    ppermute x4, starting transfers between devices, exchange(): other = lax.ppermute(block, 'tm', [(i, i ^ step) for i in range(devices)])  11 us
    ppermute x3, starting transfers between devices, per_device(): received.append(lax.ppermute(part, 'mp', pairs))  7.23 us
    ppermute x1, starting transfers between devices, per_device(): t_after = lax.ppermute(sent, 'tm', shift_pairs(tm_size, -1))  4.87 us
  transfers between devices with their start and end apart: 16, of which 10 were waited for; matrix products, arithmetic and copies ran while one was open for 6% of the time, Pallas kernels for 13%

profile of v19, /device:TPU:37, one launch (start us, length us, event | category | flops | bytes accessed | tf_op | source)
XLA Modules:
  0.0 168.8 jit_solution(10266370252832960967)
XLA Ops:
  0.0 0.0 copy-start
  0.0 3.5 %collective-permute-start.2 = (bf16[2,384,768]{2,1,0:T(8,128)(2,1)}, bf16[2,384,768]{2,1,0:T(8,128)(2,1)S(1)}, u32[]{:S(2)}, u32[]{:S(2)}) collective-permute-start(bf16[2,384,768]{2,1,0:T(8,128)(2,1)} %bitcast.2.rest_1_), channel_id=1, source_target_pairs={{0,4},{4,8},{8,12},{1,5},{5,9},{9,13},{2,6},{6,10},{10,14},{3,7},{... | collective-permute-start | bytes 3538952 | tf_op jit(solution)/shard_map/ppermute | solution.py:209
  3.5 1.9 %collective-permute-start.3 = (bf16[2,384,768]{2,1,0:T(8,128)(2,1)}, bf16[2,384,768]{2,1,0:T(8,128)(2,1)S(1)}, u32[]{:S(2)}, u32[]{:S(2)}) collective-permute-start(bf16[2,384,768]{2,1,0:T(8,128)(2,1)} %bitcast.2.rest_1_), channel_id=1, source_target_pairs={{4,0},{8,4},{12,8},{5,1},{9,5},{13,9},{6,2},{10,6},{14,10},{7,3},{... | collective-permute-start | bytes 3538952 | tf_op jit(solution)/shard_map/ppermute | solution.py:210
  5.5 0.0 copy-done
  5.5 0.6 collective-permute-start
  6.1 0.8 pad_dynamic-slice_fusion
  6.9 0.1 copy.16
  7.0 0.1 lt.113
  7.1 0.1 copy.17
  7.2 0.1 lt.118
  7.2 0.7 and_select_fusion.rest_4_.rest_2_
  7.9 0.6 slice.12
  8.5 0.6 slice.13
  9.1 9.2 %collective-permute-done = bf16[2,16,384]{2,1,0:T(8,128)(2,1)S(1)} collective-permute-done((bf16[2,16,384]{2,1,0:T(8,128)(2,1)S(1)}, bf16[2,16,384]{2,1,0:T(8,128)(2,1)S(1)}, u32[]{:S(2)}, u32[]{:S(2)}) %collective-permute-start) | collective-permute-done | bytes 24608 | tf_op jit(solution)/shard_map/ppermute | solution.py:50
  18.4 0.1 collective-permute-start.1
  18.5 1.3 fusion.8
  19.8 2.6 %collective-permute-done.1 = bf16[2,32,384]{2,1,0:T(8,128)(2,1)S(1)} collective-permute-done((bf16[2,32,384]{2,1,0:T(8,128)(2,1)S(1)}, bf16[2,32,384]{2,1,0:T(8,128)(2,1)S(1)}, u32[]{:S(2)}, u32[]{:S(2)}) %collective-permute-start.1) | collective-permute-done | bytes 49184 | tf_op jit(solution)/shard_map/ppermute | solution.py:50
  22.4 0.0 collective-permute-done.2.rest_2_
  22.4 0.0 copy-start.3
  22.4 13.8 %collective-permute-done.3.rest_3_ = bf16[2,384,768]{2,1,0:T(8,128)(2,1)S(1)} collective-permute-done((bf16[2,384,768]{2,1,0:T(8,128)(2,1)}, bf16[2,384,768]{2,1,0:T(8,128)(2,1)S(1)}, u32[]{:S(2)}, u32[]{:S(2)}) %collective-permute-start.3) | collective-permute-done | bytes 1179680 | tf_op jit(solution)/shard_map/ppermute | solution.py:210
  36.3 1.9 %collective-permute-start.4 = (bf16[2,384,768]{2,1,0:T(8,128)(2,1)}, bf16[2,384,768]{2,1,0:T(8,128)(2,1)}, u32[]{:S(2)}, u32[]{:S(2)}) collective-permute-start(bf16[2,384,768]{2,1,0:T(8,128)(2,1)} %bitcast.2.rest_1_), channel_id=1, source_target_pairs={{0,16},{16,32},{32,48},{48,64},{64,80},{80,96},{96,112},{112,128},... | collective-permute-start | bytes 3538952 | tf_op jit(solution)/shard_map/ppermute | solution.py:228
  38.2 4.9 %collective-permute-start.5 = (bf16[2,384,768]{2,1,0:T(8,128)(2,1)}, bf16[2,384,768]{2,1,0:T(8,128)(2,1)}, u32[]{:S(2)}, u32[]{:S(2)}) collective-permute-start(bf16[2,384,768]{2,1,0:T(8,128)(2,1)} %bitcast.2.rest_1_), channel_id=1, source_target_pairs={{16,0},{32,16},{48,32},{64,48},{80,64},{96,80},{112,96},{128,112},... | collective-permute-start | bytes 3538952 | tf_op jit(solution)/shard_map/ppermute | solution.py:229
  43.1 4.4 %collective-permute-start.6 = (bf16[2,64,384]{2,1,0:T(8,128)(2,1)S(1)}, bf16[2,64,384]{2,1,0:T(8,128)(2,1)S(1)}, u32[]{:S(2)}, u32[]{:S(2)}) collective-permute-start(bf16[2,64,384]{2,1,0:T(8,128)(2,1)S(1)} %maximum_select_fusion.3), channel_id=1, source_target_pairs={{0,64},{16,80},{32,96},{48,112},{64,0},{80,16},{96,32},{112,48},{1... | collective-permute-start | bytes 294920 | tf_op jit(solution)/shard_map/ppermute | solution.py:50
  47.4 10.5 %collective-permute-done.6 = bf16[2,64,384]{2,1,0:T(8,128)(2,1)S(1)} collective-permute-done((bf16[2,64,384]{2,1,0:T(8,128)(2,1)S(1)}, bf16[2,64,384]{2,1,0:T(8,128)(2,1)S(1)}, u32[]{:S(2)}, u32[]{:S(2)}) %collective-permute-start.6) | collective-permute-done | bytes 98336 | tf_op jit(solution)/shard_map/ppermute | solution.py:50
  58.0 5.9 %collective-permute-start.7 = (bf16[2,128,384]{2,1,0:T(8,128)(2,1)S(1)}, bf16[2,128,384]{2,1,0:T(8,128)(2,1)S(1)}, u32[]{:S(2)}, u32[]{:S(2)}) collective-permute-start(bf16[2,128,384]{2,1,0:T(8,128)(2,1)S(1)} %maximum_select_fusion.2), channel_id=1, source_target_pairs={{0,128},{16,144},{32,160},{48,176},{64,192},{80,208},{96,224},{112... | collective-permute-start | bytes 589832 | tf_op jit(solution)/shard_map/ppermute | solution.py:50
  63.9 3.1 %collective-permute-done.7 = bf16[2,128,384]{2,1,0:T(8,128)(2,1)S(1)} collective-permute-done((bf16[2,128,384]{2,1,0:T(8,128)(2,1)S(1)}, bf16[2,128,384]{2,1,0:T(8,128)(2,1)S(1)}, u32[]{:S(2)}, u32[]{:S(2)}) %collective-permute-start.7) | collective-permute-done | bytes 196640 | tf_op jit(solution)/shard_map/ppermute | solution.py:50
  67.0 0.1 maximum_select_fusion.1
  67.1 0.1 collective-permute-start.8
  67.2 0.0 copy-done.7
  67.2 0.7 copy.22.reach_ref
  67.9 1.0 collective-permute-done.8
  68.9 1.1 maximum_select_fusion.rest_0_
  70.0 0.0 copy-done.3
  70.0 0.0 copy-done.4
  70.0 13.7 %shard_map.82 = (f32[6,384,1]{2,1,0:T(8,128)}, f32[6,384,1]{2,1,0:T(8,128)}, f32[384,768]{1,0:T(8,128)}) custom-call(s32[6,2]{1,0:T(8,128)} %copy.22.reach_ref, bf16[384,768]{1,0:T(8,128)(2,1)} %bitcast.13, bf16[2,256,768]{2,1,0:T(8,128)(2,1)} %maximum_select_fusion.rest_0_, bf16[2,384,768]{2,1,0:T(8,128)(2,1)} %bitcast.2.rest_1_, ...), custom_call_target="tpu_custom_call" | custom-call | tf_op jit(solution)/shard_map/pallas_call | solution.py:198
  83.7 0.0 collective-permute-done.4.rest_0_
  83.7 0.0 collective-permute-done.5.rest_1_
  83.7 0.2 collective-permute-start.11
  83.9 15.2 %collective-permute-start.12 = (bf16[2,384,768]{2,1,0:T(8,128)(2,1)}, bf16[2,384,768]{2,1,0:T(8,128)(2,1)}, u32[]{:S(2)}, u32[]{:S(2)}) collective-permute-start(bf16[2,384,768]{2,1,0:T(8,128)(2,1)} %bitcast.2.rest_1_), channel_id=1, source_target_pairs={{20,8},{24,4},{36,24},{40,20},{52,40},{56,36},{68,56},{72,52},{84,... | collective-permute-start | bytes 3538952 | tf_op jit(solution)/shard_map/ppermute | solution.py:241
  99.1 1.9 %collective-permute-start.10 = (bf16[2,384,768]{2,1,0:T(8,128)(2,1)}, bf16[2,384,768]{2,1,0:T(8,128)(2,1)S(1)}, u32[]{:S(2)}, u32[]{:S(2)}) collective-permute-start(bf16[2,384,768]{2,1,0:T(8,128)(2,1)} %collective-permute-done.4.rest_0_), channel_id=1, source_target_pairs={{4,0},{8,4},{12,8},{5,1},{9,5},{13,9},{6,2},{10,6},{14,10},{7,3},{... | collective-permute-start | bytes 3538952 | tf_op jit(solution)/shard_map/ppermute | solution.py:239
  101.1 3.6 %collective-permute-start.9 = (bf16[2,384,768]{2,1,0:T(8,128)(2,1)}, bf16[2,384,768]{2,1,0:T(8,128)(2,1)S(1)}, u32[]{:S(2)}, u32[]{:S(2)}) collective-permute-start(bf16[2,384,768]{2,1,0:T(8,128)(2,1)} %collective-permute-done.4.rest_0_), channel_id=1, source_target_pairs={{0,4},{4,8},{8,12},{1,5},{5,9},{9,13},{2,6},{6,10},{10,14},{3,7},{... | collective-permute-start | bytes 3538952 | tf_op jit(solution)/shard_map/ppermute | solution.py:238
  104.8 0.8 copy.23.rest_8_
  105.6 8.3 %shard_map.83 = (f32[6,384,1]{2,1,0:T(8,128)}, f32[6,384,1]{2,1,0:T(8,128)}, f32[384,768]{1,0:T(8,128)}) custom-call(s32[6,2]{1,0:T(8,128)} %copy.22.reach_ref, bf16[384,768]{1,0:T(8,128)(2,1)} %bitcast.14, bf16[2,384,768]{2,1,0:T(8,128)(2,1)} %collective-permute-done.4.rest_0_, bf16[2,384,768]{2,1,0:T(8,128)(2,1)} %collective-permute-done.5.rest_1_, ...), custom_call_target="tpu_custom_call" | custom-call | tf_op jit(solution)/shard_map/pallas_call | solution.py:198
  113.9 0.0 collective-permute-done.11
  113.9 0.0 collective-permute-done.12
  113.9 3.2 %broadcast_select_fusion = (bf16[2,384,768]{2,1,0:T(8,128)(2,1)}, bf16[2,384,768]{2,1,0:T(8,128)(2,1)}) fusion(bf16[2,384,768]{2,1,0:T(8,128)(2,1)} %collective-permute-done.12, bf16[2,384,768]{2,1,0:T(8,128)(2,1)} %collective-permute-done.11, pred[]{:T(512)S(6)} %eq.32), kind=kLoop, calls=%fused_computation.3 | loop fusion | flops 1179648 | bytes 4718593 | tf_op jit(solution)/shard_map/jit(_where)/select_n | solution.py:249
  117.1 0.0 collective-permute-done.10.rest_1_
  117.1 1.1 collective-permute-done.9.rest_0_
  118.2 0.0 copy-done.1
  118.2 1.0 copy-done.2
  119.2 8.7 %shard_map.84 = bf16[384,768]{1,0:T(8,128)(2,1)} custom-call(s32[6,2]{1,0:T(8,128)} %copy.22.reach_ref, bf16[384,768]{1,0:T(8,128)(2,1)} %bitcast.15, bf16[2,384,768]{2,1,0:T(8,128)(2,1)} %copy-done.2, bf16[2,384,768]{2,1,0:T(8,128)(2,1)} %copy-done.1, bf16[2,384,768]{2,1,0:T(8,128)(2,1)} %get-tuple-element.45.rest_2_, ...), custom_call_target="tpu_custom_call" | custom-call | tf_op jit(solution)/shard_map/pallas_call | solution.py:198
  127.9 4.5 %convolution_convert_fusion = bf16[384,3072]{1,0:T(8,128)(2,1)S(1)} fusion(bf16[384,768]{1,0:T(8,128)(2,1)} %shard_map.84, bf16[768,3072]{1,0:T(8,128)(2,1)} %param.12), kind=kOutput, calls=%fused_computation | convolution fusion | flops 1813118976 | bytes 7667712 | tf_op jit(solution)/shard_map/dot_general | solution.py:255
  132.4 0.0 copy-start.5
  132.4 0.0 copy-start.6
  132.4 1.3 constant_dynamic-slice_fusion.2
  133.7 4.6 %collective-permute-start.13 = (bf16[384,768]{1,0:T(8,128)(2,1)}, bf16[384,768]{1,0:T(8,128)(2,1)}, u32[]{:S(2)}, u32[]{:S(2)}) collective-permute-start(bf16[384,768]{1,0:T(8,128)(2,1)} %get-tuple-element.41), channel_id=1, source_target_pairs={{0,2},{1,3},{2,0},{3,1},{4,6},{5,7},{6,4},{7,5},{8,10},{9,11},{10,... | collective-permute-start | bytes 1769480 | tf_op jit(solution)/shard_map/ppermute | solution.py:262
  138.3 2.0 %collective-permute-start.14 = (bf16[384,768]{1,0:T(8,128)(2,1)}, bf16[384,768]{1,0:T(8,128)(2,1)}, u32[]{:S(2)}, u32[]{:S(2)}) collective-permute-start(bf16[384,768]{1,0:T(8,128)(2,1)} %get-tuple-element.43), channel_id=1, source_target_pairs={{0,1},{1,2},{2,3},{3,0},{4,5},{5,6},{6,7},{7,4},{8,9},{9,10},{10,1... | collective-permute-start | bytes 1769480 | tf_op jit(solution)/shard_map/ppermute | solution.py:262
  140.2 0.7 collective-permute-start.15
  140.9 11.3 %collective-permute-done.13 = bf16[384,768]{1,0:T(8,128)(2,1)} collective-permute-done((bf16[384,768]{1,0:T(8,128)(2,1)}, bf16[384,768]{1,0:T(8,128)(2,1)}, u32[]{:S(2)}, u32[]{:S(2)}) %collective-permute-start.13) | collective-permute-done | bytes 589856 | tf_op jit(solution)/shard_map/ppermute | solution.py:262
  152.3 11.1 %collective-permute-done.14 = bf16[384,768]{1,0:T(8,128)(2,1)} collective-permute-done((bf16[384,768]{1,0:T(8,128)(2,1)}, bf16[384,768]{1,0:T(8,128)(2,1)}, u32[]{:S(2)}, u32[]{:S(2)}) %collective-permute-start.14) | collective-permute-done | bytes 589856 | tf_op jit(solution)/shard_map/ppermute | solution.py:262
  163.4 2.7 %collective-permute-done.15 = bf16[384,768]{1,0:T(8,128)(2,1)} collective-permute-done((bf16[384,768]{1,0:T(8,128)(2,1)}, bf16[384,768]{1,0:T(8,128)(2,1)}, u32[]{:S(2)}, u32[]{:S(2)}) %collective-permute-start.15) | collective-permute-done | bytes 589856 | tf_op jit(solution)/shard_map/ppermute | solution.py:262
  166.1 0.0 copy-done.5
  166.1 0.0 copy-done.6
  166.1 2.6 %fusion.1 = bf16[1,1,384,768]{3,2,1,0:T(8,128)(2,1)} fusion(bf16[384,768]{1,0:T(8,128)(2,1)} %collective-permute-done.15, bf16[384,768]{1,0:T(8,128)(2,1)} %collective-permute-done.14, bf16[384,768]{1,0:T(8,128)(2,1)} %collective-permute-done.13, bf16[1,1,384,768]{3,2,1,0:T(8,128)(2,1)S(1)} %copy-done.5, bf16[384,3072]{1,0:T(8,128)(2,1)S(1)} %convolution_convert_fusion, ...), kind=kLoop, calls=%fused_computation.6 | loop fusion | flops 3244032 | bytes 3542020 | tf_op jit(solution)/shard_map/broadcast_in_dim | solution.py:267
  (9 shorter events, 0.1 us)
Async XLA Ops:
  0.0 5.5 %copy-start = (bf16[2,16,768]{2,1,0:T(8,128)(2,1)S(1)}, bf16[2,16,768]{2,1,0:T(8,128)(2,1)}, u32[]{:S(2)}) copy-start(bf16[2,16,768]{2,1,0:T(8,128)(2,1)} %param.10) | copy-start | bytes 147460
  0.0 67.2 %copy-start.7 = (s32[6,2]{0,1:T(2,128)S(1)}, s32[6,2]{0,1:T(2,128)}, u32[]{:S(2)}) copy-start(s32[6,2]{0,1:T(2,128)} %param.14) | copy-start | bytes 148
  0.0 22.4 %collective-permute-start.2 = (bf16[2,384,768]{2,1,0:T(8,128)(2,1)}, bf16[2,384,768]{2,1,0:T(8,128)(2,1)S(1)}, u32[]{:S(2)}, u32[]{:S(2)}) collective-permute-start(bf16[2,384,768]{2,1,0:T(8,128)(2,1)} %bitcast.2.rest_1_), channel_id=1, source_target_pairs={{0,4},{4,8},{8,12},{1,5},{5,9},{9,13},{2,6},{6,10},{10,14},{3,7},{... | collective-permute-start | bytes 3538952 | tf_op jit(solution)/shard_map/ppermute | solution.py:209
  3.5 32.7 %collective-permute-start.3 = (bf16[2,384,768]{2,1,0:T(8,128)(2,1)}, bf16[2,384,768]{2,1,0:T(8,128)(2,1)S(1)}, u32[]{:S(2)}, u32[]{:S(2)}) collective-permute-start(bf16[2,384,768]{2,1,0:T(8,128)(2,1)} %bitcast.2.rest_1_), channel_id=1, source_target_pairs={{4,0},{8,4},{12,8},{5,1},{9,5},{13,9},{6,2},{10,6},{14,10},{7,3},{... | collective-permute-start | bytes 3538952 | tf_op jit(solution)/shard_map/ppermute | solution.py:210
  5.5 12.8 %collective-permute-start = (bf16[2,16,384]{2,1,0:T(8,128)(2,1)S(1)}, bf16[2,16,384]{2,1,0:T(8,128)(2,1)S(1)}, u32[]{:S(2)}, u32[]{:S(2)}) collective-permute-start(bf16[2,16,384]{2,1,0:T(8,128)(2,1)S(1)} %constant_dynamic-slice_fusion.3), channel_id=1, source_target_pairs={{0,16},{16,0},{32,48},{48,32},{64,80},{80,64},{96,112},{112,96},{1... | collective-permute-start | bytes 73736 | tf_op jit(solution)/shard_map/ppermute | solution.py:50
  18.4 4.0 %collective-permute-start.1 = (bf16[2,32,384]{2,1,0:T(8,128)(2,1)S(1)}, bf16[2,32,384]{2,1,0:T(8,128)(2,1)S(1)}, u32[]{:S(2)}, u32[]{:S(2)}) collective-permute-start(bf16[2,32,384]{2,1,0:T(8,128)(2,1)S(1)} %maximum_select_fusion.4), channel_id=1, source_target_pairs={{0,32},{16,48},{32,0},{48,16},{64,96},{80,112},{96,64},{112,80},{1... | collective-permute-start | bytes 147464 | tf_op jit(solution)/shard_map/ppermute | solution.py:50
  22.4 47.6 %copy-start.3 = (bf16[2,384,768]{2,1,0:T(8,128)(2,1)}, bf16[2,384,768]{2,1,0:T(8,128)(2,1)S(1)}, u32[]{:S(2)}) copy-start(bf16[2,384,768]{2,1,0:T(8,128)(2,1)S(1)} %collective-permute-done.2.rest_2_) | copy-start | bytes 3538948
  36.3 33.7 %copy-start.4 = (bf16[2,384,768]{2,1,0:T(8,128)(2,1)}, bf16[2,384,768]{2,1,0:T(8,128)(2,1)S(1)}, u32[]{:S(2)}) copy-start(bf16[2,384,768]{2,1,0:T(8,128)(2,1)S(1)} %collective-permute-done.3.rest_3_) | copy-start | bytes 3538948
  36.3 47.4 %collective-permute-start.4 = (bf16[2,384,768]{2,1,0:T(8,128)(2,1)}, bf16[2,384,768]{2,1,0:T(8,128)(2,1)}, u32[]{:S(2)}, u32[]{:S(2)}) collective-permute-start(bf16[2,384,768]{2,1,0:T(8,128)(2,1)} %bitcast.2.rest_1_), channel_id=1, source_target_pairs={{0,16},{16,32},{32,48},{48,64},{64,80},{80,96},{96,112},{112,128},... | collective-permute-start | bytes 3538952 | tf_op jit(solution)/shard_map/ppermute | solution.py:228
  38.2 45.5 %collective-permute-start.5 = (bf16[2,384,768]{2,1,0:T(8,128)(2,1)}, bf16[2,384,768]{2,1,0:T(8,128)(2,1)}, u32[]{:S(2)}, u32[]{:S(2)}) collective-permute-start(bf16[2,384,768]{2,1,0:T(8,128)(2,1)} %bitcast.2.rest_1_), channel_id=1, source_target_pairs={{16,0},{32,16},{48,32},{64,48},{80,64},{96,80},{112,96},{128,112},... | collective-permute-start | bytes 3538952 | tf_op jit(solution)/shard_map/ppermute | solution.py:229
  43.1 14.9 %collective-permute-start.6 = (bf16[2,64,384]{2,1,0:T(8,128)(2,1)S(1)}, bf16[2,64,384]{2,1,0:T(8,128)(2,1)S(1)}, u32[]{:S(2)}, u32[]{:S(2)}) collective-permute-start(bf16[2,64,384]{2,1,0:T(8,128)(2,1)S(1)} %maximum_select_fusion.3), channel_id=1, source_target_pairs={{0,64},{16,80},{32,96},{48,112},{64,0},{80,16},{96,32},{112,48},{1... | collective-permute-start | bytes 294920 | tf_op jit(solution)/shard_map/ppermute | solution.py:50
  58.0 9.0 %collective-permute-start.7 = (bf16[2,128,384]{2,1,0:T(8,128)(2,1)S(1)}, bf16[2,128,384]{2,1,0:T(8,128)(2,1)S(1)}, u32[]{:S(2)}, u32[]{:S(2)}) collective-permute-start(bf16[2,128,384]{2,1,0:T(8,128)(2,1)S(1)} %maximum_select_fusion.2), channel_id=1, source_target_pairs={{0,128},{16,144},{32,160},{48,176},{64,192},{80,208},{96,224},{112... | collective-permute-start | bytes 589832 | tf_op jit(solution)/shard_map/ppermute | solution.py:50
  67.1 1.8 %collective-permute-start.8 = (bf16[2,256,384]{2,1,0:T(8,128)(2,1)S(1)}, bf16[2,256,384]{2,1,0:T(8,128)(2,1)S(1)}, u32[]{:S(2)}, u32[]{:S(2)}) collective-permute-start(bf16[2,256,384]{2,1,0:T(8,128)(2,1)S(1)} %maximum_select_fusion.1), channel_id=1, source_target_pairs={{0,4},{4,0},{8,12},{12,8},{1,5},{5,1},{9,13},{13,9},{2,6},{6,2},{1... | collective-permute-start | bytes 1179656 | tf_op jit(solution)/shard_map/ppermute | solution.py:59
  83.7 30.2 %collective-permute-start.11 = (bf16[2,384,768]{2,1,0:T(8,128)(2,1)}, bf16[2,384,768]{2,1,0:T(8,128)(2,1)}, u32[]{:S(2)}, u32[]{:S(2)}) collective-permute-start(bf16[2,384,768]{2,1,0:T(8,128)(2,1)} %collective-permute-done.5.rest_1_), channel_id=1, source_target_pairs={{0,4},{4,0},{8,12},{12,8},{1,5},{5,1},{9,13},{13,9},{2,6},{6,2},{1... | collective-permute-start | bytes 3538952 | tf_op jit(solution)/shard_map/ppermute | solution.py:240
  83.9 30.0 %collective-permute-start.12 = (bf16[2,384,768]{2,1,0:T(8,128)(2,1)}, bf16[2,384,768]{2,1,0:T(8,128)(2,1)}, u32[]{:S(2)}, u32[]{:S(2)}) collective-permute-start(bf16[2,384,768]{2,1,0:T(8,128)(2,1)} %bitcast.2.rest_1_), channel_id=1, source_target_pairs={{20,8},{24,4},{36,24},{40,20},{52,40},{56,36},{68,56},{72,52},{84,... | collective-permute-start | bytes 3538952 | tf_op jit(solution)/shard_map/ppermute | solution.py:241
  99.1 17.9 %collective-permute-start.10 = (bf16[2,384,768]{2,1,0:T(8,128)(2,1)}, bf16[2,384,768]{2,1,0:T(8,128)(2,1)S(1)}, u32[]{:S(2)}, u32[]{:S(2)}) collective-permute-start(bf16[2,384,768]{2,1,0:T(8,128)(2,1)} %collective-permute-done.4.rest_0_), channel_id=1, source_target_pairs={{4,0},{8,4},{12,8},{5,1},{9,5},{13,9},{6,2},{10,6},{14,10},{7,3},{... | collective-permute-start | bytes 3538952 | tf_op jit(solution)/shard_map/ppermute | solution.py:239
  101.1 17.1 %collective-permute-start.9 = (bf16[2,384,768]{2,1,0:T(8,128)(2,1)}, bf16[2,384,768]{2,1,0:T(8,128)(2,1)S(1)}, u32[]{:S(2)}, u32[]{:S(2)}) collective-permute-start(bf16[2,384,768]{2,1,0:T(8,128)(2,1)} %collective-permute-done.4.rest_0_), channel_id=1, source_target_pairs={{0,4},{4,8},{8,12},{1,5},{5,9},{9,13},{2,6},{6,10},{10,14},{3,7},{... | collective-permute-start | bytes 3538952 | tf_op jit(solution)/shard_map/ppermute | solution.py:238
  117.1 1.1 copy-start.1
  118.2 1.0 copy-start.2
  132.4 33.8 %copy-start.5 = (bf16[1,1,384,768]{3,2,1,0:T(8,128)(2,1)S(1)}, bf16[1,1,384,768]{3,2,1,0:T(8,128)(2,1)}, u32[]{:S(2)}) copy-start(bf16[1,1,384,768]{3,2,1,0:T(8,128)(2,1)} %param.11) | copy-start | bytes 1769476
  132.4 33.7 %copy-start.6 = (f32[768]{0:T(1024)S(1)}, f32[768]{0:T(1024)}, u32[]{:S(2)}) copy-start(f32[768]{0:T(1024)} %param.13) | copy-start | bytes 9220
  133.7 18.6 %collective-permute-start.13 = (bf16[384,768]{1,0:T(8,128)(2,1)}, bf16[384,768]{1,0:T(8,128)(2,1)}, u32[]{:S(2)}, u32[]{:S(2)}) collective-permute-start(bf16[384,768]{1,0:T(8,128)(2,1)} %get-tuple-element.41), channel_id=1, source_target_pairs={{0,2},{1,3},{2,0},{3,1},{4,6},{5,7},{6,4},{7,5},{8,10},{9,11},{10,... | collective-permute-start | bytes 1769480 | tf_op jit(solution)/shard_map/ppermute | solution.py:262
  138.3 25.1 %collective-permute-start.14 = (bf16[384,768]{1,0:T(8,128)(2,1)}, bf16[384,768]{1,0:T(8,128)(2,1)}, u32[]{:S(2)}, u32[]{:S(2)}) collective-permute-start(bf16[384,768]{1,0:T(8,128)(2,1)} %get-tuple-element.43), channel_id=1, source_target_pairs={{0,1},{1,2},{2,3},{3,0},{4,5},{5,6},{6,7},{7,4},{8,9},{9,10},{10,1... | collective-permute-start | bytes 1769480 | tf_op jit(solution)/shard_map/ppermute | solution.py:262
  140.2 25.9 %collective-permute-start.15 = (bf16[384,768]{1,0:T(8,128)(2,1)}, bf16[384,768]{1,0:T(8,128)(2,1)}, u32[]{:S(2)}, u32[]{:S(2)}) collective-permute-start(bf16[384,768]{1,0:T(8,128)(2,1)} %get-tuple-element.42), channel_id=1, source_target_pairs={{0,3},{1,0},{2,1},{3,2},{4,7},{5,4},{6,5},{7,6},{8,11},{9,8},{10,9... | collective-permute-start | bytes 1769480 | tf_op jit(solution)/shard_map/ppermute | solution.py:262

commit v20 on v17

--- a/solution.py
+++ b/solution.py
@@ -226,10 +226,9 @@
     h_after = lax.ppermute(own, "height", shift_pairs(height_size, -1))
     text_group = text_halves(text_kv)
     step = 1
-    while step < tm_size:
+    while 2 * step < tm_size:
         text_group = exchange(text_group, tm_size, step)
         step *= 2
-    text = join_halves(text_group)
     time_start = lax.axis_index("tm")
     height_start = lax.axis_index("height")
     zero_index = jnp.int32(0)
@@ -239,11 +238,14 @@
     bias = jnp.where(key_valid, 0.0, NEG).astype(jnp.float32).reshape(9, 1, tile_len)
     qvalid = key_valid[1, 1].astype(jnp.float32).reshape(tile_len, 1)
 
-    sent, text, h_before, h_after, bias, qvalid = lax.optimization_barrier(
-        (own, text, h_before, h_after, bias, qvalid)
+    sent, text_group, h_before, h_after, bias, qvalid = lax.optimization_barrier(
+        (own, text_group, h_before, h_after, bias, qvalid)
     )
     t_before = lax.ppermute(sent, "tm", shift_pairs(tm_size, 1))
     t_after = lax.ppermute(sent, "tm", shift_pairs(tm_size, -1))
+    if step < tm_size:
+        text_group = exchange(text_group, tm_size, step)
+    text = join_halves(text_group)
     queries = image_q[0, 0]
     odd = (lax.axis_index("height") % 2).astype(head_reach.dtype)
     reach_odd = jnp.concatenate([head_reach, jnp.stack([odd, odd])[None]], axis=0)

time: 170 us -> 157 us (0.924)
  the two profiles are of different devices: /device:TPU:33 before, /device:TPU:97 now
where the time goes in v20:
time: 157 us; the launch traced here: 155 us
  waiting for transfers between devices  70.1 us (45%)
  starting transfers between devices  37.8 us (24%)
  Pallas kernels  30.4 us (19%)
  other arithmetic  6.6 us (4%)
  local copies, waits for them, and re-layouts  5.68 us (4%)
  matrix products  4.52 us (3%)
    ppermute x4, waiting for transfers between devices, exchange(): other = lax.ppermute(block, 'tm', [(i, i ^ step) for i in range(devices)])  43.2 us
    pallas_call x3, Pallas kernels, attend(): pl.pallas_call(kernel, grid_spec=grid_spec, out_shape=out_shape)  30.4 us
    ppermute x3, waiting for transfers between devices, per_device(): received.append(lax.ppermute(part, 'mp', pairs))  22 us
    ppermute x3, starting transfers between devices, per_device(): received.append(lax.ppermute(part, 'mp', pairs))  9.08 us
    ppermute x4, starting transfers between devices, exchange(): other = lax.ppermute(block, 'tm', [(i, i ^ step) for i in range(devices)])  7.02 us
    dot_general x1, matrix products, per_device(): jnp.dot(attended, out_weight, preferred_element_type=jnp.float32)  4.52 us
    ppermute x1, starting transfers between devices, per_device(): earlier_low = lax.ppermute(t_before, 'height', shift_pairs(height_size, 1))  4.15 us
    ppermute x1, starting transfers between devices, per_device(): t_after = lax.ppermute(sent, 'tm', shift_pairs(tm_size, -1))  3.92 us
  transfers between devices with their start and end apart: 16, of which 10 were waited for; matrix products, arithmetic and copies ran while one was open for 5% of the time, Pallas kernels for 14%

profile of v20, /device:TPU:97, one launch (start us, length us, event | category | flops | bytes accessed | tf_op | source)
XLA Modules:
  0.0 155.4 jit_solution(13320080867144837651)
XLA Ops:
  0.0 0.0 copy-start
  0.0 3.8 %collective-permute-start.3 = (bf16[2,384,768]{2,1,0:T(8,128)(2,1)}, bf16[2,384,768]{2,1,0:T(8,128)(2,1)S(1)}, u32[]{:S(2)}, u32[]{:S(2)}) collective-permute-start(bf16[2,384,768]{2,1,0:T(8,128)(2,1)} %bitcast.19), channel_id=1, source_target_pairs={{0,4},{4,8},{8,12},{1,5},{5,9},{9,13},{2,6},{6,10},{10,14},{3,7},{... | collective-permute-start | bytes 3538952 | tf_op jit(solution)/shard_map/ppermute | solution.py:225
  3.8 1.9 %collective-permute-start.4 = (bf16[2,384,768]{2,1,0:T(8,128)(2,1)}, bf16[2,384,768]{2,1,0:T(8,128)(2,1)S(1)}, u32[]{:S(2)}, u32[]{:S(2)}) collective-permute-start(bf16[2,384,768]{2,1,0:T(8,128)(2,1)} %bitcast.20), channel_id=1, source_target_pairs={{4,0},{8,4},{12,8},{5,1},{9,5},{13,9},{6,2},{10,6},{14,10},{7,3},{... | collective-permute-start | bytes 3538952 | tf_op jit(solution)/shard_map/ppermute | solution.py:226
  5.8 0.0 copy-done
  5.8 2.5 %collective-permute-start = (bf16[2,16,384]{2,1,0:T(8,128)(2,1)S(1)}, bf16[2,16,384]{2,1,0:T(8,128)(2,1)S(1)}, u32[]{:S(2)}, u32[]{:S(2)}) collective-permute-start(bf16[2,16,384]{2,1,0:T(8,128)(2,1)S(1)} %constant_dynamic-slice_fusion.3), channel_id=1, source_target_pairs={{0,16},{16,0},{32,48},{48,32},{64,80},{80,64},{96,112},{112,96},{1... | collective-permute-start | bytes 73736 | tf_op jit(solution)/shard_map/ppermute | solution.py:50
  8.3 0.8 pad_dynamic-slice_fusion
  9.1 0.1 copy.34
  9.2 0.1 lt.113
  9.3 0.1 copy.35
  9.4 0.1 lt.118
  9.5 11.1 %collective-permute-done = bf16[2,16,384]{2,1,0:T(8,128)(2,1)S(1)} collective-permute-done((bf16[2,16,384]{2,1,0:T(8,128)(2,1)S(1)}, bf16[2,16,384]{2,1,0:T(8,128)(2,1)S(1)}, u32[]{:S(2)}, u32[]{:S(2)}) %collective-permute-start) | collective-permute-done | bytes 24608 | tf_op jit(solution)/shard_map/ppermute | solution.py:50
  20.6 0.1 collective-permute-start.1
  20.7 0.7 and_select_fusion.rest_4_.rest_2_.rest_6_
  21.4 0.6 slice.12
  22.0 0.6 slice.13
  22.6 1.0 collective-permute-done.1
  23.6 0.1 collective-permute-start.2
  23.7 1.3 fusion.8
  25.0 4.5 %collective-permute-done.2 = bf16[2,64,384]{2,1,0:T(8,128)(2,1)S(1)} collective-permute-done((bf16[2,64,384]{2,1,0:T(8,128)(2,1)S(1)}, bf16[2,64,384]{2,1,0:T(8,128)(2,1)S(1)}, u32[]{:S(2)}, u32[]{:S(2)}) %collective-permute-start.2) | collective-permute-done | bytes 98336 | tf_op jit(solution)/shard_map/ppermute | solution.py:50
  29.6 0.0 collective-permute-done.3.rest_2_
  29.6 0.0 copy-start.3
  29.6 0.0 collective-permute-done.4.rest_3_
  29.6 0.0 copy-start.4
  29.6 3.8 %collective-permute-start.5 = (bf16[2,384,768]{2,1,0:T(8,128)(2,1)}, bf16[2,384,768]{2,1,0:T(8,128)(2,1)}, u32[]{:S(2)}, u32[]{:S(2)}) collective-permute-start(bf16[2,384,768]{2,1,0:T(8,128)(2,1)} %bitcast.21), channel_id=1, source_target_pairs={{0,16},{16,32},{32,48},{48,64},{64,80},{80,96},{96,112},{112,128},... | collective-permute-start | bytes 3538952 | tf_op jit(solution)/shard_map/ppermute | solution.py:244
  33.4 3.9 %collective-permute-start.6 = (bf16[2,384,768]{2,1,0:T(8,128)(2,1)}, bf16[2,384,768]{2,1,0:T(8,128)(2,1)}, u32[]{:S(2)}, u32[]{:S(2)}) collective-permute-start(bf16[2,384,768]{2,1,0:T(8,128)(2,1)} %bitcast.22), channel_id=1, source_target_pairs={{16,0},{32,16},{48,32},{64,48},{80,64},{96,80},{112,96},{128,112},... | collective-permute-start | bytes 3538952 | tf_op jit(solution)/shard_map/ppermute | solution.py:245
  37.3 4.3 %collective-permute-start.7 = (bf16[2,128,384]{2,1,0:T(8,128)(2,1)S(1)}, bf16[2,128,384]{2,1,0:T(8,128)(2,1)S(1)}, u32[]{:S(2)}, u32[]{:S(2)}) collective-permute-start(bf16[2,128,384]{2,1,0:T(8,128)(2,1)S(1)} %maximum_select_fusion.2), channel_id=1, source_target_pairs={{0,128},{16,144},{32,160},{48,176},{64,192},{80,208},{96,224},{112... | collective-permute-start | bytes 589832 | tf_op jit(solution)/shard_map/ppermute | solution.py:50
  41.6 26.6 %collective-permute-done.7 = bf16[2,128,384]{2,1,0:T(8,128)(2,1)S(1)} collective-permute-done((bf16[2,128,384]{2,1,0:T(8,128)(2,1)S(1)}, bf16[2,128,384]{2,1,0:T(8,128)(2,1)S(1)}, u32[]{:S(2)}, u32[]{:S(2)}) %collective-permute-start.7) | collective-permute-done | bytes 196640 | tf_op jit(solution)/shard_map/ppermute | solution.py:50
  68.2 0.1 maximum_select_fusion.1
  68.3 0.1 collective-permute-start.8
  68.4 0.0 copy-done.8
  68.5 0.7 copy.33.reach_ref
  69.1 1.0 collective-permute-done.8
  70.2 1.1 maximum_select_fusion.rest_0_
  71.3 0.0 copy-done.3
  71.3 0.0 copy-done.4
  71.3 13.0 %shard_map.82 = (f32[6,384,1]{2,1,0:T(8,128)}, f32[6,384,1]{2,1,0:T(8,128)}, f32[384,768]{1,0:T(8,128)}) custom-call(s32[6,2]{1,0:T(8,128)} %copy.33.reach_ref, bf16[384,768]{1,0:T(8,128)(2,1)} %bitcast.16, bf16[2,256,768]{2,1,0:T(8,128)(2,1)} %maximum_select_fusion.rest_0_, bf16[2,384,768]{2,1,0:T(8,128)(2,1)} %bitcast.23, bf16[2,384,768]{2,1,0:T(8,128)(2,1)} %copy-done.3, ...), custom_call_target="tpu_custom_call" | custom-call | tf_op jit(solution)/shard_map/pallas_call | solution.py:214
  84.3 0.0 collective-permute-done.5.rest_0_
  84.3 0.0 collective-permute-done.6.rest_1_
  84.3 2.0 %collective-permute-start.10 = (bf16[2,384,768]{2,1,0:T(8,128)(2,1)}, bf16[2,384,768]{2,1,0:T(8,128)(2,1)}, u32[]{:S(2)}, u32[]{:S(2)}) collective-permute-start(bf16[2,384,768]{2,1,0:T(8,128)(2,1)} %collective-permute-done.5.rest_0_), channel_id=1, source_target_pairs={{4,0},{8,4},{12,8},{5,1},{9,5},{13,9},{6,2},{10,6},{14,10},{7,3},{... | collective-permute-start | bytes 3538952 | tf_op jit(solution)/shard_map/ppermute | solution.py:256
  86.4 0.1 collective-permute-start.11
  86.5 1.9 %collective-permute-start.12 = (bf16[2,384,768]{2,1,0:T(8,128)(2,1)}, bf16[2,384,768]{2,1,0:T(8,128)(2,1)S(1)}, u32[]{:S(2)}, u32[]{:S(2)}) collective-permute-start(bf16[2,384,768]{2,1,0:T(8,128)(2,1)} %bitcast.24), channel_id=1, source_target_pairs={{20,8},{24,4},{36,24},{40,20},{52,40},{56,36},{68,56},{72,52},{84,... | collective-permute-start | bytes 3538952 | tf_op jit(solution)/shard_map/ppermute | solution.py:258
  88.4 4.1 %collective-permute-start.9 = (bf16[2,384,768]{2,1,0:T(8,128)(2,1)}, bf16[2,384,768]{2,1,0:T(8,128)(2,1)}, u32[]{:S(2)}, u32[]{:S(2)}) collective-permute-start(bf16[2,384,768]{2,1,0:T(8,128)(2,1)} %collective-permute-done.5.rest_0_), channel_id=1, source_target_pairs={{0,4},{4,8},{8,12},{1,5},{5,9},{9,13},{2,6},{6,10},{10,14},{3,7},{... | collective-permute-start | bytes 3538952 | tf_op jit(solution)/shard_map/ppermute | solution.py:255
  92.6 0.1 add_bitcast_fusion
  92.7 0.6 pad_add_fusion.reach_ref
  93.3 0.8 copy.40.rest_10_
  94.1 8.0 %shard_map.83 = (f32[6,384,1]{2,1,0:T(8,128)}, f32[6,384,1]{2,1,0:T(8,128)}, f32[384,768]{1,0:T(8,128)}) custom-call(s32[6,2]{1,0:T(8,128)} %copy.33.reach_ref, bf16[384,768]{1,0:T(8,128)(2,1)} %bitcast.17, bf16[2,384,768]{2,1,0:T(8,128)(2,1)} %collective-permute-done.5.rest_0_, bf16[2,384,768]{2,1,0:T(8,128)(2,1)} %collective-permute-done.6.rest_1_, ...), custom_call_target="tpu_custom_call" | custom-call | tf_op jit(solution)/shard_map/pallas_call | solution.py:214
  102.1 0.1 collective-permute-done.10.rest_1_
  102.1 0.0 collective-permute-done.11.rest_2_.rest_5_
  102.2 3.3 %collective-permute-done.12.rest_3_.rest_4_ = bf16[2,384,768]{2,1,0:T(8,128)(2,1)S(1)} collective-permute-done((bf16[2,384,768]{2,1,0:T(8,128)(2,1)}, bf16[2,384,768]{2,1,0:T(8,128)(2,1)S(1)}, u32[]{:S(2)}, u32[]{:S(2)}) %collective-permute-start.12) | collective-permute-done | bytes 1179680 | tf_op jit(solution)/shard_map/ppermute | solution.py:258
  105.4 0.6 collective-permute-done.9.rest_0_
  106.0 0.5 copy-done.2
  106.5 9.3 %shard_map.84 = bf16[384,768]{1,0:T(8,128)(2,1)} custom-call(s32[7,2]{1,0:T(8,128)} %pad_add_fusion.reach_ref, bf16[384,768]{1,0:T(8,128)(2,1)} %bitcast.18, bf16[2,384,768]{2,1,0:T(8,128)(2,1)} %collective-permute-done.9.rest_0_, bf16[2,384,768]{2,1,0:T(8,128)(2,1)} %collective-permute-done.10.rest_1_, bf16[2,384,768]{2,1,0:T(8,128)(2,1)} %copy-done.1, ...), custom_call_target="tpu_custom_call" | custom-call | tf_op jit(solution)/shard_map/pallas_call | solution.py:214
  115.8 4.5 %convolution_convert_fusion = bf16[384,3072]{1,0:T(8,128)(2,1)S(1)} fusion(bf16[384,768]{1,0:T(8,128)(2,1)} %shard_map.84, bf16[768,3072]{1,0:T(8,128)(2,1)} %param.12), kind=kOutput, calls=%fused_computation | convolution fusion | flops 1813118976 | bytes 7667712 | tf_op jit(solution)/shard_map/dot_general | solution.py:267
  120.4 0.0 copy-start.5
  120.4 0.0 copy-start.7
  120.4 1.3 constant_dynamic-slice_fusion.2
  121.7 6.4 %collective-permute-start.13 = (bf16[384,768]{1,0:T(8,128)(2,1)}, bf16[384,768]{1,0:T(8,128)(2,1)}, u32[]{:S(2)}, u32[]{:S(2)}) collective-permute-start(bf16[384,768]{1,0:T(8,128)(2,1)} %get-tuple-element.41), channel_id=1, source_target_pairs={{0,2},{1,3},{2,0},{3,1},{4,6},{5,7},{6,4},{7,5},{8,10},{9,11},{10,... | collective-permute-start | bytes 1769480 | tf_op jit(solution)/shard_map/ppermute | solution.py:274
  128.1 0.0 collective-permute-start.14
  128.1 2.7 %collective-permute-start.15 = (bf16[384,768]{1,0:T(8,128)(2,1)}, bf16[384,768]{1,0:T(8,128)(2,1)}, u32[]{:S(2)}, u32[]{:S(2)}) collective-permute-start(bf16[384,768]{1,0:T(8,128)(2,1)} %get-tuple-element.42), channel_id=1, source_target_pairs={{0,3},{1,0},{2,1},{3,2},{4,7},{5,4},{6,5},{7,6},{8,11},{9,8},{10,9... | collective-permute-start | bytes 1769480 | tf_op jit(solution)/shard_map/ppermute | solution.py:274
  130.7 11.3 %collective-permute-done.13 = bf16[384,768]{1,0:T(8,128)(2,1)} collective-permute-done((bf16[384,768]{1,0:T(8,128)(2,1)}, bf16[384,768]{1,0:T(8,128)(2,1)}, u32[]{:S(2)}, u32[]{:S(2)}) %collective-permute-start.13) | collective-permute-done | bytes 589856 | tf_op jit(solution)/shard_map/ppermute | solution.py:274
  142.1 10.7 %collective-permute-done.14 = bf16[384,768]{1,0:T(8,128)(2,1)} collective-permute-done((bf16[384,768]{1,0:T(8,128)(2,1)}, bf16[384,768]{1,0:T(8,128)(2,1)}, u32[]{:S(2)}, u32[]{:S(2)}) %collective-permute-start.14) | collective-permute-done | bytes 589856 | tf_op jit(solution)/shard_map/ppermute | solution.py:274
  152.8 0.0 collective-permute-done.15
  152.8 0.0 copy-done.5
  152.8 2.6 %fusion.1 = bf16[1,1,384,768]{3,2,1,0:T(8,128)(2,1)} fusion(bf16[384,768]{1,0:T(8,128)(2,1)} %collective-permute-done.15, bf16[384,768]{1,0:T(8,128)(2,1)} %collective-permute-done.14, bf16[384,768]{1,0:T(8,128)(2,1)} %collective-permute-done.13, bf16[1,1,384,768]{3,2,1,0:T(8,128)(2,1)S(1)} %copy-done.5, bf16[384,3072]{1,0:T(8,128)(2,1)S(1)} %convolution_convert_fusion, ...), kind=kLoop, calls=%fused_computation.4 | loop fusion | flops 3244032 | bytes 3542020 | tf_op jit(solution)/shard_map/broadcast_in_dim | solution.py:279
  (12 shorter events, 0.1 us)
Async XLA Ops:
  0.0 5.8 %copy-start = (bf16[2,16,768]{2,1,0:T(8,128)(2,1)S(1)}, bf16[2,16,768]{2,1,0:T(8,128)(2,1)}, u32[]{:S(2)}) copy-start(bf16[2,16,768]{2,1,0:T(8,128)(2,1)} %param.10) | copy-start | bytes 147460
  0.0 68.4 %copy-start.8 = (s32[6,2]{0,1:T(2,128)S(1)}, s32[6,2]{0,1:T(2,128)}, u32[]{:S(2)}) copy-start(s32[6,2]{0,1:T(2,128)} %param.14) | copy-start | bytes 148
  0.0 29.6 %collective-permute-start.3 = (bf16[2,384,768]{2,1,0:T(8,128)(2,1)}, bf16[2,384,768]{2,1,0:T(8,128)(2,1)S(1)}, u32[]{:S(2)}, u32[]{:S(2)}) collective-permute-start(bf16[2,384,768]{2,1,0:T(8,128)(2,1)} %bitcast.19), channel_id=1, source_target_pairs={{0,4},{4,8},{8,12},{1,5},{5,9},{9,13},{2,6},{6,10},{10,14},{3,7},{... | collective-permute-start | bytes 3538952 | tf_op jit(solution)/shard_map/ppermute | solution.py:225
  3.8 25.8 %collective-permute-start.4 = (bf16[2,384,768]{2,1,0:T(8,128)(2,1)}, bf16[2,384,768]{2,1,0:T(8,128)(2,1)S(1)}, u32[]{:S(2)}, u32[]{:S(2)}) collective-permute-start(bf16[2,384,768]{2,1,0:T(8,128)(2,1)} %bitcast.20), channel_id=1, source_target_pairs={{4,0},{8,4},{12,8},{5,1},{9,5},{13,9},{6,2},{10,6},{14,10},{7,3},{... | collective-permute-start | bytes 3538952 | tf_op jit(solution)/shard_map/ppermute | solution.py:226
  5.8 14.8 %collective-permute-start = (bf16[2,16,384]{2,1,0:T(8,128)(2,1)S(1)}, bf16[2,16,384]{2,1,0:T(8,128)(2,1)S(1)}, u32[]{:S(2)}, u32[]{:S(2)}) collective-permute-start(bf16[2,16,384]{2,1,0:T(8,128)(2,1)S(1)} %constant_dynamic-slice_fusion.3), channel_id=1, source_target_pairs={{0,16},{16,0},{32,48},{48,32},{64,80},{80,64},{96,112},{112,96},{1... | collective-permute-start | bytes 73736 | tf_op jit(solution)/shard_map/ppermute | solution.py:50
  20.6 3.0 %collective-permute-start.1 = (bf16[2,32,384]{2,1,0:T(8,128)(2,1)S(1)}, bf16[2,32,384]{2,1,0:T(8,128)(2,1)S(1)}, u32[]{:S(2)}, u32[]{:S(2)}) collective-permute-start(bf16[2,32,384]{2,1,0:T(8,128)(2,1)S(1)} %maximum_select_fusion.4), channel_id=1, source_target_pairs={{0,32},{16,48},{32,0},{48,16},{64,96},{80,112},{96,64},{112,80},{1... | collective-permute-start | bytes 147464 | tf_op jit(solution)/shard_map/ppermute | solution.py:50
  23.6 5.9 %collective-permute-start.2 = (bf16[2,64,384]{2,1,0:T(8,128)(2,1)S(1)}, bf16[2,64,384]{2,1,0:T(8,128)(2,1)S(1)}, u32[]{:S(2)}, u32[]{:S(2)}) collective-permute-start(bf16[2,64,384]{2,1,0:T(8,128)(2,1)S(1)} %maximum_select_fusion.3), channel_id=1, source_target_pairs={{0,64},{16,80},{32,96},{48,112},{64,0},{80,16},{96,32},{112,48},{1... | collective-permute-start | bytes 294920 | tf_op jit(solution)/shard_map/ppermute | solution.py:50
  29.6 41.7 %copy-start.3 = (bf16[2,384,768]{2,1,0:T(8,128)(2,1)}, bf16[2,384,768]{2,1,0:T(8,128)(2,1)S(1)}, u32[]{:S(2)}) copy-start(bf16[2,384,768]{2,1,0:T(8,128)(2,1)S(1)} %collective-permute-done.3.rest_2_) | copy-start | bytes 3538948
  29.6 41.6 %copy-start.4 = (bf16[2,384,768]{2,1,0:T(8,128)(2,1)}, bf16[2,384,768]{2,1,0:T(8,128)(2,1)S(1)}, u32[]{:S(2)}) copy-start(bf16[2,384,768]{2,1,0:T(8,128)(2,1)S(1)} %collective-permute-done.4.rest_3_) | copy-start | bytes 3538948
  29.6 54.7 %collective-permute-start.5 = (bf16[2,384,768]{2,1,0:T(8,128)(2,1)}, bf16[2,384,768]{2,1,0:T(8,128)(2,1)}, u32[]{:S(2)}, u32[]{:S(2)}) collective-permute-start(bf16[2,384,768]{2,1,0:T(8,128)(2,1)} %bitcast.21), channel_id=1, source_target_pairs={{0,16},{16,32},{32,48},{48,64},{64,80},{80,96},{96,112},{112,128},... | collective-permute-start | bytes 3538952 | tf_op jit(solution)/shard_map/ppermute | solution.py:244
  33.4 50.9 %collective-permute-start.6 = (bf16[2,384,768]{2,1,0:T(8,128)(2,1)}, bf16[2,384,768]{2,1,0:T(8,128)(2,1)}, u32[]{:S(2)}, u32[]{:S(2)}) collective-permute-start(bf16[2,384,768]{2,1,0:T(8,128)(2,1)} %bitcast.22), channel_id=1, source_target_pairs={{16,0},{32,16},{48,32},{64,48},{80,64},{96,80},{112,96},{128,112},... | collective-permute-start | bytes 3538952 | tf_op jit(solution)/shard_map/ppermute | solution.py:245
  37.3 30.9 %collective-permute-start.7 = (bf16[2,128,384]{2,1,0:T(8,128)(2,1)S(1)}, bf16[2,128,384]{2,1,0:T(8,128)(2,1)S(1)}, u32[]{:S(2)}, u32[]{:S(2)}) collective-permute-start(bf16[2,128,384]{2,1,0:T(8,128)(2,1)S(1)} %maximum_select_fusion.2), channel_id=1, source_target_pairs={{0,128},{16,144},{32,160},{48,176},{64,192},{80,208},{96,224},{112... | collective-permute-start | bytes 589832 | tf_op jit(solution)/shard_map/ppermute | solution.py:50
  68.3 1.8 %collective-permute-start.8 = (bf16[2,256,384]{2,1,0:T(8,128)(2,1)S(1)}, bf16[2,256,384]{2,1,0:T(8,128)(2,1)S(1)}, u32[]{:S(2)}, u32[]{:S(2)}) collective-permute-start(bf16[2,256,384]{2,1,0:T(8,128)(2,1)S(1)} %maximum_select_fusion.1), channel_id=1, source_target_pairs={{0,4},{4,0},{8,12},{12,8},{1,5},{5,1},{9,13},{13,9},{2,6},{6,2},{1... | collective-permute-start | bytes 1179656 | tf_op jit(solution)/shard_map/ppermute | solution.py:59
  71.3 21.4 %copy-start.6 = (s32[6,2]{1,0:T(8,128)S(1)}, s32[6,2]{1,0:T(8,128)}, u32[]{:S(2)}) copy-start(s32[6,2]{1,0:T(8,128)} %copy.33.reach_ref) | copy-start | bytes 148
  84.3 17.8 %collective-permute-start.10 = (bf16[2,384,768]{2,1,0:T(8,128)(2,1)}, bf16[2,384,768]{2,1,0:T(8,128)(2,1)}, u32[]{:S(2)}, u32[]{:S(2)}) collective-permute-start(bf16[2,384,768]{2,1,0:T(8,128)(2,1)} %collective-permute-done.5.rest_0_), channel_id=1, source_target_pairs={{4,0},{8,4},{12,8},{5,1},{9,5},{13,9},{6,2},{10,6},{14,10},{7,3},{... | collective-permute-start | bytes 3538952 | tf_op jit(solution)/shard_map/ppermute | solution.py:256
  86.4 15.8 %collective-permute-start.11 = (bf16[2,384,768]{2,1,0:T(8,128)(2,1)}, bf16[2,384,768]{2,1,0:T(8,128)(2,1)S(1)}, u32[]{:S(2)}, u32[]{:S(2)}) collective-permute-start(bf16[2,384,768]{2,1,0:T(8,128)(2,1)} %collective-permute-done.6.rest_1_), channel_id=1, source_target_pairs={{0,4},{4,0},{8,12},{12,8},{1,5},{5,1},{9,13},{13,9},{2,6},{6,2},{1... | collective-permute-start | bytes 3538952 | tf_op jit(solution)/shard_map/ppermute | solution.py:257
  86.5 18.9 %collective-permute-start.12 = (bf16[2,384,768]{2,1,0:T(8,128)(2,1)}, bf16[2,384,768]{2,1,0:T(8,128)(2,1)S(1)}, u32[]{:S(2)}, u32[]{:S(2)}) collective-permute-start(bf16[2,384,768]{2,1,0:T(8,128)(2,1)} %bitcast.24), channel_id=1, source_target_pairs={{20,8},{24,4},{36,24},{40,20},{52,40},{56,36},{68,56},{72,52},{84,... | collective-permute-start | bytes 3538952 | tf_op jit(solution)/shard_map/ppermute | solution.py:258
  88.4 17.6 %collective-permute-start.9 = (bf16[2,384,768]{2,1,0:T(8,128)(2,1)}, bf16[2,384,768]{2,1,0:T(8,128)(2,1)}, u32[]{:S(2)}, u32[]{:S(2)}) collective-permute-start(bf16[2,384,768]{2,1,0:T(8,128)(2,1)} %collective-permute-done.5.rest_0_), channel_id=1, source_target_pairs={{0,4},{4,8},{8,12},{1,5},{5,9},{9,13},{2,6},{6,10},{10,14},{3,7},{... | collective-permute-start | bytes 3538952 | tf_op jit(solution)/shard_map/ppermute | solution.py:255
  102.1 3.8 %copy-start.1 = (bf16[2,384,768]{2,1,0:T(8,128)(2,1)}, bf16[2,384,768]{2,1,0:T(8,128)(2,1)S(1)}, u32[]{:S(2)}) copy-start(bf16[2,384,768]{2,1,0:T(8,128)(2,1)S(1)} %collective-permute-done.11.rest_2_.rest_5_) | copy-start | bytes 3538948
  105.4 1.1 copy-start.2
  120.4 32.4 %copy-start.5 = (bf16[1,1,384,768]{3,2,1,0:T(8,128)(2,1)S(1)}, bf16[1,1,384,768]{3,2,1,0:T(8,128)(2,1)}, u32[]{:S(2)}) copy-start(bf16[1,1,384,768]{3,2,1,0:T(8,128)(2,1)} %param.11) | copy-start | bytes 1769476
  120.4 32.4 %copy-start.7 = (f32[768]{0:T(1024)S(1)}, f32[768]{0:T(1024)}, u32[]{:S(2)}) copy-start(f32[768]{0:T(1024)} %param.13) | copy-start | bytes 9220
  121.7 20.4 %collective-permute-start.13 = (bf16[384,768]{1,0:T(8,128)(2,1)}, bf16[384,768]{1,0:T(8,128)(2,1)}, u32[]{:S(2)}, u32[]{:S(2)}) collective-permute-start(bf16[384,768]{1,0:T(8,128)(2,1)} %get-tuple-element.41), channel_id=1, source_target_pairs={{0,2},{1,3},{2,0},{3,1},{4,6},{5,7},{6,4},{7,5},{8,10},{9,11},{10,... | collective-permute-start | bytes 1769480 | tf_op jit(solution)/shard_map/ppermute | solution.py:274
  128.1 24.7 %collective-permute-start.14 = (bf16[384,768]{1,0:T(8,128)(2,1)}, bf16[384,768]{1,0:T(8,128)(2,1)}, u32[]{:S(2)}, u32[]{:S(2)}) collective-permute-start(bf16[384,768]{1,0:T(8,128)(2,1)} %get-tuple-element.43), channel_id=1, source_target_pairs={{0,1},{1,2},{2,3},{3,0},{4,5},{5,6},{6,7},{7,4},{8,9},{9,10},{10,1... | collective-permute-start | bytes 1769480 | tf_op jit(solution)/shard_map/ppermute | solution.py:274
  128.1 24.7 %collective-permute-start.15 = (bf16[384,768]{1,0:T(8,128)(2,1)}, bf16[384,768]{1,0:T(8,128)(2,1)}, u32[]{:S(2)}, u32[]{:S(2)}) collective-permute-start(bf16[384,768]{1,0:T(8,128)(2,1)} %get-tuple-element.42), channel_id=1, source_target_pairs={{0,3},{1,0},{2,1},{3,2},{4,7},{5,4},{6,5},{7,6},{8,11},{9,8},{10,9... | collective-permute-start | bytes 1769480 | tf_op jit(solution)/shard_map/ppermute | solution.py:274
